TPU v7x, 32 devices: a whole 2x2x4 slice. The times are simulated.
32 devices in a mesh: seq: 16 (over z, x, core), head: 2 (over y).
Axes of the slice: x: 2, y: 2, z: 4, core: 2. Of those that a mesh axis runs over, the one named last changes fastest.
Arguments:
- queries: bfloat16 [4096, 4096], P('seq', 'head'), may hold values from -6 to 6
- keys: bfloat16 [4096, 4096], P('seq', 'head'), may hold values from -6 to 6
- values: bfloat16 [4096, 4096], P('seq', 'head'), may hold values from -6 to 6
- out_weight: bfloat16 [4096, 4096], P('head'), may hold values from -0.09375 to 0.09375
- cotangent: bfloat16 [4096, 4096], P(('seq', 'head')), may hold values from -6 to 6
- offsets: int32 [16, 32], P('head'), may hold values from 0 to 127, as said below
Outputs:
- attention: bfloat16 [4096, 4096], P('seq', 'head')
- query_grad: bfloat16 [4096, 4096], P('seq', 'head')
- key_grad: bfloat16 [4096, 4096], P('seq', 'head')
- value_grad: bfloat16 [4096, 4096], P('seq', 'head')
Inputs may be any that keep to these rules, and one draw needn't show every extreme that they name: Each row holds 32 distinct offsets in rising order, the last one 128 - 1.
All inputs are finite; a program needn't handle non-finite values.
Results may differ from a plain program's by a relative error of at most 0.011.
Values may be sent and summed in bfloat16 or wider, within the bound.
No kernel may reach another device: no remote copies, remote signals or barrier semaphores. Data moves between devices by JAX's collectives and lax.ppermute only.
A program may use at most 128 MiB of HBM per device.

v0:
```python
import functools

import jax
import jax.numpy as jnp
from jax import lax
from jax.experimental import pallas as pl
from jax.experimental.pallas import tpu as pltpu
from jax.sharding import PartitionSpec as P

WIN = 256
BLOCK = 128
SUMM = 32


NEG = -1e30


def passed_along(value, axis, steps):
    count = lax.axis_size(axis)
    first, last = (max(0, -steps), min(count, count - steps))
    return lax.ppermute(value, axis, [(source, source + steps) for source in range(first, last)])


def seq_reduce_scatter(parts, axis):
    count = lax.axis_size("seq")
    if count & (count - 1):
        return lax.psum_scatter(
            parts.astype(jnp.bfloat16), "seq", scatter_dimension=axis, tiled=True
        )
    me = lax.axis_index("seq")
    bits = count.bit_length() - 1
    chunk = parts.shape[axis] // count
    held = parts.reshape(parts.shape[:axis] + (2,) * bits + (chunk,) + parts.shape[axis + 1 :])
    for bit in range(bits):
        where = axis + bits - 1 - bit
        mine = (me >> bit) & 1
        keep = lax.dynamic_index_in_dim(held, mine, where, keepdims=False)
        send = lax.dynamic_index_in_dim(held, 1 - mine, where, keepdims=False)
        arrived = lax.ppermute(
            send.astype(jnp.bfloat16), "seq", [(source, source ^ (1 << bit)) for source in range(count)]
        )
        held = keep + arrived.astype(jnp.float32)
    return held.astype(jnp.bfloat16)


def nt(left, right):
    return lax.dot_general(left, right, (((1,), (1,)), ((), ())), preferred_element_type=jnp.float32)


def tn(left, right):
    return lax.dot_general(left, right, (((0,), (0,)), ((), ())), preferred_element_type=jnp.float32)


def nn(left, right):
    return lax.dot_general(left, right, (((1,), (0,)), ((), ())), preferred_element_type=jnp.float32)


def two_part_attention(q, g, first, second, scale):
    (k_a, v_a, mask_a), (k_b, v_b, mask_b) = first, second
    s_a = jnp.where(mask_a, nt(q, k_a) * scale, NEG)
    s_b = jnp.where(mask_b, nt(q, k_b) * scale, NEG)
    row_max = jnp.maximum(s_a.max(-1, keepdims=True), s_b.max(-1, keepdims=True))
    w_a = jnp.exp(s_a - row_max)
    w_b = jnp.exp(s_b - row_max)
    row_sum = w_a.sum(-1, keepdims=True) + w_b.sum(-1, keepdims=True)
    mixed = nn(w_a.astype(jnp.bfloat16), v_a) + nn(w_b.astype(jnp.bfloat16), v_b)
    out = (mixed / row_sum).astype(jnp.bfloat16)
    log_total = row_max + jnp.log(row_sum)
    delta = jnp.sum(g.astype(jnp.float32) * out.astype(jnp.float32), -1, keepdims=True)
    p_a = jnp.exp(s_a - log_total)
    p_b = jnp.exp(s_b - log_total)
    gs_a = (p_a * (nt(g, v_a) - delta)).astype(jnp.bfloat16)
    gs_b = (p_b * (nt(g, v_b) - delta)).astype(jnp.bfloat16)
    dq = ((nn(gs_a, k_a) + nn(gs_b, k_b)) * scale).astype(jnp.bfloat16)
    dk_a = tn(gs_a, q) * scale
    dk_b = tn(gs_b, q) * scale
    dv_a = tn(p_a.astype(jnp.bfloat16), g)
    dv_b = tn(p_b.astype(jnp.bfloat16), g)
    return out, dq, (dk_a, dv_a), (dk_b, dv_b)


def pair_kernel(
    seq_ref,
    q_ref,
    k_ref,
    v_ref,
    g_ref,
    kp_ref,
    vp_ref,
    kf_ref,
    vf_ref,
    out_ref,
    dq_ref,
    dk_ref,
    dv_ref,
    dkp_ref,
    dvp_ref,
    dkvf_ref,
    *,
    head_dim,
    scale,
):
    rows = q_ref.shape[0]
    far_rows = kf_ref.shape[0]
    start = seq_ref[0] * rows
    hd = head_dim
    qi = lax.broadcasted_iota(jnp.int32, (rows, rows), 0)
    kj = lax.broadcasted_iota(jnp.int32, (rows, rows), 1)
    causal = kj <= qi
    prev_mask = (kj > qi) & (seq_ref[0] > 0)
    own_band = causal & (qi - kj < WIN)
    out_b, dq_b, (dkp, dvp), (dko, dvo) = two_part_attention(
        q_ref[:, :hd],
        g_ref[:, :hd],
        (kp_ref[:, :hd], vp_ref[:, :hd], prev_mask),
        (k_ref[:, :hd], v_ref[:, :hd], own_band),
        scale,
    )
    out_ref[:, :hd] = out_b
    dq_ref[:, :hd] = dq_b
    dk_ref[:, :hd] = dko
    dv_ref[:, :hd] = dvo
    dkp_ref[...] = dkp.astype(dkp_ref.dtype)
    dvp_ref[...] = dvp.astype(dvp_ref.dtype)
    own_fixed = causal & ((qi // BLOCK) == (kj // BLOCK))
    fq = lax.broadcasted_iota(jnp.int32, (rows, far_rows), 0)
    fr = lax.broadcasted_iota(jnp.int32, (rows, far_rows), 1)
    far_mask = (fr // SUMM) < ((start + fq) // BLOCK)
    out_f, dq_f, (dkf_own, dvf_own), (dkf, dvf) = two_part_attention(
        q_ref[:, hd:],
        g_ref[:, hd:],
        (k_ref[:, hd:], v_ref[:, hd:], own_fixed),
        (kf_ref[...], vf_ref[...], far_mask),
        scale,
    )
    out_ref[:, hd:] = out_f
    dq_ref[:, hd:] = dq_f
    dk_ref[:, hd:] = dkf_own
    dv_ref[:, hd:] = dvf_own
    dkvf_ref[0] = dkf
    dkvf_ref[1] = dvf


def pair_attention(seq_index, q, k, v, g, k_prev, v_prev, far_kv, head_pairs, head_dim, scale):
    rows = q.shape[0]
    far_rows = far_kv.shape[0]
    pair = 2 * head_dim

    def col(width):
        return pl.BlockSpec((rows, width), lambda p, s: (0, p))

    far_k_spec = pl.BlockSpec((far_rows, head_dim), lambda p, s: (0, p))
    far_v_spec = pl.BlockSpec((far_rows, head_dim), lambda p, s: (0, head_pairs + p))
    flops = 2 * rows * head_dim * (2 * rows + rows + far_rows) * 7 * head_pairs
    cost = pl.CostEstimate(
        flops=flops,
        transcendentals=2 * rows * (3 * rows + far_rows) * head_pairs,
        bytes_accessed=rows * pair * 2 * 16 * head_pairs + far_rows * head_dim * 12 * head_pairs,
    )
    grid_spec = pltpu.PrefetchScalarGridSpec(
        num_scalar_prefetch=1,
        grid=(head_pairs,),
        in_specs=[col(pair)] * 6 + [far_k_spec, far_v_spec],
        out_specs=[
            col(pair),
            col(pair),
            col(pair),
            col(pair),
            col(head_dim),
            col(head_dim),
            pl.BlockSpec((2, far_rows, head_dim), lambda p, s: (0, 0, p)),
        ],
    )
    width = head_pairs * pair
    return pl.pallas_call(
        functools.partial(pair_kernel, head_dim=head_dim, scale=scale),
        grid_spec=grid_spec,
        out_shape=[
            jax.ShapeDtypeStruct((rows, width), jnp.bfloat16),
            jax.ShapeDtypeStruct((rows, width), jnp.bfloat16),
            jax.ShapeDtypeStruct((rows, width), jnp.float32),
            jax.ShapeDtypeStruct((rows, width), jnp.float32),
            jax.ShapeDtypeStruct((rows, head_pairs * head_dim), jnp.bfloat16),
            jax.ShapeDtypeStruct((rows, head_pairs * head_dim), jnp.bfloat16),
            jax.ShapeDtypeStruct((2, far_rows, head_pairs * head_dim), jnp.float32),
        ],
        compiler_params=pltpu.CompilerParams(vmem_limit_bytes=48 * 1024 * 1024),
        cost_estimate=cost,
    )(seq_index, q, k, v, g, k_prev, v_prev, far_kv, far_kv)


def on_device(queries, keys, values, out_weight, cotangent, offsets):
    seq_rows = queries.shape[0]
    full_width = queries.shape[1]
    head_pairs = offsets.shape[0]
    head_dim = full_width // (2 * head_pairs)
    score_scale = head_dim ** (-0.5)
    assert seq_rows == WIN and seq_rows % BLOCK == 0
    seq_index = lax.axis_index("seq")
    split_k = keys.reshape(seq_rows, head_pairs, 2, head_dim)
    split_v = values.reshape(seq_rows, head_pairs, 2, head_dim)
    fixed_k = split_k[:, :, 1]
    fixed_v = split_v[:, :, 1]
    prev_k, prev_v = passed_along((keys, values), "seq", 1)
    digest_count = seq_rows // BLOCK * SUMM
    offset_table = jnp.tile(offsets.T, (seq_rows // BLOCK, 1))
    digest_rows = (jnp.arange(digest_count, dtype=jnp.int32) // SUMM * BLOCK)[
        :, None
    ] + offset_table
    select = (
        digest_rows.T[:, :, None] == jnp.arange(seq_rows, dtype=jnp.int32)[None, None, :]
    ).astype(jnp.bfloat16)
    digest_k = jnp.einsum(
        "hjr,rhc->jhc", select, fixed_k, preferred_element_type=jnp.float32
    ).astype(jnp.bfloat16)
    digest_v = jnp.einsum(
        "hjr,rhc->jhc", select, fixed_v, preferred_element_type=jnp.float32
    ).astype(jnp.bfloat16)
    pair_width = head_pairs * head_dim
    far_kv = lax.all_gather(
        jnp.concatenate(
            [
                digest_k.reshape(digest_count, pair_width),
                digest_v.reshape(digest_count, pair_width),
            ],
            1,
        ),
        "seq",
        axis=0,
        tiled=True,
    )
    head_count = lax.axis_size("head")
    head_index = lax.axis_index("head")
    pieces = [cotangent] + [
        lax.ppermute(
            cotangent, "head", [(source, (source + shift) % head_count) for source in range(head_count)]
        )
        for shift in range(1, head_count)
    ]
    doubled = jnp.stack(pieces[::-1] + pieces[::-1], 0)
    gathered = lax.dynamic_slice_in_dim(doubled, head_count - 1 - head_index, head_count, 0)
    grad_out = lax.dot_general(
        gathered.reshape(seq_rows, cotangent.shape[1]),
        out_weight,
        (((1,), (1,)), ((), ())),
        preferred_element_type=jnp.float32,
    ).astype(jnp.bfloat16)
    attention, query_grad, own_dk, own_dv, back_k, back_v, far_dkv = pair_attention(
        seq_index.reshape(1).astype(jnp.int32),
        queries,
        keys,
        values,
        grad_out,
        prev_k,
        prev_v,
        far_kv,
        head_pairs,
        head_dim,
        score_scale,
    )
    back_k, back_v = passed_along((back_k, back_v), "seq", -1)
    digest_dkv = seq_reduce_scatter(far_dkv, 1)
    digest_dk = digest_dkv[0].reshape(digest_count, head_pairs, head_dim)
    digest_dv = digest_dkv[1].reshape(digest_count, head_pairs, head_dim)
    fixed_dk = jnp.einsum("hjr,jhc->rhc", select, digest_dk, preferred_element_type=jnp.float32)
    fixed_dv = jnp.einsum("hjr,jhc->rhc", select, digest_dv, preferred_element_type=jnp.float32)

    def with_extra(own, band_extra, fixed_extra):
        extra = jnp.stack(
            [band_extra.reshape(seq_rows, head_pairs, head_dim).astype(jnp.float32), fixed_extra], 2
        ).reshape(seq_rows, full_width)
        return (own + extra).astype(jnp.bfloat16)

    return (
        attention,
        query_grad,
        with_extra(own_dk, back_k, fixed_dk),
        with_extra(own_dv, back_v, fixed_dv),
    )


def solution(mesh):
    in_specs = (
        P("seq", "head"),
        P("seq", "head"),
        P("seq", "head"),
        P("head", None),
        P(("seq", "head"), None),
        P("head", None),
    )
    out_specs = (P("seq", "head"), P("seq", "head"), P("seq", "head"), P("seq", "head"))
    return jax.shard_map(
        on_device, mesh=mesh, in_specs=in_specs, out_specs=out_specs, check_vma=False
    )
```

profile of v0, /device:TPU:3, one launch (start us, length us, event | category | flops | bytes accessed | tf_op | source)
XLA Modules:
  0.0 198.9 jit_solution(4414042936299157009)
XLA Ops:
  8.1 2.3 %copy.16 = bf16[256,2048]{0,1:T(8,128)(2,1)} copy(bf16[256,2048]{1,0:T(8,128)(2,1)} %k_ref.1) | data formatting | bytes 2097152 | tf_op args[1]
  10.3 1.3 copy.19
  11.7 1.4 fusion.4
  13.0 1.4 fusion.5
  15.2 1.3 collective-permute-start
  16.5 4.0 %collective-permute-start.1 = (bf16[256,2048]{1,0:T(8,128)(2,1)S(1)}, bf16[256,2048]{1,0:T(8,128)(2,1)}, u32[]{:S(2)}, u32[]{:S(2)}) collective-permute-start(bf16[256,2048]{1,0:T(8,128)(2,1)S(1)} %copy-done), channel_id=1, source_target_pairs={{0,2},{2,4},{4,6},{6,8},{8,10},{10,12},{12,14},{14,16},{16,18},{18... | collective-permute-start | bytes 3145736 | tf_op jit(solution)/shard_map/ppermute | solution.py:21
  20.6 1.9 collective-permute-start.2
  22.5 16.9 %collective-permute-done = bf16[128,4096]{1,0:T(8,128)(2,1)} collective-permute-done((bf16[128,4096]{1,0:T(8,128)(2,1)S(1)}, bf16[128,4096]{1,0:T(8,128)(2,1)}, u32[]{:S(2)}, u32[]{:S(2)}) %collective-permute-start) | collective-permute-done | bytes 1048608 | tf_op jit(solution)/shard_map/ppermute | solution.py:235
  39.4 4.0 %fusion.3 = bf16[2,128,4096]{2,1,0:T(8,128)(2,1)} fusion(s32[]{:T(128)S(6)} %select_n.40, bf16[1,128,4096]{2,1,0:T(8,128)(2,1)} %bitcast.1, bf16[1,128,4096]{2,1,0:T(8,128)(2,1)S(1)} %bitcast.73), kind=kLoop, calls=%fused_computation.10 | loop fusion | flops 3145728 | bytes 4194308 | tf_op jit(solution)/shard_map/stack | solution.py:240
  43.5 12.5 %convolution_convert_fusion.g_ref = bf16[256,2048]{1,0:T(8,128)(2,1)} fusion(bf16[256,4096]{1,0:T(8,128)(2,1)} %bitcast.72, bf16[2048,4096]{1,0:T(8,128)(2,1)} %param.9), kind=kOutput, calls=%fused_computation.6 | convolution fusion | flops 4295491584 | bytes 19922944 | tf_op jit(solution)/shard_map/dot_general | solution.py:242
  56.0 9.4 %collective-permute-done.2.vp_ref = bf16[256,2048]{1,0:T(8,128)(2,1)} collective-permute-done((bf16[256,2048]{1,0:T(8,128)(2,1)S(1)}, bf16[256,2048]{1,0:T(8,128)(2,1)}, u32[]{:S(2)}, u32[]{:S(2)}) %collective-permute-start.2) | collective-permute-done | bytes 1048608 | tf_op jit(solution)/shard_map/ppermute | solution.py:21
  65.4 4.0 %all-gather.2.cloned.1.call-done.kf_ref.vf_ref = bf16[1024,2048]{1,0:T(8,128)(2,1)} async-done(((bf16[64,2048]{1,0:T(8,128)(2,1)}), bf16[1024,2048]{1,0:T(8,128)(2,1)}) %all-gather.2.cloned.1.call-update) | async-done | bytes 4194320 | tf_op jit(solution)/shard_map/all_gather | solution.py:220
  70.6 22.8 %shard_map.93 = (bf16[256,2048]{1,0:T(8,128)(2,1)}, bf16[256,2048]{1,0:T(8,128)(2,1)}, f32[256,2048]{1,0:T(8,128)}, f32[256,2048]{1,0:T(8,128)}, bf16[256,1024]{...) custom-call(s32[1]{0:T(128)} %bitcast.seq_ref, bf16[256,2048]{1,0:T(8,128)(2,1)S(1)} %copy-done.2, ...), custom_call_target="tpu_custom_call" | custom-call | flops 6576668672 | bytes 29360128 | tf_op jit(solution)/shard_map/pallas_call | solution.py:175
  93.5 2.9 %fusion = bf16[2,2,2,2,64,1024]{5,4,0,1,2,3:T(8,128)(2,1)S(1)} fusion(f32[2,2,2,2,2,64,1024]{6,5,4,3,2,1,0:T(8,128)} %bitcast.68, s32[]{:T(128)S(6)} %select_n.43), kind=kLoop, calls=%fused_computation.7 | loop fusion | bytes 4194308 | tf_op jit(solution)/shard_map/convert_element_type | solution.py:40
  96.7 4.0 %collective-permute-done.4 = bf16[2,2,2,2,64,1024]{5,4,0,1,2,3:T(8,128)(2,1)} collective-permute-done((bf16[2,2,2,2,64,1024]{5,4,0,1,2,3:T(8,128)(2,1)S(1)}, bf16[2,2,2,2,64,1024]{5,4,0,1,2,3:T(8,128)(2,1)}, u32[]{:S(2)}, u32[]{:S(2)}) %collective-permute-start.4) | collective-permute-done | bytes 2097184 | tf_op jit(solution)/shard_map/ppermute | solution.py:39
  100.8 3.5 %bitcast_add_fusion = f32[2,2,2,2,64,1024]{5,4,0,1,2,3:T(8,128)S(1)} fusion(bf16[2,2,2,2,64,1024]{5,4,0,1,2,3:T(8,128)(2,1)} %collective-permute-done.4, f32[2,2,2,2,2,64,1024]{6,5,4,3,2,1,0:T(8,128)} %bitcast.69, s32[]{:T(128)S(6)} %select_n.42), kind=kLoop, calls=%fused_computation.5 | loop fusion | flops 2097152 | bytes 10485764 | tf_op jit(solution)/shard_map/add | solution.py:42
  104.3 1.9 copy-done.8
  106.4 4.9 %collective-permute-start.5 = (bf16[2,2,2,64,1024]{4,3,0,1,2:T(8,128)(2,1)S(1)}, bf16[2,2,2,64,1024]{4,3,0,1,2:T(8,128)(2,1)}, u32[]{:S(2)}, u32[]{:S(2)}) collective-permute-start(bf16[2,2,2,64,1024]{4,3,0,1,2:T(8,128)(2,1)S(1)} %fusion.6), channel_id=1, source_target_pairs={{0,4},{2,6},{4,0},{6,2},{8,12},{10,14},{12,8},{14,10},{16,20},{18,... | collective-permute-start | bytes 3145736 | tf_op jit(solution)/shard_map/ppermute | solution.py:39
  111.3 23.5 %collective-permute-done.5 = bf16[2,2,2,64,1024]{4,3,0,1,2:T(8,128)(2,1)} collective-permute-done((bf16[2,2,2,64,1024]{4,3,0,1,2:T(8,128)(2,1)S(1)}, bf16[2,2,2,64,1024]{4,3,0,1,2:T(8,128)(2,1)}, u32[]{:S(2)}, u32[]{:S(2)}) %collective-permute-start.5) | collective-permute-done | bytes 1048608 | tf_op jit(solution)/shard_map/ppermute | solution.py:39
  134.7 2.2 %bitcast_add_fusion.1 = f32[2,2,2,64,1024]{4,3,0,1,2:T(8,128)S(1)} fusion(bf16[2,2,2,64,1024]{4,3,0,1,2:T(8,128)(2,1)} %collective-permute-done.5, f32[2,2,2,2,64,1024]{5,4,0,1,2,3:T(8,128)} %copy-done.8, s32[]{:T(128)S(6)} %select_n.44), kind=kLoop, calls=%fused_computation.13 | loop fusion | flops 1048576 | bytes 5242884 | tf_op jit(solution)/shard_map/add | solution.py:42
  137.8 3.0 %collective-permute-start.8 = (bf16[256,1024]{1,0:T(8,128)(2,1)S(1)}, bf16[256,1024]{1,0:T(8,128)(2,1)}, u32[]{:S(2)}, u32[]{:S(2)}) collective-permute-start(bf16[256,1024]{1,0:T(8,128)(2,1)S(1)} %copy-done.6), channel_id=1, source_target_pairs={{2,0},{4,2},{6,4},{8,6},{10,8},{12,10},{14,12},{16,14},{18,16},{20... | collective-permute-start | bytes 1572872 | tf_op jit(solution)/shard_map/ppermute | solution.py:21
  140.9 2.5 %collective-permute-start.3 = (bf16[256,1024]{1,0:T(8,128)(2,1)S(1)}, bf16[256,1024]{1,0:T(8,128)(2,1)}, u32[]{:S(2)}, u32[]{:S(2)}) collective-permute-start(bf16[256,1024]{1,0:T(8,128)(2,1)S(1)} %copy-done.4), channel_id=1, source_target_pairs={{2,0},{4,2},{6,4},{8,6},{10,8},{12,10},{14,12},{16,14},{18,16},{20... | collective-permute-start | bytes 1572872 | tf_op jit(solution)/shard_map/ppermute | solution.py:21
  143.4 7.5 %collective-permute-done.6 = bf16[2,2,64,1024]{3,2,0,1:T(8,128)(2,1)} collective-permute-done((bf16[2,2,64,1024]{3,2,0,1:T(8,128)(2,1)}, bf16[2,2,64,1024]{3,2,0,1:T(8,128)(2,1)}, u32[]{:S(2)}, u32[]{:S(2)}) %collective-permute-start.6) | collective-permute-done | bytes 524320 | tf_op jit(solution)/shard_map/ppermute | solution.py:39
  153.2 6.4 %collective-permute-done.8 = bf16[256,1024]{1,0:T(8,128)(2,1)} collective-permute-done((bf16[256,1024]{1,0:T(8,128)(2,1)S(1)}, bf16[256,1024]{1,0:T(8,128)(2,1)}, u32[]{:S(2)}, u32[]{:S(2)}) %collective-permute-start.8) | collective-permute-done | bytes 524320 | tf_op jit(solution)/shard_map/ppermute | solution.py:21
  159.5 2.2 %copy.31 = f32[256,1024]{0,1:T(8,128)} copy(bf16[256,1024]{1,0:T(8,128)(2,1)} %collective-permute-done.8) | data formatting | bytes 1572864 | tf_op jit(solution)/shard_map/convert_element_type | solution.py:270
  161.8 7.7 %collective-permute-done.3 = bf16[256,1024]{1,0:T(8,128)(2,1)} collective-permute-done((bf16[256,1024]{1,0:T(8,128)(2,1)S(1)}, bf16[256,1024]{1,0:T(8,128)(2,1)}, u32[]{:S(2)}, u32[]{:S(2)}) %collective-permute-start.3) | collective-permute-done | bytes 524320 | tf_op jit(solution)/shard_map/ppermute | solution.py:21
  172.5 2.4 %copy.29 = f32[256,8,2,128]{3,2,1,0:T(2,128)} copy(f32[256,8,2,128]{0,3,1,2:T(8,128)S(1)} %pad_maximum_fusion.1) | data formatting | bytes 4194304 | tf_op jit(solution)/shard_map/stack | solution.py:269
  174.9 2.9 %reshape.92 = f32[256,2048]{1,0:T(8,128)S(1)} reshape(f32[256,8,2,128]{3,2,1,0:T(2,128)} %copy.29) | data formatting | bytes 4194304 | tf_op jit(solution)/shard_map/reshape | solution.py:271
  178.3 1.5 pad_maximum_fusion
  179.8 4.2 %copy.26 = f32[256,8,2,128]{3,2,1,0:T(2,128)} copy(f32[256,8,2,128]{0,3,1,2:T(8,128)} %pad_maximum_fusion) | data formatting | bytes 4194304 | tf_op jit(solution)/shard_map/stack | solution.py:269
  184.0 3.9 %reshape.91 = f32[256,2048]{1,0:T(8,128)} reshape(f32[256,8,2,128]{3,2,1,0:T(2,128)} %copy.26) | data formatting | bytes 4194304 | tf_op jit(solution)/shard_map/reshape | solution.py:271
  187.8 2.9 %add_convert_fusion = bf16[256,2048]{1,0:T(8,128)(2,1)} fusion(f32[256,2048]{1,0:T(8,128)} %get-tuple-element.16, f32[256,2048]{1,0:T(8,128)S(1)} %reshape.92), kind=kLoop, calls=%fused_computation.14 | loop fusion | flops 1048576 | bytes 5242880 | tf_op jit(solution)/shard_map/convert_element_type | solution.py:272
  (55 shorter events, 11.2 us)
Async XLA Ops:
  7.2 3.2 %copy-start.1 = (bf16[256,2048]{1,0:T(8,128)(2,1)S(1)}, bf16[256,2048]{1,0:T(8,128)(2,1)}, u32[]{:S(2)}) copy-start(bf16[256,2048]{1,0:T(8,128)(2,1)} %v_ref.1) | copy-start | bytes 3145732
  7.2 62.2 %all-gather.2.cloned.1.call-start = ((), (), s32[]{:S(2)}) async-start(), calls=%async_computation | async-start | bytes 4456448 | tf_op jit(solution)/shard_map/all_gather | solution.py:220
  10.3 4.9 %copy-start.14 = (bf16[128,4096]{1,0:T(8,128)(2,1)S(1)}, bf16[128,4096]{1,0:T(8,128)(2,1)}, u32[]{:S(2)}) copy-start(bf16[128,4096]{1,0:T(8,128)(2,1)} %param.10) | copy-start | bytes 3145732
  10.3 6.2 %copy-start = (bf16[256,2048]{1,0:T(8,128)(2,1)S(1)}, bf16[256,2048]{1,0:T(8,128)(2,1)}, u32[]{:S(2)}) copy-start(bf16[256,2048]{1,0:T(8,128)(2,1)} %k_ref.1) | copy-start | bytes 3145732
  15.2 24.2 %collective-permute-start = (bf16[128,4096]{1,0:T(8,128)(2,1)S(1)}, bf16[128,4096]{1,0:T(8,128)(2,1)}, u32[]{:S(2)}, u32[]{:S(2)}) collective-permute-start(bf16[128,4096]{1,0:T(8,128)(2,1)S(1)} %copy-done.14), channel_id=1, source_target_pairs={{0,1},{1,0},{2,3},{3,2},{4,5},{5,4},{6,7},{7,6},{8,9},{9,8},{10,11... | collective-permute-start | bytes 3145736 | tf_op jit(solution)/shard_map/ppermute | solution.py:235
  16.5 39.4 %collective-permute-start.1 = (bf16[256,2048]{1,0:T(8,128)(2,1)S(1)}, bf16[256,2048]{1,0:T(8,128)(2,1)}, u32[]{:S(2)}, u32[]{:S(2)}) collective-permute-start(bf16[256,2048]{1,0:T(8,128)(2,1)S(1)} %copy-done), channel_id=1, source_target_pairs={{0,2},{2,4},{4,6},{6,8},{8,10},{10,12},{12,14},{14,16},{16,18},{18... | collective-permute-start | bytes 3145736 | tf_op jit(solution)/shard_map/ppermute | solution.py:21
  20.6 44.9 %collective-permute-start.2 = (bf16[256,2048]{1,0:T(8,128)(2,1)S(1)}, bf16[256,2048]{1,0:T(8,128)(2,1)}, u32[]{:S(2)}, u32[]{:S(2)}) collective-permute-start(bf16[256,2048]{1,0:T(8,128)(2,1)S(1)} %copy-done.1), channel_id=1, source_target_pairs={{0,2},{2,4},{4,6},{6,8},{8,10},{10,12},{12,14},{14,16},{16,18},{18... | collective-permute-start | bytes 3145736 | tf_op jit(solution)/shard_map/ppermute | solution.py:21
  43.5 26.0 %copy-start.2 = (bf16[256,2048]{1,0:T(8,128)(2,1)S(1)}, bf16[256,2048]{1,0:T(8,128)(2,1)}, u32[]{:S(2)}) copy-start(bf16[256,2048]{1,0:T(8,128)(2,1)} %q_ref.1) | copy-start | bytes 3145732
  69.4 1.2 copy-start.7
  93.5 2.9 %copy-start.3 = (bf16[256,1024]{1,0:T(8,128)(2,1)}, bf16[256,1024]{1,0:T(8,128)(2,1)S(1)}, u32[]{:S(2)}) copy-start(bf16[256,1024]{1,0:T(8,128)(2,1)S(1)} %get-tuple-element.14) | copy-start | bytes 1572868
  93.5 2.9 %copy-start.5 = (bf16[256,1024]{1,0:T(8,128)(2,1)}, bf16[256,1024]{1,0:T(8,128)(2,1)S(1)}, u32[]{:S(2)}) copy-start(bf16[256,1024]{1,0:T(8,128)(2,1)S(1)} %get-tuple-element.17) | copy-start | bytes 1572868
  96.4 4.4 %collective-permute-start.4 = (bf16[2,2,2,2,64,1024]{5,4,0,1,2,3:T(8,128)(2,1)S(1)}, bf16[2,2,2,2,64,1024]{5,4,0,1,2,3:T(8,128)(2,1)}, u32[]{:S(2)}, u32[]{:S(2)}) collective-permute-start(bf16[2,2,2,2,64,1024]{5,4,0,1,2,3:T(8,128)(2,1)S(1)} %fusion), channel_id=1, source_target_pairs={{0,2},{2,0},{4,6},{6,4},{8,10},{10,8},{12,14},{14,12},{16,18},{18,... | collective-permute-start | bytes 6291464 | tf_op jit(solution)/shard_map/ppermute | solution.py:39
  104.3 2.0 copy-start.8
  106.4 28.3 %collective-permute-start.5 = (bf16[2,2,2,64,1024]{4,3,0,1,2:T(8,128)(2,1)S(1)}, bf16[2,2,2,64,1024]{4,3,0,1,2:T(8,128)(2,1)}, u32[]{:S(2)}, u32[]{:S(2)}) collective-permute-start(bf16[2,2,2,64,1024]{4,3,0,1,2:T(8,128)(2,1)S(1)} %fusion.6), channel_id=1, source_target_pairs={{0,4},{2,6},{4,0},{6,2},{8,12},{10,14},{12,8},{14,10},{16,20},{18,... | collective-permute-start | bytes 3145736 | tf_op jit(solution)/shard_map/ppermute | solution.py:39
  111.3 26.6 %copy-start.6 = (bf16[256,1024]{1,0:T(8,128)(2,1)S(1)}, bf16[256,1024]{1,0:T(8,128)(2,1)}, u32[]{:S(2)}) copy-start(bf16[256,1024]{1,0:T(8,128)(2,1)} %copy-done.5) | copy-start | bytes 1572868
  111.3 29.6 %copy-start.4 = (bf16[256,1024]{1,0:T(8,128)(2,1)S(1)}, bf16[256,1024]{1,0:T(8,128)(2,1)}, u32[]{:S(2)}) copy-start(bf16[256,1024]{1,0:T(8,128)(2,1)} %copy-done.3) | copy-start | bytes 1572868
  137.8 13.0 %collective-permute-start.6 = (bf16[2,2,64,1024]{3,2,0,1:T(8,128)(2,1)}, bf16[2,2,64,1024]{3,2,0,1:T(8,128)(2,1)}, u32[]{:S(2)}, u32[]{:S(2)}) collective-permute-start(bf16[2,2,64,1024]{3,2,0,1:T(8,128)(2,1)} %fusion.7), channel_id=1, source_target_pairs={{0,8},{2,10},{4,12},{6,14},{8,0},{10,2},{12,4},{14,6},{16,24},{18,... | collective-permute-start | bytes 1572872 | tf_op jit(solution)/shard_map/ppermute | solution.py:39
  137.8 21.7 %collective-permute-start.8 = (bf16[256,1024]{1,0:T(8,128)(2,1)S(1)}, bf16[256,1024]{1,0:T(8,128)(2,1)}, u32[]{:S(2)}, u32[]{:S(2)}) collective-permute-start(bf16[256,1024]{1,0:T(8,128)(2,1)S(1)} %copy-done.6), channel_id=1, source_target_pairs={{2,0},{4,2},{6,4},{8,6},{10,8},{12,10},{14,12},{16,14},{18,16},{20... | collective-permute-start | bytes 1572872 | tf_op jit(solution)/shard_map/ppermute | solution.py:21
  140.9 28.6 %collective-permute-start.3 = (bf16[256,1024]{1,0:T(8,128)(2,1)S(1)}, bf16[256,1024]{1,0:T(8,128)(2,1)}, u32[]{:S(2)}, u32[]{:S(2)}) collective-permute-start(bf16[256,1024]{1,0:T(8,128)(2,1)S(1)} %copy-done.4), channel_id=1, source_target_pairs={{2,0},{4,2},{6,4},{8,6},{10,8},{12,10},{14,12},{16,14},{18,16},{20... | collective-permute-start | bytes 1572872 | tf_op jit(solution)/shard_map/ppermute | solution.py:21
  152.1 1.0 copy-start.11
  153.1 17.7 %copy-start.12 = (f32[2,2,64,1024]{3,2,0,1:T(8,128)S(1)}, f32[2,2,64,1024]{3,2,0,1:T(8,128)}, u32[]{:S(2)}) copy-start(f32[2,2,64,1024]{3,2,0,1:T(8,128)} %copy-done.11) | copy-start | bytes 3145732
  153.1 17.7 %collective-permute-start.7 = (bf16[2,64,1024]{2,1,0:T(8,128)(2,1)S(1)}, bf16[2,64,1024]{2,1,0:T(8,128)(2,1)}, u32[]{:S(2)}, u32[]{:S(2)}) collective-permute-start(bf16[2,64,1024]{2,1,0:T(8,128)(2,1)S(1)} %fusion.9), channel_id=1, source_target_pairs={{0,16},{2,18},{4,20},{6,22},{8,24},{10,26},{12,28},{14,30},{16,0},... | collective-permute-start | bytes 786440 | tf_op jit(solution)/shard_map/ppermute | solution.py:39
  170.8 1.6 copy-start.10
  187.8 3.0 %copy-start.9 = (f32[256,2048]{1,0:T(8,128)S(1)}, f32[256,2048]{1,0:T(8,128)}, u32[]{:S(2)}) copy-start(f32[256,2048]{1,0:T(8,128)} %reshape.91) | copy-start | bytes 6291460
  187.8 3.0 %copy-start.13 = (f32[256,2048]{1,0:T(8,128)S(1)}, f32[256,2048]{1,0:T(8,128)}, u32[]{:S(2)}) copy-start(f32[256,2048]{1,0:T(8,128)} %get-tuple-element.13) | copy-start | bytes 6291460
Sparse Core Ops, SparseCore 0:
  15.3 54.0 all-gather.1
where the time goes:
time: 200 us; the launch traced here: 199 us
  waiting for transfers between devices  79.5 us (40%)
  local copies, waits for them, and re-layouts  29.5 us (15%)
  Pallas kernels  22.8 us (11%)
  other arithmetic  18.6 us (9%)
  starting transfers between devices  18.1 us (9%)
  matrix products  16.1 us (8%)
  between operations  14.3 us (7%)
    ppermute x4, waiting for transfers between devices, seq_reduce_scatter(): lax.ppermute(send.astype(jnp.bfloat16), 'seq', [(source, source ^ 1 << bi...  35 us
    ppermute x4, waiting for transfers between devices, passed_along(): lax.ppermute(value, axis, [(source, source + steps) for source in range(f...  23.5 us
    pallas_call x1, Pallas kernels, pair_attention(): pl.pallas_call(functools.partial(pair_kernel, head_dim=head_dim, scale=sc...  22.8 us
    ppermute x1, waiting for transfers between devices, on_device(): lax.ppermute(cotangent, 'head', [(source, (source + shift) % head_count)...  16.9 us
    dot_general x1, matrix products, on_device(): lax.dot_general(gathered.reshape(seq_rows, cotangent.shape[1]), out_weigh...  12.5 us
    ppermute x4, starting transfers between devices, passed_along(): lax.ppermute(value, axis, [(source, source + steps) for source in range(f...  11.5 us
    unnamed x35, local copies, waits for them, and re-layouts  7.82 us
    add x3, other arithmetic, seq_reduce_scatter(): held = keep + arrived.astype(jnp.float32)  6.93 us
  transfers between devices with their start and end apart: 10, of which 8 were waited for; matrix products, arithmetic and copies ran while one was open for 11% of the time, Pallas kernels for 0%

commit v1 on v0

--- a/solution.py
+++ b/solution.py
@@ -141,26 +141,36 @@
     dkvf_ref[1] = dvf
 
 
-def pair_attention(seq_index, q, k, v, g, k_prev, v_prev, far_kv, head_pairs, head_dim, scale):
+def pair_attention(
+    seq_index, q, k, v, g, k_prev, v_prev, far_kv, first_pair, pairs, head_pairs, head_dim, scale, earlier
+):
     rows = q.shape[0]
     far_rows = far_kv.shape[0]
     pair = 2 * head_dim
 
     def col(width):
-        return pl.BlockSpec((rows, width), lambda p, s: (0, p))
+        return pl.BlockSpec((rows, width), lambda p, s: (0, first_pair + p))
 
     far_k_spec = pl.BlockSpec((far_rows, head_dim), lambda p, s: (0, p))
-    far_v_spec = pl.BlockSpec((far_rows, head_dim), lambda p, s: (0, head_pairs + p))
-    flops = 2 * rows * head_dim * (2 * rows + rows + far_rows) * 7 * head_pairs
+    far_v_spec = pl.BlockSpec((far_rows, head_dim), lambda p, s: (0, pairs + p))
+    flops = 2 * rows * head_dim * (2 * rows + rows + far_rows) * 7 * pairs
     cost = pl.CostEstimate(
         flops=flops,
-        transcendentals=2 * rows * (3 * rows + far_rows) * head_pairs,
-        bytes_accessed=rows * pair * 2 * 16 * head_pairs + far_rows * head_dim * 12 * head_pairs,
-    )
+        transcendentals=2 * rows * (3 * rows + far_rows) * pairs,
+        bytes_accessed=rows * pair * 2 * 16 * pairs + far_rows * head_dim * 12 * pairs,
+    )
+    in_specs = [col(pair)] * 6 + [far_k_spec, far_v_spec]
+    operands = [seq_index, q, k, v, g, k_prev, v_prev, far_kv, far_kv]
+    aliases = {}
+    if earlier is not None:
+        for number, array in enumerate(earlier):
+            aliases[len(operands) + number] = number
+        in_specs = in_specs + [pl.BlockSpec(memory_space=pl.ANY)] * len(earlier)
+        operands = operands + list(earlier)
     grid_spec = pltpu.PrefetchScalarGridSpec(
         num_scalar_prefetch=1,
-        grid=(head_pairs,),
-        in_specs=[col(pair)] * 6 + [far_k_spec, far_v_spec],
+        grid=(pairs,),
+        in_specs=in_specs,
         out_specs=[
             col(pair),
             col(pair),
@@ -172,8 +182,11 @@
         ],
     )
     width = head_pairs * pair
-    return pl.pallas_call(
-        functools.partial(pair_kernel, head_dim=head_dim, scale=scale),
+    kernel = functools.partial(pair_kernel, head_dim=head_dim, scale=scale)
+    if earlier is not None:
+        kernel = functools.partial(skip_tail, kernel, len(earlier))
+    outs = pl.pallas_call(
+        kernel,
         grid_spec=grid_spec,
         out_shape=[
             jax.ShapeDtypeStruct((rows, width), jnp.bfloat16),
@@ -182,11 +195,57 @@
             jax.ShapeDtypeStruct((rows, width), jnp.float32),
             jax.ShapeDtypeStruct((rows, head_pairs * head_dim), jnp.bfloat16),
             jax.ShapeDtypeStruct((rows, head_pairs * head_dim), jnp.bfloat16),
-            jax.ShapeDtypeStruct((2, far_rows, head_pairs * head_dim), jnp.float32),
+            jax.ShapeDtypeStruct((2, far_rows, pairs * head_dim), jnp.float32),
         ],
+        input_output_aliases=aliases,
         compiler_params=pltpu.CompilerParams(vmem_limit_bytes=48 * 1024 * 1024),
         cost_estimate=cost,
-    )(seq_index, q, k, v, g, k_prev, v_prev, far_kv, far_kv)
+    )(*operands)
+    return outs[:6], outs[6]
+
+
+def skip_tail(kernel, unused, *refs):
+    inputs = refs[: 9]
+    outputs = refs[9 + unused :]
+    kernel(*inputs, *outputs)
+
+
+def finalize_kernel(own_k_ref, own_v_ref, back_k_ref, back_v_ref, digest_ref, select_ref, k_out, v_out):
+    hd = back_k_ref.shape[1]
+    pick = select_ref[0]
+    for own_ref, back_ref, side, out_ref in (
+        (own_k_ref, back_k_ref, 0, k_out),
+        (own_v_ref, back_v_ref, 1, v_out),
+    ):
+        out_ref[:, :hd] = (own_ref[:, :hd] + back_ref[...].astype(jnp.float32)).astype(out_ref.dtype)
+        summary = tn(pick, digest_ref[side])
+        out_ref[:, hd:] = (own_ref[:, hd:] + summary).astype(out_ref.dtype)
+
+
+def finalize(own_k, own_v, back_k, back_v, digest, select, head_pairs, head_dim):
+    rows = own_k.shape[0]
+    digest_rows = digest.shape[1]
+    wide = pl.BlockSpec((rows, 2 * head_dim), lambda p: (0, p))
+    narrow = pl.BlockSpec((rows, head_dim), lambda p: (0, p))
+    return pl.pallas_call(
+        finalize_kernel,
+        grid=(head_pairs,),
+        in_specs=[
+            wide,
+            wide,
+            narrow,
+            narrow,
+            pl.BlockSpec((2, digest_rows, head_dim), lambda p: (0, 0, p)),
+            pl.BlockSpec((1, digest_rows, rows), lambda p: (p, 0, 0)),
+        ],
+        out_specs=[wide, wide],
+        out_shape=[jax.ShapeDtypeStruct(own_k.shape, jnp.bfloat16)] * 2,
+        cost_estimate=pl.CostEstimate(
+            flops=4 * rows * digest_rows * head_dim * head_pairs,
+            transcendentals=0,
+            bytes_accessed=rows * head_dim * head_pairs * 20,
+        ),
+    )(own_k, own_v, back_k, back_v, digest, select)
 
 
 def on_device(queries, keys, values, out_weight, cotangent, offsets):
@@ -216,19 +275,19 @@
     digest_v = jnp.einsum(
         "hjr,rhc->jhc", select, fixed_v, preferred_element_type=jnp.float32
     ).astype(jnp.bfloat16)
-    pair_width = head_pairs * head_dim
-    far_kv = lax.all_gather(
-        jnp.concatenate(
-            [
-                digest_k.reshape(digest_count, pair_width),
-                digest_v.reshape(digest_count, pair_width),
-            ],
-            1,
-        ),
-        "seq",
-        axis=0,
-        tiled=True,
-    )
+    chunks = 2 if head_pairs % 2 == 0 else 1
+    pairs = head_pairs // chunks
+    split_dk = digest_k.reshape(digest_count, chunks, pairs * head_dim)
+    split_dv = digest_v.reshape(digest_count, chunks, pairs * head_dim)
+    far_parts = [
+        lax.all_gather(
+            jnp.concatenate([split_dk[:, chunk], split_dv[:, chunk]], 1),
+            "seq",
+            axis=0,
+            tiled=True,
+        )
+        for chunk in range(chunks)
+    ]
     head_count = lax.axis_size("head")
     head_index = lax.axis_index("head")
     pieces = [cotangent] + [
@@ -245,38 +304,34 @@
         (((1,), (1,)), ((), ())),
         preferred_element_type=jnp.float32,
     ).astype(jnp.bfloat16)
-    attention, query_grad, own_dk, own_dv, back_k, back_v, far_dkv = pair_attention(
-        seq_index.reshape(1).astype(jnp.int32),
-        queries,
-        keys,
-        values,
-        grad_out,
-        prev_k,
-        prev_v,
-        far_kv,
-        head_pairs,
-        head_dim,
-        score_scale,
-    )
+    seq_scalar = seq_index.reshape(1).astype(jnp.int32)
+    outputs = None
+    digests = []
+    for chunk in range(chunks):
+        outputs, far_dkv = pair_attention(
+            seq_scalar,
+            queries,
+            keys,
+            values,
+            grad_out,
+            prev_k,
+            prev_v,
+            far_parts[chunk],
+            chunk * pairs,
+            pairs,
+            head_pairs,
+            head_dim,
+            score_scale,
+            outputs,
+        )
+        digests.append(seq_reduce_scatter(far_dkv, 1))
+    attention, query_grad, own_dk, own_dv, back_k, back_v = outputs
     back_k, back_v = passed_along((back_k, back_v), "seq", -1)
-    digest_dkv = seq_reduce_scatter(far_dkv, 1)
-    digest_dk = digest_dkv[0].reshape(digest_count, head_pairs, head_dim)
-    digest_dv = digest_dkv[1].reshape(digest_count, head_pairs, head_dim)
-    fixed_dk = jnp.einsum("hjr,jhc->rhc", select, digest_dk, preferred_element_type=jnp.float32)
-    fixed_dv = jnp.einsum("hjr,jhc->rhc", select, digest_dv, preferred_element_type=jnp.float32)
-
-    def with_extra(own, band_extra, fixed_extra):
-        extra = jnp.stack(
-            [band_extra.reshape(seq_rows, head_pairs, head_dim).astype(jnp.float32), fixed_extra], 2
-        ).reshape(seq_rows, full_width)
-        return (own + extra).astype(jnp.bfloat16)
-
-    return (
-        attention,
-        query_grad,
-        with_extra(own_dk, back_k, fixed_dk),
-        with_extra(own_dv, back_v, fixed_dv),
-    )
+    digest_dkv = jnp.concatenate(digests, 2) if chunks > 1 else digests[0]
+    key_grad, value_grad = finalize(
+        own_dk, own_dv, back_k, back_v, digest_dkv, select, head_pairs, head_dim
+    )
+    return attention, query_grad, key_grad, value_grad
 
 
 def solution(mesh):

time: 200 us -> 196 us (0.980)
  the two profiles are of different devices: /device:TPU:3 before, /device:TPU:0 now
where the time goes in v1:
time: 196 us; the launch traced here: 195 us
  waiting for transfers between devices  89 us (45%)
  Pallas kernels  31.9 us (16%)
  local copies, waits for them, and re-layouts  19.4 us (10%)
  starting transfers between devices  16.3 us (8%)
  between operations  14.3 us (7%)
  matrix products  14 us (7%)
  other arithmetic  10.3 us (5%)
    ppermute x8, waiting for transfers between devices, seq_reduce_scatter(): lax.ppermute(send.astype(jnp.bfloat16), 'seq', [(source, source ^ 1 << bi...  44.1 us
    all_gather x2, waiting for transfers between devices, on_device(): lax.all_gather(jnp.concatenate([split_dk[:, chunk], split_dv[:, chunk]],...  28.1 us
    pallas_call x2, Pallas kernels, pair_attention(): pl.pallas_call(kernel, grid_spec=grid_spec, out_shape=[jax.ShapeDtypeStru...  25 us
    ppermute x1, waiting for transfers between devices, on_device(): lax.ppermute(cotangent, 'head', [(source, (source + shift) % head_count)...  16.8 us
    dot_general x1, matrix products, on_device(): lax.dot_general(gathered.reshape(seq_rows, cotangent.shape[1]), out_weigh...  12.1 us
    unnamed x36, local copies, waits for them, and re-layouts  11.6 us
    ppermute x4, starting transfers between devices, passed_along(): lax.ppermute(value, axis, [(source, source + steps) for source in range(f...  8.98 us
    pallas_call x1, Pallas kernels, finalize(): pl.pallas_call(finalize_kernel, grid=(head_pairs,), in_specs=[wide, wide,...  6.89 us
  transfers between devices with their start and end apart: 15, of which 7 were waited for; matrix products, arithmetic and copies ran while one was open for 14% of the time, Pallas kernels for 13%

profile of v1, /device:TPU:0, one launch (start us, length us, event | category | flops | bytes accessed | tf_op | source)
XLA Modules:
  0.0 195.3 jit_solution(7998105065701463224)
XLA Ops:
  8.1 1.5 copy.16
  10.1 0.8 fusion.19
  10.9 1.3 copy.20
  12.2 1.5 fusion.4
  14.1 0.9 copy_bitcast_fusion
  16.5 3.0 %collective-permute-start = (bf16[128,4096]{1,0:T(8,128)(2,1)S(1)}, bf16[128,4096]{1,0:T(8,128)(2,1)}, u32[]{:S(2)}, u32[]{:S(2)}) collective-permute-start(bf16[128,4096]{1,0:T(8,128)(2,1)S(1)} %copy-done.14), channel_id=1, source_target_pairs={{0,1},{1,0},{2,3},{3,2},{4,5},{5,4},{6,7},{7,6},{8,9},{9,8},{10,11... | collective-permute-start | bytes 3145736 | tf_op jit(solution)/shard_map/ppermute | solution.py:294
  19.5 2.5 %collective-permute-start.1 = (bf16[256,2048]{1,0:T(8,128)(2,1)S(1)}, bf16[256,2048]{1,0:T(8,128)(2,1)}, u32[]{:S(2)}, u32[]{:S(2)}) collective-permute-start(bf16[256,2048]{1,0:T(8,128)(2,1)S(1)} %copy-done), channel_id=1, source_target_pairs={{0,2},{2,4},{4,6},{6,8},{8,10},{10,12},{12,14},{14,16},{16,18},{18... | collective-permute-start | bytes 3145736 | tf_op jit(solution)/shard_map/ppermute | solution.py:21
  22.0 4.0 %collective-permute-start.2 = (bf16[256,2048]{1,0:T(8,128)(2,1)S(1)}, bf16[256,2048]{1,0:T(8,128)(2,1)}, u32[]{:S(2)}, u32[]{:S(2)}) collective-permute-start(bf16[256,2048]{1,0:T(8,128)(2,1)S(1)} %copy-done.1), channel_id=1, source_target_pairs={{0,2},{2,4},{4,6},{6,8},{8,10},{10,12},{12,14},{14,16},{16,18},{18... | collective-permute-start | bytes 3145736 | tf_op jit(solution)/shard_map/ppermute | solution.py:21
  26.0 16.8 %collective-permute-done = bf16[128,4096]{1,0:T(8,128)(2,1)} collective-permute-done((bf16[128,4096]{1,0:T(8,128)(2,1)S(1)}, bf16[128,4096]{1,0:T(8,128)(2,1)}, u32[]{:S(2)}, u32[]{:S(2)}) %collective-permute-start) | collective-permute-done | bytes 1048608 | tf_op jit(solution)/shard_map/ppermute | solution.py:294
  42.8 4.1 %fusion.2 = bf16[2,128,4096]{2,1,0:T(8,128)(2,1)} fusion(s32[]{:T(128)S(6)} %select_n.48, bf16[1,128,4096]{2,1,0:T(8,128)(2,1)} %bitcast.1, bf16[1,128,4096]{2,1,0:T(8,128)(2,1)S(1)} %bitcast.76), kind=kLoop, calls=%fused_computation.7 | loop fusion | flops 3145728 | bytes 4194308 | tf_op jit(solution)/shard_map/stack | solution.py:299
  46.9 12.1 %convolution_convert_fusion.g_ref.refs_4_ = bf16[256,2048]{1,0:T(8,128)(2,1)} fusion(bf16[256,4096]{1,0:T(8,128)(2,1)} %bitcast.75, bf16[2048,4096]{1,0:T(8,128)(2,1)} %param.9), kind=kOutput, calls=%fused_computation.4 | convolution fusion | flops 4295491584 | bytes 19922944 | tf_op jit(solution)/shard_map/dot_general | solution.py:301
  59.0 3.8 %all-gather.5.cloned.1.call-done.kf_ref.vf_ref = bf16[1024,1024]{1,0:T(8,128)(2,1)} async-done(((bf16[64,1024]{1,0:T(8,128)(2,1)}), bf16[1024,1024]{1,0:T(8,128)(2,1)}) %all-gather.5.cloned.1.call-update) | async-done | bytes 2097168 | tf_op jit(solution)/shard_map/all_gather | solution.py:283
  62.8 1.2 copy-done.3
  64.1 12.4 %shard_map.93 = (bf16[256,2048]{1,0:T(8,128)(2,1)}, bf16[256,2048]{1,0:T(8,128)(2,1)}, f32[256,2048]{1,0:T(8,128)}, f32[256,2048]{1,0:T(8,128)}, bf16[256,1024]{...) custom-call(s32[1]{0:T(128)} %bitcast.seq_ref.refs_0_, bf16[256,2048]{1,0:T(8,128)(2,1)S(1)} %copy-done.2, ...), custom_call_target="tpu_custom_call" | custom-call | flops 3288334336 | bytes 14680064 | tf_op jit(solution)/shard_map/pallas_call | solution.py:188
  78.1 2.7 %fusion.5 = bf16[2,2,2,2,64,512]{5,4,0,1,2,3:T(8,128)(2,1)} fusion(f32[2,2,2,2,2,64,512]{6,5,4,3,2,1,0:T(8,128)} %bitcast.71, s32[]{:T(128)S(6)} %select_n.51), kind=kLoop, calls=%fused_computation.16 | loop fusion | bytes 2097156 | tf_op jit(solution)/shard_map/convert_element_type | solution.py:40
  81.1 24.2 %all-gather.3.cloned.1.call-done.refs_7_.refs_8_ = bf16[1024,1024]{1,0:T(8,128)(2,1)} async-done(((bf16[64,1024]{1,0:T(8,128)(2,1)}), bf16[1024,1024]{1,0:T(8,128)(2,1)}) %all-gather.3.cloned.1.call-update) | async-done | bytes 2097168 | tf_op jit(solution)/shard_map/all_gather | solution.py:283
  105.3 1.2 copy-done.4
  106.6 1.0 copy-done.6
  107.6 1.0 copy-done.10
  108.6 12.5 %shard_map.94 = (bf16[256,2048]{1,0:T(8,128)(2,1)}, bf16[256,2048]{1,0:T(8,128)(2,1)}, f32[256,2048]{1,0:T(8,128)}, f32[256,2048]{1,0:T(8,128)}, bf16[256,1024]{...) custom-call(s32[1]{0:T(128)} %bitcast.seq_ref.refs_0_, ...), custom_call_target="tpu_custom_call", output_to_operand_aliasing={{0}: (9, {}), {1}: (10, {}), {2}: (11, {}), {3}: (12, {}), ... | custom-call | flops 3288334336 | bytes 14680064 | tf_op jit(solution)/shard_map/pallas_call | solution.py:188
  122.0 0.8 copy-done.11
  122.8 1.7 fusion.6
  124.9 2.4 %bitcast_add_fusion.1 = f32[2,2,2,2,64,512]{5,4,0,1,2,3:T(8,128)S(1)} fusion(bf16[2,2,2,2,64,512]{5,4,0,1,2,3:T(8,128)(2,1)} %collective-permute-done.5, f32[2,2,2,2,2,64,512]{6,5,4,3,2,1,0:T(8,128)} %bitcast.72, s32[]{:T(128)S(6)} %select_n.50), kind=kLoop, calls=%fused_computation.11 | loop fusion | flops 1048576 | bytes 5242884 | tf_op jit(solution)/shard_map/add | solution.py:42
  128.5 1.5 collective-permute-start.10
  130.0 0.8 fusion.9.select_ref
  130.9 1.3 collective-permute-start.3
  132.2 1.3 collective-permute-start.4
  133.5 18.1 %collective-permute-done.6 = bf16[2,2,2,64,512]{4,3,0,1,2:T(8,128)(2,1)S(1)} collective-permute-done((bf16[2,2,2,64,512]{4,3,0,1,2:T(8,128)(2,1)S(1)}, bf16[2,2,2,64,512]{4,3,0,1,2:T(8,128)(2,1)S(1)}, u32[]{:S(2)}, u32[]{:S(2)}) %collective-permute-start.6) | collective-permute-done | bytes 524320 | tf_op jit(solution)/shard_map/ppermute | solution.py:39
  152.3 9.8 %collective-permute-done.10 = bf16[2,2,2,64,512]{4,3,0,1,2:T(8,128)(2,1)S(1)} collective-permute-done((bf16[2,2,2,64,512]{4,3,0,1,2:T(8,128)(2,1)S(1)}, bf16[2,2,2,64,512]{4,3,0,1,2:T(8,128)(2,1)S(1)}, u32[]{:S(2)}, u32[]{:S(2)}) %collective-permute-start.10) | collective-permute-done | bytes 524320 | tf_op jit(solution)/shard_map/ppermute | solution.py:39
  163.3 9.6 %collective-permute-done.11 = bf16[2,2,64,512]{3,2,0,1:T(8,128)(2,1)S(1)} collective-permute-done((bf16[2,2,64,512]{3,2,0,1:T(8,128)(2,1)S(1)}, bf16[2,2,64,512]{3,2,0,1:T(8,128)(2,1)S(1)}, u32[]{:S(2)}, u32[]{:S(2)}) %collective-permute-start.11) | collective-permute-done | bytes 262176 | tf_op jit(solution)/shard_map/ppermute | solution.py:39
  173.1 6.7 %collective-permute-done.12 = bf16[2,64,512]{2,1,0:T(8,128)(2,1)S(1)} collective-permute-done((bf16[2,64,512]{2,1,0:T(8,128)(2,1)S(1)}, bf16[2,64,512]{2,1,0:T(8,128)(2,1)S(1)}, u32[]{:S(2)}, u32[]{:S(2)}) %collective-permute-start.12) | collective-permute-done | bytes 131104 | tf_op jit(solution)/shard_map/ppermute | solution.py:39
  181.5 6.9 %shard_map.95 = (bf16[256,2048]{1,0:T(8,128)(2,1)}, bf16[256,2048]{1,0:T(8,128)(2,1)}) custom-call(f32[256,2048]{1,0:T(8,128)} %get-tuple-element.28.own_k_ref, f32[256,2048]{1,0:T(8,128)} %get-tuple-element.29.own_v_ref, bf16[256,1024]{1,0:T(8,128)(2,1)} %copy-done.15, bf16[256,1024]{1,0:T(8,128)(2,1)} %copy-done.16, ...), custom_call_target="tpu_custom_call" | custom-call | flops 67108864 | bytes 5242880 | tf_op jit(solution)/shard_map/pallas_call | solution.py:230
  (75 shorter events, 11.2 us)
Async XLA Ops:
  7.2 3.8 %copy-start.1 = (bf16[256,2048]{1,0:T(8,128)(2,1)S(1)}, bf16[256,2048]{1,0:T(8,128)(2,1)}, u32[]{:S(2)}) copy-start(bf16[256,2048]{1,0:T(8,128)(2,1)} %refs_3_.1) | copy-start | bytes 3145732
  7.2 55.6 %all-gather.5.cloned.1.call-start = ((), (), s32[]{:S(2)}) async-start(), calls=%async_computation.1 | async-start | bytes 2228224 | tf_op jit(solution)/shard_map/all_gather | solution.py:283
  12.2 4.3 %copy-start.14 = (bf16[128,4096]{1,0:T(8,128)(2,1)S(1)}, bf16[128,4096]{1,0:T(8,128)(2,1)}, u32[]{:S(2)}) copy-start(bf16[128,4096]{1,0:T(8,128)(2,1)} %param.10) | copy-start | bytes 3145732
  12.2 7.3 %copy-start = (bf16[256,2048]{1,0:T(8,128)(2,1)S(1)}, bf16[256,2048]{1,0:T(8,128)(2,1)}, u32[]{:S(2)}) copy-start(bf16[256,2048]{1,0:T(8,128)(2,1)} %refs_2_.1) | copy-start | bytes 3145732
  15.7 89.6 %all-gather.3.cloned.1.call-start = ((), (), s32[]{:S(2)}) async-start(), calls=%async_computation | async-start | bytes 2228224 | tf_op jit(solution)/shard_map/all_gather | solution.py:283
  16.5 26.3 %collective-permute-start = (bf16[128,4096]{1,0:T(8,128)(2,1)S(1)}, bf16[128,4096]{1,0:T(8,128)(2,1)}, u32[]{:S(2)}, u32[]{:S(2)}) collective-permute-start(bf16[128,4096]{1,0:T(8,128)(2,1)S(1)} %copy-done.14), channel_id=1, source_target_pairs={{0,1},{1,0},{2,3},{3,2},{4,5},{5,4},{6,7},{7,6},{8,9},{9,8},{10,11... | collective-permute-start | bytes 3145736 | tf_op jit(solution)/shard_map/ppermute | solution.py:294
  19.5 39.5 %collective-permute-start.1 = (bf16[256,2048]{1,0:T(8,128)(2,1)S(1)}, bf16[256,2048]{1,0:T(8,128)(2,1)}, u32[]{:S(2)}, u32[]{:S(2)}) collective-permute-start(bf16[256,2048]{1,0:T(8,128)(2,1)S(1)} %copy-done), channel_id=1, source_target_pairs={{0,2},{2,4},{4,6},{6,8},{8,10},{10,12},{12,14},{14,16},{16,18},{18... | collective-permute-start | bytes 3145736 | tf_op jit(solution)/shard_map/ppermute | solution.py:21
  22.0 37.0 %collective-permute-start.2 = (bf16[256,2048]{1,0:T(8,128)(2,1)S(1)}, bf16[256,2048]{1,0:T(8,128)(2,1)}, u32[]{:S(2)}, u32[]{:S(2)}) collective-permute-start(bf16[256,2048]{1,0:T(8,128)(2,1)S(1)} %copy-done.1), channel_id=1, source_target_pairs={{0,2},{2,4},{4,6},{6,8},{8,10},{10,12},{12,14},{14,16},{16,18},{18... | collective-permute-start | bytes 3145736 | tf_op jit(solution)/shard_map/ppermute | solution.py:21
  46.9 15.9 %copy-start.2 = (bf16[256,2048]{1,0:T(8,128)(2,1)S(1)}, bf16[256,2048]{1,0:T(8,128)(2,1)}, u32[]{:S(2)}) copy-start(bf16[256,2048]{1,0:T(8,128)(2,1)} %refs_1_.1) | copy-start | bytes 3145732
  62.8 1.2 copy-start.3
  76.5 0.8 copy-start.5
  77.3 0.8 copy-start.9
  80.8 44.1 %collective-permute-start.5 = (bf16[2,2,2,2,64,512]{5,4,0,1,2,3:T(8,128)(2,1)}, bf16[2,2,2,2,64,512]{5,4,0,1,2,3:T(8,128)(2,1)}, u32[]{:S(2)}, u32[]{:S(2)}) collective-permute-start(bf16[2,2,2,2,64,512]{5,4,0,1,2,3:T(8,128)(2,1)} %fusion.5), channel_id=1, source_target_pairs={{0,2},{2,0},{4,6},{6,4},{8,10},{10,8},{12,14},{14,12},{16,18},{18,... | collective-permute-start | bytes 3145736 | tf_op jit(solution)/shard_map/ppermute | solution.py:39
  105.3 1.2 copy-start.4
  106.6 1.0 copy-start.6
  107.6 1.0 copy-start.10
  121.2 0.8 copy-start.7
  122.0 0.8 copy-start.11
  124.6 3.5 %collective-permute-start.9 = (bf16[2,2,2,2,64,512]{5,4,0,1,2,3:T(8,128)(2,1)S(1)}, bf16[2,2,2,2,64,512]{5,4,0,1,2,3:T(8,128)(2,1)S(1)}, u32[]{:S(2)}, u32[]{:S(2)}) collective-permute-start(bf16[2,2,2,2,64,512]{5,4,0,1,2,3:T(8,128)(2,1)S(1)} %fusion.6), channel_id=1, source_target_pairs={{0,2},{2,0},{4,6},{6,4},{8,10},{10,8},{12,14},{14,12},{16,18},{18,... | collective-permute-start | bytes 3145736 | tf_op jit(solution)/shard_map/ppermute | solution.py:39
  124.9 3.1 %copy-start.13 = (f32[2,1024,512]{2,1,0:T(8,128)S(1)}, f32[2,1024,512]{2,1,0:T(8,128)}, u32[]{:S(2)}) copy-start(f32[2,1024,512]{2,1,0:T(8,128)} %get-tuple-element.33) | copy-start | bytes 12582916
  127.4 3.5 %copy-start.8 = (bf16[256,1024]{1,0:T(8,128)(2,1)S(1)}, bf16[256,1024]{1,0:T(8,128)(2,1)}, u32[]{:S(2)}) copy-start(bf16[256,1024]{1,0:T(8,128)(2,1)} %copy-done.7) | copy-start | bytes 1572868
  127.4 4.8 %copy-start.12 = (bf16[256,1024]{1,0:T(8,128)(2,1)S(1)}, bf16[256,1024]{1,0:T(8,128)(2,1)}, u32[]{:S(2)}) copy-start(bf16[256,1024]{1,0:T(8,128)(2,1)} %copy-done.11) | copy-start | bytes 1572868
  127.4 24.1 %collective-permute-start.6 = (bf16[2,2,2,64,512]{4,3,0,1,2:T(8,128)(2,1)S(1)}, bf16[2,2,2,64,512]{4,3,0,1,2:T(8,128)(2,1)S(1)}, u32[]{:S(2)}, u32[]{:S(2)}) collective-permute-start(bf16[2,2,2,64,512]{4,3,0,1,2:T(8,128)(2,1)S(1)} %fusion.7), channel_id=1, source_target_pairs={{0,4},{2,6},{4,0},{6,2},{8,12},{10,14},{12,8},{14,10},{16,20},{18,... | collective-permute-start | bytes 1572872 | tf_op jit(solution)/shard_map/ppermute | solution.py:39
  128.5 33.6 %collective-permute-start.10 = (bf16[2,2,2,64,512]{4,3,0,1,2:T(8,128)(2,1)S(1)}, bf16[2,2,2,64,512]{4,3,0,1,2:T(8,128)(2,1)S(1)}, u32[]{:S(2)}, u32[]{:S(2)}) collective-permute-start(bf16[2,2,2,64,512]{4,3,0,1,2:T(8,128)(2,1)S(1)} %fusion.8), channel_id=1, source_target_pairs={{0,4},{2,6},{4,0},{6,2},{8,12},{10,14},{12,8},{14,10},{16,20},{18,... | collective-permute-start | bytes 1572872 | tf_op jit(solution)/shard_map/ppermute | solution.py:39
  130.9 49.7 %collective-permute-start.3 = (bf16[256,1024]{1,0:T(8,128)(2,1)S(1)}, bf16[256,1024]{1,0:T(8,128)(2,1)S(1)}, u32[]{:S(2)}, u32[]{:S(2)}) collective-permute-start(bf16[256,1024]{1,0:T(8,128)(2,1)S(1)} %copy-done.8), channel_id=1, source_target_pairs={{2,0},{4,2},{6,4},{8,6},{10,8},{12,10},{14,12},{16,14},{18,16},{20... | collective-permute-start | bytes 1572872 | tf_op jit(solution)/shard_map/ppermute | solution.py:21
  132.2 48.4 %collective-permute-start.4 = (bf16[256,1024]{1,0:T(8,128)(2,1)S(1)}, bf16[256,1024]{1,0:T(8,128)(2,1)S(1)}, u32[]{:S(2)}, u32[]{:S(2)}) collective-permute-start(bf16[256,1024]{1,0:T(8,128)(2,1)S(1)} %copy-done.12), channel_id=1, source_target_pairs={{2,0},{4,2},{6,4},{8,6},{10,8},{12,10},{14,12},{16,14},{18,16},{20... | collective-permute-start | bytes 1572872 | tf_op jit(solution)/shard_map/ppermute | solution.py:21
  151.7 11.2 %collective-permute-start.7 = (bf16[2,2,64,512]{3,2,0,1:T(8,128)(2,1)S(1)}, bf16[2,2,64,512]{3,2,0,1:T(8,128)(2,1)S(1)}, u32[]{:S(2)}, u32[]{:S(2)}) collective-permute-start(bf16[2,2,64,512]{3,2,0,1:T(8,128)(2,1)S(1)} %fusion.10), channel_id=1, source_target_pairs={{0,8},{2,10},{4,12},{6,14},{8,0},{10,2},{12,4},{14,6},{16,24},{18,... | collective-permute-start | bytes 786440 | tf_op jit(solution)/shard_map/ppermute | solution.py:39
  162.3 10.5 %collective-permute-start.11 = (bf16[2,2,64,512]{3,2,0,1:T(8,128)(2,1)S(1)}, bf16[2,2,64,512]{3,2,0,1:T(8,128)(2,1)S(1)}, u32[]{:S(2)}, u32[]{:S(2)}) collective-permute-start(bf16[2,2,64,512]{3,2,0,1:T(8,128)(2,1)S(1)} %fusion.11), channel_id=1, source_target_pairs={{0,8},{2,10},{4,12},{6,14},{8,0},{10,2},{12,4},{14,6},{16,24},{18,... | collective-permute-start | bytes 786440 | tf_op jit(solution)/shard_map/ppermute | solution.py:39
  163.0 10.0 %collective-permute-start.8 = (bf16[2,64,512]{2,1,0:T(8,128)(2,1)S(1)}, bf16[2,64,512]{2,1,0:T(8,128)(2,1)S(1)}, u32[]{:S(2)}, u32[]{:S(2)}) collective-permute-start(bf16[2,64,512]{2,1,0:T(8,128)(2,1)S(1)} %fusion.16), channel_id=1, source_target_pairs={{0,16},{2,18},{4,20},{6,22},{8,24},{10,26},{12,28},{14,30},{16,0},... | collective-permute-start | bytes 393224 | tf_op jit(solution)/shard_map/ppermute | solution.py:39
  173.0 6.8 %collective-permute-start.12 = (bf16[2,64,512]{2,1,0:T(8,128)(2,1)S(1)}, bf16[2,64,512]{2,1,0:T(8,128)(2,1)S(1)}, u32[]{:S(2)}, u32[]{:S(2)}) collective-permute-start(bf16[2,64,512]{2,1,0:T(8,128)(2,1)S(1)} %fusion.17), channel_id=1, source_target_pairs={{0,16},{2,18},{4,20},{6,22},{8,24},{10,26},{12,28},{14,30},{16,0},... | collective-permute-start | bytes 393224 | tf_op jit(solution)/shard_map/ppermute | solution.py:39
  180.5 0.8 copy-start.15
  180.5 1.0 copy-start.16
Sparse Core Ops, SparseCore 0:
  15.9 46.9 all-gather.4
  65.0 40.3 all-gather.2

commit v2 on v1

--- a/solution.py
+++ b/solution.py
@@ -79,114 +79,74 @@
     return out, dq, (dk_a, dv_a), (dk_b, dv_b)
 
 
-def pair_kernel(
-    seq_ref,
-    q_ref,
-    k_ref,
-    v_ref,
-    g_ref,
-    kp_ref,
-    vp_ref,
-    kf_ref,
-    vf_ref,
-    out_ref,
-    dq_ref,
-    dk_ref,
-    dv_ref,
-    dkp_ref,
-    dvp_ref,
-    dkvf_ref,
-    *,
-    head_dim,
-    scale,
-):
+def band_kernel(seq_ref, q_ref, k_ref, v_ref, g_ref, kp_ref, vp_ref, out_ref, dq_ref, dk_ref, dv_ref, dkp_ref, dvp_ref, *, scale):
+    rows = q_ref.shape[0]
+    qi = lax.broadcasted_iota(jnp.int32, (rows, rows), 0)
+    kj = lax.broadcasted_iota(jnp.int32, (rows, rows), 1)
+    prev_mask = (kj > qi) & (seq_ref[0] > 0)
+    own_mask = (kj <= qi) & (qi - kj < WIN)
+    out, dq, (dkp, dvp), (dko, dvo) = two_part_attention(
+        q_ref[...],
+        g_ref[...],
+        (kp_ref[...], vp_ref[...], prev_mask),
+        (k_ref[...], v_ref[...], own_mask),
+        scale,
+    )
+    out_ref[...] = out
+    dq_ref[...] = dq
+    dk_ref[...] = dko
+    dv_ref[...] = dvo
+    dkp_ref[...] = dkp.astype(dkp_ref.dtype)
+    dvp_ref[...] = dvp.astype(dvp_ref.dtype)
+
+
+def fixed_kernel(seq_ref, q_ref, k_ref, v_ref, g_ref, kf_ref, vf_ref, *refs, scale, unused):
+    out_ref, dq_ref, dk_ref, dv_ref, dkvf_ref = refs[unused:]
     rows = q_ref.shape[0]
     far_rows = kf_ref.shape[0]
     start = seq_ref[0] * rows
-    hd = head_dim
     qi = lax.broadcasted_iota(jnp.int32, (rows, rows), 0)
     kj = lax.broadcasted_iota(jnp.int32, (rows, rows), 1)
-    causal = kj <= qi
-    prev_mask = (kj > qi) & (seq_ref[0] > 0)
-    own_band = causal & (qi - kj < WIN)
-    out_b, dq_b, (dkp, dvp), (dko, dvo) = two_part_attention(
-        q_ref[:, :hd],
-        g_ref[:, :hd],
-        (kp_ref[:, :hd], vp_ref[:, :hd], prev_mask),
-        (k_ref[:, :hd], v_ref[:, :hd], own_band),
-        scale,
-    )
-    out_ref[:, :hd] = out_b
-    dq_ref[:, :hd] = dq_b
-    dk_ref[:, :hd] = dko
-    dv_ref[:, :hd] = dvo
-    dkp_ref[...] = dkp.astype(dkp_ref.dtype)
-    dvp_ref[...] = dvp.astype(dvp_ref.dtype)
-    own_fixed = causal & ((qi // BLOCK) == (kj // BLOCK))
+    own_mask = (kj <= qi) & ((qi // BLOCK) == (kj // BLOCK))
     fq = lax.broadcasted_iota(jnp.int32, (rows, far_rows), 0)
     fr = lax.broadcasted_iota(jnp.int32, (rows, far_rows), 1)
     far_mask = (fr // SUMM) < ((start + fq) // BLOCK)
-    out_f, dq_f, (dkf_own, dvf_own), (dkf, dvf) = two_part_attention(
-        q_ref[:, hd:],
-        g_ref[:, hd:],
-        (k_ref[:, hd:], v_ref[:, hd:], own_fixed),
+    out, dq, (dko, dvo), (dkf, dvf) = two_part_attention(
+        q_ref[...],
+        g_ref[...],
+        (k_ref[...], v_ref[...], own_mask),
         (kf_ref[...], vf_ref[...], far_mask),
         scale,
     )
-    out_ref[:, hd:] = out_f
-    dq_ref[:, hd:] = dq_f
-    dk_ref[:, hd:] = dkf_own
-    dv_ref[:, hd:] = dvf_own
+    out_ref[...] = out
+    dq_ref[...] = dq
+    dk_ref[...] = dko
+    dv_ref[...] = dvo
     dkvf_ref[0] = dkf
     dkvf_ref[1] = dvf
 
 
-def pair_attention(
-    seq_index, q, k, v, g, k_prev, v_prev, far_kv, first_pair, pairs, head_pairs, head_dim, scale, earlier
-):
+def attention_cost(rows, keys, head_dim, heads):
+    return pl.CostEstimate(
+        flops=2 * rows * keys * head_dim * 7 * heads,
+        transcendentals=3 * rows * keys * heads,
+        bytes_accessed=(rows * 16 + keys * 6) * head_dim * heads,
+    )
+
+
+def band_attention(seq_index, q, k, v, g, k_prev, v_prev, head_pairs, head_dim, scale):
     rows = q.shape[0]
-    far_rows = far_kv.shape[0]
-    pair = 2 * head_dim
-
-    def col(width):
-        return pl.BlockSpec((rows, width), lambda p, s: (0, first_pair + p))
-
-    far_k_spec = pl.BlockSpec((far_rows, head_dim), lambda p, s: (0, p))
-    far_v_spec = pl.BlockSpec((far_rows, head_dim), lambda p, s: (0, pairs + p))
-    flops = 2 * rows * head_dim * (2 * rows + rows + far_rows) * 7 * pairs
-    cost = pl.CostEstimate(
-        flops=flops,
-        transcendentals=2 * rows * (3 * rows + far_rows) * pairs,
-        bytes_accessed=rows * pair * 2 * 16 * pairs + far_rows * head_dim * 12 * pairs,
-    )
-    in_specs = [col(pair)] * 6 + [far_k_spec, far_v_spec]
-    operands = [seq_index, q, k, v, g, k_prev, v_prev, far_kv, far_kv]
-    aliases = {}
-    if earlier is not None:
-        for number, array in enumerate(earlier):
-            aliases[len(operands) + number] = number
-        in_specs = in_specs + [pl.BlockSpec(memory_space=pl.ANY)] * len(earlier)
-        operands = operands + list(earlier)
+    block = pl.BlockSpec((rows, head_dim), lambda p, s: (0, 2 * p))
+    narrow = pl.BlockSpec((rows, head_dim), lambda p, s: (0, p))
+    width = 2 * head_pairs * head_dim
     grid_spec = pltpu.PrefetchScalarGridSpec(
         num_scalar_prefetch=1,
-        grid=(pairs,),
-        in_specs=in_specs,
-        out_specs=[
-            col(pair),
-            col(pair),
-            col(pair),
-            col(pair),
-            col(head_dim),
-            col(head_dim),
-            pl.BlockSpec((2, far_rows, head_dim), lambda p, s: (0, 0, p)),
-        ],
-    )
-    width = head_pairs * pair
-    kernel = functools.partial(pair_kernel, head_dim=head_dim, scale=scale)
-    if earlier is not None:
-        kernel = functools.partial(skip_tail, kernel, len(earlier))
-    outs = pl.pallas_call(
-        kernel,
+        grid=(head_pairs,),
+        in_specs=[block] * 6,
+        out_specs=[block] * 4 + [narrow] * 2,
+    )
+    return pl.pallas_call(
+        functools.partial(band_kernel, scale=scale),
         grid_spec=grid_spec,
         out_shape=[
             jax.ShapeDtypeStruct((rows, width), jnp.bfloat16),
@@ -195,19 +155,36 @@
             jax.ShapeDtypeStruct((rows, width), jnp.float32),
             jax.ShapeDtypeStruct((rows, head_pairs * head_dim), jnp.bfloat16),
             jax.ShapeDtypeStruct((rows, head_pairs * head_dim), jnp.bfloat16),
-            jax.ShapeDtypeStruct((2, far_rows, pairs * head_dim), jnp.float32),
         ],
+        compiler_params=pltpu.CompilerParams(vmem_limit_bytes=48 * 1024 * 1024),
+        cost_estimate=attention_cost(rows, 2 * rows, head_dim, head_pairs),
+    )(seq_index, q, k, v, g, k_prev, v_prev)
+
+
+def fixed_attention(seq_index, q, k, v, g, far_kv, first_pair, pairs, head_pairs, head_dim, scale, earlier):
+    rows = q.shape[0]
+    far_rows = far_kv.shape[0]
+    block = pl.BlockSpec((rows, head_dim), lambda p, s: (0, 2 * (first_pair + p) + 1))
+    far_k_spec = pl.BlockSpec((far_rows, head_dim), lambda p, s: (0, first_pair + p))
+    far_v_spec = pl.BlockSpec((far_rows, head_dim), lambda p, s: (0, head_pairs + first_pair + p))
+    operands = [seq_index, q, k, v, g, far_kv, far_kv] + list(earlier)
+    aliases = {7 + number: number for number in range(len(earlier))}
+    grid_spec = pltpu.PrefetchScalarGridSpec(
+        num_scalar_prefetch=1,
+        grid=(pairs,),
+        in_specs=[block] * 4 + [far_k_spec, far_v_spec]
+        + [pl.BlockSpec(memory_space=pl.ANY)] * len(earlier),
+        out_specs=[block] * 4 + [pl.BlockSpec((2, far_rows, head_dim), lambda p, s: (0, 0, p))],
+    )
+    return pl.pallas_call(
+        functools.partial(fixed_kernel, scale=scale, unused=len(earlier)),
+        grid_spec=grid_spec,
+        out_shape=[jax.ShapeDtypeStruct(array.shape, array.dtype) for array in earlier]
+        + [jax.ShapeDtypeStruct((2, far_rows, pairs * head_dim), jnp.float32)],
         input_output_aliases=aliases,
         compiler_params=pltpu.CompilerParams(vmem_limit_bytes=48 * 1024 * 1024),
-        cost_estimate=cost,
+        cost_estimate=attention_cost(rows, rows + far_rows, head_dim, pairs),
     )(*operands)
-    return outs[:6], outs[6]
-
-
-def skip_tail(kernel, unused, *refs):
-    inputs = refs[: 9]
-    outputs = refs[9 + unused :]
-    kernel(*inputs, *outputs)
 
 
 def finalize_kernel(own_k_ref, own_v_ref, back_k_ref, back_v_ref, digest_ref, select_ref, k_out, v_out):
@@ -275,19 +252,19 @@
     digest_v = jnp.einsum(
         "hjr,rhc->jhc", select, fixed_v, preferred_element_type=jnp.float32
     ).astype(jnp.bfloat16)
-    chunks = 2 if head_pairs % 2 == 0 else 1
-    pairs = head_pairs // chunks
-    split_dk = digest_k.reshape(digest_count, chunks, pairs * head_dim)
-    split_dv = digest_v.reshape(digest_count, chunks, pairs * head_dim)
-    far_parts = [
-        lax.all_gather(
-            jnp.concatenate([split_dk[:, chunk], split_dv[:, chunk]], 1),
-            "seq",
-            axis=0,
-            tiled=True,
-        )
-        for chunk in range(chunks)
-    ]
+    pair_width = head_pairs * head_dim
+    far_kv = lax.all_gather(
+        jnp.concatenate(
+            [
+                digest_k.reshape(digest_count, pair_width),
+                digest_v.reshape(digest_count, pair_width),
+            ],
+            1,
+        ),
+        "seq",
+        axis=0,
+        tiled=True,
+    )
     head_count = lax.axis_size("head")
     head_index = lax.axis_index("head")
     pieces = [cotangent] + [
@@ -305,18 +282,21 @@
         preferred_element_type=jnp.float32,
     ).astype(jnp.bfloat16)
     seq_scalar = seq_index.reshape(1).astype(jnp.int32)
-    outputs = None
+    attention, query_grad, own_dk, own_dv, back_k, back_v = band_attention(
+        seq_scalar, queries, keys, values, grad_out, prev_k, prev_v, head_pairs, head_dim, score_scale
+    )
+    chunks = 2 if head_pairs % 2 == 0 else 1
+    pairs = head_pairs // chunks
+    outputs = (attention, query_grad, own_dk, own_dv)
     digests = []
     for chunk in range(chunks):
-        outputs, far_dkv = pair_attention(
+        *outputs, far_dkv = fixed_attention(
             seq_scalar,
             queries,
             keys,
             values,
             grad_out,
-            prev_k,
-            prev_v,
-            far_parts[chunk],
+            far_kv,
             chunk * pairs,
             pairs,
             head_pairs,
@@ -325,7 +305,7 @@
             outputs,
         )
         digests.append(seq_reduce_scatter(far_dkv, 1))
-    attention, query_grad, own_dk, own_dv, back_k, back_v = outputs
+    attention, query_grad, own_dk, own_dv = outputs
     back_k, back_v = passed_along((back_k, back_v), "seq", -1)
     digest_dkv = jnp.concatenate(digests, 2) if chunks > 1 else digests[0]
     key_grad, value_grad = finalize(

time: 196 us -> 180 us (0.918)
  waiting for transfers between devices: 89 us -> 59.3 us
  starting transfers between devices: 16.3 us -> 32.4 us
  local copies, waits for them, and re-layouts: 19.4 us -> 14.2 us
  Pallas kernels: 31.9 us -> 34.5 us
    all_gather x2 -> x1, waiting for transfers between devices: 28.1 us -> 4.44 us  [on_device(): lax.all_gather(jnp.concatenate([digest_k.reshape(digest_count, pair_width...]
    ppermute x8, starting transfers between devices: 4.23 us -> 20.3 us  [seq_reduce_scatter(): lax.ppermute(send.astype(jnp.bfloat16), 'seq', [(source, source ^ 1 << bi...]
    ppermute x8, waiting for transfers between devices: 44.1 us -> 38.1 us  [seq_reduce_scatter(): lax.ppermute(send.astype(jnp.bfloat16), 'seq', [(source, source ^ 1 << bi...]
    unnamed x36 -> x28, local copies, waits for them, and re-layouts: 11.6 us -> 8.6 us
    pallas_call x2 -> x3, Pallas kernels: 25 us -> 27.6 us  [the longest x2 17.8 us: fixed_attention(): pl.pallas_call(functools.partial(fixed_kernel, scale=scale, unused=len(ea...]
  transfers between devices with their start and end apart: 15 -> 14, of which waited for: 7 -> 6; matrix products, arithmetic and copies ran while one was open for 14% -> 13% of each run, Pallas kernels for 13% -> 10%
where the time goes in v2:
time: 180 us; the launch traced here: 179 us
  waiting for transfers between devices  59.3 us (33%)
  Pallas kernels  34.5 us (19%)
  starting transfers between devices  32.4 us (18%)
  matrix products  15.1 us (8%)
  between operations  14.3 us (8%)
  local copies, waits for them, and re-layouts  14.2 us (8%)
  other arithmetic  9.61 us (5%)
    ppermute x8, waiting for transfers between devices, seq_reduce_scatter(): lax.ppermute(send.astype(jnp.bfloat16), 'seq', [(source, source ^ 1 << bi...  38.1 us
    ppermute x8, starting transfers between devices, seq_reduce_scatter(): lax.ppermute(send.astype(jnp.bfloat16), 'seq', [(source, source ^ 1 << bi...  20.3 us
    pallas_call x2, Pallas kernels, fixed_attention(): pl.pallas_call(functools.partial(fixed_kernel, scale=scale, unused=len(ea...  17.8 us
    ppermute x1, waiting for transfers between devices, on_device(): lax.ppermute(cotangent, 'head', [(source, (source + shift) % head_count)...  16.8 us
    dot_general x1, matrix products, on_device(): lax.dot_general(gathered.reshape(seq_rows, cotangent.shape[1]), out_weigh...  12.3 us
    pallas_call x1, Pallas kernels, band_attention(): pl.pallas_call(functools.partial(band_kernel, scale=scale), grid_spec=gri...  9.82 us
    ppermute x4, starting transfers between devices, passed_along(): lax.ppermute(value, axis, [(source, source + steps) for source in range(f...  9.08 us
    unnamed x28, local copies, waits for them, and re-layouts  8.6 us
  transfers between devices with their start and end apart: 14, of which 6 were waited for; matrix products, arithmetic and copies ran while one was open for 13% of the time, Pallas kernels for 10%

profile of v2, /device:TPU:0, one launch (start us, length us, event | category | flops | bytes accessed | tf_op | source)
XLA Modules:
  0.0 179.4 jit_solution(10052070445752559132)
XLA Ops:
  8.1 2.3 %copy.20 = bf16[256,2048]{0,1:T(8,128)(2,1)} copy(bf16[256,2048]{1,0:T(8,128)(2,1)} %k_ref.5) | data formatting | bytes 2097152 | tf_op args[1]
  10.3 1.3 copy.23
  11.7 1.4 fusion.3
  13.0 1.4 fusion.4
  15.2 3.0 %collective-permute-start = (bf16[128,4096]{1,0:T(8,128)(2,1)S(1)}, bf16[128,4096]{1,0:T(8,128)(2,1)}, u32[]{:S(2)}, u32[]{:S(2)}) collective-permute-start(bf16[128,4096]{1,0:T(8,128)(2,1)S(1)} %copy-done.10), channel_id=1, source_target_pairs={{0,1},{1,0},{2,3},{3,2},{4,5},{5,4},{6,7},{7,6},{8,9},{9,8},{10,11... | collective-permute-start | bytes 3145736 | tf_op jit(solution)/shard_map/ppermute | solution.py:271
  18.3 2.4 %collective-permute-start.1 = (bf16[256,2048]{1,0:T(8,128)(2,1)S(1)}, bf16[256,2048]{1,0:T(8,128)(2,1)}, u32[]{:S(2)}, u32[]{:S(2)}) collective-permute-start(bf16[256,2048]{1,0:T(8,128)(2,1)S(1)} %copy-done), channel_id=1, source_target_pairs={{0,2},{2,4},{4,6},{6,8},{8,10},{10,12},{12,14},{14,16},{16,18},{18... | collective-permute-start | bytes 3145736 | tf_op jit(solution)/shard_map/ppermute | solution.py:21
  20.7 4.1 %collective-permute-start.2 = (bf16[256,2048]{1,0:T(8,128)(2,1)S(1)}, bf16[256,2048]{1,0:T(8,128)(2,1)}, u32[]{:S(2)}, u32[]{:S(2)}) collective-permute-start(bf16[256,2048]{1,0:T(8,128)(2,1)S(1)} %copy-done.1), channel_id=1, source_target_pairs={{0,2},{2,4},{4,6},{6,8},{8,10},{10,12},{12,14},{14,16},{16,18},{18... | collective-permute-start | bytes 3145736 | tf_op jit(solution)/shard_map/ppermute | solution.py:21
  24.8 16.8 %collective-permute-done = bf16[128,4096]{1,0:T(8,128)(2,1)} collective-permute-done((bf16[128,4096]{1,0:T(8,128)(2,1)S(1)}, bf16[128,4096]{1,0:T(8,128)(2,1)}, u32[]{:S(2)}, u32[]{:S(2)}) %collective-permute-start) | collective-permute-done | bytes 1048608 | tf_op jit(solution)/shard_map/ppermute | solution.py:271
  41.5 4.1 %fusion.2 = bf16[2,128,4096]{2,1,0:T(8,128)(2,1)} fusion(s32[]{:T(128)S(6)} %select_n.48, bf16[1,128,4096]{2,1,0:T(8,128)(2,1)} %bitcast.1, bf16[1,128,4096]{2,1,0:T(8,128)(2,1)S(1)} %bitcast.74), kind=kLoop, calls=%fused_computation.7 | loop fusion | flops 3145728 | bytes 4194308 | tf_op jit(solution)/shard_map/stack | solution.py:276
  45.6 12.3 %convolution_convert_fusion.g_ref = bf16[256,2048]{1,0:T(8,128)(2,1)} fusion(bf16[256,4096]{1,0:T(8,128)(2,1)} %bitcast.73, bf16[2048,4096]{1,0:T(8,128)(2,1)} %param.9), kind=kOutput, calls=%fused_computation.4 | convolution fusion | flops 4295491584 | bytes 19922944 | tf_op jit(solution)/shard_map/dot_general | solution.py:278
  57.9 1.2 copy-done.3
  59.1 9.8 %shard_map.93 = (bf16[256,2048]{1,0:T(8,128)(2,1)}, bf16[256,2048]{1,0:T(8,128)(2,1)}, f32[256,2048]{1,0:T(8,128)}, f32[256,2048]{1,0:T(8,128)}, bf16[256,1024]{...) custom-call(s32[1]{0:T(128)} %bitcast.seq_ref, bf16[256,2048]{1,0:T(8,128)(2,1)S(1)} %copy-done.2, ...), custom_call_target="tpu_custom_call" | custom-call | flops 1879048192 | bytes 7340032 | tf_op jit(solution)/shard_map/pallas_call | solution.py:148
  70.5 4.4 %all-gather.2.cloned.1.call-done.kf_ref.vf_ref = bf16[1024,2048]{1,0:T(8,128)(2,1)} async-done(((bf16[64,2048]{1,0:T(8,128)(2,1)}), bf16[1024,2048]{1,0:T(8,128)(2,1)}) %all-gather.2.cloned.1.call-update) | async-done | bytes 4194320 | tf_op jit(solution)/shard_map/all_gather | solution.py:256
  75.0 1.2 copy-done.4
  76.2 8.9 %shard_map.94 = (bf16[256,2048]{1,0:T(8,128)(2,1)}, bf16[256,2048]{1,0:T(8,128)(2,1)}, f32[256,2048]{1,0:T(8,128)}, f32[256,2048]{1,0:T(8,128)}, f32[2,1024,512]{2,1,0:T(8,128)}) custom-call(s32[1]{0:T(128)} %bitcast.seq_ref, bf16[256,2048]{1,0:T(8,128)(2,1)S(1)} %copy-done.2, ...), custom_call_target="tpu_custom_call", output_to_operand_aliasing={{0}: (7, {}), {1}: (8, {}), {2}: (9, {}), {3}: (10, {})} | custom-call | flops 2348810240 | bytes 6029312 | tf_op jit(solution)/shard_map/pallas_call | solution.py:179
  85.1 2.7 %fusion.5 = bf16[2,2,2,2,64,512]{5,4,0,1,2,3:T(8,128)(2,1)} fusion(f32[2,2,2,2,2,64,512]{6,5,4,3,2,1,0:T(8,128)} %bitcast.71, s32[]{:T(128)S(6)} %select_n.51), kind=kLoop, calls=%fused_computation.16 | loop fusion | bytes 2097156 | tf_op jit(solution)/shard_map/convert_element_type | solution.py:40
  88.1 8.8 %shard_map.95 = (bf16[256,2048]{1,0:T(8,128)(2,1)}, bf16[256,2048]{1,0:T(8,128)(2,1)}, f32[256,2048]{1,0:T(8,128)}, f32[256,2048]{1,0:T(8,128)}, f32[2,1024,512]{2,1,0:T(8,128)}) custom-call(s32[1]{0:T(128)} %bitcast.seq_ref, bf16[256,2048]{1,0:T(8,128)(2,1)S(1)} %copy-done.2, ...), custom_call_target="tpu_custom_call", output_to_operand_aliasing={{0}: (7, {}), {1}: (8, {}), {2}: (9, {}), {3}: (10, {})} | custom-call | flops 2348810240 | bytes 6029312 | tf_op jit(solution)/shard_map/pallas_call | solution.py:179
  96.9 1.7 fusion.6
  99.0 2.4 %bitcast_add_fusion.1 = f32[2,2,2,2,64,512]{5,4,0,1,2,3:T(8,128)S(1)} fusion(bf16[2,2,2,2,64,512]{5,4,0,1,2,3:T(8,128)(2,1)} %collective-permute-done.5, f32[2,2,2,2,2,64,512]{6,5,4,3,2,1,0:T(8,128)} %bitcast.72, s32[]{:T(128)S(6)} %select_n.50), kind=kLoop, calls=%fused_computation.11 | loop fusion | flops 1048576 | bytes 5242884 | tf_op jit(solution)/shard_map/add | solution.py:42
  101.5 5.5 %collective-permute-start.6 = (bf16[2,2,2,64,512]{4,3,0,1,2:T(8,128)(2,1)S(1)}, bf16[2,2,2,64,512]{4,3,0,1,2:T(8,128)(2,1)S(1)}, u32[]{:S(2)}, u32[]{:S(2)}) collective-permute-start(bf16[2,2,2,64,512]{4,3,0,1,2:T(8,128)(2,1)S(1)} %fusion.7), channel_id=1, source_target_pairs={{0,4},{2,6},{4,0},{6,2},{8,12},{10,14},{12,8},{14,10},{16,20},{18,... | collective-permute-start | bytes 1572872 | tf_op jit(solution)/shard_map/ppermute | solution.py:39
  108.1 0.8 fusion.9.select_ref
  108.9 1.3 collective-permute-start.3
  110.2 1.3 collective-permute-start.4
  111.5 19.0 %collective-permute-done.6 = bf16[2,2,2,64,512]{4,3,0,1,2:T(8,128)(2,1)S(1)} collective-permute-done((bf16[2,2,2,64,512]{4,3,0,1,2:T(8,128)(2,1)S(1)}, bf16[2,2,2,64,512]{4,3,0,1,2:T(8,128)(2,1)S(1)}, u32[]{:S(2)}, u32[]{:S(2)}) %collective-permute-start.6) | collective-permute-done | bytes 524320 | tf_op jit(solution)/shard_map/ppermute | solution.py:39
  130.7 5.0 %collective-permute-start.7 = (bf16[2,2,64,512]{3,2,0,1:T(8,128)(2,1)S(1)}, bf16[2,2,64,512]{3,2,0,1:T(8,128)(2,1)S(1)}, u32[]{:S(2)}, u32[]{:S(2)}) collective-permute-start(bf16[2,2,64,512]{3,2,0,1:T(8,128)(2,1)S(1)} %fusion.10), channel_id=1, source_target_pairs={{0,8},{2,10},{4,12},{6,14},{8,0},{10,2},{12,4},{14,6},{16,24},{18,... | collective-permute-start | bytes 786440 | tf_op jit(solution)/shard_map/ppermute | solution.py:39
  135.7 5.6 %collective-permute-done.10 = bf16[2,2,2,64,512]{4,3,0,1,2:T(8,128)(2,1)S(1)} collective-permute-done((bf16[2,2,2,64,512]{4,3,0,1,2:T(8,128)(2,1)S(1)}, bf16[2,2,2,64,512]{4,3,0,1,2:T(8,128)(2,1)S(1)}, u32[]{:S(2)}, u32[]{:S(2)}) %collective-permute-start.10) | collective-permute-done | bytes 524320 | tf_op jit(solution)/shard_map/ppermute | solution.py:39
  141.5 5.0 %collective-permute-start.11 = (bf16[2,2,64,512]{3,2,0,1:T(8,128)(2,1)S(1)}, bf16[2,2,64,512]{3,2,0,1:T(8,128)(2,1)S(1)}, u32[]{:S(2)}, u32[]{:S(2)}) collective-permute-start(bf16[2,2,64,512]{3,2,0,1:T(8,128)(2,1)S(1)} %fusion.11), channel_id=1, source_target_pairs={{0,8},{2,10},{4,12},{6,14},{8,0},{10,2},{12,4},{14,6},{16,24},{18,... | collective-permute-start | bytes 786440 | tf_op jit(solution)/shard_map/ppermute | solution.py:39
  146.6 1.7 collective-permute-start.8
  148.4 7.1 %collective-permute-done.11 = bf16[2,2,64,512]{3,2,0,1:T(8,128)(2,1)S(1)} collective-permute-done((bf16[2,2,64,512]{3,2,0,1:T(8,128)(2,1)S(1)}, bf16[2,2,64,512]{3,2,0,1:T(8,128)(2,1)S(1)}, u32[]{:S(2)}, u32[]{:S(2)}) %collective-permute-start.11) | collective-permute-done | bytes 262176 | tf_op jit(solution)/shard_map/ppermute | solution.py:39
  155.6 1.9 %collective-permute-start.12 = (bf16[2,64,512]{2,1,0:T(8,128)(2,1)S(1)}, bf16[2,64,512]{2,1,0:T(8,128)(2,1)S(1)}, u32[]{:S(2)}, u32[]{:S(2)}) collective-permute-start(bf16[2,64,512]{2,1,0:T(8,128)(2,1)S(1)} %fusion.17), channel_id=1, source_target_pairs={{0,16},{2,18},{4,20},{6,22},{8,24},{10,26},{12,28},{14,30},{16,0},... | collective-permute-start | bytes 393224 | tf_op jit(solution)/shard_map/ppermute | solution.py:39
  157.5 6.4 %collective-permute-done.12 = bf16[2,64,512]{2,1,0:T(8,128)(2,1)S(1)} collective-permute-done((bf16[2,64,512]{2,1,0:T(8,128)(2,1)S(1)}, bf16[2,64,512]{2,1,0:T(8,128)(2,1)S(1)}, u32[]{:S(2)}, u32[]{:S(2)}) %collective-permute-start.12) | collective-permute-done | bytes 131104 | tf_op jit(solution)/shard_map/ppermute | solution.py:39
  165.6 6.9 %shard_map.96 = (bf16[256,2048]{1,0:T(8,128)(2,1)}, bf16[256,2048]{1,0:T(8,128)(2,1)}) custom-call(f32[256,2048]{1,0:T(8,128)} %get-tuple-element.32.own_k_ref, f32[256,2048]{1,0:T(8,128)} %get-tuple-element.33.own_v_ref, bf16[256,1024]{1,0:T(8,128)(2,1)} %copy-done.11, bf16[256,1024]{1,0:T(8,128)(2,1)} %copy-done.12, ...), custom_call_target="tpu_custom_call" | custom-call | flops 67108864 | bytes 5242880 | tf_op jit(solution)/shard_map/pallas_call | solution.py:207
  (57 shorter events, 7.4 us)
Async XLA Ops:
  7.2 3.2 %copy-start.1 = (bf16[256,2048]{1,0:T(8,128)(2,1)S(1)}, bf16[256,2048]{1,0:T(8,128)(2,1)}, u32[]{:S(2)}) copy-start(bf16[256,2048]{1,0:T(8,128)(2,1)} %v_ref.5) | copy-start | bytes 3145732
  7.2 67.8 %all-gather.2.cloned.1.call-start = ((), (), s32[]{:S(2)}) async-start(), calls=%async_computation | async-start | bytes 4456448 | tf_op jit(solution)/shard_map/all_gather | solution.py:256
  10.3 4.9 %copy-start.10 = (bf16[128,4096]{1,0:T(8,128)(2,1)S(1)}, bf16[128,4096]{1,0:T(8,128)(2,1)}, u32[]{:S(2)}) copy-start(bf16[128,4096]{1,0:T(8,128)(2,1)} %param.10) | copy-start | bytes 3145732
  10.3 7.9 %copy-start = (bf16[256,2048]{1,0:T(8,128)(2,1)S(1)}, bf16[256,2048]{1,0:T(8,128)(2,1)}, u32[]{:S(2)}) copy-start(bf16[256,2048]{1,0:T(8,128)(2,1)} %k_ref.5) | copy-start | bytes 3145732
  15.2 26.3 %collective-permute-start = (bf16[128,4096]{1,0:T(8,128)(2,1)S(1)}, bf16[128,4096]{1,0:T(8,128)(2,1)}, u32[]{:S(2)}, u32[]{:S(2)}) collective-permute-start(bf16[128,4096]{1,0:T(8,128)(2,1)S(1)} %copy-done.10), channel_id=1, source_target_pairs={{0,1},{1,0},{2,3},{3,2},{4,5},{5,4},{6,7},{7,6},{8,9},{9,8},{10,11... | collective-permute-start | bytes 3145736 | tf_op jit(solution)/shard_map/ppermute | solution.py:271
  18.3 39.6 %collective-permute-start.1 = (bf16[256,2048]{1,0:T(8,128)(2,1)S(1)}, bf16[256,2048]{1,0:T(8,128)(2,1)}, u32[]{:S(2)}, u32[]{:S(2)}) collective-permute-start(bf16[256,2048]{1,0:T(8,128)(2,1)S(1)} %copy-done), channel_id=1, source_target_pairs={{0,2},{2,4},{4,6},{6,8},{8,10},{10,12},{12,14},{14,16},{16,18},{18... | collective-permute-start | bytes 3145736 | tf_op jit(solution)/shard_map/ppermute | solution.py:21
  20.7 37.2 %collective-permute-start.2 = (bf16[256,2048]{1,0:T(8,128)(2,1)S(1)}, bf16[256,2048]{1,0:T(8,128)(2,1)}, u32[]{:S(2)}, u32[]{:S(2)}) collective-permute-start(bf16[256,2048]{1,0:T(8,128)(2,1)S(1)} %copy-done.1), channel_id=1, source_target_pairs={{0,2},{2,4},{4,6},{6,8},{8,10},{10,12},{12,14},{14,16},{16,18},{18... | collective-permute-start | bytes 3145736 | tf_op jit(solution)/shard_map/ppermute | solution.py:21
  45.6 12.3 %copy-start.2 = (bf16[256,2048]{1,0:T(8,128)(2,1)S(1)}, bf16[256,2048]{1,0:T(8,128)(2,1)}, u32[]{:S(2)}) copy-start(bf16[256,2048]{1,0:T(8,128)(2,1)} %q_ref.5) | copy-start | bytes 3145732
  57.9 1.2 copy-start.3
  68.9 0.8 copy-start.5
  69.7 0.8 copy-start.7
  75.0 1.2 copy-start.4
  87.8 11.2 %collective-permute-start.5 = (bf16[2,2,2,2,64,512]{5,4,0,1,2,3:T(8,128)(2,1)}, bf16[2,2,2,2,64,512]{5,4,0,1,2,3:T(8,128)(2,1)}, u32[]{:S(2)}, u32[]{:S(2)}) collective-permute-start(bf16[2,2,2,2,64,512]{5,4,0,1,2,3:T(8,128)(2,1)} %fusion.5), channel_id=1, source_target_pairs={{0,2},{2,0},{4,6},{6,4},{8,10},{10,8},{12,14},{14,12},{16,18},{18,... | collective-permute-start | bytes 3145736 | tf_op jit(solution)/shard_map/ppermute | solution.py:39
  98.7 8.4 %collective-permute-start.9 = (bf16[2,2,2,2,64,512]{5,4,0,1,2,3:T(8,128)(2,1)S(1)}, bf16[2,2,2,2,64,512]{5,4,0,1,2,3:T(8,128)(2,1)S(1)}, u32[]{:S(2)}, u32[]{:S(2)}) collective-permute-start(bf16[2,2,2,2,64,512]{5,4,0,1,2,3:T(8,128)(2,1)S(1)} %fusion.6), channel_id=1, source_target_pairs={{0,2},{2,0},{4,6},{6,4},{8,10},{10,8},{12,14},{14,12},{16,18},{18,... | collective-permute-start | bytes 3145736 | tf_op jit(solution)/shard_map/ppermute | solution.py:39
  99.0 8.0 %copy-start.9 = (f32[2,1024,512]{2,1,0:T(8,128)S(1)}, f32[2,1024,512]{2,1,0:T(8,128)}, u32[]{:S(2)}) copy-start(f32[2,1024,512]{2,1,0:T(8,128)} %get-tuple-element.37) | copy-start | bytes 12582916
  101.5 7.4 %copy-start.8 = (bf16[256,1024]{1,0:T(8,128)(2,1)S(1)}, bf16[256,1024]{1,0:T(8,128)(2,1)}, u32[]{:S(2)}) copy-start(bf16[256,1024]{1,0:T(8,128)(2,1)} %copy-done.7) | copy-start | bytes 1572868
  101.5 8.7 %copy-start.6 = (bf16[256,1024]{1,0:T(8,128)(2,1)S(1)}, bf16[256,1024]{1,0:T(8,128)(2,1)}, u32[]{:S(2)}) copy-start(bf16[256,1024]{1,0:T(8,128)(2,1)} %copy-done.5) | copy-start | bytes 1572868
  101.5 29.0 %collective-permute-start.6 = (bf16[2,2,2,64,512]{4,3,0,1,2:T(8,128)(2,1)S(1)}, bf16[2,2,2,64,512]{4,3,0,1,2:T(8,128)(2,1)S(1)}, u32[]{:S(2)}, u32[]{:S(2)}) collective-permute-start(bf16[2,2,2,64,512]{4,3,0,1,2:T(8,128)(2,1)S(1)} %fusion.7), channel_id=1, source_target_pairs={{0,4},{2,6},{4,0},{6,2},{8,12},{10,14},{12,8},{14,10},{16,20},{18,... | collective-permute-start | bytes 1572872 | tf_op jit(solution)/shard_map/ppermute | solution.py:39
  107.5 33.8 %collective-permute-start.10 = (bf16[2,2,2,64,512]{4,3,0,1,2:T(8,128)(2,1)S(1)}, bf16[2,2,2,64,512]{4,3,0,1,2:T(8,128)(2,1)S(1)}, u32[]{:S(2)}, u32[]{:S(2)}) collective-permute-start(bf16[2,2,2,64,512]{4,3,0,1,2:T(8,128)(2,1)S(1)} %fusion.8), channel_id=1, source_target_pairs={{0,4},{2,6},{4,0},{6,2},{8,12},{10,14},{12,8},{14,10},{16,20},{18,... | collective-permute-start | bytes 1572872 | tf_op jit(solution)/shard_map/ppermute | solution.py:39
  108.9 55.7 %collective-permute-start.3 = (bf16[256,1024]{1,0:T(8,128)(2,1)S(1)}, bf16[256,1024]{1,0:T(8,128)(2,1)S(1)}, u32[]{:S(2)}, u32[]{:S(2)}) collective-permute-start(bf16[256,1024]{1,0:T(8,128)(2,1)S(1)} %copy-done.8), channel_id=1, source_target_pairs={{2,0},{4,2},{6,4},{8,6},{10,8},{12,10},{14,12},{16,14},{18,16},{20... | collective-permute-start | bytes 1572872 | tf_op jit(solution)/shard_map/ppermute | solution.py:21
  110.2 54.4 %collective-permute-start.4 = (bf16[256,1024]{1,0:T(8,128)(2,1)S(1)}, bf16[256,1024]{1,0:T(8,128)(2,1)S(1)}, u32[]{:S(2)}, u32[]{:S(2)}) collective-permute-start(bf16[256,1024]{1,0:T(8,128)(2,1)S(1)} %copy-done.6), channel_id=1, source_target_pairs={{2,0},{4,2},{6,4},{8,6},{10,8},{12,10},{14,12},{16,14},{18,16},{20... | collective-permute-start | bytes 1572872 | tf_op jit(solution)/shard_map/ppermute | solution.py:21
  130.7 15.8 %collective-permute-start.7 = (bf16[2,2,64,512]{3,2,0,1:T(8,128)(2,1)S(1)}, bf16[2,2,64,512]{3,2,0,1:T(8,128)(2,1)S(1)}, u32[]{:S(2)}, u32[]{:S(2)}) collective-permute-start(bf16[2,2,64,512]{3,2,0,1:T(8,128)(2,1)S(1)} %fusion.10), channel_id=1, source_target_pairs={{0,8},{2,10},{4,12},{6,14},{8,0},{10,2},{12,4},{14,6},{16,24},{18,... | collective-permute-start | bytes 786440 | tf_op jit(solution)/shard_map/ppermute | solution.py:39
  141.5 14.0 %collective-permute-start.11 = (bf16[2,2,64,512]{3,2,0,1:T(8,128)(2,1)S(1)}, bf16[2,2,64,512]{3,2,0,1:T(8,128)(2,1)S(1)}, u32[]{:S(2)}, u32[]{:S(2)}) collective-permute-start(bf16[2,2,64,512]{3,2,0,1:T(8,128)(2,1)S(1)} %fusion.11), channel_id=1, source_target_pairs={{0,8},{2,10},{4,12},{6,14},{8,0},{10,2},{12,4},{14,6},{16,24},{18,... | collective-permute-start | bytes 786440 | tf_op jit(solution)/shard_map/ppermute | solution.py:39
  146.6 10.8 %collective-permute-start.8 = (bf16[2,64,512]{2,1,0:T(8,128)(2,1)S(1)}, bf16[2,64,512]{2,1,0:T(8,128)(2,1)S(1)}, u32[]{:S(2)}, u32[]{:S(2)}) collective-permute-start(bf16[2,64,512]{2,1,0:T(8,128)(2,1)S(1)} %fusion.16), channel_id=1, source_target_pairs={{0,16},{2,18},{4,20},{6,22},{8,24},{10,26},{12,28},{14,30},{16,0},... | collective-permute-start | bytes 393224 | tf_op jit(solution)/shard_map/ppermute | solution.py:39
  155.6 8.3 %collective-permute-start.12 = (bf16[2,64,512]{2,1,0:T(8,128)(2,1)S(1)}, bf16[2,64,512]{2,1,0:T(8,128)(2,1)S(1)}, u32[]{:S(2)}, u32[]{:S(2)}) collective-permute-start(bf16[2,64,512]{2,1,0:T(8,128)(2,1)S(1)} %fusion.17), channel_id=1, source_target_pairs={{0,16},{2,18},{4,20},{6,22},{8,24},{10,26},{12,28},{14,30},{16,0},... | collective-permute-start | bytes 393224 | tf_op jit(solution)/shard_map/ppermute | solution.py:39
  164.7 0.8 copy-start.11
  164.7 1.0 copy-start.12
Sparse Core Ops, SparseCore 0:
  15.3 59.5 all-gather.1

commit v3 on v2

--- a/solution.py
+++ b/solution.py
@@ -21,7 +21,7 @@
     return lax.ppermute(value, axis, [(source, source + steps) for source in range(first, last)])
 
 
-def seq_reduce_scatter(parts, axis):
+def seq_reduce_scatter(parts, axis, rotate=0):
     count = lax.axis_size("seq")
     if count & (count - 1):
         return lax.psum_scatter(
@@ -31,8 +31,14 @@
     bits = count.bit_length() - 1
     chunk = parts.shape[axis] // count
     held = parts.reshape(parts.shape[:axis] + (2,) * bits + (chunk,) + parts.shape[axis + 1 :])
-    for bit in range(bits):
-        where = axis + bits - 1 - bit
+    if bits > 2:
+        order = [0] + sorted(range(1, bits - 1), key=lambda b: (b - 1 - rotate) % (bits - 2)) + [bits - 1]
+    else:
+        order = list(range(bits))
+    gone = []
+    for bit in order:
+        where = axis + bits - 1 - bit - sum(1 for done in gone if done > bit)
+        gone.append(bit)
         mine = (me >> bit) & 1
         keep = lax.dynamic_index_in_dim(held, mine, where, keepdims=False)
         send = lax.dynamic_index_in_dim(held, 1 - mine, where, keepdims=False)
@@ -304,7 +310,7 @@
             score_scale,
             outputs,
         )
-        digests.append(seq_reduce_scatter(far_dkv, 1))
+        digests.append(seq_reduce_scatter(far_dkv, 1, chunk))
     attention, query_grad, own_dk, own_dv = outputs
     back_k, back_v = passed_along((back_k, back_v), "seq", -1)
     digest_dkv = jnp.concatenate(digests, 2) if chunks > 1 else digests[0]

time: 180 us -> 172 us (0.956)
  waiting for transfers between devices: 59.3 us -> 38.3 us
  starting transfers between devices: 32.4 us -> 45.4 us
    ppermute x8, waiting for transfers between devices: 38.1 us -> 17.1 us  [seq_reduce_scatter(): lax.ppermute(send.astype(jnp.bfloat16), 'seq', [(source, source ^ 1 << bi...]
    ppermute x8, starting transfers between devices: 20.3 us -> 33.2 us  [seq_reduce_scatter(): lax.ppermute(send.astype(jnp.bfloat16), 'seq', [(source, source ^ 1 << bi...]
  transfers between devices with their start and end apart: 14 -> 14, of which waited for: 6 -> 6; matrix products, arithmetic and copies ran while one was open for 13% -> 14% of each run, Pallas kernels for 10% -> 11%
where the time goes in v3:
time: 172 us; the launch traced here: 171 us
  starting transfers between devices  45.4 us (26%)
  waiting for transfers between devices  38.3 us (22%)
  Pallas kernels  34.5 us (20%)
  matrix products  15.1 us (9%)
  between operations  14.3 us (8%)
  local copies, waits for them, and re-layouts  14.2 us (8%)
  other arithmetic  9.61 us (6%)
    ppermute x8, starting transfers between devices, seq_reduce_scatter(): lax.ppermute(send.astype(jnp.bfloat16), 'seq', [(source, source ^ 1 << bi...  33.2 us
    pallas_call x2, Pallas kernels, fixed_attention(): pl.pallas_call(functools.partial(fixed_kernel, scale=scale, unused=len(ea...  17.8 us
    ppermute x8, waiting for transfers between devices, seq_reduce_scatter(): lax.ppermute(send.astype(jnp.bfloat16), 'seq', [(source, source ^ 1 << bi...  17.1 us
    ppermute x1, waiting for transfers between devices, on_device(): lax.ppermute(cotangent, 'head', [(source, (source + shift) % head_count)...  16.8 us
    dot_general x1, matrix products, on_device(): lax.dot_general(gathered.reshape(seq_rows, cotangent.shape[1]), out_weigh...  12.3 us
    pallas_call x1, Pallas kernels, band_attention(): pl.pallas_call(functools.partial(band_kernel, scale=scale), grid_spec=gri...  9.82 us
    ppermute x4, starting transfers between devices, passed_along(): lax.ppermute(value, axis, [(source, source + steps) for source in range(f...  9.08 us
    unnamed x28, local copies, waits for them, and re-layouts  8.6 us
  transfers between devices with their start and end apart: 14, of which 6 were waited for; matrix products, arithmetic and copies ran while one was open for 14% of the time, Pallas kernels for 11%

profile of v3, /device:TPU:0, one launch (start us, length us, event | category | flops | bytes accessed | tf_op | source)
XLA Modules:
  0.0 171.3 jit_solution(15018054279401785544)
XLA Ops:
  8.1 2.3 %copy.20 = bf16[256,2048]{0,1:T(8,128)(2,1)} copy(bf16[256,2048]{1,0:T(8,128)(2,1)} %k_ref.5) | data formatting | bytes 2097152 | tf_op args[1]
  10.3 1.3 copy.23
  11.7 1.4 fusion.3
  13.0 1.4 fusion.4
  15.2 3.0 %collective-permute-start = (bf16[128,4096]{1,0:T(8,128)(2,1)S(1)}, bf16[128,4096]{1,0:T(8,128)(2,1)}, u32[]{:S(2)}, u32[]{:S(2)}) collective-permute-start(bf16[128,4096]{1,0:T(8,128)(2,1)S(1)} %copy-done.10), channel_id=1, source_target_pairs={{0,1},{1,0},{2,3},{3,2},{4,5},{5,4},{6,7},{7,6},{8,9},{9,8},{10,11... | collective-permute-start | bytes 3145736 | tf_op jit(solution)/shard_map/ppermute | solution.py:277
  18.3 2.4 %collective-permute-start.1 = (bf16[256,2048]{1,0:T(8,128)(2,1)S(1)}, bf16[256,2048]{1,0:T(8,128)(2,1)}, u32[]{:S(2)}, u32[]{:S(2)}) collective-permute-start(bf16[256,2048]{1,0:T(8,128)(2,1)S(1)} %copy-done), channel_id=1, source_target_pairs={{0,2},{2,4},{4,6},{6,8},{8,10},{10,12},{12,14},{14,16},{16,18},{18... | collective-permute-start | bytes 3145736 | tf_op jit(solution)/shard_map/ppermute | solution.py:21
  20.7 4.1 %collective-permute-start.2 = (bf16[256,2048]{1,0:T(8,128)(2,1)S(1)}, bf16[256,2048]{1,0:T(8,128)(2,1)}, u32[]{:S(2)}, u32[]{:S(2)}) collective-permute-start(bf16[256,2048]{1,0:T(8,128)(2,1)S(1)} %copy-done.1), channel_id=1, source_target_pairs={{0,2},{2,4},{4,6},{6,8},{8,10},{10,12},{12,14},{14,16},{16,18},{18... | collective-permute-start | bytes 3145736 | tf_op jit(solution)/shard_map/ppermute | solution.py:21
  24.8 16.8 %collective-permute-done = bf16[128,4096]{1,0:T(8,128)(2,1)} collective-permute-done((bf16[128,4096]{1,0:T(8,128)(2,1)S(1)}, bf16[128,4096]{1,0:T(8,128)(2,1)}, u32[]{:S(2)}, u32[]{:S(2)}) %collective-permute-start) | collective-permute-done | bytes 1048608 | tf_op jit(solution)/shard_map/ppermute | solution.py:277
  41.5 4.1 %fusion.2 = bf16[2,128,4096]{2,1,0:T(8,128)(2,1)} fusion(s32[]{:T(128)S(6)} %select_n.49, bf16[1,128,4096]{2,1,0:T(8,128)(2,1)} %bitcast.1, bf16[1,128,4096]{2,1,0:T(8,128)(2,1)S(1)} %bitcast.74), kind=kLoop, calls=%fused_computation.7 | loop fusion | flops 3145728 | bytes 4194308 | tf_op jit(solution)/shard_map/stack | solution.py:282
  45.6 12.3 %convolution_convert_fusion.g_ref = bf16[256,2048]{1,0:T(8,128)(2,1)} fusion(bf16[256,4096]{1,0:T(8,128)(2,1)} %bitcast.73, bf16[2048,4096]{1,0:T(8,128)(2,1)} %param.9), kind=kOutput, calls=%fused_computation.4 | convolution fusion | flops 4295491584 | bytes 19922944 | tf_op jit(solution)/shard_map/dot_general | solution.py:284
  57.9 1.2 copy-done.3
  59.1 9.8 %shard_map.93 = (bf16[256,2048]{1,0:T(8,128)(2,1)}, bf16[256,2048]{1,0:T(8,128)(2,1)}, f32[256,2048]{1,0:T(8,128)}, f32[256,2048]{1,0:T(8,128)}, bf16[256,1024]{...) custom-call(s32[1]{0:T(128)} %bitcast.seq_ref, bf16[256,2048]{1,0:T(8,128)(2,1)S(1)} %copy-done.2, ...), custom_call_target="tpu_custom_call" | custom-call | flops 1879048192 | bytes 7340032 | tf_op jit(solution)/shard_map/pallas_call | solution.py:154
  70.5 4.4 %all-gather.2.cloned.1.call-done.kf_ref.vf_ref = bf16[1024,2048]{1,0:T(8,128)(2,1)} async-done(((bf16[64,2048]{1,0:T(8,128)(2,1)}), bf16[1024,2048]{1,0:T(8,128)(2,1)}) %all-gather.2.cloned.1.call-update) | async-done | bytes 4194320 | tf_op jit(solution)/shard_map/all_gather | solution.py:262
  75.0 1.2 copy-done.4
  76.2 8.9 %shard_map.94 = (bf16[256,2048]{1,0:T(8,128)(2,1)}, bf16[256,2048]{1,0:T(8,128)(2,1)}, f32[256,2048]{1,0:T(8,128)}, f32[256,2048]{1,0:T(8,128)}, f32[2,1024,512]{2,1,0:T(8,128)}) custom-call(s32[1]{0:T(128)} %bitcast.seq_ref, bf16[256,2048]{1,0:T(8,128)(2,1)S(1)} %copy-done.2, ...), custom_call_target="tpu_custom_call", output_to_operand_aliasing={{0}: (7, {}), {1}: (8, {}), {2}: (9, {}), {3}: (10, {})} | custom-call | flops 2348810240 | bytes 6029312 | tf_op jit(solution)/shard_map/pallas_call | solution.py:185
  85.1 2.7 %fusion.5 = bf16[2,2,2,2,64,512]{5,4,0,1,2,3:T(8,128)(2,1)} fusion(f32[2,2,2,2,2,64,512]{6,5,4,3,2,1,0:T(8,128)} %bitcast.71, s32[]{:T(128)S(6)} %select_n.52), kind=kLoop, calls=%fused_computation.16 | loop fusion | bytes 2097156 | tf_op jit(solution)/shard_map/convert_element_type | solution.py:46
  88.1 8.8 %shard_map.95 = (bf16[256,2048]{1,0:T(8,128)(2,1)}, bf16[256,2048]{1,0:T(8,128)(2,1)}, f32[256,2048]{1,0:T(8,128)}, f32[256,2048]{1,0:T(8,128)}, f32[2,1024,512]{2,1,0:T(8,128)}) custom-call(s32[1]{0:T(128)} %bitcast.seq_ref, bf16[256,2048]{1,0:T(8,128)(2,1)S(1)} %copy-done.2, ...), custom_call_target="tpu_custom_call", output_to_operand_aliasing={{0}: (7, {}), {1}: (8, {}), {2}: (9, {}), {3}: (10, {})} | custom-call | flops 2348810240 | bytes 6029312 | tf_op jit(solution)/shard_map/pallas_call | solution.py:185
  96.9 1.7 %fusion.6 = bf16[2,2,2,2,64,512]{5,4,0,1,3,2:T(8,128)(2,1)S(1)} fusion(f32[2,2,2,2,2,64,512]{6,5,4,3,2,1,0:T(8,128)} %bitcast.69, s32[]{:T(128)S(6)} %select_n.52), kind=kLoop, calls=%fused_computation.17 | loop fusion | bytes 2097156 | tf_op jit(solution)/shard_map/convert_element_type | solution.py:46
  99.0 2.4 %bitcast_add_fusion.1 = f32[2,2,2,2,64,512]{5,4,0,1,2,3:T(8,128)S(1)} fusion(bf16[2,2,2,2,64,512]{5,4,0,1,2,3:T(8,128)(2,1)} %collective-permute-done.5, f32[2,2,2,2,2,64,512]{6,5,4,3,2,1,0:T(8,128)} %bitcast.72, s32[]{:T(128)S(6)} %select_n.51), kind=kLoop, calls=%fused_computation.11 | loop fusion | flops 1048576 | bytes 5242884 | tf_op jit(solution)/shard_map/add | solution.py:48
  101.5 5.5 %collective-permute-start.6 = (bf16[2,2,2,64,512]{4,3,0,1,2:T(8,128)(2,1)S(1)}, bf16[2,2,2,64,512]{4,3,0,1,2:T(8,128)(2,1)S(1)}, u32[]{:S(2)}, u32[]{:S(2)}) collective-permute-start(bf16[2,2,2,64,512]{4,3,0,1,2:T(8,128)(2,1)S(1)} %fusion.7), channel_id=1, source_target_pairs={{0,4},{2,6},{4,0},{6,2},{8,12},{10,14},{12,8},{14,10},{16,20},{18,... | collective-permute-start | bytes 1572872 | tf_op jit(solution)/shard_map/ppermute | solution.py:45
  107.5 5.0 %collective-permute-start.10 = (bf16[2,2,2,64,512]{4,3,0,1,2:T(8,128)(2,1)S(1)}, bf16[2,2,2,64,512]{4,3,0,1,2:T(8,128)(2,1)S(1)}, u32[]{:S(2)}, u32[]{:S(2)}) collective-permute-start(bf16[2,2,2,64,512]{4,3,0,1,2:T(8,128)(2,1)S(1)} %fusion.8), channel_id=1, source_target_pairs={{0,8},{2,10},{4,12},{6,14},{8,0},{10,2},{12,4},{14,6},{16,24},{18,... | collective-permute-start | bytes 1572872 | tf_op jit(solution)/shard_map/ppermute | solution.py:45
  112.5 0.8 fusion.9.select_ref
  113.3 1.3 collective-permute-start.3
  114.6 1.3 collective-permute-start.4
  115.9 3.7 %collective-permute-done.6 = bf16[2,2,2,64,512]{4,3,0,1,2:T(8,128)(2,1)S(1)} collective-permute-done((bf16[2,2,2,64,512]{4,3,0,1,2:T(8,128)(2,1)S(1)}, bf16[2,2,2,64,512]{4,3,0,1,2:T(8,128)(2,1)S(1)}, u32[]{:S(2)}, u32[]{:S(2)}) %collective-permute-start.6) | collective-permute-done | bytes 524320 | tf_op jit(solution)/shard_map/ppermute | solution.py:45
  119.8 15.5 %collective-permute-start.7 = (bf16[2,2,64,512]{3,2,0,1:T(8,128)(2,1)S(1)}, bf16[2,2,64,512]{3,2,0,1:T(8,128)(2,1)S(1)}, u32[]{:S(2)}, u32[]{:S(2)}) collective-permute-start(bf16[2,2,64,512]{3,2,0,1:T(8,128)(2,1)S(1)} %fusion.10), channel_id=1, source_target_pairs={{0,8},{2,10},{4,12},{6,14},{8,0},{10,2},{12,4},{14,6},{16,24},{18,... | collective-permute-start | bytes 786440 | tf_op jit(solution)/shard_map/ppermute | solution.py:45
  135.5 2.5 %collective-permute-start.11 = (bf16[2,2,64,512]{3,2,0,1:T(8,128)(2,1)S(1)}, bf16[2,2,64,512]{3,2,0,1:T(8,128)(2,1)S(1)}, u32[]{:S(2)}, u32[]{:S(2)}) collective-permute-start(bf16[2,2,64,512]{3,2,0,1:T(8,128)(2,1)S(1)} %fusion.11), channel_id=1, source_target_pairs={{0,4},{2,6},{4,0},{6,2},{8,12},{10,14},{12,8},{14,10},{16,20},{18,... | collective-permute-start | bytes 786440 | tf_op jit(solution)/shard_map/ppermute | solution.py:45
  138.1 3.6 %collective-permute-done.7 = bf16[2,2,64,512]{3,2,0,1:T(8,128)(2,1)S(1)} collective-permute-done((bf16[2,2,64,512]{3,2,0,1:T(8,128)(2,1)S(1)}, bf16[2,2,64,512]{3,2,0,1:T(8,128)(2,1)S(1)}, u32[]{:S(2)}, u32[]{:S(2)}) %collective-permute-start.7) | collective-permute-done | bytes 262176 | tf_op jit(solution)/shard_map/ppermute | solution.py:45
  141.7 4.0 %collective-permute-start.8 = (bf16[2,64,512]{2,1,0:T(8,128)(2,1)S(1)}, bf16[2,64,512]{2,1,0:T(8,128)(2,1)S(1)}, u32[]{:S(2)}, u32[]{:S(2)}) collective-permute-start(bf16[2,64,512]{2,1,0:T(8,128)(2,1)S(1)} %fusion.16), channel_id=1, source_target_pairs={{0,16},{2,18},{4,20},{6,22},{8,24},{10,26},{12,28},{14,30},{16,0},... | collective-permute-start | bytes 393224 | tf_op jit(solution)/shard_map/ppermute | solution.py:45
  145.9 7.7 %collective-permute-done.8 = bf16[2,64,512]{2,1,0:T(8,128)(2,1)S(1)} collective-permute-done((bf16[2,64,512]{2,1,0:T(8,128)(2,1)S(1)}, bf16[2,64,512]{2,1,0:T(8,128)(2,1)S(1)}, u32[]{:S(2)}, u32[]{:S(2)}) %collective-permute-start.8) | collective-permute-done | bytes 131104 | tf_op jit(solution)/shard_map/ppermute | solution.py:45
  153.7 2.1 %collective-permute-done.12 = bf16[2,64,512]{2,1,0:T(8,128)(2,1)S(1)} collective-permute-done((bf16[2,64,512]{2,1,0:T(8,128)(2,1)S(1)}, bf16[2,64,512]{2,1,0:T(8,128)(2,1)S(1)}, u32[]{:S(2)}, u32[]{:S(2)}) %collective-permute-start.12) | collective-permute-done | bytes 131104 | tf_op jit(solution)/shard_map/ppermute | solution.py:45
  157.6 6.9 %shard_map.96 = (bf16[256,2048]{1,0:T(8,128)(2,1)}, bf16[256,2048]{1,0:T(8,128)(2,1)}) custom-call(f32[256,2048]{1,0:T(8,128)} %get-tuple-element.32.own_k_ref, f32[256,2048]{1,0:T(8,128)} %get-tuple-element.33.own_v_ref, bf16[256,1024]{1,0:T(8,128)(2,1)} %copy-done.11, bf16[256,1024]{1,0:T(8,128)(2,1)} %copy-done.12, ...), custom_call_target="tpu_custom_call" | custom-call | flops 67108864 | bytes 5242880 | tf_op jit(solution)/shard_map/pallas_call | solution.py:213
  (57 shorter events, 6.8 us)
Async XLA Ops:
  7.2 3.2 %copy-start.1 = (bf16[256,2048]{1,0:T(8,128)(2,1)S(1)}, bf16[256,2048]{1,0:T(8,128)(2,1)}, u32[]{:S(2)}) copy-start(bf16[256,2048]{1,0:T(8,128)(2,1)} %v_ref.5) | copy-start | bytes 3145732
  7.2 67.8 %all-gather.2.cloned.1.call-start = ((), (), s32[]{:S(2)}) async-start(), calls=%async_computation | async-start | bytes 4456448 | tf_op jit(solution)/shard_map/all_gather | solution.py:262
  10.3 4.9 %copy-start.10 = (bf16[128,4096]{1,0:T(8,128)(2,1)S(1)}, bf16[128,4096]{1,0:T(8,128)(2,1)}, u32[]{:S(2)}) copy-start(bf16[128,4096]{1,0:T(8,128)(2,1)} %param.10) | copy-start | bytes 3145732
  10.3 7.9 %copy-start = (bf16[256,2048]{1,0:T(8,128)(2,1)S(1)}, bf16[256,2048]{1,0:T(8,128)(2,1)}, u32[]{:S(2)}) copy-start(bf16[256,2048]{1,0:T(8,128)(2,1)} %k_ref.5) | copy-start | bytes 3145732
  15.2 26.3 %collective-permute-start = (bf16[128,4096]{1,0:T(8,128)(2,1)S(1)}, bf16[128,4096]{1,0:T(8,128)(2,1)}, u32[]{:S(2)}, u32[]{:S(2)}) collective-permute-start(bf16[128,4096]{1,0:T(8,128)(2,1)S(1)} %copy-done.10), channel_id=1, source_target_pairs={{0,1},{1,0},{2,3},{3,2},{4,5},{5,4},{6,7},{7,6},{8,9},{9,8},{10,11... | collective-permute-start | bytes 3145736 | tf_op jit(solution)/shard_map/ppermute | solution.py:277
  18.3 39.6 %collective-permute-start.1 = (bf16[256,2048]{1,0:T(8,128)(2,1)S(1)}, bf16[256,2048]{1,0:T(8,128)(2,1)}, u32[]{:S(2)}, u32[]{:S(2)}) collective-permute-start(bf16[256,2048]{1,0:T(8,128)(2,1)S(1)} %copy-done), channel_id=1, source_target_pairs={{0,2},{2,4},{4,6},{6,8},{8,10},{10,12},{12,14},{14,16},{16,18},{18... | collective-permute-start | bytes 3145736 | tf_op jit(solution)/shard_map/ppermute | solution.py:21
  20.7 37.2 %collective-permute-start.2 = (bf16[256,2048]{1,0:T(8,128)(2,1)S(1)}, bf16[256,2048]{1,0:T(8,128)(2,1)}, u32[]{:S(2)}, u32[]{:S(2)}) collective-permute-start(bf16[256,2048]{1,0:T(8,128)(2,1)S(1)} %copy-done.1), channel_id=1, source_target_pairs={{0,2},{2,4},{4,6},{6,8},{8,10},{10,12},{12,14},{14,16},{16,18},{18... | collective-permute-start | bytes 3145736 | tf_op jit(solution)/shard_map/ppermute | solution.py:21
  45.6 12.3 %copy-start.2 = (bf16[256,2048]{1,0:T(8,128)(2,1)S(1)}, bf16[256,2048]{1,0:T(8,128)(2,1)}, u32[]{:S(2)}) copy-start(bf16[256,2048]{1,0:T(8,128)(2,1)} %q_ref.5) | copy-start | bytes 3145732
  57.9 1.2 copy-start.3
  68.9 0.8 copy-start.5
  69.7 0.8 copy-start.7
  75.0 1.2 copy-start.4
  87.8 11.2 %collective-permute-start.5 = (bf16[2,2,2,2,64,512]{5,4,0,1,2,3:T(8,128)(2,1)}, bf16[2,2,2,2,64,512]{5,4,0,1,2,3:T(8,128)(2,1)}, u32[]{:S(2)}, u32[]{:S(2)}) collective-permute-start(bf16[2,2,2,2,64,512]{5,4,0,1,2,3:T(8,128)(2,1)} %fusion.5), channel_id=1, source_target_pairs={{0,2},{2,0},{4,6},{6,4},{8,10},{10,8},{12,14},{14,12},{16,18},{18,... | collective-permute-start | bytes 3145736 | tf_op jit(solution)/shard_map/ppermute | solution.py:45
  98.7 8.4 %collective-permute-start.9 = (bf16[2,2,2,2,64,512]{5,4,0,1,3,2:T(8,128)(2,1)S(1)}, bf16[2,2,2,2,64,512]{5,4,0,1,3,2:T(8,128)(2,1)S(1)}, u32[]{:S(2)}, u32[]{:S(2)}) collective-permute-start(bf16[2,2,2,2,64,512]{5,4,0,1,3,2:T(8,128)(2,1)S(1)} %fusion.6), channel_id=1, source_target_pairs={{0,2},{2,0},{4,6},{6,4},{8,10},{10,8},{12,14},{14,12},{16,18},{18,... | collective-permute-start | bytes 3145736 | tf_op jit(solution)/shard_map/ppermute | solution.py:45
  99.0 8.0 %copy-start.9 = (f32[2,1024,512]{2,1,0:T(8,128)S(1)}, f32[2,1024,512]{2,1,0:T(8,128)}, u32[]{:S(2)}) copy-start(f32[2,1024,512]{2,1,0:T(8,128)} %get-tuple-element.37) | copy-start | bytes 12582916
  101.5 11.8 %copy-start.8 = (bf16[256,1024]{1,0:T(8,128)(2,1)S(1)}, bf16[256,1024]{1,0:T(8,128)(2,1)}, u32[]{:S(2)}) copy-start(bf16[256,1024]{1,0:T(8,128)(2,1)} %copy-done.7) | copy-start | bytes 1572868
  101.5 13.1 %copy-start.6 = (bf16[256,1024]{1,0:T(8,128)(2,1)S(1)}, bf16[256,1024]{1,0:T(8,128)(2,1)}, u32[]{:S(2)}) copy-start(bf16[256,1024]{1,0:T(8,128)(2,1)} %copy-done.5) | copy-start | bytes 1572868
  101.5 18.1 %collective-permute-start.6 = (bf16[2,2,2,64,512]{4,3,0,1,2:T(8,128)(2,1)S(1)}, bf16[2,2,2,64,512]{4,3,0,1,2:T(8,128)(2,1)S(1)}, u32[]{:S(2)}, u32[]{:S(2)}) collective-permute-start(bf16[2,2,2,64,512]{4,3,0,1,2:T(8,128)(2,1)S(1)} %fusion.7), channel_id=1, source_target_pairs={{0,4},{2,6},{4,0},{6,2},{8,12},{10,14},{12,8},{14,10},{16,20},{18,... | collective-permute-start | bytes 1572872 | tf_op jit(solution)/shard_map/ppermute | solution.py:45
  107.5 27.8 %collective-permute-start.10 = (bf16[2,2,2,64,512]{4,3,0,1,2:T(8,128)(2,1)S(1)}, bf16[2,2,2,64,512]{4,3,0,1,2:T(8,128)(2,1)S(1)}, u32[]{:S(2)}, u32[]{:S(2)}) collective-permute-start(bf16[2,2,2,64,512]{4,3,0,1,2:T(8,128)(2,1)S(1)} %fusion.8), channel_id=1, source_target_pairs={{0,8},{2,10},{4,12},{6,14},{8,0},{10,2},{12,4},{14,6},{16,24},{18,... | collective-permute-start | bytes 1572872 | tf_op jit(solution)/shard_map/ppermute | solution.py:45
  113.3 43.3 %collective-permute-start.3 = (bf16[256,1024]{1,0:T(8,128)(2,1)S(1)}, bf16[256,1024]{1,0:T(8,128)(2,1)S(1)}, u32[]{:S(2)}, u32[]{:S(2)}) collective-permute-start(bf16[256,1024]{1,0:T(8,128)(2,1)S(1)} %copy-done.8), channel_id=1, source_target_pairs={{2,0},{4,2},{6,4},{8,6},{10,8},{12,10},{14,12},{16,14},{18,16},{20... | collective-permute-start | bytes 1572872 | tf_op jit(solution)/shard_map/ppermute | solution.py:21
  114.6 42.0 %collective-permute-start.4 = (bf16[256,1024]{1,0:T(8,128)(2,1)S(1)}, bf16[256,1024]{1,0:T(8,128)(2,1)S(1)}, u32[]{:S(2)}, u32[]{:S(2)}) collective-permute-start(bf16[256,1024]{1,0:T(8,128)(2,1)S(1)} %copy-done.6), channel_id=1, source_target_pairs={{2,0},{4,2},{6,4},{8,6},{10,8},{12,10},{14,12},{16,14},{18,16},{20... | collective-permute-start | bytes 1572872 | tf_op jit(solution)/shard_map/ppermute | solution.py:21
  119.8 21.8 %collective-permute-start.7 = (bf16[2,2,64,512]{3,2,0,1:T(8,128)(2,1)S(1)}, bf16[2,2,64,512]{3,2,0,1:T(8,128)(2,1)S(1)}, u32[]{:S(2)}, u32[]{:S(2)}) collective-permute-start(bf16[2,2,64,512]{3,2,0,1:T(8,128)(2,1)S(1)} %fusion.10), channel_id=1, source_target_pairs={{0,8},{2,10},{4,12},{6,14},{8,0},{10,2},{12,4},{14,6},{16,24},{18,... | collective-permute-start | bytes 786440 | tf_op jit(solution)/shard_map/ppermute | solution.py:45
  135.5 10.2 %collective-permute-start.11 = (bf16[2,2,64,512]{3,2,0,1:T(8,128)(2,1)S(1)}, bf16[2,2,64,512]{3,2,0,1:T(8,128)(2,1)S(1)}, u32[]{:S(2)}, u32[]{:S(2)}) collective-permute-start(bf16[2,2,64,512]{3,2,0,1:T(8,128)(2,1)S(1)} %fusion.11), channel_id=1, source_target_pairs={{0,4},{2,6},{4,0},{6,2},{8,12},{10,14},{12,8},{14,10},{16,20},{18,... | collective-permute-start | bytes 786440 | tf_op jit(solution)/shard_map/ppermute | solution.py:45
  141.7 11.9 %collective-permute-start.8 = (bf16[2,64,512]{2,1,0:T(8,128)(2,1)S(1)}, bf16[2,64,512]{2,1,0:T(8,128)(2,1)S(1)}, u32[]{:S(2)}, u32[]{:S(2)}) collective-permute-start(bf16[2,64,512]{2,1,0:T(8,128)(2,1)S(1)} %fusion.16), channel_id=1, source_target_pairs={{0,16},{2,18},{4,20},{6,22},{8,24},{10,26},{12,28},{14,30},{16,0},... | collective-permute-start | bytes 393224 | tf_op jit(solution)/shard_map/ppermute | solution.py:45
  145.9 10.0 %collective-permute-start.12 = (bf16[2,64,512]{2,1,0:T(8,128)(2,1)S(1)}, bf16[2,64,512]{2,1,0:T(8,128)(2,1)S(1)}, u32[]{:S(2)}, u32[]{:S(2)}) collective-permute-start(bf16[2,64,512]{2,1,0:T(8,128)(2,1)S(1)} %fusion.17), channel_id=1, source_target_pairs={{0,16},{2,18},{4,20},{6,22},{8,24},{10,26},{12,28},{14,30},{16,0},... | collective-permute-start | bytes 393224 | tf_op jit(solution)/shard_map/ppermute | solution.py:45
  156.6 0.8 copy-start.11
  156.6 1.0 copy-start.12
Sparse Core Ops, SparseCore 0:
  15.3 59.5 all-gather.1

commit v4 on v3

--- a/solution.py
+++ b/solution.py
@@ -291,7 +291,7 @@
     attention, query_grad, own_dk, own_dv, back_k, back_v = band_attention(
         seq_scalar, queries, keys, values, grad_out, prev_k, prev_v, head_pairs, head_dim, score_scale
     )
-    chunks = 2 if head_pairs % 2 == 0 else 1
+    chunks = 4 if head_pairs % 4 == 0 else (2 if head_pairs % 2 == 0 else 1)
     pairs = head_pairs // chunks
     outputs = (attention, query_grad, own_dk, own_dv)
     digests = []

time: 172 us -> 167 us (0.971)
  waiting for transfers between devices: 38.3 us -> 31.2 us
  Pallas kernels: 34.5 us -> 38.2 us
  other arithmetic: 9.61 us -> 7.27 us
  starting transfers between devices: 45.4 us -> 47.3 us
    ppermute x8 -> x16, waiting for transfers between devices: 17.1 us -> 11.9 us  [seq_reduce_scatter(): lax.ppermute(send.astype(jnp.bfloat16), 'seq', [(source, source ^ 1 << bi...]
    pallas_call x2 -> x4, Pallas kernels: 17.8 us -> 21.6 us  [fixed_attention(): pl.pallas_call(functools.partial(fixed_kernel, scale=scale, unused=len(ea...]
    unnamed x28 -> x22, local copies, waits for them, and re-layouts: 8.6 us -> 6.04 us
    add x6 -> x12, other arithmetic: 3.21 us -> 0.84 us  [seq_reduce_scatter(): held = keep + arrived.astype(jnp.float32)]
    ppermute x8 -> x16, starting transfers between devices: 33.2 us -> 34.9 us  [seq_reduce_scatter(): lax.ppermute(send.astype(jnp.bfloat16), 'seq', [(source, source ^ 1 << bi...]
    convert_element_type x8 -> x16, local copies, waits for them, and re-layouts: 4.73 us -> 5.6 us  [seq_reduce_scatter(): send.astype(jnp.bfloat16)]
  transfers between devices with their start and end apart: 14 -> 22, of which waited for: 6 -> 9; matrix products, arithmetic and copies ran while one was open for 14% -> 15% of each run, Pallas kernels for 11% -> 19%
where the time goes in v4:
time: 167 us; the launch traced here: 166 us
  starting transfers between devices  47.3 us (28%)
  Pallas kernels  38.2 us (23%)
  waiting for transfers between devices  31.2 us (19%)
  matrix products  15.1 us (9%)
  between operations  14.4 us (9%)
  local copies, waits for them, and re-layouts  12.5 us (7%)
  other arithmetic  7.27 us (4%)
    ppermute x16, starting transfers between devices, seq_reduce_scatter(): lax.ppermute(send.astype(jnp.bfloat16), 'seq', [(source, source ^ 1 << bi...  34.9 us
    pallas_call x4, Pallas kernels, fixed_attention(): pl.pallas_call(functools.partial(fixed_kernel, scale=scale, unused=len(ea...  21.6 us
    ppermute x1, waiting for transfers between devices, on_device(): lax.ppermute(cotangent, 'head', [(source, (source + shift) % head_count)...  15.9 us
    dot_general x1, matrix products, on_device(): lax.dot_general(gathered.reshape(seq_rows, cotangent.shape[1]), out_weigh...  12.3 us
    ppermute x16, waiting for transfers between devices, seq_reduce_scatter(): lax.ppermute(send.astype(jnp.bfloat16), 'seq', [(source, source ^ 1 << bi...  11.9 us
    pallas_call x1, Pallas kernels, band_attention(): pl.pallas_call(functools.partial(band_kernel, scale=scale), grid_spec=gri...  9.64 us
    ppermute x4, starting transfers between devices, passed_along(): lax.ppermute(value, axis, [(source, source + steps) for source in range(f...  9.26 us
    pallas_call x1, Pallas kernels, finalize(): pl.pallas_call(finalize_kernel, grid=(head_pairs,), in_specs=[wide, wide,...  6.9 us
  transfers between devices with their start and end apart: 22, of which 9 were waited for; matrix products, arithmetic and copies ran while one was open for 15% of the time, Pallas kernels for 19%

profile of v4, /device:TPU:0, one launch (start us, length us, event | category | flops | bytes accessed | tf_op | source)
XLA Modules:
  0.0 166.0 jit_solution(9663850762477169008)
XLA Ops:
  8.1 2.3 %copy.28 = bf16[256,2048]{0,1:T(8,128)(2,1)} copy(bf16[256,2048]{1,0:T(8,128)(2,1)} %k_ref.9) | data formatting | bytes 2097152 | tf_op args[1]
  10.3 1.3 copy.31
  11.7 1.4 fusion.3
  13.0 1.4 fusion.4
  15.2 3.0 %collective-permute-start = (bf16[128,4096]{1,0:T(8,128)(2,1)S(1)}, bf16[128,4096]{1,0:T(8,128)(2,1)}, u32[]{:S(2)}, u32[]{:S(2)}) collective-permute-start(bf16[128,4096]{1,0:T(8,128)(2,1)S(1)} %copy-done.9), channel_id=1, source_target_pairs={{0,1},{1,0},{2,3},{3,2},{4,5},{5,4},{6,7},{7,6},{8,9},{9,8},{10,11... | collective-permute-start | bytes 3145736 | tf_op jit(solution)/shard_map/ppermute | solution.py:277
  18.3 2.4 %collective-permute-start.1 = (bf16[256,2048]{1,0:T(8,128)(2,1)S(1)}, bf16[256,2048]{1,0:T(8,128)(2,1)}, u32[]{:S(2)}, u32[]{:S(2)}) collective-permute-start(bf16[256,2048]{1,0:T(8,128)(2,1)S(1)} %copy-done), channel_id=1, source_target_pairs={{0,2},{2,4},{4,6},{6,8},{8,10},{10,12},{12,14},{14,16},{16,18},{18... | collective-permute-start | bytes 3145736 | tf_op jit(solution)/shard_map/ppermute | solution.py:21
  20.7 4.1 %collective-permute-start.2 = (bf16[256,2048]{1,0:T(8,128)(2,1)S(1)}, bf16[256,2048]{1,0:T(8,128)(2,1)}, u32[]{:S(2)}, u32[]{:S(2)}) collective-permute-start(bf16[256,2048]{1,0:T(8,128)(2,1)S(1)} %copy-done.1), channel_id=1, source_target_pairs={{0,2},{2,4},{4,6},{6,8},{8,10},{10,12},{12,14},{14,16},{16,18},{18... | collective-permute-start | bytes 3145736 | tf_op jit(solution)/shard_map/ppermute | solution.py:21
  25.6 15.9 %collective-permute-done = bf16[128,4096]{1,0:T(8,128)(2,1)} collective-permute-done((bf16[128,4096]{1,0:T(8,128)(2,1)S(1)}, bf16[128,4096]{1,0:T(8,128)(2,1)}, u32[]{:S(2)}, u32[]{:S(2)}) %collective-permute-start) | collective-permute-done | bytes 1048608 | tf_op jit(solution)/shard_map/ppermute | solution.py:277
  41.5 4.1 %fusion.2 = bf16[2,128,4096]{2,1,0:T(8,128)(2,1)} fusion(s32[]{:T(128)S(6)} %select_n.65, bf16[1,128,4096]{2,1,0:T(8,128)(2,1)} %bitcast.1, bf16[1,128,4096]{2,1,0:T(8,128)(2,1)S(1)} %bitcast.116), kind=kLoop, calls=%fused_computation.7 | loop fusion | flops 3145728 | bytes 4194308 | tf_op jit(solution)/shard_map/stack | solution.py:282
  45.6 12.3 %convolution_convert_fusion.g_ref = bf16[256,2048]{1,0:T(8,128)(2,1)} fusion(bf16[256,4096]{1,0:T(8,128)(2,1)} %bitcast.107, bf16[2048,4096]{1,0:T(8,128)(2,1)} %param.9), kind=kOutput, calls=%fused_computation.4 | convolution fusion | flops 4295491584 | bytes 19922944 | tf_op jit(solution)/shard_map/dot_general | solution.py:284
  59.1 9.6 %shard_map.93 = (bf16[256,2048]{1,0:T(8,128)(2,1)}, bf16[256,2048]{1,0:T(8,128)(2,1)}, f32[256,2048]{1,0:T(8,128)}, f32[256,2048]{1,0:T(8,128)}, bf16[256,1024]{1,0:T(8,128)(2,1)}, /*index=5*/bf16[256,1024]{1,0:T(8,128)(2,1)}) custom-call(s32[1]{0:T(128)} %bitcast.seq_ref, bf16[256,2048]{1,0:T(8,128)(2,1)S(1)} %copy-done.2, bf16[256,2048]{1,0:T(8,128)(2,1)S(1)} %copy-done, ...), custom_call_target="tpu_custom_call" | custom-call | flops 1879048192 | bytes 7340032 | tf_op jit(solution)/shard_map/pallas_call | solution.py:154
  68.8 1.3 collective-permute-start.3
  70.1 1.5 collective-permute-start.4
  71.5 3.4 %all-gather.2.cloned.1.call-done.kf_ref.vf_ref = bf16[1024,2048]{1,0:T(8,128)(2,1)} async-done(((bf16[64,2048]{1,0:T(8,128)(2,1)}), bf16[1024,2048]{1,0:T(8,128)(2,1)}) %all-gather.2.cloned.1.call-update) | async-done | bytes 4194320 | tf_op jit(solution)/shard_map/all_gather | solution.py:262
  76.2 5.4 %shard_map.94 = (bf16[256,2048]{1,0:T(8,128)(2,1)}, bf16[256,2048]{1,0:T(8,128)(2,1)}, f32[256,2048]{1,0:T(8,128)}, f32[256,2048]{1,0:T(8,128)}, f32[2,1024,256]{2,1,0:T(8,128)}) custom-call(s32[1]{0:T(128)} %bitcast.seq_ref, bf16[256,2048]{1,0:T(8,128)(2,1)S(1)} %copy-done.2, ...), custom_call_target="tpu_custom_call", output_to_operand_aliasing={{0}: (7, {}), {1}: (8, {}), {2}: (9, {}), {3}: (10, {})} | custom-call | flops 1174405120 | bytes 3014656 | tf_op jit(solution)/shard_map/pallas_call | solution.py:185
  83.2 5.4 %shard_map.95 = (bf16[256,2048]{1,0:T(8,128)(2,1)}, bf16[256,2048]{1,0:T(8,128)(2,1)}, f32[256,2048]{1,0:T(8,128)}, f32[256,2048]{1,0:T(8,128)}, f32[2,1024,256]{2,1,0:T(8,128)}) custom-call(s32[1]{0:T(128)} %bitcast.seq_ref, bf16[256,2048]{1,0:T(8,128)(2,1)S(1)} %copy-done.2, ...), custom_call_target="tpu_custom_call", output_to_operand_aliasing={{0}: (7, {}), {1}: (8, {}), {2}: (9, {}), {3}: (10, {})} | custom-call | flops 1174405120 | bytes 3014656 | tf_op jit(solution)/shard_map/pallas_call | solution.py:185
  88.6 1.3 fusion.6
  90.2 5.4 %shard_map.96 = (bf16[256,2048]{1,0:T(8,128)(2,1)}, bf16[256,2048]{1,0:T(8,128)(2,1)}, f32[256,2048]{1,0:T(8,128)}, f32[256,2048]{1,0:T(8,128)}, f32[2,1024,256]{2,1,0:T(8,128)}) custom-call(s32[1]{0:T(128)} %bitcast.seq_ref, bf16[256,2048]{1,0:T(8,128)(2,1)S(1)} %copy-done.2, ...), custom_call_target="tpu_custom_call", output_to_operand_aliasing={{0}: (7, {}), {1}: (8, {}), {2}: (9, {}), {3}: (10, {})} | custom-call | flops 1174405120 | bytes 3014656 | tf_op jit(solution)/shard_map/pallas_call | solution.py:185
  97.2 5.5 %shard_map.97 = (bf16[256,2048]{1,0:T(8,128)(2,1)}, bf16[256,2048]{1,0:T(8,128)(2,1)}, f32[256,2048]{1,0:T(8,128)}, f32[256,2048]{1,0:T(8,128)}, f32[2,1024,256]{2,1,0:T(8,128)}) custom-call(s32[1]{0:T(128)} %bitcast.seq_ref, bf16[256,2048]{1,0:T(8,128)(2,1)S(1)} %copy-done.2, ...), custom_call_target="tpu_custom_call", output_to_operand_aliasing={{0}: (7, {}), {1}: (8, {}), {2}: (9, {}), {3}: (10, {})} | custom-call | flops 1174405120 | bytes 3014656 | tf_op jit(solution)/shard_map/pallas_call | solution.py:185
  102.7 1.4 fusion.8
  104.6 7.9 %collective-permute-start.6 = (bf16[2,2,2,64,256]{4,3,0,1,2:T(8,128)(2,1)S(1)}, bf16[2,2,2,64,256]{4,3,0,1,2:T(8,128)(2,1)S(1)}, u32[]{:S(2)}, u32[]{:S(2)}) collective-permute-start(bf16[2,2,2,64,256]{4,3,0,1,2:T(8,128)(2,1)S(1)} %fusion.10), channel_id=1, source_target_pairs={{0,4},{2,6},{4,0},{6,2},{8,12},{10,14},{12,8},{14,10},{16,20},{18,... | collective-permute-start | bytes 786440 | tf_op jit(solution)/shard_map/ppermute | solution.py:45
  112.7 5.0 %collective-permute-start.10 = (bf16[2,2,2,64,256]{4,3,0,1,2:T(8,128)(2,1)S(1)}, bf16[2,2,2,64,256]{4,3,0,1,2:T(8,128)(2,1)S(1)}, u32[]{:S(2)}, u32[]{:S(2)}) collective-permute-start(bf16[2,2,2,64,256]{4,3,0,1,2:T(8,128)(2,1)S(1)} %fusion.11), channel_id=1, source_target_pairs={{0,8},{2,10},{4,12},{6,14},{8,0},{10,2},{12,4},{14,6},{16,24},{18,... | collective-permute-start | bytes 786440 | tf_op jit(solution)/shard_map/ppermute | solution.py:45
  119.4 5.2 %collective-permute-start.18 = (bf16[2,2,2,64,256]{4,3,0,1,2:T(8,128)(2,1)S(1)}, bf16[2,2,2,64,256]{4,3,0,1,2:T(8,128)(2,1)S(1)}, u32[]{:S(2)}, u32[]{:S(2)}) collective-permute-start(bf16[2,2,2,64,256]{4,3,0,1,2:T(8,128)(2,1)S(1)} %fusion.13), channel_id=1, source_target_pairs={{0,8},{2,10},{4,12},{6,14},{8,0},{10,2},{12,4},{14,6},{16,24},{18,... | collective-permute-start | bytes 786440 | tf_op jit(solution)/shard_map/ppermute | solution.py:45
  124.7 1.4 collective-permute-start.7
  127.0 4.8 %collective-permute-done.18 = bf16[2,2,2,64,256]{4,3,0,1,2:T(8,128)(2,1)S(1)} collective-permute-done((bf16[2,2,2,64,256]{4,3,0,1,2:T(8,128)(2,1)S(1)}, bf16[2,2,2,64,256]{4,3,0,1,2:T(8,128)(2,1)S(1)}, u32[]{:S(2)}, u32[]{:S(2)}) %collective-permute-start.18) | collective-permute-done | bytes 262176 | tf_op jit(solution)/shard_map/ppermute | solution.py:45
  131.8 2.0 %collective-permute-start.15 = (bf16[2,2,64,256]{3,2,0,1:T(8,128)(2,1)S(1)}, bf16[2,2,64,256]{3,2,0,1:T(8,128)(2,1)S(1)}, u32[]{:S(2)}, u32[]{:S(2)}) collective-permute-start(bf16[2,2,64,256]{3,2,0,1:T(8,128)(2,1)S(1)} %fusion.18), channel_id=1, source_target_pairs={{0,8},{2,10},{4,12},{6,14},{8,0},{10,2},{12,4},{14,6},{16,24},{18,... | collective-permute-start | bytes 393224 | tf_op jit(solution)/shard_map/ppermute | solution.py:45
  134.6 1.9 %collective-permute-start.19 = (bf16[2,2,64,256]{3,2,0,1:T(8,128)(2,1)S(1)}, bf16[2,2,64,256]{3,2,0,1:T(8,128)(2,1)S(1)}, u32[]{:S(2)}, u32[]{:S(2)}) collective-permute-start(bf16[2,2,64,256]{3,2,0,1:T(8,128)(2,1)S(1)} %fusion.19), channel_id=1, source_target_pairs={{0,4},{2,6},{4,0},{6,2},{8,12},{10,14},{12,8},{14,10},{16,20},{18,... | collective-permute-start | bytes 393224 | tf_op jit(solution)/shard_map/ppermute | solution.py:45
  136.5 5.0 %collective-permute-start.8 = (bf16[2,64,256]{2,1,0:T(8,128)(2,1)S(1)}, bf16[2,64,256]{2,1,0:T(8,128)(2,1)S(1)}, u32[]{:S(2)}, u32[]{:S(2)}) collective-permute-start(bf16[2,64,256]{2,1,0:T(8,128)(2,1)S(1)} %fusion.24), channel_id=1, source_target_pairs={{0,16},{2,18},{4,20},{6,22},{8,24},{10,26},{12,28},{14,30},{16,0},... | collective-permute-start | bytes 196616 | tf_op jit(solution)/shard_map/ppermute | solution.py:45
  142.3 2.7 %collective-permute-start.16 = (bf16[2,64,256]{2,1,0:T(8,128)(2,1)S(1)}, bf16[2,64,256]{2,1,0:T(8,128)(2,1)S(1)}, u32[]{:S(2)}, u32[]{:S(2)}) collective-permute-start(bf16[2,64,256]{2,1,0:T(8,128)(2,1)S(1)} %fusion.26), channel_id=1, source_target_pairs={{0,16},{2,18},{4,20},{6,22},{8,24},{10,26},{12,28},{14,30},{16,0},... | collective-permute-start | bytes 196616 | tf_op jit(solution)/shard_map/ppermute | solution.py:45
  148.4 1.6 collective-permute-done.16
  150.1 1.4 collective-permute-done.20
  152.2 6.9 %shard_map.98 = (bf16[256,2048]{1,0:T(8,128)(2,1)}, bf16[256,2048]{1,0:T(8,128)(2,1)}) custom-call(f32[256,2048]{1,0:T(8,128)} %get-tuple-element.50.own_k_ref, f32[256,2048]{1,0:T(8,128)} %get-tuple-element.51.own_v_ref, bf16[256,1024]{1,0:T(8,128)(2,1)} %collective-permute-done.3.back_k_ref, bf16[256,1024]{1,0:T(8,128)(2,1)} %collective-permute-done.4.back_v_ref, ...), custom_call_target="tpu_custom_call" | custom-call | flops 67108864 | bytes 5242880 | tf_op jit(solution)/shard_map/pallas_call | solution.py:213
  (85 shorter events, 17.5 us)
Async XLA Ops:
  7.2 3.2 %copy-start.1 = (bf16[256,2048]{1,0:T(8,128)(2,1)S(1)}, bf16[256,2048]{1,0:T(8,128)(2,1)}, u32[]{:S(2)}) copy-start(bf16[256,2048]{1,0:T(8,128)(2,1)} %v_ref.9) | copy-start | bytes 3145732
  7.2 67.8 %all-gather.2.cloned.1.call-start = ((), (), s32[]{:S(2)}) async-start(), calls=%async_computation | async-start | bytes 4456448 | tf_op jit(solution)/shard_map/all_gather | solution.py:262
  10.3 4.9 %copy-start.9 = (bf16[128,4096]{1,0:T(8,128)(2,1)S(1)}, bf16[128,4096]{1,0:T(8,128)(2,1)}, u32[]{:S(2)}) copy-start(bf16[128,4096]{1,0:T(8,128)(2,1)} %param.10) | copy-start | bytes 3145732
  10.3 7.9 %copy-start = (bf16[256,2048]{1,0:T(8,128)(2,1)S(1)}, bf16[256,2048]{1,0:T(8,128)(2,1)}, u32[]{:S(2)}) copy-start(bf16[256,2048]{1,0:T(8,128)(2,1)} %k_ref.9) | copy-start | bytes 3145732
  15.2 26.3 %collective-permute-start = (bf16[128,4096]{1,0:T(8,128)(2,1)S(1)}, bf16[128,4096]{1,0:T(8,128)(2,1)}, u32[]{:S(2)}, u32[]{:S(2)}) collective-permute-start(bf16[128,4096]{1,0:T(8,128)(2,1)S(1)} %copy-done.9), channel_id=1, source_target_pairs={{0,1},{1,0},{2,3},{3,2},{4,5},{5,4},{6,7},{7,6},{8,9},{9,8},{10,11... | collective-permute-start | bytes 3145736 | tf_op jit(solution)/shard_map/ppermute | solution.py:277
  18.3 39.6 %collective-permute-start.1 = (bf16[256,2048]{1,0:T(8,128)(2,1)S(1)}, bf16[256,2048]{1,0:T(8,128)(2,1)}, u32[]{:S(2)}, u32[]{:S(2)}) collective-permute-start(bf16[256,2048]{1,0:T(8,128)(2,1)S(1)} %copy-done), channel_id=1, source_target_pairs={{0,2},{2,4},{4,6},{6,8},{8,10},{10,12},{12,14},{14,16},{16,18},{18... | collective-permute-start | bytes 3145736 | tf_op jit(solution)/shard_map/ppermute | solution.py:21
  20.7 37.2 %collective-permute-start.2 = (bf16[256,2048]{1,0:T(8,128)(2,1)S(1)}, bf16[256,2048]{1,0:T(8,128)(2,1)}, u32[]{:S(2)}, u32[]{:S(2)}) collective-permute-start(bf16[256,2048]{1,0:T(8,128)(2,1)S(1)} %copy-done.1), channel_id=1, source_target_pairs={{0,2},{2,4},{4,6},{6,8},{8,10},{10,12},{12,14},{14,16},{16,18},{18... | collective-permute-start | bytes 3145736 | tf_op jit(solution)/shard_map/ppermute | solution.py:21
  45.6 12.3 %copy-start.2 = (bf16[256,2048]{1,0:T(8,128)(2,1)S(1)}, bf16[256,2048]{1,0:T(8,128)(2,1)}, u32[]{:S(2)}) copy-start(bf16[256,2048]{1,0:T(8,128)(2,1)} %q_ref.9) | copy-start | bytes 3145732
  57.9 1.2 copy-start.3
  68.8 83.4 %collective-permute-start.3 = (bf16[256,1024]{1,0:T(8,128)(2,1)}, bf16[256,1024]{1,0:T(8,128)(2,1)}, u32[]{:S(2)}, u32[]{:S(2)}) collective-permute-start(bf16[256,1024]{1,0:T(8,128)(2,1)} %get-tuple-element.52), channel_id=1, source_target_pairs={{2,0},{4,2},{6,4},{8,6},{10,8},{12,10},{14,12},{16,14},{18,16},{20... | collective-permute-start | bytes 1572872 | tf_op jit(solution)/shard_map/ppermute | solution.py:21
  70.1 82.1 %collective-permute-start.4 = (bf16[256,1024]{1,0:T(8,128)(2,1)}, bf16[256,1024]{1,0:T(8,128)(2,1)}, u32[]{:S(2)}, u32[]{:S(2)}) collective-permute-start(bf16[256,1024]{1,0:T(8,128)(2,1)} %get-tuple-element.53), channel_id=1, source_target_pairs={{2,0},{4,2},{6,4},{8,6},{10,8},{12,10},{14,12},{16,14},{18,16},{20... | collective-permute-start | bytes 1572872 | tf_op jit(solution)/shard_map/ppermute | solution.py:21
  75.0 1.2 copy-start.4
  82.9 21.3 %collective-permute-start.5 = (bf16[2,2,2,2,64,256]{5,4,0,1,2,3:T(8,128)(2,1)S(1)}, bf16[2,2,2,2,64,256]{5,4,0,1,2,3:T(8,128)(2,1)S(1)}, u32[]{:S(2)}, u32[]{:S(2)}) collective-permute-start(bf16[2,2,2,2,64,256]{5,4,0,1,2,3:T(8,128)(2,1)S(1)} %fusion.5), channel_id=1, source_target_pairs={{0,2},{2,0},{4,6},{6,4},{8,10},{10,8},{12,14},{14,12},{16,18},{18,... | collective-permute-start | bytes 1572872 | tf_op jit(solution)/shard_map/ppermute | solution.py:45
  89.9 14.8 %collective-permute-start.9 = (bf16[2,2,2,2,64,256]{5,4,0,1,3,2:T(8,128)(2,1)S(1)}, bf16[2,2,2,2,64,256]{5,4,0,1,3,2:T(8,128)(2,1)S(1)}, u32[]{:S(2)}, u32[]{:S(2)}) collective-permute-start(bf16[2,2,2,2,64,256]{5,4,0,1,3,2:T(8,128)(2,1)S(1)} %fusion.6), channel_id=1, source_target_pairs={{0,2},{2,0},{4,6},{6,4},{8,10},{10,8},{12,14},{14,12},{16,18},{18,... | collective-permute-start | bytes 1572872 | tf_op jit(solution)/shard_map/ppermute | solution.py:45
  96.9 15.8 %collective-permute-start.13 = (bf16[2,2,2,2,64,256]{5,4,0,1,2,3:T(8,128)(2,1)S(1)}, bf16[2,2,2,2,64,256]{5,4,0,1,2,3:T(8,128)(2,1)S(1)}, u32[]{:S(2)}, u32[]{:S(2)}) collective-permute-start(bf16[2,2,2,2,64,256]{5,4,0,1,2,3:T(8,128)(2,1)S(1)} %fusion.7), channel_id=1, source_target_pairs={{0,2},{2,0},{4,6},{6,4},{8,10},{10,8},{12,14},{14,12},{16,18},{18,... | collective-permute-start | bytes 1572872 | tf_op jit(solution)/shard_map/ppermute | solution.py:45
  97.2 7.3 %copy-start.5 = (f32[2,1024,256]{2,1,0:T(8,128)S(1)}, f32[2,1024,256]{2,1,0:T(8,128)}, u32[]{:S(2)}) copy-start(f32[2,1024,256]{2,1,0:T(8,128)} %get-tuple-element.54) | copy-start | bytes 6291460
  102.7 9.8 %copy-start.6 = (f32[2,1024,256]{2,1,0:T(8,128)S(1)}, f32[2,1024,256]{2,1,0:T(8,128)}, u32[]{:S(2)}) copy-start(f32[2,1024,256]{2,1,0:T(8,128)} %get-tuple-element.55) | copy-start | bytes 6291460
  104.1 13.8 %collective-permute-start.17 = (bf16[2,2,2,2,64,256]{5,4,0,1,3,2:T(8,128)(2,1)S(1)}, bf16[2,2,2,2,64,256]{5,4,0,1,3,2:T(8,128)(2,1)S(1)}, u32[]{:S(2)}, u32[]{:S(2)}) collective-permute-start(bf16[2,2,2,2,64,256]{5,4,0,1,3,2:T(8,128)(2,1)S(1)} %fusion.8), channel_id=1, source_target_pairs={{0,2},{2,0},{4,6},{6,4},{8,10},{10,8},{12,14},{14,12},{16,18},{18,... | collective-permute-start | bytes 1572872 | tf_op jit(solution)/shard_map/ppermute | solution.py:45
  104.6 13.1 %copy-start.8 = (f32[2,1024,256]{2,1,0:T(8,128)S(1)}, f32[2,1024,256]{2,1,0:T(8,128)}, u32[]{:S(2)}) copy-start(f32[2,1024,256]{2,1,0:T(8,128)} %get-tuple-element.56) | copy-start | bytes 6291460
  104.6 14.8 %collective-permute-start.6 = (bf16[2,2,2,64,256]{4,3,0,1,2:T(8,128)(2,1)S(1)}, bf16[2,2,2,64,256]{4,3,0,1,2:T(8,128)(2,1)S(1)}, u32[]{:S(2)}, u32[]{:S(2)}) collective-permute-start(bf16[2,2,2,64,256]{4,3,0,1,2:T(8,128)(2,1)S(1)} %fusion.10), channel_id=1, source_target_pairs={{0,4},{2,6},{4,0},{6,2},{8,12},{10,14},{12,8},{14,10},{16,20},{18,... | collective-permute-start | bytes 786440 | tf_op jit(solution)/shard_map/ppermute | solution.py:45
  112.6 5.4 %copy-start.7 = (f32[2,1024,256]{2,1,0:T(8,128)S(1)}, f32[2,1024,256]{2,1,0:T(8,128)}, u32[]{:S(2)}) copy-start(f32[2,1024,256]{2,1,0:T(8,128)} %get-tuple-element.57) | copy-start | bytes 6291460
  112.7 12.0 %collective-permute-start.10 = (bf16[2,2,2,64,256]{4,3,0,1,2:T(8,128)(2,1)S(1)}, bf16[2,2,2,64,256]{4,3,0,1,2:T(8,128)(2,1)S(1)}, u32[]{:S(2)}, u32[]{:S(2)}) collective-permute-start(bf16[2,2,2,64,256]{4,3,0,1,2:T(8,128)(2,1)S(1)} %fusion.11), channel_id=1, source_target_pairs={{0,8},{2,10},{4,12},{6,14},{8,0},{10,2},{12,4},{14,6},{16,24},{18,... | collective-permute-start | bytes 786440 | tf_op jit(solution)/shard_map/ppermute | solution.py:45
  117.9 8.3 %collective-permute-start.14 = (bf16[2,2,2,64,256]{4,3,0,1,2:T(8,128)(2,1)S(1)}, bf16[2,2,2,64,256]{4,3,0,1,2:T(8,128)(2,1)S(1)}, u32[]{:S(2)}, u32[]{:S(2)}) collective-permute-start(bf16[2,2,2,64,256]{4,3,0,1,2:T(8,128)(2,1)S(1)} %fusion.12), channel_id=1, source_target_pairs={{0,4},{2,6},{4,0},{6,2},{8,12},{10,14},{12,8},{14,10},{16,20},{18,... | collective-permute-start | bytes 786440 | tf_op jit(solution)/shard_map/ppermute | solution.py:45
  119.4 12.4 %collective-permute-start.18 = (bf16[2,2,2,64,256]{4,3,0,1,2:T(8,128)(2,1)S(1)}, bf16[2,2,2,64,256]{4,3,0,1,2:T(8,128)(2,1)S(1)}, u32[]{:S(2)}, u32[]{:S(2)}) collective-permute-start(bf16[2,2,2,64,256]{4,3,0,1,2:T(8,128)(2,1)S(1)} %fusion.13), channel_id=1, source_target_pairs={{0,8},{2,10},{4,12},{6,14},{8,0},{10,2},{12,4},{14,6},{16,24},{18,... | collective-permute-start | bytes 786440 | tf_op jit(solution)/shard_map/ppermute | solution.py:45
  124.7 9.9 %collective-permute-start.7 = (bf16[2,2,64,256]{3,2,0,1:T(8,128)(2,1)S(1)}, bf16[2,2,64,256]{3,2,0,1:T(8,128)(2,1)S(1)}, u32[]{:S(2)}, u32[]{:S(2)}) collective-permute-start(bf16[2,2,64,256]{3,2,0,1:T(8,128)(2,1)S(1)} %fusion.16), channel_id=1, source_target_pairs={{0,8},{2,10},{4,12},{6,14},{8,0},{10,2},{12,4},{14,6},{16,24},{18,... | collective-permute-start | bytes 393224 | tf_op jit(solution)/shard_map/ppermute | solution.py:45
  126.2 10.3 %collective-permute-start.11 = (bf16[2,2,64,256]{3,2,0,1:T(8,128)(2,1)S(1)}, bf16[2,2,64,256]{3,2,0,1:T(8,128)(2,1)S(1)}, u32[]{:S(2)}, u32[]{:S(2)}) collective-permute-start(bf16[2,2,64,256]{3,2,0,1:T(8,128)(2,1)S(1)} %fusion.17), channel_id=1, source_target_pairs={{0,4},{2,6},{4,0},{6,2},{8,12},{10,14},{12,8},{14,10},{16,20},{18,... | collective-permute-start | bytes 393224 | tf_op jit(solution)/shard_map/ppermute | solution.py:45
  131.8 9.8 %collective-permute-start.15 = (bf16[2,2,64,256]{3,2,0,1:T(8,128)(2,1)S(1)}, bf16[2,2,64,256]{3,2,0,1:T(8,128)(2,1)S(1)}, u32[]{:S(2)}, u32[]{:S(2)}) collective-permute-start(bf16[2,2,64,256]{3,2,0,1:T(8,128)(2,1)S(1)} %fusion.18), channel_id=1, source_target_pairs={{0,8},{2,10},{4,12},{6,14},{8,0},{10,2},{12,4},{14,6},{16,24},{18,... | collective-permute-start | bytes 393224 | tf_op jit(solution)/shard_map/ppermute | solution.py:45
  134.6 7.8 %collective-permute-start.19 = (bf16[2,2,64,256]{3,2,0,1:T(8,128)(2,1)S(1)}, bf16[2,2,64,256]{3,2,0,1:T(8,128)(2,1)S(1)}, u32[]{:S(2)}, u32[]{:S(2)}) collective-permute-start(bf16[2,2,64,256]{3,2,0,1:T(8,128)(2,1)S(1)} %fusion.19), channel_id=1, source_target_pairs={{0,4},{2,6},{4,0},{6,2},{8,12},{10,14},{12,8},{14,10},{16,20},{18,... | collective-permute-start | bytes 393224 | tf_op jit(solution)/shard_map/ppermute | solution.py:45
  136.5 9.8 %collective-permute-start.8 = (bf16[2,64,256]{2,1,0:T(8,128)(2,1)S(1)}, bf16[2,64,256]{2,1,0:T(8,128)(2,1)S(1)}, u32[]{:S(2)}, u32[]{:S(2)}) collective-permute-start(bf16[2,64,256]{2,1,0:T(8,128)(2,1)S(1)} %fusion.24), channel_id=1, source_target_pairs={{0,16},{2,18},{4,20},{6,22},{8,24},{10,26},{12,28},{14,30},{16,0},... | collective-permute-start | bytes 196616 | tf_op jit(solution)/shard_map/ppermute | solution.py:45
  141.5 6.9 %collective-permute-start.12 = (bf16[2,64,256]{2,1,0:T(8,128)(2,1)S(1)}, bf16[2,64,256]{2,1,0:T(8,128)(2,1)S(1)}, u32[]{:S(2)}, u32[]{:S(2)}) collective-permute-start(bf16[2,64,256]{2,1,0:T(8,128)(2,1)S(1)} %fusion.25), channel_id=1, source_target_pairs={{0,16},{2,18},{4,20},{6,22},{8,24},{10,26},{12,28},{14,30},{16,0},... | collective-permute-start | bytes 196616 | tf_op jit(solution)/shard_map/ppermute | solution.py:45
  142.3 7.7 %collective-permute-start.16 = (bf16[2,64,256]{2,1,0:T(8,128)(2,1)S(1)}, bf16[2,64,256]{2,1,0:T(8,128)(2,1)S(1)}, u32[]{:S(2)}, u32[]{:S(2)}) collective-permute-start(bf16[2,64,256]{2,1,0:T(8,128)(2,1)S(1)} %fusion.26), channel_id=1, source_target_pairs={{0,16},{2,18},{4,20},{6,22},{8,24},{10,26},{12,28},{14,30},{16,0},... | collective-permute-start | bytes 196616 | tf_op jit(solution)/shard_map/ppermute | solution.py:45
  146.3 5.2 %collective-permute-start.20 = (bf16[2,64,256]{2,1,0:T(8,128)(2,1)S(1)}, bf16[2,64,256]{2,1,0:T(8,128)(2,1)S(1)}, u32[]{:S(2)}, u32[]{:S(2)}) collective-permute-start(bf16[2,64,256]{2,1,0:T(8,128)(2,1)S(1)} %fusion.27), channel_id=1, source_target_pairs={{0,16},{2,18},{4,20},{6,22},{8,24},{10,26},{12,28},{14,30},{16,0},... | collective-permute-start | bytes 196616 | tf_op jit(solution)/shard_map/ppermute | solution.py:45
Sparse Core Ops, SparseCore 0:
  15.3 59.5 all-gather.1

commit v5 on v4

--- a/solution.py
+++ b/solution.py
@@ -312,6 +312,7 @@
         )
         digests.append(seq_reduce_scatter(far_dkv, 1, chunk))
     attention, query_grad, own_dk, own_dv = outputs
+    back_k, back_v, attention = lax.optimization_barrier((back_k, back_v, attention))
     back_k, back_v = passed_along((back_k, back_v), "seq", -1)
     digest_dkv = jnp.concatenate(digests, 2) if chunks > 1 else digests[0]
     key_grad, value_grad = finalize(

time: 167 us -> 180 us (1.078)
  waiting for transfers between devices: 31.2 us -> 46.1 us
  starting transfers between devices: 47.3 us -> 42.6 us
  local copies, waits for them, and re-layouts: 12.5 us -> 15.1 us
    ppermute x16, waiting for transfers between devices: 11.9 us -> 25.7 us  [seq_reduce_scatter(): lax.ppermute(send.astype(jnp.bfloat16), 'seq', [(source, source ^ 1 << bi...]
    ppermute x16, starting transfers between devices: 34.9 us -> 30.5 us  [seq_reduce_scatter(): lax.ppermute(send.astype(jnp.bfloat16), 'seq', [(source, source ^ 1 << bi...]
    unnamed x22 -> x34, local copies, waits for them, and re-layouts: 6.04 us -> 8.64 us
  transfers between devices with their start and end apart: 22 -> 22, of which waited for: 9 -> 8; matrix products, arithmetic and copies ran while one was open for 15% -> 13% of each run, Pallas kernels for 19% -> 15%
where the time goes in v5:
time: 180 us; the launch traced here: 179 us
  waiting for transfers between devices  46.1 us (26%)
  starting transfers between devices  42.6 us (24%)
  Pallas kernels  38.4 us (21%)
  local copies, waits for them, and re-layouts  15.1 us (8%)
  matrix products  15.1 us (8%)
  between operations  14.5 us (8%)
  other arithmetic  7.33 us (4%)
    ppermute x16, starting transfers between devices, seq_reduce_scatter(): lax.ppermute(send.astype(jnp.bfloat16), 'seq', [(source, source ^ 1 << bi...  30.5 us
    ppermute x16, waiting for transfers between devices, seq_reduce_scatter(): lax.ppermute(send.astype(jnp.bfloat16), 'seq', [(source, source ^ 1 << bi...  25.7 us
    pallas_call x4, Pallas kernels, fixed_attention(): pl.pallas_call(functools.partial(fixed_kernel, scale=scale, unused=len(ea...  21.7 us
    ppermute x1, waiting for transfers between devices, on_device(): lax.ppermute(cotangent, 'head', [(source, (source + shift) % head_count)...  15.9 us
    dot_general x1, matrix products, on_device(): lax.dot_general(gathered.reshape(seq_rows, cotangent.shape[1]), out_weigh...  12.3 us
    pallas_call x1, Pallas kernels, band_attention(): pl.pallas_call(functools.partial(band_kernel, scale=scale), grid_spec=gri...  9.81 us
    ppermute x4, starting transfers between devices, passed_along(): lax.ppermute(value, axis, [(source, source + steps) for source in range(f...  9.03 us
    unnamed x34, local copies, waits for them, and re-layouts  8.64 us
  transfers between devices with their start and end apart: 22, of which 8 were waited for; matrix products, arithmetic and copies ran while one was open for 13% of the time, Pallas kernels for 15%

profile of v5, /device:TPU:0, one launch (start us, length us, event | category | flops | bytes accessed | tf_op | source)
XLA Modules:
  0.0 179.2 jit_solution(15653054780756470163)
XLA Ops:
  8.1 2.3 %copy.28 = bf16[256,2048]{0,1:T(8,128)(2,1)} copy(bf16[256,2048]{1,0:T(8,128)(2,1)} %k_ref.9) | data formatting | bytes 2097152 | tf_op args[1]
  10.3 1.3 copy.31
  11.7 1.4 fusion.3
  13.0 1.4 fusion.4
  15.3 3.0 %collective-permute-start = (bf16[128,4096]{1,0:T(8,128)(2,1)S(1)}, bf16[128,4096]{1,0:T(8,128)(2,1)}, u32[]{:S(2)}, u32[]{:S(2)}) collective-permute-start(bf16[128,4096]{1,0:T(8,128)(2,1)S(1)} %copy-done.13), channel_id=1, source_target_pairs={{0,1},{1,0},{2,3},{3,2},{4,5},{5,4},{6,7},{7,6},{8,9},{9,8},{10,11... | collective-permute-start | bytes 3145736 | tf_op jit(solution)/shard_map/ppermute | solution.py:277
  18.3 2.4 %collective-permute-start.1 = (bf16[256,2048]{1,0:T(8,128)(2,1)S(1)}, bf16[256,2048]{1,0:T(8,128)(2,1)}, u32[]{:S(2)}, u32[]{:S(2)}) collective-permute-start(bf16[256,2048]{1,0:T(8,128)(2,1)S(1)} %copy-done), channel_id=1, source_target_pairs={{0,2},{2,4},{4,6},{6,8},{8,10},{10,12},{12,14},{14,16},{16,18},{18... | collective-permute-start | bytes 3145736 | tf_op jit(solution)/shard_map/ppermute | solution.py:21
  20.7 4.0 %collective-permute-start.2 = (bf16[256,2048]{1,0:T(8,128)(2,1)S(1)}, bf16[256,2048]{1,0:T(8,128)(2,1)}, u32[]{:S(2)}, u32[]{:S(2)}) collective-permute-start(bf16[256,2048]{1,0:T(8,128)(2,1)S(1)} %copy-done.1), channel_id=1, source_target_pairs={{0,2},{2,4},{4,6},{6,8},{8,10},{10,12},{12,14},{14,16},{16,18},{18... | collective-permute-start | bytes 3145736 | tf_op jit(solution)/shard_map/ppermute | solution.py:21
  25.6 15.9 %collective-permute-done = bf16[128,4096]{1,0:T(8,128)(2,1)} collective-permute-done((bf16[128,4096]{1,0:T(8,128)(2,1)S(1)}, bf16[128,4096]{1,0:T(8,128)(2,1)}, u32[]{:S(2)}, u32[]{:S(2)}) %collective-permute-start) | collective-permute-done | bytes 1048608 | tf_op jit(solution)/shard_map/ppermute | solution.py:277
  41.6 4.0 %fusion.2 = bf16[2,128,4096]{2,1,0:T(8,128)(2,1)} fusion(s32[]{:T(128)S(6)} %select_n.65, bf16[1,128,4096]{2,1,0:T(8,128)(2,1)} %bitcast.1, bf16[1,128,4096]{2,1,0:T(8,128)(2,1)S(1)} %bitcast.116), kind=kLoop, calls=%fused_computation.7 | loop fusion | flops 3145728 | bytes 4194308 | tf_op jit(solution)/shard_map/stack | solution.py:282
  45.6 12.3 %convolution_convert_fusion.g_ref = bf16[256,2048]{1,0:T(8,128)(2,1)} fusion(bf16[256,4096]{1,0:T(8,128)(2,1)} %bitcast.107, bf16[2048,4096]{1,0:T(8,128)(2,1)} %param.9), kind=kOutput, calls=%fused_computation.4 | convolution fusion | flops 4295491584 | bytes 19922944 | tf_op jit(solution)/shard_map/dot_general | solution.py:284
  59.1 9.8 %shard_map.93 = (bf16[256,2048]{1,0:T(8,128)(2,1)}, bf16[256,2048]{1,0:T(8,128)(2,1)}, f32[256,2048]{1,0:T(8,128)}, f32[256,2048]{1,0:T(8,128)}, bf16[256,1024]{...) custom-call(s32[1]{0:T(128)} %bitcast.seq_ref, bf16[256,2048]{1,0:T(8,128)(2,1)S(1)} %copy-done.2, ...), custom_call_target="tpu_custom_call" | custom-call | flops 1879048192 | bytes 7340032 | tf_op jit(solution)/shard_map/pallas_call | solution.py:154
  70.5 4.4 %all-gather.2.cloned.1.call-done.kf_ref.vf_ref = bf16[1024,2048]{1,0:T(8,128)(2,1)} async-done(((bf16[64,2048]{1,0:T(8,128)(2,1)}), bf16[1024,2048]{1,0:T(8,128)(2,1)}) %all-gather.2.cloned.1.call-update) | async-done | bytes 4194320 | tf_op jit(solution)/shard_map/all_gather | solution.py:262
  76.2 5.4 %shard_map.94 = (bf16[256,2048]{1,0:T(8,128)(2,1)}, bf16[256,2048]{1,0:T(8,128)(2,1)}, f32[256,2048]{1,0:T(8,128)}, f32[256,2048]{1,0:T(8,128)}, f32[2,1024,256]{2,1,0:T(8,128)}) custom-call(s32[1]{0:T(128)} %bitcast.seq_ref, bf16[256,2048]{1,0:T(8,128)(2,1)S(1)} %copy-done.2, ...), custom_call_target="tpu_custom_call", output_to_operand_aliasing={{0}: (7, {}), {1}: (8, {}), {2}: (9, {}), {3}: (10, {})} | custom-call | flops 1174405120 | bytes 3014656 | tf_op jit(solution)/shard_map/pallas_call | solution.py:185
  83.2 5.4 %shard_map.95 = (bf16[256,2048]{1,0:T(8,128)(2,1)}, bf16[256,2048]{1,0:T(8,128)(2,1)}, f32[256,2048]{1,0:T(8,128)}, f32[256,2048]{1,0:T(8,128)}, f32[2,1024,256]{2,1,0:T(8,128)}) custom-call(s32[1]{0:T(128)} %bitcast.seq_ref, bf16[256,2048]{1,0:T(8,128)(2,1)S(1)} %copy-done.2, ...), custom_call_target="tpu_custom_call", output_to_operand_aliasing={{0}: (7, {}), {1}: (8, {}), {2}: (9, {}), {3}: (10, {})} | custom-call | flops 1174405120 | bytes 3014656 | tf_op jit(solution)/shard_map/pallas_call | solution.py:185
  90.2 5.4 %shard_map.96 = (bf16[256,2048]{1,0:T(8,128)(2,1)}, bf16[256,2048]{1,0:T(8,128)(2,1)}, f32[256,2048]{1,0:T(8,128)}, f32[256,2048]{1,0:T(8,128)}, f32[2,1024,256]{2,1,0:T(8,128)}) custom-call(s32[1]{0:T(128)} %bitcast.seq_ref, bf16[256,2048]{1,0:T(8,128)(2,1)S(1)} %copy-done.2, ...), custom_call_target="tpu_custom_call", output_to_operand_aliasing={{0}: (7, {}), {1}: (8, {}), {2}: (9, {}), {3}: (10, {})} | custom-call | flops 1174405120 | bytes 3014656 | tf_op jit(solution)/shard_map/pallas_call | solution.py:185
  97.2 5.6 %shard_map.97 = (bf16[256,2048]{1,0:T(8,128)(2,1)}, bf16[256,2048]{1,0:T(8,128)(2,1)}, f32[256,2048]{1,0:T(8,128)}, f32[256,2048]{1,0:T(8,128)}, f32[2,1024,256]{2,1,0:T(8,128)}) custom-call(s32[1]{0:T(128)} %bitcast.seq_ref, bf16[256,2048]{1,0:T(8,128)(2,1)S(1)} %copy-done.2, ...), custom_call_target="tpu_custom_call", output_to_operand_aliasing={{0}: (7, {}), {1}: (8, {}), {2}: (9, {}), {3}: (10, {})} | custom-call | flops 1174405120 | bytes 3014656 | tf_op jit(solution)/shard_map/pallas_call | solution.py:185
  102.8 1.4 fusion.8
  105.9 1.3 collective-permute-start.4
  107.4 6.8 %collective-permute-start.6 = (bf16[2,2,2,64,256]{4,3,0,1,2:T(8,128)(2,1)S(1)}, bf16[2,2,2,64,256]{4,3,0,1,2:T(8,128)(2,1)S(1)}, u32[]{:S(2)}, u32[]{:S(2)}) collective-permute-start(bf16[2,2,2,64,256]{4,3,0,1,2:T(8,128)(2,1)S(1)} %fusion.10), channel_id=1, source_target_pairs={{0,4},{2,6},{4,0},{6,2},{8,12},{10,14},{12,8},{14,10},{16,20},{18,... | collective-permute-start | bytes 786440 | tf_op jit(solution)/shard_map/ppermute | solution.py:45
  114.4 5.0 %collective-permute-start.10 = (bf16[2,2,2,64,256]{4,3,0,1,2:T(8,128)(2,1)S(1)}, bf16[2,2,2,64,256]{4,3,0,1,2:T(8,128)(2,1)S(1)}, u32[]{:S(2)}, u32[]{:S(2)}) collective-permute-start(bf16[2,2,2,64,256]{4,3,0,1,2:T(8,128)(2,1)S(1)} %fusion.11), channel_id=1, source_target_pairs={{0,8},{2,10},{4,12},{6,14},{8,0},{10,2},{12,4},{14,6},{16,24},{18,... | collective-permute-start | bytes 786440 | tf_op jit(solution)/shard_map/ppermute | solution.py:45
  119.9 13.3 %collective-permute-done.6 = bf16[2,2,2,64,256]{4,3,0,1,2:T(8,128)(2,1)S(1)} collective-permute-done((bf16[2,2,2,64,256]{4,3,0,1,2:T(8,128)(2,1)S(1)}, bf16[2,2,2,64,256]{4,3,0,1,2:T(8,128)(2,1)S(1)}, u32[]{:S(2)}, u32[]{:S(2)}) %collective-permute-start.6) | collective-permute-done | bytes 262176 | tf_op jit(solution)/shard_map/ppermute | solution.py:45
  133.1 4.9 %collective-permute-start.18 = (bf16[2,2,2,64,256]{4,3,0,1,2:T(8,128)(2,1)S(1)}, bf16[2,2,2,64,256]{4,3,0,1,2:T(8,128)(2,1)S(1)}, u32[]{:S(2)}, u32[]{:S(2)}) collective-permute-start(bf16[2,2,2,64,256]{4,3,0,1,2:T(8,128)(2,1)S(1)} %fusion.13), channel_id=1, source_target_pairs={{0,8},{2,10},{4,12},{6,14},{8,0},{10,2},{12,4},{14,6},{16,24},{18,... | collective-permute-start | bytes 786440 | tf_op jit(solution)/shard_map/ppermute | solution.py:45
  138.3 1.4 collective-permute-start.11
  139.8 4.7 %collective-permute-done.18 = bf16[2,2,2,64,256]{4,3,0,1,2:T(8,128)(2,1)S(1)} collective-permute-done((bf16[2,2,2,64,256]{4,3,0,1,2:T(8,128)(2,1)S(1)}, bf16[2,2,2,64,256]{4,3,0,1,2:T(8,128)(2,1)S(1)}, u32[]{:S(2)}, u32[]{:S(2)}) %collective-permute-start.18) | collective-permute-done | bytes 262176 | tf_op jit(solution)/shard_map/ppermute | solution.py:45
  144.5 1.7 collective-permute-start.15
  146.4 2.6 %collective-permute-start.19 = (bf16[2,2,64,256]{3,2,0,1:T(8,128)(2,1)S(1)}, bf16[2,2,64,256]{3,2,0,1:T(8,128)(2,1)S(1)}, u32[]{:S(2)}, u32[]{:S(2)}) collective-permute-start(bf16[2,2,64,256]{3,2,0,1:T(8,128)(2,1)S(1)} %fusion.19), channel_id=1, source_target_pairs={{0,4},{2,6},{4,0},{6,2},{8,12},{10,14},{12,8},{14,10},{16,20},{18,... | collective-permute-start | bytes 393224 | tf_op jit(solution)/shard_map/ppermute | solution.py:45
  149.0 3.6 %collective-permute-start.8 = (bf16[2,64,256]{2,1,0:T(8,128)(2,1)S(1)}, bf16[2,64,256]{2,1,0:T(8,128)(2,1)S(1)}, u32[]{:S(2)}, u32[]{:S(2)}) collective-permute-start(bf16[2,64,256]{2,1,0:T(8,128)(2,1)S(1)} %fusion.24), channel_id=1, source_target_pairs={{0,16},{2,18},{4,20},{6,22},{8,24},{10,26},{12,28},{14,30},{16,0},... | collective-permute-start | bytes 196616 | tf_op jit(solution)/shard_map/ppermute | solution.py:45
  154.0 1.8 collective-permute-start.16
  155.9 2.6 %collective-permute-done.8 = bf16[2,64,256]{2,1,0:T(8,128)(2,1)S(1)} collective-permute-done((bf16[2,64,256]{2,1,0:T(8,128)(2,1)S(1)}, bf16[2,64,256]{2,1,0:T(8,128)(2,1)S(1)}, u32[]{:S(2)}, u32[]{:S(2)}) %collective-permute-start.8) | collective-permute-done | bytes 65568 | tf_op jit(solution)/shard_map/ppermute | solution.py:45
  158.5 2.1 %collective-permute-done.12 = bf16[2,64,256]{2,1,0:T(8,128)(2,1)S(1)} collective-permute-done((bf16[2,64,256]{2,1,0:T(8,128)(2,1)S(1)}, bf16[2,64,256]{2,1,0:T(8,128)(2,1)S(1)}, u32[]{:S(2)}, u32[]{:S(2)}) %collective-permute-start.12) | collective-permute-done | bytes 65568 | tf_op jit(solution)/shard_map/ppermute | solution.py:45
  161.4 2.3 %collective-permute-done.20 = bf16[2,64,256]{2,1,0:T(8,128)(2,1)S(1)} collective-permute-done((bf16[2,64,256]{2,1,0:T(8,128)(2,1)S(1)}, bf16[2,64,256]{2,1,0:T(8,128)(2,1)S(1)}, u32[]{:S(2)}, u32[]{:S(2)}) %collective-permute-start.20) | collective-permute-done | bytes 65568 | tf_op jit(solution)/shard_map/ppermute | solution.py:45
  165.5 6.9 %shard_map.98 = (bf16[256,2048]{1,0:T(8,128)(2,1)}, bf16[256,2048]{1,0:T(8,128)(2,1)}) custom-call(f32[256,2048]{1,0:T(8,128)} %get-tuple-element.56.own_k_ref, f32[256,2048]{1,0:T(8,128)} %get-tuple-element.57.own_v_ref, bf16[256,1024]{1,0:T(8,128)(2,1)} %copy-done.14, bf16[256,1024]{1,0:T(8,128)(2,1)} %copy-done.15, ...), custom_call_target="tpu_custom_call" | custom-call | flops 67108864 | bytes 5242880 | tf_op jit(solution)/shard_map/pallas_call | solution.py:213
  (97 shorter events, 18.2 us)
Async XLA Ops:
  7.2 3.2 %copy-start.1 = (bf16[256,2048]{1,0:T(8,128)(2,1)S(1)}, bf16[256,2048]{1,0:T(8,128)(2,1)}, u32[]{:S(2)}) copy-start(bf16[256,2048]{1,0:T(8,128)(2,1)} %v_ref.9) | copy-start | bytes 3145732
  7.2 67.8 %all-gather.2.cloned.1.call-start = ((), (), s32[]{:S(2)}) async-start(), calls=%async_computation | async-start | bytes 4456448 | tf_op jit(solution)/shard_map/all_gather | solution.py:262
  10.3 4.9 %copy-start.13 = (bf16[128,4096]{1,0:T(8,128)(2,1)S(1)}, bf16[128,4096]{1,0:T(8,128)(2,1)}, u32[]{:S(2)}) copy-start(bf16[128,4096]{1,0:T(8,128)(2,1)} %param.10) | copy-start | bytes 3145732
  10.3 7.9 %copy-start = (bf16[256,2048]{1,0:T(8,128)(2,1)S(1)}, bf16[256,2048]{1,0:T(8,128)(2,1)}, u32[]{:S(2)}) copy-start(bf16[256,2048]{1,0:T(8,128)(2,1)} %k_ref.9) | copy-start | bytes 3145732
  15.3 26.3 %collective-permute-start = (bf16[128,4096]{1,0:T(8,128)(2,1)S(1)}, bf16[128,4096]{1,0:T(8,128)(2,1)}, u32[]{:S(2)}, u32[]{:S(2)}) collective-permute-start(bf16[128,4096]{1,0:T(8,128)(2,1)S(1)} %copy-done.13), channel_id=1, source_target_pairs={{0,1},{1,0},{2,3},{3,2},{4,5},{5,4},{6,7},{7,6},{8,9},{9,8},{10,11... | collective-permute-start | bytes 3145736 | tf_op jit(solution)/shard_map/ppermute | solution.py:277
  18.3 39.6 %collective-permute-start.1 = (bf16[256,2048]{1,0:T(8,128)(2,1)S(1)}, bf16[256,2048]{1,0:T(8,128)(2,1)}, u32[]{:S(2)}, u32[]{:S(2)}) collective-permute-start(bf16[256,2048]{1,0:T(8,128)(2,1)S(1)} %copy-done), channel_id=1, source_target_pairs={{0,2},{2,4},{4,6},{6,8},{8,10},{10,12},{12,14},{14,16},{16,18},{18... | collective-permute-start | bytes 3145736 | tf_op jit(solution)/shard_map/ppermute | solution.py:21
  20.7 37.2 %collective-permute-start.2 = (bf16[256,2048]{1,0:T(8,128)(2,1)S(1)}, bf16[256,2048]{1,0:T(8,128)(2,1)}, u32[]{:S(2)}, u32[]{:S(2)}) collective-permute-start(bf16[256,2048]{1,0:T(8,128)(2,1)S(1)} %copy-done.1), channel_id=1, source_target_pairs={{0,2},{2,4},{4,6},{6,8},{8,10},{10,12},{12,14},{14,16},{16,18},{18... | collective-permute-start | bytes 3145736 | tf_op jit(solution)/shard_map/ppermute | solution.py:21
  45.6 12.3 %copy-start.2 = (bf16[256,2048]{1,0:T(8,128)(2,1)S(1)}, bf16[256,2048]{1,0:T(8,128)(2,1)}, u32[]{:S(2)}) copy-start(bf16[256,2048]{1,0:T(8,128)(2,1)} %q_ref.9) | copy-start | bytes 3145732
  82.9 23.0 %collective-permute-start.5 = (bf16[2,2,2,2,64,256]{5,4,0,1,2,3:T(8,128)(2,1)S(1)}, bf16[2,2,2,2,64,256]{5,4,0,1,2,3:T(8,128)(2,1)S(1)}, u32[]{:S(2)}, u32[]{:S(2)}) collective-permute-start(bf16[2,2,2,2,64,256]{5,4,0,1,2,3:T(8,128)(2,1)S(1)} %fusion.5), channel_id=1, source_target_pairs={{0,2},{2,0},{4,6},{6,4},{8,10},{10,8},{12,14},{14,12},{16,18},{18,... | collective-permute-start | bytes 1572872 | tf_op jit(solution)/shard_map/ppermute | solution.py:45
  89.9 17.5 %collective-permute-start.9 = (bf16[2,2,2,2,64,256]{5,4,0,1,3,2:T(8,128)(2,1)S(1)}, bf16[2,2,2,2,64,256]{5,4,0,1,3,2:T(8,128)(2,1)S(1)}, u32[]{:S(2)}, u32[]{:S(2)}) collective-permute-start(bf16[2,2,2,2,64,256]{5,4,0,1,3,2:T(8,128)(2,1)S(1)} %fusion.6), channel_id=1, source_target_pairs={{0,2},{2,0},{4,6},{6,4},{8,10},{10,8},{12,14},{14,12},{16,18},{18,... | collective-permute-start | bytes 1572872 | tf_op jit(solution)/shard_map/ppermute | solution.py:45
  96.9 17.5 %collective-permute-start.13 = (bf16[2,2,2,2,64,256]{5,4,0,1,2,3:T(8,128)(2,1)S(1)}, bf16[2,2,2,2,64,256]{5,4,0,1,2,3:T(8,128)(2,1)S(1)}, u32[]{:S(2)}, u32[]{:S(2)}) collective-permute-start(bf16[2,2,2,2,64,256]{5,4,0,1,2,3:T(8,128)(2,1)S(1)} %fusion.7), channel_id=1, source_target_pairs={{0,2},{2,0},{4,6},{6,4},{8,10},{10,8},{12,14},{14,12},{16,18},{18,... | collective-permute-start | bytes 1572872 | tf_op jit(solution)/shard_map/ppermute | solution.py:45
  97.2 7.4 %copy-start.8 = (bf16[256,1024]{1,0:T(8,128)(2,1)S(1)}, bf16[256,1024]{1,0:T(8,128)(2,1)}, u32[]{:S(2)}) copy-start(bf16[256,1024]{1,0:T(8,128)(2,1)} %copy-done.7) | copy-start | bytes 1572868
  97.2 8.7 %copy-start.6 = (bf16[256,1024]{1,0:T(8,128)(2,1)S(1)}, bf16[256,1024]{1,0:T(8,128)(2,1)}, u32[]{:S(2)}) copy-start(bf16[256,1024]{1,0:T(8,128)(2,1)} %copy-done.5) | copy-start | bytes 1572868
  97.2 10.0 %copy-start.9 = (f32[2,1024,256]{2,1,0:T(8,128)S(1)}, f32[2,1024,256]{2,1,0:T(8,128)}, u32[]{:S(2)}) copy-start(f32[2,1024,256]{2,1,0:T(8,128)} %get-tuple-element.60) | copy-start | bytes 6291460
  102.8 11.4 %copy-start.10 = (f32[2,1024,256]{2,1,0:T(8,128)S(1)}, f32[2,1024,256]{2,1,0:T(8,128)}, u32[]{:S(2)}) copy-start(f32[2,1024,256]{2,1,0:T(8,128)} %get-tuple-element.61) | copy-start | bytes 6291460
  104.2 15.3 %collective-permute-start.17 = (bf16[2,2,2,2,64,256]{5,4,0,1,3,2:T(8,128)(2,1)S(1)}, bf16[2,2,2,2,64,256]{5,4,0,1,3,2:T(8,128)(2,1)S(1)}, u32[]{:S(2)}, u32[]{:S(2)}) collective-permute-start(bf16[2,2,2,2,64,256]{5,4,0,1,3,2:T(8,128)(2,1)S(1)} %fusion.8), channel_id=1, source_target_pairs={{0,2},{2,0},{4,6},{6,4},{8,10},{10,8},{12,14},{14,12},{16,18},{18,... | collective-permute-start | bytes 1572872 | tf_op jit(solution)/shard_map/ppermute | solution.py:45
  104.6 59.9 %collective-permute-start.3 = (bf16[256,1024]{1,0:T(8,128)(2,1)S(1)}, bf16[256,1024]{1,0:T(8,128)(2,1)S(1)}, u32[]{:S(2)}, u32[]{:S(2)}) collective-permute-start(bf16[256,1024]{1,0:T(8,128)(2,1)S(1)} %copy-done.8), channel_id=1, source_target_pairs={{2,0},{4,2},{6,4},{8,6},{10,8},{12,10},{14,12},{16,14},{18,16},{20... | collective-permute-start | bytes 1572872 | tf_op jit(solution)/shard_map/ppermute | solution.py:21
  105.9 58.6 %collective-permute-start.4 = (bf16[256,1024]{1,0:T(8,128)(2,1)S(1)}, bf16[256,1024]{1,0:T(8,128)(2,1)S(1)}, u32[]{:S(2)}, u32[]{:S(2)}) collective-permute-start(bf16[256,1024]{1,0:T(8,128)(2,1)S(1)} %copy-done.6), channel_id=1, source_target_pairs={{2,0},{4,2},{6,4},{8,6},{10,8},{12,10},{14,12},{16,14},{18,16},{20... | collective-permute-start | bytes 1572872 | tf_op jit(solution)/shard_map/ppermute | solution.py:21
  107.3 12.1 %copy-start.12 = (f32[2,1024,256]{2,1,0:T(8,128)S(1)}, f32[2,1024,256]{2,1,0:T(8,128)}, u32[]{:S(2)}) copy-start(f32[2,1024,256]{2,1,0:T(8,128)} %get-tuple-element.62) | copy-start | bytes 6291460
  107.4 25.7 %collective-permute-start.6 = (bf16[2,2,2,64,256]{4,3,0,1,2:T(8,128)(2,1)S(1)}, bf16[2,2,2,64,256]{4,3,0,1,2:T(8,128)(2,1)S(1)}, u32[]{:S(2)}, u32[]{:S(2)}) collective-permute-start(bf16[2,2,2,64,256]{4,3,0,1,2:T(8,128)(2,1)S(1)} %fusion.10), channel_id=1, source_target_pairs={{0,4},{2,6},{4,0},{6,2},{8,12},{10,14},{12,8},{14,10},{16,20},{18,... | collective-permute-start | bytes 786440 | tf_op jit(solution)/shard_map/ppermute | solution.py:45
  114.3 5.4 %copy-start.11 = (f32[2,1024,256]{2,1,0:T(8,128)S(1)}, f32[2,1024,256]{2,1,0:T(8,128)}, u32[]{:S(2)}) copy-start(f32[2,1024,256]{2,1,0:T(8,128)} %get-tuple-element.63) | copy-start | bytes 6291460
  114.4 23.8 %collective-permute-start.10 = (bf16[2,2,2,64,256]{4,3,0,1,2:T(8,128)(2,1)S(1)}, bf16[2,2,2,64,256]{4,3,0,1,2:T(8,128)(2,1)S(1)}, u32[]{:S(2)}, u32[]{:S(2)}) collective-permute-start(bf16[2,2,2,64,256]{4,3,0,1,2:T(8,128)(2,1)S(1)} %fusion.11), channel_id=1, source_target_pairs={{0,8},{2,10},{4,12},{6,14},{8,0},{10,2},{12,4},{14,6},{16,24},{18,... | collective-permute-start | bytes 786440 | tf_op jit(solution)/shard_map/ppermute | solution.py:45
  119.6 18.8 %collective-permute-start.14 = (bf16[2,2,2,64,256]{4,3,0,1,2:T(8,128)(2,1)S(1)}, bf16[2,2,2,64,256]{4,3,0,1,2:T(8,128)(2,1)S(1)}, u32[]{:S(2)}, u32[]{:S(2)}) collective-permute-start(bf16[2,2,2,64,256]{4,3,0,1,2:T(8,128)(2,1)S(1)} %fusion.12), channel_id=1, source_target_pairs={{0,4},{2,6},{4,0},{6,2},{8,12},{10,14},{12,8},{14,10},{16,20},{18,... | collective-permute-start | bytes 786440 | tf_op jit(solution)/shard_map/ppermute | solution.py:45
  133.1 11.4 %collective-permute-start.18 = (bf16[2,2,2,64,256]{4,3,0,1,2:T(8,128)(2,1)S(1)}, bf16[2,2,2,64,256]{4,3,0,1,2:T(8,128)(2,1)S(1)}, u32[]{:S(2)}, u32[]{:S(2)}) collective-permute-start(bf16[2,2,2,64,256]{4,3,0,1,2:T(8,128)(2,1)S(1)} %fusion.13), channel_id=1, source_target_pairs={{0,8},{2,10},{4,12},{6,14},{8,0},{10,2},{12,4},{14,6},{16,24},{18,... | collective-permute-start | bytes 786440 | tf_op jit(solution)/shard_map/ppermute | solution.py:45
  138.2 8.2 %collective-permute-start.7 = (bf16[2,2,64,256]{3,2,0,1:T(8,128)(2,1)S(1)}, bf16[2,2,64,256]{3,2,0,1:T(8,128)(2,1)S(1)}, u32[]{:S(2)}, u32[]{:S(2)}) collective-permute-start(bf16[2,2,64,256]{3,2,0,1:T(8,128)(2,1)S(1)} %fusion.16), channel_id=1, source_target_pairs={{0,8},{2,10},{4,12},{6,14},{8,0},{10,2},{12,4},{14,6},{16,24},{18,... | collective-permute-start | bytes 393224 | tf_op jit(solution)/shard_map/ppermute | solution.py:45
  138.3 10.7 %collective-permute-start.11 = (bf16[2,2,64,256]{3,2,0,1:T(8,128)(2,1)S(1)}, bf16[2,2,64,256]{3,2,0,1:T(8,128)(2,1)S(1)}, u32[]{:S(2)}, u32[]{:S(2)}) collective-permute-start(bf16[2,2,64,256]{3,2,0,1:T(8,128)(2,1)S(1)} %fusion.17), channel_id=1, source_target_pairs={{0,4},{2,6},{4,0},{6,2},{8,12},{10,14},{12,8},{14,10},{16,20},{18,... | collective-permute-start | bytes 393224 | tf_op jit(solution)/shard_map/ppermute | solution.py:45
  144.5 8.2 %collective-permute-start.15 = (bf16[2,2,64,256]{3,2,0,1:T(8,128)(2,1)S(1)}, bf16[2,2,64,256]{3,2,0,1:T(8,128)(2,1)S(1)}, u32[]{:S(2)}, u32[]{:S(2)}) collective-permute-start(bf16[2,2,64,256]{3,2,0,1:T(8,128)(2,1)S(1)} %fusion.18), channel_id=1, source_target_pairs={{0,8},{2,10},{4,12},{6,14},{8,0},{10,2},{12,4},{14,6},{16,24},{18,... | collective-permute-start | bytes 393224 | tf_op jit(solution)/shard_map/ppermute | solution.py:45
  146.4 7.7 %collective-permute-start.19 = (bf16[2,2,64,256]{3,2,0,1:T(8,128)(2,1)S(1)}, bf16[2,2,64,256]{3,2,0,1:T(8,128)(2,1)S(1)}, u32[]{:S(2)}, u32[]{:S(2)}) collective-permute-start(bf16[2,2,64,256]{3,2,0,1:T(8,128)(2,1)S(1)} %fusion.19), channel_id=1, source_target_pairs={{0,4},{2,6},{4,0},{6,2},{8,12},{10,14},{12,8},{14,10},{16,20},{18,... | collective-permute-start | bytes 393224 | tf_op jit(solution)/shard_map/ppermute | solution.py:45
  149.0 9.5 %collective-permute-start.8 = (bf16[2,64,256]{2,1,0:T(8,128)(2,1)S(1)}, bf16[2,64,256]{2,1,0:T(8,128)(2,1)S(1)}, u32[]{:S(2)}, u32[]{:S(2)}) collective-permute-start(bf16[2,64,256]{2,1,0:T(8,128)(2,1)S(1)} %fusion.24), channel_id=1, source_target_pairs={{0,16},{2,18},{4,20},{6,22},{8,24},{10,26},{12,28},{14,30},{16,0},... | collective-permute-start | bytes 196616 | tf_op jit(solution)/shard_map/ppermute | solution.py:45
  152.7 7.9 %collective-permute-start.12 = (bf16[2,64,256]{2,1,0:T(8,128)(2,1)S(1)}, bf16[2,64,256]{2,1,0:T(8,128)(2,1)S(1)}, u32[]{:S(2)}, u32[]{:S(2)}) collective-permute-start(bf16[2,64,256]{2,1,0:T(8,128)(2,1)S(1)} %fusion.25), channel_id=1, source_target_pairs={{0,16},{2,18},{4,20},{6,22},{8,24},{10,26},{12,28},{14,30},{16,0},... | collective-permute-start | bytes 196616 | tf_op jit(solution)/shard_map/ppermute | solution.py:45
  154.0 7.3 %collective-permute-start.16 = (bf16[2,64,256]{2,1,0:T(8,128)(2,1)S(1)}, bf16[2,64,256]{2,1,0:T(8,128)(2,1)S(1)}, u32[]{:S(2)}, u32[]{:S(2)}) collective-permute-start(bf16[2,64,256]{2,1,0:T(8,128)(2,1)S(1)} %fusion.26), channel_id=1, source_target_pairs={{0,16},{2,18},{4,20},{6,22},{8,24},{10,26},{12,28},{14,30},{16,0},... | collective-permute-start | bytes 196616 | tf_op jit(solution)/shard_map/ppermute | solution.py:45
  158.5 5.2 %collective-permute-start.20 = (bf16[2,64,256]{2,1,0:T(8,128)(2,1)S(1)}, bf16[2,64,256]{2,1,0:T(8,128)(2,1)S(1)}, u32[]{:S(2)}, u32[]{:S(2)}) collective-permute-start(bf16[2,64,256]{2,1,0:T(8,128)(2,1)S(1)} %fusion.27), channel_id=1, source_target_pairs={{0,16},{2,18},{4,20},{6,22},{8,24},{10,26},{12,28},{14,30},{16,0},... | collective-permute-start | bytes 196616 | tf_op jit(solution)/shard_map/ppermute | solution.py:45
  (6 other events, 5.9 us)
Sparse Core Ops, SparseCore 0:
  15.4 59.5 all-gather.1

commit v6 on v4

--- a/solution.py
+++ b/solution.py
@@ -148,7 +148,7 @@
     grid_spec = pltpu.PrefetchScalarGridSpec(
         num_scalar_prefetch=1,
         grid=(head_pairs,),
-        in_specs=[block] * 6,
+        in_specs=[block] * 4 + [narrow] * 2,
         out_specs=[block] * 4 + [narrow] * 2,
     )
     return pl.pallas_call(
@@ -243,7 +243,9 @@
     split_v = values.reshape(seq_rows, head_pairs, 2, head_dim)
     fixed_k = split_k[:, :, 1]
     fixed_v = split_v[:, :, 1]
-    prev_k, prev_v = passed_along((keys, values), "seq", 1)
+    band_k = split_k[:, :, 0].reshape(seq_rows, head_pairs * head_dim)
+    band_v = split_v[:, :, 0].reshape(seq_rows, head_pairs * head_dim)
+    prev_k, prev_v = passed_along((band_k, band_v), "seq", 1)
     digest_count = seq_rows // BLOCK * SUMM
     offset_table = jnp.tile(offsets.T, (seq_rows // BLOCK, 1))
     digest_rows = (jnp.arange(digest_count, dtype=jnp.int32) // SUMM * BLOCK)[

time: 167 us -> 149 us (0.89)
  starting transfers between devices: 47.3 us -> 35 us
  waiting for transfers between devices: 31.2 us -> 27.2 us
  matrix products: 15.1 us -> 12.8 us
    ppermute x16, starting transfers between devices: 34.9 us -> 23 us  [seq_reduce_scatter(): lax.ppermute(send.astype(jnp.bfloat16), 'seq', [(source, source ^ 1 << bi...]
    all_gather x1, waiting for transfers between devices: 3.43 us -> 0.02 us  [on_device(): lax.all_gather(jnp.concatenate([digest_k.reshape(digest_count, pair_width...]
    ppermute x1, waiting for transfers between devices: 15.9 us -> 12.5 us  [on_device(): lax.ppermute(cotangent, 'head', [(source, (source + shift) % head_count)...]
    another operation x0 -> x2, local copies, waits for them, and re-layouts: none -> 3.04 us  [the longest x1 2.04 us: on_device(): band_k = split_k[:, :, 0].reshape(seq_rows, head_pairs * head_dim)]
    ppermute x16, waiting for transfers between devices: 11.9 us -> 14.7 us  [seq_reduce_scatter(): lax.ppermute(send.astype(jnp.bfloat16), 'seq', [(source, source ^ 1 << bi...]
    unnamed x22, local copies, waits for them, and re-layouts: 6.04 us -> 3.34 us
  transfers between devices with their start and end apart: 22 -> 22, of which waited for: 9 -> 9; matrix products, arithmetic and copies ran while one was open for 15% -> 19% of each run, Pallas kernels for 19% -> 21%
where the time goes in v6:
time: 149 us; the launch traced here: 148 us
  Pallas kernels  38.2 us (26%)
  starting transfers between devices  35 us (23%)
  waiting for transfers between devices  27.2 us (18%)
  between operations  14.5 us (10%)
  local copies, waits for them, and re-layouts  13 us (9%)
  matrix products  12.8 us (9%)
  other arithmetic  7.26 us (5%)
    ppermute x16, starting transfers between devices, seq_reduce_scatter(): lax.ppermute(send.astype(jnp.bfloat16), 'seq', [(source, source ^ 1 << bi...  23 us
    pallas_call x4, Pallas kernels, fixed_attention(): pl.pallas_call(functools.partial(fixed_kernel, scale=scale, unused=len(ea...  21.6 us
    ppermute x16, waiting for transfers between devices, seq_reduce_scatter(): lax.ppermute(send.astype(jnp.bfloat16), 'seq', [(source, source ^ 1 << bi...  14.7 us
    ppermute x1, waiting for transfers between devices, on_device(): lax.ppermute(cotangent, 'head', [(source, (source + shift) % head_count)...  12.5 us
    dot_general x1, matrix products, on_device(): lax.dot_general(gathered.reshape(seq_rows, cotangent.shape[1]), out_weigh...  12.1 us
    pallas_call x1, Pallas kernels, band_attention(): pl.pallas_call(functools.partial(band_kernel, scale=scale), grid_spec=gri...  9.65 us
    ppermute x4, starting transfers between devices, passed_along(): lax.ppermute(value, axis, [(source, source + steps) for source in range(f...  8.97 us
    pallas_call x1, Pallas kernels, finalize(): pl.pallas_call(finalize_kernel, grid=(head_pairs,), in_specs=[wide, wide,...  6.9 us
  transfers between devices with their start and end apart: 22, of which 9 were waited for; matrix products, arithmetic and copies ran while one was open for 19% of the time, Pallas kernels for 21%

profile of v6, /device:TPU:0, one launch (start us, length us, event | category | flops | bytes accessed | tf_op | source)
XLA Modules:
  0.0 148.0 jit_solution(3784655274561830095)
XLA Ops:
  7.2 1.6 %copy.30 = bf16[256,2048]{0,1:T(8,128)(2,1)S(1)} copy(bf16[256,2048]{1,0:T(8,128)(2,1)} %k_ref.9) | data formatting | bytes 2097152 | tf_op args[1]
  10.9 3.0 %collective-permute-start = (bf16[128,4096]{1,0:T(8,128)(2,1)}, bf16[128,4096]{1,0:T(8,128)(2,1)}, u32[]{:S(2)}, u32[]{:S(2)}) collective-permute-start(bf16[128,4096]{1,0:T(8,128)(2,1)} %param.10), channel_id=1, source_target_pairs={{0,1},{1,0},{2,3},{3,2},{4,5},{5,4},{6,7},{7,6},{8,9},{9,8},{10,11... | collective-permute-start | bytes 3145736 | tf_op jit(solution)/shard_map/ppermute | solution.py:279
  14.8 2.0 %copy.46 = bf16[256,1024]{1,0:T(8,128)(2,1)} copy(bf16[256,1024]{0,1:T(8,128)(2,1)} %bitcast.116) | data formatting | bytes 1048576 | tf_op jit(solution)/shard_map/reshape;squeeze | solution.py:246
  16.9 2.3 %collective-permute-start.1 = (bf16[256,1024]{1,0:T(8,128)(2,1)}, bf16[256,1024]{1,0:T(8,128)(2,1)}, u32[]{:S(2)}, u32[]{:S(2)}) collective-permute-start(bf16[256,1024]{1,0:T(8,128)(2,1)} %copy.46), channel_id=1, source_target_pairs={{0,2},{2,4},{4,6},{6,8},{8,10},{10,12},{12,14},{14,16},{16,18},{18... | collective-permute-start | bytes 1572872 | tf_op jit(solution)/shard_map/ppermute | solution.py:21
  20.2 4.0 %collective-permute-start.2 = (bf16[256,1024]{1,0:T(8,128)(2,1)}, bf16[256,1024]{1,0:T(8,128)(2,1)}, u32[]{:S(2)}, u32[]{:S(2)}) collective-permute-start(bf16[256,1024]{1,0:T(8,128)(2,1)} %copy.47), channel_id=1, source_target_pairs={{0,2},{2,4},{4,6},{6,8},{8,10},{10,12},{12,14},{14,16},{16,18},{18... | collective-permute-start | bytes 1572872 | tf_op jit(solution)/shard_map/ppermute | solution.py:21
  24.9 12.5 %collective-permute-done = bf16[128,4096]{1,0:T(8,128)(2,1)} collective-permute-done((bf16[128,4096]{1,0:T(8,128)(2,1)}, bf16[128,4096]{1,0:T(8,128)(2,1)}, u32[]{:S(2)}, u32[]{:S(2)}) %collective-permute-start) | collective-permute-done | bytes 1048608 | tf_op jit(solution)/shard_map/ppermute | solution.py:279
  37.5 4.1 %fusion.2 = bf16[2,128,4096]{2,1,0:T(8,128)(2,1)} fusion(s32[]{:T(128)S(6)} %select_n.65, bf16[1,128,4096]{2,1,0:T(8,128)(2,1)} %bitcast.1, bf16[1,128,4096]{2,1,0:T(8,128)(2,1)S(1)} %bitcast.126), kind=kLoop, calls=%fused_computation.7 | loop fusion | flops 3145728 | bytes 4194308 | tf_op jit(solution)/shard_map/stack | solution.py:284
  41.5 12.1 %convolution_convert_fusion.g_ref = bf16[256,2048]{1,0:T(8,128)(2,1)} fusion(bf16[256,4096]{1,0:T(8,128)(2,1)} %bitcast.115, bf16[2048,4096]{1,0:T(8,128)(2,1)} %param.9), kind=kOutput, calls=%fused_computation.4 | convolution fusion | flops 4295491584 | bytes 19922944 | tf_op jit(solution)/shard_map/dot_general | solution.py:286
  53.7 9.7 %shard_map.93 = (bf16[256,2048]{1,0:T(8,128)(2,1)}, bf16[256,2048]{1,0:T(8,128)(2,1)}, f32[256,2048]{1,0:T(8,128)}, f32[256,2048]{1,0:T(8,128)}, bf16[256,1024]{1,0:T(8,128)(2,1)}, /*index=5*/bf16[256,1024]{1,0:T(8,128)(2,1)}) custom-call(s32[1]{0:T(128)} %bitcast.seq_ref, bf16[256,2048]{1,0:T(8,128)(2,1)S(1)} %copy-done.2, bf16[256,2048]{1,0:T(8,128)(2,1)S(1)} %copy-done, ...), custom_call_target="tpu_custom_call" | custom-call | flops 1879048192 | bytes 7340032 | tf_op jit(solution)/shard_map/pallas_call | solution.py:154
  63.3 1.3 collective-permute-start.3
  64.6 1.5 collective-permute-start.4
  67.4 5.4 %shard_map.94 = (bf16[256,2048]{1,0:T(8,128)(2,1)}, bf16[256,2048]{1,0:T(8,128)(2,1)}, f32[256,2048]{1,0:T(8,128)}, f32[256,2048]{1,0:T(8,128)}, f32[2,1024,256]{2,1,0:T(8,128)}) custom-call(s32[1]{0:T(128)} %bitcast.seq_ref, bf16[256,2048]{1,0:T(8,128)(2,1)S(1)} %copy-done.2, ...), custom_call_target="tpu_custom_call", output_to_operand_aliasing={{0}: (7, {}), {1}: (8, {}), {2}: (9, {}), {3}: (10, {})} | custom-call | flops 1174405120 | bytes 3014656 | tf_op jit(solution)/shard_map/pallas_call | solution.py:185
  74.0 1.8 %collective-permute-start.5 = (bf16[2,2,2,2,64,256]{5,4,0,1,2,3:T(8,128)(2,1)S(1)}, bf16[2,2,2,2,64,256]{5,4,0,1,2,3:T(8,128)(2,1)S(1)}, u32[]{:S(2)}, u32[]{:S(2)}) collective-permute-start(bf16[2,2,2,2,64,256]{5,4,0,1,2,3:T(8,128)(2,1)S(1)} %fusion.5), channel_id=1, source_target_pairs={{0,2},{2,0},{4,6},{6,4},{8,10},{10,8},{12,14},{14,12},{16,18},{18,... | collective-permute-start | bytes 1572872 | tf_op jit(solution)/shard_map/ppermute | solution.py:45
  75.9 5.4 %shard_map.95 = (bf16[256,2048]{1,0:T(8,128)(2,1)}, bf16[256,2048]{1,0:T(8,128)(2,1)}, f32[256,2048]{1,0:T(8,128)}, f32[256,2048]{1,0:T(8,128)}, f32[2,1024,256]{2,1,0:T(8,128)}) custom-call(s32[1]{0:T(128)} %bitcast.seq_ref, bf16[256,2048]{1,0:T(8,128)(2,1)S(1)} %copy-done.2, ...), custom_call_target="tpu_custom_call", output_to_operand_aliasing={{0}: (7, {}), {1}: (8, {}), {2}: (9, {}), {3}: (10, {})} | custom-call | flops 1174405120 | bytes 3014656 | tf_op jit(solution)/shard_map/pallas_call | solution.py:185
  82.6 5.4 %shard_map.96 = (bf16[256,2048]{1,0:T(8,128)(2,1)}, bf16[256,2048]{1,0:T(8,128)(2,1)}, f32[256,2048]{1,0:T(8,128)}, f32[256,2048]{1,0:T(8,128)}, f32[2,1024,256]{2,1,0:T(8,128)}) custom-call(s32[1]{0:T(128)} %bitcast.seq_ref, bf16[256,2048]{1,0:T(8,128)(2,1)S(1)} %copy-done.2, ...), custom_call_target="tpu_custom_call", output_to_operand_aliasing={{0}: (7, {}), {1}: (8, {}), {2}: (9, {}), {3}: (10, {})} | custom-call | flops 1174405120 | bytes 3014656 | tf_op jit(solution)/shard_map/pallas_call | solution.py:185
  89.9 5.5 %shard_map.97 = (bf16[256,2048]{1,0:T(8,128)(2,1)}, bf16[256,2048]{1,0:T(8,128)(2,1)}, f32[256,2048]{1,0:T(8,128)}, f32[256,2048]{1,0:T(8,128)}, f32[2,1024,256]{2,1,0:T(8,128)}) custom-call(s32[1]{0:T(128)} %bitcast.seq_ref, bf16[256,2048]{1,0:T(8,128)(2,1)S(1)} %copy-done.2, ...), custom_call_target="tpu_custom_call", output_to_operand_aliasing={{0}: (7, {}), {1}: (8, {}), {2}: (9, {}), {3}: (10, {})} | custom-call | flops 1174405120 | bytes 3014656 | tf_op jit(solution)/shard_map/pallas_call | solution.py:185
  95.4 1.4 fusion.8
  97.1 2.1 %collective-permute-start.6 = (bf16[2,2,2,64,256]{4,3,0,1,2:T(8,128)(2,1)S(1)}, bf16[2,2,2,64,256]{4,3,0,1,2:T(8,128)(2,1)S(1)}, u32[]{:S(2)}, u32[]{:S(2)}) collective-permute-start(bf16[2,2,2,64,256]{4,3,0,1,2:T(8,128)(2,1)S(1)} %fusion.10), channel_id=1, source_target_pairs={{0,4},{2,6},{4,0},{6,2},{8,12},{10,14},{12,8},{14,10},{16,20},{18,... | collective-permute-start | bytes 786440 | tf_op jit(solution)/shard_map/ppermute | solution.py:45
  99.5 1.9 %collective-permute-start.10 = (bf16[2,2,2,64,256]{4,3,0,1,2:T(8,128)(2,1)S(1)}, bf16[2,2,2,64,256]{4,3,0,1,2:T(8,128)(2,1)S(1)}, u32[]{:S(2)}, u32[]{:S(2)}) collective-permute-start(bf16[2,2,2,64,256]{4,3,0,1,2:T(8,128)(2,1)S(1)} %fusion.11), channel_id=1, source_target_pairs={{0,8},{2,10},{4,12},{6,14},{8,0},{10,2},{12,4},{14,6},{16,24},{18,... | collective-permute-start | bytes 786440 | tf_op jit(solution)/shard_map/ppermute | solution.py:45
  101.6 1.5 %collective-permute-start.14 = (bf16[2,2,2,64,256]{4,3,0,1,2:T(8,128)(2,1)S(1)}, bf16[2,2,2,64,256]{4,3,0,1,2:T(8,128)(2,1)S(1)}, u32[]{:S(2)}, u32[]{:S(2)}) collective-permute-start(bf16[2,2,2,64,256]{4,3,0,1,2:T(8,128)(2,1)S(1)} %fusion.12), channel_id=1, source_target_pairs={{0,4},{2,6},{4,0},{6,2},{8,12},{10,14},{12,8},{14,10},{16,20},{18,... | collective-permute-start | bytes 786440 | tf_op jit(solution)/shard_map/ppermute | solution.py:45
  103.3 3.1 %collective-permute-done.6 = bf16[2,2,2,64,256]{4,3,0,1,2:T(8,128)(2,1)S(1)} collective-permute-done((bf16[2,2,2,64,256]{4,3,0,1,2:T(8,128)(2,1)S(1)}, bf16[2,2,2,64,256]{4,3,0,1,2:T(8,128)(2,1)S(1)}, u32[]{:S(2)}, u32[]{:S(2)}) %collective-permute-start.6) | collective-permute-done | bytes 262176 | tf_op jit(solution)/shard_map/ppermute | solution.py:45
  106.4 3.3 %collective-permute-start.18 = (bf16[2,2,2,64,256]{4,3,0,1,2:T(8,128)(2,1)S(1)}, bf16[2,2,2,64,256]{4,3,0,1,2:T(8,128)(2,1)S(1)}, u32[]{:S(2)}, u32[]{:S(2)}) collective-permute-start(bf16[2,2,2,64,256]{4,3,0,1,2:T(8,128)(2,1)S(1)} %fusion.13), channel_id=1, source_target_pairs={{0,8},{2,10},{4,12},{6,14},{8,0},{10,2},{12,4},{14,6},{16,24},{18,... | collective-permute-start | bytes 786440 | tf_op jit(solution)/shard_map/ppermute | solution.py:45
  110.0 1.6 %collective-permute-done.14 = bf16[2,2,2,64,256]{4,3,0,1,2:T(8,128)(2,1)S(1)} collective-permute-done((bf16[2,2,2,64,256]{4,3,0,1,2:T(8,128)(2,1)S(1)}, bf16[2,2,2,64,256]{4,3,0,1,2:T(8,128)(2,1)S(1)}, u32[]{:S(2)}, u32[]{:S(2)}) %collective-permute-start.14) | collective-permute-done | bytes 262176 | tf_op jit(solution)/shard_map/ppermute | solution.py:45
  111.6 1.7 %collective-permute-start.11 = (bf16[2,2,64,256]{3,2,0,1:T(8,128)(2,1)S(1)}, bf16[2,2,64,256]{3,2,0,1:T(8,128)(2,1)S(1)}, u32[]{:S(2)}, u32[]{:S(2)}) collective-permute-start(bf16[2,2,64,256]{3,2,0,1:T(8,128)(2,1)S(1)} %fusion.17), channel_id=1, source_target_pairs={{0,4},{2,6},{4,0},{6,2},{8,12},{10,14},{12,8},{14,10},{16,20},{18,... | collective-permute-start | bytes 393224 | tf_op jit(solution)/shard_map/ppermute | solution.py:45
  113.4 3.2 %collective-permute-done.18 = bf16[2,2,2,64,256]{4,3,0,1,2:T(8,128)(2,1)S(1)} collective-permute-done((bf16[2,2,2,64,256]{4,3,0,1,2:T(8,128)(2,1)S(1)}, bf16[2,2,2,64,256]{4,3,0,1,2:T(8,128)(2,1)S(1)}, u32[]{:S(2)}, u32[]{:S(2)}) %collective-permute-start.18) | collective-permute-done | bytes 262176 | tf_op jit(solution)/shard_map/ppermute | solution.py:45
  116.6 1.9 %collective-permute-start.15 = (bf16[2,2,64,256]{3,2,0,1:T(8,128)(2,1)S(1)}, bf16[2,2,64,256]{3,2,0,1:T(8,128)(2,1)S(1)}, u32[]{:S(2)}, u32[]{:S(2)}) collective-permute-start(bf16[2,2,64,256]{3,2,0,1:T(8,128)(2,1)S(1)} %fusion.18), channel_id=1, source_target_pairs={{0,8},{2,10},{4,12},{6,14},{8,0},{10,2},{12,4},{14,6},{16,24},{18,... | collective-permute-start | bytes 393224 | tf_op jit(solution)/shard_map/ppermute | solution.py:45
  119.5 3.4 %collective-permute-start.8 = (bf16[2,64,256]{2,1,0:T(8,128)(2,1)S(1)}, bf16[2,64,256]{2,1,0:T(8,128)(2,1)S(1)}, u32[]{:S(2)}, u32[]{:S(2)}) collective-permute-start(bf16[2,64,256]{2,1,0:T(8,128)(2,1)S(1)} %fusion.24), channel_id=1, source_target_pairs={{0,16},{2,18},{4,20},{6,22},{8,24},{10,26},{12,28},{14,30},{16,0},... | collective-permute-start | bytes 196616 | tf_op jit(solution)/shard_map/ppermute | solution.py:45
  124.3 2.0 %collective-permute-start.16 = (bf16[2,64,256]{2,1,0:T(8,128)(2,1)S(1)}, bf16[2,64,256]{2,1,0:T(8,128)(2,1)S(1)}, u32[]{:S(2)}, u32[]{:S(2)}) collective-permute-start(bf16[2,64,256]{2,1,0:T(8,128)(2,1)S(1)} %fusion.26), channel_id=1, source_target_pairs={{0,16},{2,18},{4,20},{6,22},{8,24},{10,26},{12,28},{14,30},{16,0},... | collective-permute-start | bytes 196616 | tf_op jit(solution)/shard_map/ppermute | solution.py:45
  126.4 1.9 %collective-permute-done.8 = bf16[2,64,256]{2,1,0:T(8,128)(2,1)S(1)} collective-permute-done((bf16[2,64,256]{2,1,0:T(8,128)(2,1)S(1)}, bf16[2,64,256]{2,1,0:T(8,128)(2,1)S(1)}, u32[]{:S(2)}, u32[]{:S(2)}) %collective-permute-start.8) | collective-permute-done | bytes 65568 | tf_op jit(solution)/shard_map/ppermute | solution.py:45
  128.7 2.4 %collective-permute-done.12 = bf16[2,64,256]{2,1,0:T(8,128)(2,1)S(1)} collective-permute-done((bf16[2,64,256]{2,1,0:T(8,128)(2,1)S(1)}, bf16[2,64,256]{2,1,0:T(8,128)(2,1)S(1)}, u32[]{:S(2)}, u32[]{:S(2)}) %collective-permute-start.12) | collective-permute-done | bytes 65568 | tf_op jit(solution)/shard_map/ppermute | solution.py:45
  131.9 1.6 %collective-permute-done.20 = bf16[2,64,256]{2,1,0:T(8,128)(2,1)S(1)} collective-permute-done((bf16[2,64,256]{2,1,0:T(8,128)(2,1)S(1)}, bf16[2,64,256]{2,1,0:T(8,128)(2,1)S(1)}, u32[]{:S(2)}, u32[]{:S(2)}) %collective-permute-start.20) | collective-permute-done | bytes 65568 | tf_op jit(solution)/shard_map/ppermute | solution.py:45
  134.2 6.9 %shard_map.98 = (bf16[256,2048]{1,0:T(8,128)(2,1)}, bf16[256,2048]{1,0:T(8,128)(2,1)}) custom-call(f32[256,2048]{1,0:T(8,128)} %get-tuple-element.50.own_k_ref, f32[256,2048]{1,0:T(8,128)} %get-tuple-element.51.own_v_ref, bf16[256,1024]{1,0:T(8,128)(2,1)} %collective-permute-done.3.back_k_ref, bf16[256,1024]{1,0:T(8,128)(2,1)} %collective-permute-done.4.back_v_ref, ...), custom_call_target="tpu_custom_call" | custom-call | flops 67108864 | bytes 5242880 | tf_op jit(solution)/shard_map/pallas_call | solution.py:213
  (90 shorter events, 15.9 us)
Async XLA Ops:
  7.2 1.6 %copy-start.1 = (bf16[256,2048]{1,0:T(8,128)(2,1)S(1)}, bf16[256,2048]{1,0:T(8,128)(2,1)}, u32[]{:S(2)}) copy-start(bf16[256,2048]{1,0:T(8,128)(2,1)} %v_ref.9) | copy-start | bytes 3145732
  7.2 59.0 %all-gather.2.cloned.1.call-start = ((), (), s32[]{:S(2)}) async-start(), calls=%async_computation | async-start | bytes 4456448 | tf_op jit(solution)/shard_map/all_gather | solution.py:264
  7.2 2.1 %copy-start.9 = (s32[8,32]{1,0:T(8,128)S(1)}, s32[8,32]{1,0:T(8,128)}, u32[]{:S(2)}) copy-start(s32[8,32]{1,0:T(8,128)} %param.11) | copy-start | bytes 3076
  10.9 26.5 %collective-permute-start = (bf16[128,4096]{1,0:T(8,128)(2,1)}, bf16[128,4096]{1,0:T(8,128)(2,1)}, u32[]{:S(2)}, u32[]{:S(2)}) collective-permute-start(bf16[128,4096]{1,0:T(8,128)(2,1)} %param.10), channel_id=1, source_target_pairs={{0,1},{1,0},{2,3},{3,2},{4,5},{5,4},{6,7},{7,6},{8,9},{9,8},{10,11... | collective-permute-start | bytes 3145736 | tf_op jit(solution)/shard_map/ppermute | solution.py:279
  16.9 36.8 %collective-permute-start.1 = (bf16[256,1024]{1,0:T(8,128)(2,1)}, bf16[256,1024]{1,0:T(8,128)(2,1)}, u32[]{:S(2)}, u32[]{:S(2)}) collective-permute-start(bf16[256,1024]{1,0:T(8,128)(2,1)} %copy.46), channel_id=1, source_target_pairs={{0,2},{2,4},{4,6},{6,8},{8,10},{10,12},{12,14},{14,16},{16,18},{18... | collective-permute-start | bytes 1572872 | tf_op jit(solution)/shard_map/ppermute | solution.py:21
  19.1 18.3 %copy-start.8 = (bf16[128,4096]{1,0:T(8,128)(2,1)S(1)}, bf16[128,4096]{1,0:T(8,128)(2,1)}, u32[]{:S(2)}) copy-start(bf16[128,4096]{1,0:T(8,128)(2,1)} %param.10) | copy-start | bytes 3145732
  20.2 33.5 %collective-permute-start.2 = (bf16[256,1024]{1,0:T(8,128)(2,1)}, bf16[256,1024]{1,0:T(8,128)(2,1)}, u32[]{:S(2)}, u32[]{:S(2)}) collective-permute-start(bf16[256,1024]{1,0:T(8,128)(2,1)} %copy.47), channel_id=1, source_target_pairs={{0,2},{2,4},{4,6},{6,8},{8,10},{10,12},{12,14},{14,16},{16,18},{18... | collective-permute-start | bytes 1572872 | tf_op jit(solution)/shard_map/ppermute | solution.py:21
  41.5 12.1 %copy-start = (bf16[256,2048]{1,0:T(8,128)(2,1)S(1)}, bf16[256,2048]{1,0:T(8,128)(2,1)}, u32[]{:S(2)}) copy-start(bf16[256,2048]{1,0:T(8,128)(2,1)} %k_ref.9) | copy-start | bytes 3145732
  41.5 12.1 %copy-start.2 = (bf16[256,2048]{1,0:T(8,128)(2,1)S(1)}, bf16[256,2048]{1,0:T(8,128)(2,1)}, u32[]{:S(2)}) copy-start(bf16[256,2048]{1,0:T(8,128)(2,1)} %q_ref.9) | copy-start | bytes 3145732
  63.3 70.9 %collective-permute-start.3 = (bf16[256,1024]{1,0:T(8,128)(2,1)}, bf16[256,1024]{1,0:T(8,128)(2,1)}, u32[]{:S(2)}, u32[]{:S(2)}) collective-permute-start(bf16[256,1024]{1,0:T(8,128)(2,1)} %get-tuple-element.52), channel_id=1, source_target_pairs={{2,0},{4,2},{6,4},{8,6},{10,8},{12,10},{14,12},{16,14},{18,16},{20... | collective-permute-start | bytes 1572872 | tf_op jit(solution)/shard_map/ppermute | solution.py:21
  64.6 69.6 %collective-permute-start.4 = (bf16[256,1024]{1,0:T(8,128)(2,1)}, bf16[256,1024]{1,0:T(8,128)(2,1)}, u32[]{:S(2)}, u32[]{:S(2)}) collective-permute-start(bf16[256,1024]{1,0:T(8,128)(2,1)} %get-tuple-element.53), channel_id=1, source_target_pairs={{2,0},{4,2},{6,4},{8,6},{10,8},{12,10},{14,12},{16,14},{18,16},{20... | collective-permute-start | bytes 1572872 | tf_op jit(solution)/shard_map/ppermute | solution.py:21
  66.1 1.2 copy-start.3
  74.0 22.8 %collective-permute-start.5 = (bf16[2,2,2,2,64,256]{5,4,0,1,2,3:T(8,128)(2,1)S(1)}, bf16[2,2,2,2,64,256]{5,4,0,1,2,3:T(8,128)(2,1)S(1)}, u32[]{:S(2)}, u32[]{:S(2)}) collective-permute-start(bf16[2,2,2,2,64,256]{5,4,0,1,2,3:T(8,128)(2,1)S(1)} %fusion.5), channel_id=1, source_target_pairs={{0,2},{2,0},{4,6},{6,4},{8,10},{10,8},{12,14},{14,12},{16,18},{18,... | collective-permute-start | bytes 1572872 | tf_op jit(solution)/shard_map/ppermute | solution.py:45
  82.5 14.6 %collective-permute-start.9 = (bf16[2,2,2,2,64,256]{5,4,0,1,3,2:T(8,128)(2,1)S(1)}, bf16[2,2,2,2,64,256]{5,4,0,1,3,2:T(8,128)(2,1)S(1)}, u32[]{:S(2)}, u32[]{:S(2)}) collective-permute-start(bf16[2,2,2,2,64,256]{5,4,0,1,3,2:T(8,128)(2,1)S(1)} %fusion.6), channel_id=1, source_target_pairs={{0,2},{2,0},{4,6},{6,4},{8,10},{10,8},{12,14},{14,12},{16,18},{18,... | collective-permute-start | bytes 1572872 | tf_op jit(solution)/shard_map/ppermute | solution.py:45
  89.3 10.1 %collective-permute-start.13 = (bf16[2,2,2,2,64,256]{5,4,0,1,2,3:T(8,128)(2,1)S(1)}, bf16[2,2,2,2,64,256]{5,4,0,1,2,3:T(8,128)(2,1)S(1)}, u32[]{:S(2)}, u32[]{:S(2)}) collective-permute-start(bf16[2,2,2,2,64,256]{5,4,0,1,2,3:T(8,128)(2,1)S(1)} %fusion.7), channel_id=1, source_target_pairs={{0,2},{2,0},{4,6},{6,4},{8,10},{10,8},{12,14},{14,12},{16,18},{18,... | collective-permute-start | bytes 1572872 | tf_op jit(solution)/shard_map/ppermute | solution.py:45
  89.9 7.1 %copy-start.4 = (f32[2,1024,256]{2,1,0:T(8,128)S(1)}, f32[2,1024,256]{2,1,0:T(8,128)}, u32[]{:S(2)}) copy-start(f32[2,1024,256]{2,1,0:T(8,128)} %get-tuple-element.54) | copy-start | bytes 6291460
  95.3 3.9 %copy-start.5 = (f32[2,1024,256]{2,1,0:T(8,128)S(1)}, f32[2,1024,256]{2,1,0:T(8,128)}, u32[]{:S(2)}) copy-start(f32[2,1024,256]{2,1,0:T(8,128)} %get-tuple-element.55) | copy-start | bytes 6291460
  96.8 4.8 %collective-permute-start.17 = (bf16[2,2,2,2,64,256]{5,4,0,1,3,2:T(8,128)(2,1)S(1)}, bf16[2,2,2,2,64,256]{5,4,0,1,3,2:T(8,128)(2,1)S(1)}, u32[]{:S(2)}, u32[]{:S(2)}) collective-permute-start(bf16[2,2,2,2,64,256]{5,4,0,1,3,2:T(8,128)(2,1)S(1)} %fusion.8), channel_id=1, source_target_pairs={{0,2},{2,0},{4,6},{6,4},{8,10},{10,8},{12,14},{14,12},{16,18},{18,... | collective-permute-start | bytes 1572872 | tf_op jit(solution)/shard_map/ppermute | solution.py:45
  97.1 4.3 %copy-start.7 = (f32[2,1024,256]{2,1,0:T(8,128)S(1)}, f32[2,1024,256]{2,1,0:T(8,128)}, u32[]{:S(2)}) copy-start(f32[2,1024,256]{2,1,0:T(8,128)} %get-tuple-element.56) | copy-start | bytes 6291460
  97.1 9.2 %collective-permute-start.6 = (bf16[2,2,2,64,256]{4,3,0,1,2:T(8,128)(2,1)S(1)}, bf16[2,2,2,64,256]{4,3,0,1,2:T(8,128)(2,1)S(1)}, u32[]{:S(2)}, u32[]{:S(2)}) collective-permute-start(bf16[2,2,2,64,256]{4,3,0,1,2:T(8,128)(2,1)S(1)} %fusion.10), channel_id=1, source_target_pairs={{0,4},{2,6},{4,0},{6,2},{8,12},{10,14},{12,8},{14,10},{16,20},{18,... | collective-permute-start | bytes 786440 | tf_op jit(solution)/shard_map/ppermute | solution.py:45
  99.4 3.7 %copy-start.6 = (f32[2,1024,256]{2,1,0:T(8,128)S(1)}, f32[2,1024,256]{2,1,0:T(8,128)}, u32[]{:S(2)}) copy-start(f32[2,1024,256]{2,1,0:T(8,128)} %get-tuple-element.57) | copy-start | bytes 6291460
  99.5 10.3 %collective-permute-start.10 = (bf16[2,2,2,64,256]{4,3,0,1,2:T(8,128)(2,1)S(1)}, bf16[2,2,2,64,256]{4,3,0,1,2:T(8,128)(2,1)S(1)}, u32[]{:S(2)}, u32[]{:S(2)}) collective-permute-start(bf16[2,2,2,64,256]{4,3,0,1,2:T(8,128)(2,1)S(1)} %fusion.11), channel_id=1, source_target_pairs={{0,8},{2,10},{4,12},{6,14},{8,0},{10,2},{12,4},{14,6},{16,24},{18,... | collective-permute-start | bytes 786440 | tf_op jit(solution)/shard_map/ppermute | solution.py:45
  101.6 10.0 %collective-permute-start.14 = (bf16[2,2,2,64,256]{4,3,0,1,2:T(8,128)(2,1)S(1)}, bf16[2,2,2,64,256]{4,3,0,1,2:T(8,128)(2,1)S(1)}, u32[]{:S(2)}, u32[]{:S(2)}) collective-permute-start(bf16[2,2,2,64,256]{4,3,0,1,2:T(8,128)(2,1)S(1)} %fusion.12), channel_id=1, source_target_pairs={{0,4},{2,6},{4,0},{6,2},{8,12},{10,14},{12,8},{14,10},{16,20},{18,... | collective-permute-start | bytes 786440 | tf_op jit(solution)/shard_map/ppermute | solution.py:45
  106.4 10.3 %collective-permute-start.18 = (bf16[2,2,2,64,256]{4,3,0,1,2:T(8,128)(2,1)S(1)}, bf16[2,2,2,64,256]{4,3,0,1,2:T(8,128)(2,1)S(1)}, u32[]{:S(2)}, u32[]{:S(2)}) collective-permute-start(bf16[2,2,2,64,256]{4,3,0,1,2:T(8,128)(2,1)S(1)} %fusion.13), channel_id=1, source_target_pairs={{0,8},{2,10},{4,12},{6,14},{8,0},{10,2},{12,4},{14,6},{16,24},{18,... | collective-permute-start | bytes 786440 | tf_op jit(solution)/shard_map/ppermute | solution.py:45
  109.8 8.9 %collective-permute-start.7 = (bf16[2,2,64,256]{3,2,0,1:T(8,128)(2,1)S(1)}, bf16[2,2,64,256]{3,2,0,1:T(8,128)(2,1)S(1)}, u32[]{:S(2)}, u32[]{:S(2)}) collective-permute-start(bf16[2,2,64,256]{3,2,0,1:T(8,128)(2,1)S(1)} %fusion.16), channel_id=1, source_target_pairs={{0,8},{2,10},{4,12},{6,14},{8,0},{10,2},{12,4},{14,6},{16,24},{18,... | collective-permute-start | bytes 393224 | tf_op jit(solution)/shard_map/ppermute | solution.py:45
  111.6 8.0 %collective-permute-start.11 = (bf16[2,2,64,256]{3,2,0,1:T(8,128)(2,1)S(1)}, bf16[2,2,64,256]{3,2,0,1:T(8,128)(2,1)S(1)}, u32[]{:S(2)}, u32[]{:S(2)}) collective-permute-start(bf16[2,2,64,256]{3,2,0,1:T(8,128)(2,1)S(1)} %fusion.17), channel_id=1, source_target_pairs={{0,4},{2,6},{4,0},{6,2},{8,12},{10,14},{12,8},{14,10},{16,20},{18,... | collective-permute-start | bytes 393224 | tf_op jit(solution)/shard_map/ppermute | solution.py:45
  116.6 6.4 %collective-permute-start.15 = (bf16[2,2,64,256]{3,2,0,1:T(8,128)(2,1)S(1)}, bf16[2,2,64,256]{3,2,0,1:T(8,128)(2,1)S(1)}, u32[]{:S(2)}, u32[]{:S(2)}) collective-permute-start(bf16[2,2,64,256]{3,2,0,1:T(8,128)(2,1)S(1)} %fusion.18), channel_id=1, source_target_pairs={{0,8},{2,10},{4,12},{6,14},{8,0},{10,2},{12,4},{14,6},{16,24},{18,... | collective-permute-start | bytes 393224 | tf_op jit(solution)/shard_map/ppermute | solution.py:45
  118.7 5.6 %collective-permute-start.19 = (bf16[2,2,64,256]{3,2,0,1:T(8,128)(2,1)S(1)}, bf16[2,2,64,256]{3,2,0,1:T(8,128)(2,1)S(1)}, u32[]{:S(2)}, u32[]{:S(2)}) collective-permute-start(bf16[2,2,64,256]{3,2,0,1:T(8,128)(2,1)S(1)} %fusion.19), channel_id=1, source_target_pairs={{0,4},{2,6},{4,0},{6,2},{8,12},{10,14},{12,8},{14,10},{16,20},{18,... | collective-permute-start | bytes 393224 | tf_op jit(solution)/shard_map/ppermute | solution.py:45
  119.5 8.8 %collective-permute-start.8 = (bf16[2,64,256]{2,1,0:T(8,128)(2,1)S(1)}, bf16[2,64,256]{2,1,0:T(8,128)(2,1)S(1)}, u32[]{:S(2)}, u32[]{:S(2)}) collective-permute-start(bf16[2,64,256]{2,1,0:T(8,128)(2,1)S(1)} %fusion.24), channel_id=1, source_target_pairs={{0,16},{2,18},{4,20},{6,22},{8,24},{10,26},{12,28},{14,30},{16,0},... | collective-permute-start | bytes 196616 | tf_op jit(solution)/shard_map/ppermute | solution.py:45
  123.1 8.1 %collective-permute-start.12 = (bf16[2,64,256]{2,1,0:T(8,128)(2,1)S(1)}, bf16[2,64,256]{2,1,0:T(8,128)(2,1)S(1)}, u32[]{:S(2)}, u32[]{:S(2)}) collective-permute-start(bf16[2,64,256]{2,1,0:T(8,128)(2,1)S(1)} %fusion.25), channel_id=1, source_target_pairs={{0,16},{2,18},{4,20},{6,22},{8,24},{10,26},{12,28},{14,30},{16,0},... | collective-permute-start | bytes 196616 | tf_op jit(solution)/shard_map/ppermute | solution.py:45
  124.3 7.5 %collective-permute-start.16 = (bf16[2,64,256]{2,1,0:T(8,128)(2,1)S(1)}, bf16[2,64,256]{2,1,0:T(8,128)(2,1)S(1)}, u32[]{:S(2)}, u32[]{:S(2)}) collective-permute-start(bf16[2,64,256]{2,1,0:T(8,128)(2,1)S(1)} %fusion.26), channel_id=1, source_target_pairs={{0,16},{2,18},{4,20},{6,22},{8,24},{10,26},{12,28},{14,30},{16,0},... | collective-permute-start | bytes 196616 | tf_op jit(solution)/shard_map/ppermute | solution.py:45
  128.3 5.2 %collective-permute-start.20 = (bf16[2,64,256]{2,1,0:T(8,128)(2,1)S(1)}, bf16[2,64,256]{2,1,0:T(8,128)(2,1)S(1)}, u32[]{:S(2)}, u32[]{:S(2)}) collective-permute-start(bf16[2,64,256]{2,1,0:T(8,128)(2,1)S(1)} %fusion.27), channel_id=1, source_target_pairs={{0,16},{2,18},{4,20},{6,22},{8,24},{10,26},{12,28},{14,30},{16,0},... | collective-permute-start | bytes 196616 | tf_op jit(solution)/shard_map/ppermute | solution.py:45
Sparse Core Ops, SparseCore 0:
  11.1 54.6 all-gather.1

commit v7 on v6

--- a/solution.py
+++ b/solution.py
@@ -193,6 +193,78 @@
     )(*operands)
 
 
+def prep_kernel(k_ref, v_ref, select_ref, bk_ref, bv_ref, dk_ref, dv_ref):
+    hd = bk_ref.shape[1]
+    pick = select_ref[0]
+    bk_ref[...] = k_ref[:, :hd]
+    bv_ref[...] = v_ref[:, :hd]
+    dk_ref[...] = nn(pick, k_ref[:, hd:]).astype(dk_ref.dtype)
+    dv_ref[...] = nn(pick, v_ref[:, hd:]).astype(dv_ref.dtype)
+
+
+def prep(keys, values, select, head_pairs, head_dim):
+    rows = keys.shape[0]
+    digest_rows = select.shape[1]
+    wide = pl.BlockSpec((rows, 2 * head_dim), lambda p: (0, p))
+    narrow = pl.BlockSpec((rows, head_dim), lambda p: (0, p))
+    digest = pl.BlockSpec((digest_rows, head_dim), lambda p: (0, p))
+    width = head_pairs * head_dim
+    return pl.pallas_call(
+        prep_kernel,
+        grid=(head_pairs,),
+        in_specs=[wide, wide, pl.BlockSpec((1, digest_rows, rows), lambda p: (p, 0, 0))],
+        out_specs=[narrow, narrow, digest, digest],
+        out_shape=[
+            jax.ShapeDtypeStruct((rows, width), keys.dtype),
+            jax.ShapeDtypeStruct((rows, width), keys.dtype),
+            jax.ShapeDtypeStruct((digest_rows, width), keys.dtype),
+            jax.ShapeDtypeStruct((digest_rows, width), keys.dtype),
+        ],
+        cost_estimate=pl.CostEstimate(
+            flops=4 * digest_rows * rows * head_dim * head_pairs,
+            transcendentals=0,
+            bytes_accessed=rows * head_dim * head_pairs * 12,
+        ),
+    )(keys, values, select)
+
+
+def grad_out_kernel(head_ref, *refs):
+    pieces = refs[:-2]
+    w_ref, out_ref = refs[-2:]
+    count = len(pieces)
+    piece_rows = pieces[0].shape[0]
+    block = w_ref[...]
+    for shift, piece in enumerate(pieces):
+        owner = lax.rem(head_ref[0] - shift + count, count)
+        start = pl.multiple_of(owner * piece_rows, piece_rows)
+        out_ref[pl.ds(start, piece_rows), :] = nt(piece[...], block).astype(out_ref.dtype)
+
+
+def grad_out_matmul(head_index, pieces, out_weight):
+    piece_rows, model = pieces[0].shape
+    width = out_weight.shape[0]
+    tile = 256 if width % 256 == 0 else width
+    rows = piece_rows * len(pieces)
+    grid_spec = pltpu.PrefetchScalarGridSpec(
+        num_scalar_prefetch=1,
+        grid=(width // tile,),
+        in_specs=[pl.BlockSpec((piece_rows, model), lambda j, h: (0, 0))] * len(pieces)
+        + [pl.BlockSpec((tile, model), lambda j, h: (j, 0))],
+        out_specs=pl.BlockSpec((rows, tile), lambda j, h: (0, j)),
+    )
+    return pl.pallas_call(
+        grad_out_kernel,
+        grid_spec=grid_spec,
+        out_shape=jax.ShapeDtypeStruct((rows, width), jnp.bfloat16),
+        compiler_params=pltpu.CompilerParams(vmem_limit_bytes=48 * 1024 * 1024),
+        cost_estimate=pl.CostEstimate(
+            flops=2 * rows * model * width,
+            transcendentals=0,
+            bytes_accessed=2 * (width * model + rows * model + rows * width),
+        ),
+    )(head_index, *pieces, out_weight)
+
+
 def finalize_kernel(own_k_ref, own_v_ref, back_k_ref, back_v_ref, digest_ref, select_ref, k_out, v_out):
     hd = back_k_ref.shape[1]
     pick = select_ref[0]
@@ -239,13 +311,6 @@
     score_scale = head_dim ** (-0.5)
     assert seq_rows == WIN and seq_rows % BLOCK == 0
     seq_index = lax.axis_index("seq")
-    split_k = keys.reshape(seq_rows, head_pairs, 2, head_dim)
-    split_v = values.reshape(seq_rows, head_pairs, 2, head_dim)
-    fixed_k = split_k[:, :, 1]
-    fixed_v = split_v[:, :, 1]
-    band_k = split_k[:, :, 0].reshape(seq_rows, head_pairs * head_dim)
-    band_v = split_v[:, :, 0].reshape(seq_rows, head_pairs * head_dim)
-    prev_k, prev_v = passed_along((band_k, band_v), "seq", 1)
     digest_count = seq_rows // BLOCK * SUMM
     offset_table = jnp.tile(offsets.T, (seq_rows // BLOCK, 1))
     digest_rows = (jnp.arange(digest_count, dtype=jnp.int32) // SUMM * BLOCK)[
@@ -254,24 +319,10 @@
     select = (
         digest_rows.T[:, :, None] == jnp.arange(seq_rows, dtype=jnp.int32)[None, None, :]
     ).astype(jnp.bfloat16)
-    digest_k = jnp.einsum(
-        "hjr,rhc->jhc", select, fixed_k, preferred_element_type=jnp.float32
-    ).astype(jnp.bfloat16)
-    digest_v = jnp.einsum(
-        "hjr,rhc->jhc", select, fixed_v, preferred_element_type=jnp.float32
-    ).astype(jnp.bfloat16)
-    pair_width = head_pairs * head_dim
+    band_k, band_v, digest_k, digest_v = prep(keys, values, select, head_pairs, head_dim)
+    prev_k, prev_v = passed_along((band_k, band_v), "seq", 1)
     far_kv = lax.all_gather(
-        jnp.concatenate(
-            [
-                digest_k.reshape(digest_count, pair_width),
-                digest_v.reshape(digest_count, pair_width),
-            ],
-            1,
-        ),
-        "seq",
-        axis=0,
-        tiled=True,
+        jnp.concatenate([digest_k, digest_v], 1), "seq", axis=0, tiled=True
     )
     head_count = lax.axis_size("head")
     head_index = lax.axis_index("head")
@@ -281,14 +332,7 @@
         )
         for shift in range(1, head_count)
     ]
-    doubled = jnp.stack(pieces[::-1] + pieces[::-1], 0)
-    gathered = lax.dynamic_slice_in_dim(doubled, head_count - 1 - head_index, head_count, 0)
-    grad_out = lax.dot_general(
-        gathered.reshape(seq_rows, cotangent.shape[1]),
-        out_weight,
-        (((1,), (1,)), ((), ())),
-        preferred_element_type=jnp.float32,
-    ).astype(jnp.bfloat16)
+    grad_out = grad_out_matmul(head_index.reshape(1).astype(jnp.int32), pieces, out_weight)
     seq_scalar = seq_index.reshape(1).astype(jnp.int32)
     attention, query_grad, own_dk, own_dv, back_k, back_v = band_attention(
         seq_scalar, queries, keys, values, grad_out, prev_k, prev_v, head_pairs, head_dim, score_scale

time: 149 us -> 156 us (1.047)
  Pallas kernels: 38.2 us -> 58.3 us
  matrix products: 12.8 us -> 0 us
  waiting for transfers between devices: 27.2 us -> 31.7 us
  other arithmetic: 7.26 us -> 4.22 us
  local copies, waits for them, and re-layouts: 13 us -> 10.9 us
    pallas_call x0 -> x2, Pallas kernels: none -> 20 us  [the longest x1 14.1 us: grad_out_matmul(): pl.pallas_call(grad_out_kernel, grid_spec=grid_spec, out_shape=jax.ShapeD...]
    dot_general x3 -> x0, matrix products: 12.8 us -> none  [the longest x1 12.1 us: on_device(): lax.dot_general(gathered.reshape(seq_rows, cotangent.shape[1]), out_weigh...]
    ppermute x1, waiting for transfers between devices: 12.5 us -> 16.9 us  [on_device(): lax.ppermute(cotangent, 'head', [(source, (source + shift) % head_count)...]
    another operation x1 -> x0, other arithmetic: 4.06 us -> none  [on_device(): doubled = jnp.stack(pieces[::-1] + pieces[::-1], 0)]
    another operation x2 -> x0, local copies, waits for them, and re-layouts: 3.04 us -> none  [the longest x1 2.04 us: on_device(): band_k = split_k[:, :, 0].reshape(seq_rows, head_pairs * head_dim)]
    unnamed x22 -> x26, local copies, waits for them, and re-layouts: 3.34 us -> 4.41 us
  transfers between devices with their start and end apart: 22 -> 22, of which waited for: 9 -> 9; matrix products, arithmetic and copies ran while one was open for 19% -> 5% of each run, Pallas kernels for 21% -> 29%
where the time goes in v7:
time: 156 us; the launch traced here: 155 us
  Pallas kernels  58.3 us (37%)
  starting transfers between devices  34.9 us (22%)
  waiting for transfers between devices  31.7 us (20%)
  between operations  14.5 us (9%)
  local copies, waits for them, and re-layouts  10.9 us (7%)
  other arithmetic  4.22 us (3%)
    ppermute x16, starting transfers between devices, seq_reduce_scatter(): lax.ppermute(send.astype(jnp.bfloat16), 'seq', [(source, source ^ 1 << bi...  22.9 us
    pallas_call x4, Pallas kernels, fixed_attention(): pl.pallas_call(functools.partial(fixed_kernel, scale=scale, unused=len(ea...  21.6 us
    ppermute x1, waiting for transfers between devices, on_device(): lax.ppermute(cotangent, 'head', [(source, (source + shift) % head_count)...  16.9 us
    ppermute x16, waiting for transfers between devices, seq_reduce_scatter(): lax.ppermute(send.astype(jnp.bfloat16), 'seq', [(source, source ^ 1 << bi...  14.8 us
    pallas_call x1, Pallas kernels, grad_out_matmul(): pl.pallas_call(grad_out_kernel, grid_spec=grid_spec, out_shape=jax.ShapeD...  14.1 us
    pallas_call x1, Pallas kernels, band_attention(): pl.pallas_call(functools.partial(band_kernel, scale=scale), grid_spec=gri...  9.72 us
    ppermute x4, starting transfers between devices, passed_along(): lax.ppermute(value, axis, [(source, source + steps) for source in range(f...  9.01 us
    pallas_call x1, Pallas kernels, finalize(): pl.pallas_call(finalize_kernel, grid=(head_pairs,), in_specs=[wide, wide,...  6.9 us
  transfers between devices with their start and end apart: 22, of which 9 were waited for; matrix products, arithmetic and copies ran while one was open for 5% of the time, Pallas kernels for 29%

profile of v7, /device:TPU:0, one launch (start us, length us, event | category | flops | bytes accessed | tf_op | source)
XLA Modules:
  0.0 154.5 jit_solution(6746364040522808733)
XLA Ops:
  8.9 5.9 %shard_map.94 = (bf16[256,1024]{1,0:T(8,128)(2,1)}, bf16[256,1024]{1,0:T(8,128)(2,1)}, bf16[64,1024]{1,0:T(8,128)(2,1)}, bf16[64,1024]{1,0:T(8,128)(2,1)}) custom-call(bf16[256,2048]{1,0:T(8,128)(2,1)} %k_ref.11, bf16[256,2048]{1,0:T(8,128)(2,1)} %v_ref.11, bf16[8,64,256]{2,1,0:T(8,128)(2,1)} %fusion.4.select_ref), custom_call_target="tpu_custom_call" | custom-call | flops 67108864 | bytes 3145728 | tf_op jit(solution)/shard_map/pallas_call | solution.py:212
  14.8 1.7 %pad_maximum_fusion = bf16[64,2048]{1,0:T(8,128)(2,1)} fusion(bf16[64,1024]{1,0:T(8,128)(2,1)} %get-tuple-element.37, bf16[64,1024]{1,0:T(8,128)(2,1)} %get-tuple-element.36), kind=kLoop, calls=%fused_computation.26 | loop fusion | flops 524288 | bytes 524288 | tf_op jit(solution)/shard_map/concatenate | solution.py:325
  16.6 3.0 %collective-permute-start = (bf16[128,4096]{1,0:T(8,128)(2,1)S(1)}, bf16[128,4096]{1,0:T(8,128)(2,1)S(1)}, u32[]{:S(2)}, u32[]{:S(2)}) collective-permute-start(bf16[128,4096]{1,0:T(8,128)(2,1)S(1)} %copy-done.6), channel_id=1, source_target_pairs={{0,1},{1,0},{2,3},{3,2},{4,5},{5,4},{6,7},{7,6},{8,9},{9,8},{10,11... | collective-permute-start | bytes 3145736 | tf_op jit(solution)/shard_map/ppermute | solution.py:330
  19.6 2.3 %collective-permute-start.1 = (bf16[256,1024]{1,0:T(8,128)(2,1)}, bf16[256,1024]{1,0:T(8,128)(2,1)}, u32[]{:S(2)}, u32[]{:S(2)}) collective-permute-start(bf16[256,1024]{1,0:T(8,128)(2,1)} %get-tuple-element.38), channel_id=1, source_target_pairs={{0,2},{2,4},{4,6},{6,8},{8,10},{10,12},{12,14},{14,16},{16,18},{18... | collective-permute-start | bytes 1572872 | tf_op jit(solution)/shard_map/ppermute | solution.py:21
  21.8 4.0 %collective-permute-start.2 = (bf16[256,1024]{1,0:T(8,128)(2,1)}, bf16[256,1024]{1,0:T(8,128)(2,1)}, u32[]{:S(2)}, u32[]{:S(2)}) collective-permute-start(bf16[256,1024]{1,0:T(8,128)(2,1)} %get-tuple-element.39), channel_id=1, source_target_pairs={{0,2},{2,4},{4,6},{6,8},{8,10},{10,12},{12,14},{14,16},{16,18},{18... | collective-permute-start | bytes 1572872 | tf_op jit(solution)/shard_map/ppermute | solution.py:21
  25.8 16.9 %collective-permute-done.refs_1_ = bf16[128,4096]{1,0:T(8,128)(2,1)S(1)} collective-permute-done((bf16[128,4096]{1,0:T(8,128)(2,1)S(1)}, bf16[128,4096]{1,0:T(8,128)(2,1)S(1)}, u32[]{:S(2)}, u32[]{:S(2)}) %collective-permute-start) | collective-permute-done | bytes 1048608 | tf_op jit(solution)/shard_map/ppermute | solution.py:330
  44.9 14.1 %shard_map.93.g_ref = bf16[256,2048]{1,0:T(8,128)(2,1)S(1)} custom-call(s32[1]{0:T(128)} %bitcast.1.head_ref, bf16[128,4096]{1,0:T(8,128)(2,1)S(1)} %copy-done.6, bf16[128,4096]{1,0:T(8,128)(2,1)S(1)} %copy-done.8, bf16[2048,4096]{1,0:T(8,128)(2,1)} %refs_2_.1), custom_call_target="tpu_custom_call" | custom-call | flops 4294967296 | bytes 19922944 | tf_op jit(solution)/shard_map/pallas_call | solution.py:255
  60.1 9.7 %shard_map.95 = (bf16[256,2048]{1,0:T(8,128)(2,1)}, bf16[256,2048]{1,0:T(8,128)(2,1)}, f32[256,2048]{1,0:T(8,128)}, f32[256,2048]{1,0:T(8,128)}, bf16[256,1024]{1,0:T(8,128)(2,1)}, /*index=5*/bf16[256,1024]{1,0:T(8,128)(2,1)}) custom-call(s32[1]{0:T(128)} %bitcast.seq_ref, bf16[256,2048]{1,0:T(8,128)(2,1)S(1)} %copy-done.4, bf16[256,2048]{1,0:T(8,128)(2,1)S(1)} %copy-done, ...), custom_call_target="tpu_custom_call" | custom-call | flops 1879048192 | bytes 7340032 | tf_op jit(solution)/shard_map/pallas_call | solution.py:154
  69.8 1.3 collective-permute-start.3
  71.1 1.5 collective-permute-start.4
  73.9 5.4 %shard_map.96 = (bf16[256,2048]{1,0:T(8,128)(2,1)}, bf16[256,2048]{1,0:T(8,128)(2,1)}, f32[256,2048]{1,0:T(8,128)}, f32[256,2048]{1,0:T(8,128)}, f32[2,1024,256]{2,1,0:T(8,128)}) custom-call(s32[1]{0:T(128)} %bitcast.seq_ref, bf16[256,2048]{1,0:T(8,128)(2,1)S(1)} %copy-done.5, ...), custom_call_target="tpu_custom_call", output_to_operand_aliasing={{0}: (7, {}), {1}: (8, {}), {2}: (9, {}), {3}: (10, {})} | custom-call | flops 1174405120 | bytes 3014656 | tf_op jit(solution)/shard_map/pallas_call | solution.py:185
  79.2 1.3 fusion
  80.5 1.8 %collective-permute-start.5 = (bf16[2,2,2,2,64,256]{5,4,0,1,2,3:T(8,128)(2,1)S(1)}, bf16[2,2,2,2,64,256]{5,4,0,1,2,3:T(8,128)(2,1)S(1)}, u32[]{:S(2)}, u32[]{:S(2)}) collective-permute-start(bf16[2,2,2,2,64,256]{5,4,0,1,2,3:T(8,128)(2,1)S(1)} %fusion), channel_id=1, source_target_pairs={{0,2},{2,0},{4,6},{6,4},{8,10},{10,8},{12,14},{14,12},{16,18},{18,... | collective-permute-start | bytes 1572872 | tf_op jit(solution)/shard_map/ppermute | solution.py:45
  82.3 5.4 %shard_map.97 = (bf16[256,2048]{1,0:T(8,128)(2,1)}, bf16[256,2048]{1,0:T(8,128)(2,1)}, f32[256,2048]{1,0:T(8,128)}, f32[256,2048]{1,0:T(8,128)}, f32[2,1024,256]{2,1,0:T(8,128)}) custom-call(s32[1]{0:T(128)} %bitcast.seq_ref, bf16[256,2048]{1,0:T(8,128)(2,1)S(1)} %copy-done.5, ...), custom_call_target="tpu_custom_call", output_to_operand_aliasing={{0}: (7, {}), {1}: (8, {}), {2}: (9, {}), {3}: (10, {})} | custom-call | flops 1174405120 | bytes 3014656 | tf_op jit(solution)/shard_map/pallas_call | solution.py:185
  89.1 5.4 %shard_map.98 = (bf16[256,2048]{1,0:T(8,128)(2,1)}, bf16[256,2048]{1,0:T(8,128)(2,1)}, f32[256,2048]{1,0:T(8,128)}, f32[256,2048]{1,0:T(8,128)}, f32[2,1024,256]{2,1,0:T(8,128)}) custom-call(s32[1]{0:T(128)} %bitcast.seq_ref, bf16[256,2048]{1,0:T(8,128)(2,1)S(1)} %copy-done.5, ...), custom_call_target="tpu_custom_call", output_to_operand_aliasing={{0}: (7, {}), {1}: (8, {}), {2}: (9, {}), {3}: (10, {})} | custom-call | flops 1174405120 | bytes 3014656 | tf_op jit(solution)/shard_map/pallas_call | solution.py:185
  96.4 5.5 %shard_map.99 = (bf16[256,2048]{1,0:T(8,128)(2,1)}, bf16[256,2048]{1,0:T(8,128)(2,1)}, f32[256,2048]{1,0:T(8,128)}, f32[256,2048]{1,0:T(8,128)}, f32[2,1024,256]{2,1,0:T(8,128)}) custom-call(s32[1]{0:T(128)} %bitcast.seq_ref, bf16[256,2048]{1,0:T(8,128)(2,1)S(1)} %copy-done.5, ...), custom_call_target="tpu_custom_call", output_to_operand_aliasing={{0}: (7, {}), {1}: (8, {}), {2}: (9, {}), {3}: (10, {})} | custom-call | flops 1174405120 | bytes 3014656 | tf_op jit(solution)/shard_map/pallas_call | solution.py:185
  101.8 1.4 fusion.3
  103.7 2.1 %collective-permute-start.6 = (bf16[2,2,2,64,256]{4,3,0,1,2:T(8,128)(2,1)S(1)}, bf16[2,2,2,64,256]{4,3,0,1,2:T(8,128)(2,1)S(1)}, u32[]{:S(2)}, u32[]{:S(2)}) collective-permute-start(bf16[2,2,2,64,256]{4,3,0,1,2:T(8,128)(2,1)S(1)} %fusion.5), channel_id=1, source_target_pairs={{0,4},{2,6},{4,0},{6,2},{8,12},{10,14},{12,8},{14,10},{16,20},{18,... | collective-permute-start | bytes 786440 | tf_op jit(solution)/shard_map/ppermute | solution.py:45
  106.0 1.9 %collective-permute-start.10 = (bf16[2,2,2,64,256]{4,3,0,1,2:T(8,128)(2,1)S(1)}, bf16[2,2,2,64,256]{4,3,0,1,2:T(8,128)(2,1)S(1)}, u32[]{:S(2)}, u32[]{:S(2)}) collective-permute-start(bf16[2,2,2,64,256]{4,3,0,1,2:T(8,128)(2,1)S(1)} %fusion.6), channel_id=1, source_target_pairs={{0,8},{2,10},{4,12},{6,14},{8,0},{10,2},{12,4},{14,6},{16,24},{18,... | collective-permute-start | bytes 786440 | tf_op jit(solution)/shard_map/ppermute | solution.py:45
  108.1 1.5 collective-permute-start.14
  109.7 3.1 %collective-permute-done.6 = bf16[2,2,2,64,256]{4,3,0,1,2:T(8,128)(2,1)S(1)} collective-permute-done((bf16[2,2,2,64,256]{4,3,0,1,2:T(8,128)(2,1)S(1)}, bf16[2,2,2,64,256]{4,3,0,1,2:T(8,128)(2,1)S(1)}, u32[]{:S(2)}, u32[]{:S(2)}) %collective-permute-start.6) | collective-permute-done | bytes 262176 | tf_op jit(solution)/shard_map/ppermute | solution.py:45
  112.9 3.3 %collective-permute-start.18 = (bf16[2,2,2,64,256]{4,3,0,1,2:T(8,128)(2,1)S(1)}, bf16[2,2,2,64,256]{4,3,0,1,2:T(8,128)(2,1)S(1)}, u32[]{:S(2)}, u32[]{:S(2)}) collective-permute-start(bf16[2,2,2,64,256]{4,3,0,1,2:T(8,128)(2,1)S(1)} %fusion.8), channel_id=1, source_target_pairs={{0,8},{2,10},{4,12},{6,14},{8,0},{10,2},{12,4},{14,6},{16,24},{18,... | collective-permute-start | bytes 786440 | tf_op jit(solution)/shard_map/ppermute | solution.py:45
  116.4 1.6 %collective-permute-done.14 = bf16[2,2,2,64,256]{4,3,0,1,2:T(8,128)(2,1)S(1)} collective-permute-done((bf16[2,2,2,64,256]{4,3,0,1,2:T(8,128)(2,1)S(1)}, bf16[2,2,2,64,256]{4,3,0,1,2:T(8,128)(2,1)S(1)}, u32[]{:S(2)}, u32[]{:S(2)}) %collective-permute-start.14) | collective-permute-done | bytes 262176 | tf_op jit(solution)/shard_map/ppermute | solution.py:45
  118.0 1.7 %collective-permute-start.11 = (bf16[2,2,64,256]{3,2,0,1:T(8,128)(2,1)S(1)}, bf16[2,2,64,256]{3,2,0,1:T(8,128)(2,1)S(1)}, u32[]{:S(2)}, u32[]{:S(2)}) collective-permute-start(bf16[2,2,64,256]{3,2,0,1:T(8,128)(2,1)S(1)} %fusion.10), channel_id=1, source_target_pairs={{0,4},{2,6},{4,0},{6,2},{8,12},{10,14},{12,8},{14,10},{16,20},{18,... | collective-permute-start | bytes 393224 | tf_op jit(solution)/shard_map/ppermute | solution.py:45
  119.8 3.3 %collective-permute-done.18 = bf16[2,2,2,64,256]{4,3,0,1,2:T(8,128)(2,1)S(1)} collective-permute-done((bf16[2,2,2,64,256]{4,3,0,1,2:T(8,128)(2,1)S(1)}, bf16[2,2,2,64,256]{4,3,0,1,2:T(8,128)(2,1)S(1)}, u32[]{:S(2)}, u32[]{:S(2)}) %collective-permute-start.18) | collective-permute-done | bytes 262176 | tf_op jit(solution)/shard_map/ppermute | solution.py:45
  123.1 1.8 %collective-permute-start.15 = (bf16[2,2,64,256]{3,2,0,1:T(8,128)(2,1)S(1)}, bf16[2,2,64,256]{3,2,0,1:T(8,128)(2,1)S(1)}, u32[]{:S(2)}, u32[]{:S(2)}) collective-permute-start(bf16[2,2,64,256]{3,2,0,1:T(8,128)(2,1)S(1)} %fusion.11), channel_id=1, source_target_pairs={{0,8},{2,10},{4,12},{6,14},{8,0},{10,2},{12,4},{14,6},{16,24},{18,... | collective-permute-start | bytes 393224 | tf_op jit(solution)/shard_map/ppermute | solution.py:45
  125.9 3.7 %collective-permute-start.8 = (bf16[2,64,256]{2,1,0:T(8,128)(2,1)S(1)}, bf16[2,64,256]{2,1,0:T(8,128)(2,1)S(1)}, u32[]{:S(2)}, u32[]{:S(2)}) collective-permute-start(bf16[2,64,256]{2,1,0:T(8,128)(2,1)S(1)} %fusion.17), channel_id=1, source_target_pairs={{0,16},{2,18},{4,20},{6,22},{8,24},{10,26},{12,28},{14,30},{16,0},... | collective-permute-start | bytes 196616 | tf_op jit(solution)/shard_map/ppermute | solution.py:45
  130.9 2.0 %collective-permute-start.16 = (bf16[2,64,256]{2,1,0:T(8,128)(2,1)S(1)}, bf16[2,64,256]{2,1,0:T(8,128)(2,1)S(1)}, u32[]{:S(2)}, u32[]{:S(2)}) collective-permute-start(bf16[2,64,256]{2,1,0:T(8,128)(2,1)S(1)} %fusion.19), channel_id=1, source_target_pairs={{0,16},{2,18},{4,20},{6,22},{8,24},{10,26},{12,28},{14,30},{16,0},... | collective-permute-start | bytes 196616 | tf_op jit(solution)/shard_map/ppermute | solution.py:45
  133.0 1.8 %collective-permute-done.8 = bf16[2,64,256]{2,1,0:T(8,128)(2,1)S(1)} collective-permute-done((bf16[2,64,256]{2,1,0:T(8,128)(2,1)S(1)}, bf16[2,64,256]{2,1,0:T(8,128)(2,1)S(1)}, u32[]{:S(2)}, u32[]{:S(2)}) %collective-permute-start.8) | collective-permute-done | bytes 65568 | tf_op jit(solution)/shard_map/ppermute | solution.py:45
  135.2 2.4 %collective-permute-done.12 = bf16[2,64,256]{2,1,0:T(8,128)(2,1)S(1)} collective-permute-done((bf16[2,64,256]{2,1,0:T(8,128)(2,1)S(1)}, bf16[2,64,256]{2,1,0:T(8,128)(2,1)S(1)}, u32[]{:S(2)}, u32[]{:S(2)}) %collective-permute-start.12) | collective-permute-done | bytes 65568 | tf_op jit(solution)/shard_map/ppermute | solution.py:45
  138.4 1.6 %collective-permute-done.20 = bf16[2,64,256]{2,1,0:T(8,128)(2,1)S(1)} collective-permute-done((bf16[2,64,256]{2,1,0:T(8,128)(2,1)S(1)}, bf16[2,64,256]{2,1,0:T(8,128)(2,1)S(1)}, u32[]{:S(2)}, u32[]{:S(2)}) %collective-permute-start.20) | collective-permute-done | bytes 65568 | tf_op jit(solution)/shard_map/ppermute | solution.py:45
  140.8 6.9 %shard_map.100 = (bf16[256,2048]{1,0:T(8,128)(2,1)}, bf16[256,2048]{1,0:T(8,128)(2,1)}) custom-call(f32[256,2048]{1,0:T(8,128)} %get-tuple-element.58.own_k_ref, f32[256,2048]{1,0:T(8,128)} %get-tuple-element.59.own_v_ref, bf16[256,1024]{1,0:T(8,128)(2,1)} %collective-permute-done.3.back_k_ref, bf16[256,1024]{1,0:T(8,128)(2,1)} %collective-permute-done.4.back_v_ref, ...), custom_call_target="tpu_custom_call" | custom-call | flops 67108864 | bytes 5242880 | tf_op jit(solution)/shard_map/pallas_call | solution.py:285
  (86 shorter events, 14.8 us)
Async XLA Ops:
  7.2 9.4 %copy-start.6 = (bf16[128,4096]{1,0:T(8,128)(2,1)S(1)}, bf16[128,4096]{1,0:T(8,128)(2,1)}, u32[]{:S(2)}) copy-start(bf16[128,4096]{1,0:T(8,128)(2,1)} %refs_0_.1) | copy-start | bytes 3145732
  7.2 65.4 %all-gather.2.cloned.1.call-start = ((), (), s32[]{:S(2)}) async-start(), calls=%async_computation | async-start | bytes 4456448 | tf_op jit(solution)/shard_map/all_gather | solution.py:324
  16.6 26.2 %collective-permute-start = (bf16[128,4096]{1,0:T(8,128)(2,1)S(1)}, bf16[128,4096]{1,0:T(8,128)(2,1)S(1)}, u32[]{:S(2)}, u32[]{:S(2)}) collective-permute-start(bf16[128,4096]{1,0:T(8,128)(2,1)S(1)} %copy-done.6), channel_id=1, source_target_pairs={{0,1},{1,0},{2,3},{3,2},{4,5},{5,4},{6,7},{7,6},{8,9},{9,8},{10,11... | collective-permute-start | bytes 3145736 | tf_op jit(solution)/shard_map/ppermute | solution.py:330
  19.6 40.5 %collective-permute-start.1 = (bf16[256,1024]{1,0:T(8,128)(2,1)}, bf16[256,1024]{1,0:T(8,128)(2,1)}, u32[]{:S(2)}, u32[]{:S(2)}) collective-permute-start(bf16[256,1024]{1,0:T(8,128)(2,1)} %get-tuple-element.38), channel_id=1, source_target_pairs={{0,2},{2,4},{4,6},{6,8},{8,10},{10,12},{12,14},{14,16},{16,18},{18... | collective-permute-start | bytes 1572872 | tf_op jit(solution)/shard_map/ppermute | solution.py:21
  21.8 38.2 %collective-permute-start.2 = (bf16[256,1024]{1,0:T(8,128)(2,1)}, bf16[256,1024]{1,0:T(8,128)(2,1)}, u32[]{:S(2)}, u32[]{:S(2)}) collective-permute-start(bf16[256,1024]{1,0:T(8,128)(2,1)} %get-tuple-element.39), channel_id=1, source_target_pairs={{0,2},{2,4},{4,6},{6,8},{8,10},{10,12},{12,14},{14,16},{16,18},{18... | collective-permute-start | bytes 1572872 | tf_op jit(solution)/shard_map/ppermute | solution.py:21
  44.9 15.1 %copy-start = (bf16[256,2048]{1,0:T(8,128)(2,1)S(1)}, bf16[256,2048]{1,0:T(8,128)(2,1)}, u32[]{:S(2)}) copy-start(bf16[256,2048]{1,0:T(8,128)(2,1)} %k_ref.11) | copy-start | bytes 3145732
  44.9 15.1 %copy-start.1 = (bf16[256,2048]{1,0:T(8,128)(2,1)S(1)}, bf16[256,2048]{1,0:T(8,128)(2,1)}, u32[]{:S(2)}) copy-start(bf16[256,2048]{1,0:T(8,128)(2,1)} %v_ref.11) | copy-start | bytes 3145732
  44.9 15.1 %copy-start.4 = (bf16[256,2048]{1,0:T(8,128)(2,1)S(1)}, bf16[256,2048]{1,0:T(8,128)(2,1)}, u32[]{:S(2)}) copy-start(bf16[256,2048]{1,0:T(8,128)(2,1)} %q_ref.9) | copy-start | bytes 3145732
  60.1 12.5 %copy-start.3 = (bf16[256,2048]{1,0:T(8,128)(2,1)S(1)}, bf16[256,2048]{1,0:T(8,128)(2,1)}, u32[]{:S(2)}) copy-start(bf16[256,2048]{1,0:T(8,128)(2,1)} %copy-done.2) | copy-start | bytes 3145732
  69.8 70.9 %collective-permute-start.3 = (bf16[256,1024]{1,0:T(8,128)(2,1)}, bf16[256,1024]{1,0:T(8,128)(2,1)}, u32[]{:S(2)}, u32[]{:S(2)}) collective-permute-start(bf16[256,1024]{1,0:T(8,128)(2,1)} %get-tuple-element.60), channel_id=1, source_target_pairs={{2,0},{4,2},{6,4},{8,6},{10,8},{12,10},{14,12},{16,14},{18,16},{20... | collective-permute-start | bytes 1572872 | tf_op jit(solution)/shard_map/ppermute | solution.py:21
  71.1 69.7 %collective-permute-start.4 = (bf16[256,1024]{1,0:T(8,128)(2,1)}, bf16[256,1024]{1,0:T(8,128)(2,1)}, u32[]{:S(2)}, u32[]{:S(2)}) collective-permute-start(bf16[256,1024]{1,0:T(8,128)(2,1)} %get-tuple-element.61), channel_id=1, source_target_pairs={{2,0},{4,2},{6,4},{8,6},{10,8},{12,10},{14,12},{16,14},{18,16},{20... | collective-permute-start | bytes 1572872 | tf_op jit(solution)/shard_map/ppermute | solution.py:21
  72.6 1.2 copy-start.5
  80.5 22.8 %collective-permute-start.5 = (bf16[2,2,2,2,64,256]{5,4,0,1,2,3:T(8,128)(2,1)S(1)}, bf16[2,2,2,2,64,256]{5,4,0,1,2,3:T(8,128)(2,1)S(1)}, u32[]{:S(2)}, u32[]{:S(2)}) collective-permute-start(bf16[2,2,2,2,64,256]{5,4,0,1,2,3:T(8,128)(2,1)S(1)} %fusion), channel_id=1, source_target_pairs={{0,2},{2,0},{4,6},{6,4},{8,10},{10,8},{12,14},{14,12},{16,18},{18,... | collective-permute-start | bytes 1572872 | tf_op jit(solution)/shard_map/ppermute | solution.py:45
  89.0 14.6 %collective-permute-start.9 = (bf16[2,2,2,2,64,256]{5,4,0,1,3,2:T(8,128)(2,1)S(1)}, bf16[2,2,2,2,64,256]{5,4,0,1,3,2:T(8,128)(2,1)S(1)}, u32[]{:S(2)}, u32[]{:S(2)}) collective-permute-start(bf16[2,2,2,2,64,256]{5,4,0,1,3,2:T(8,128)(2,1)S(1)} %fusion.1), channel_id=1, source_target_pairs={{0,2},{2,0},{4,6},{6,4},{8,10},{10,8},{12,14},{14,12},{16,18},{18,... | collective-permute-start | bytes 1572872 | tf_op jit(solution)/shard_map/ppermute | solution.py:45
  95.8 10.1 %collective-permute-start.13 = (bf16[2,2,2,2,64,256]{5,4,0,1,2,3:T(8,128)(2,1)S(1)}, bf16[2,2,2,2,64,256]{5,4,0,1,2,3:T(8,128)(2,1)S(1)}, u32[]{:S(2)}, u32[]{:S(2)}) collective-permute-start(bf16[2,2,2,2,64,256]{5,4,0,1,2,3:T(8,128)(2,1)S(1)} %fusion.2), channel_id=1, source_target_pairs={{0,2},{2,0},{4,6},{6,4},{8,10},{10,8},{12,14},{14,12},{16,18},{18,... | collective-permute-start | bytes 1572872 | tf_op jit(solution)/shard_map/ppermute | solution.py:45
  96.3 7.1 %copy-start.9 = (f32[2,1024,256]{2,1,0:T(8,128)S(1)}, f32[2,1024,256]{2,1,0:T(8,128)}, u32[]{:S(2)}) copy-start(f32[2,1024,256]{2,1,0:T(8,128)} %get-tuple-element.62) | copy-start | bytes 6291460
  101.8 3.9 %copy-start.10 = (f32[2,1024,256]{2,1,0:T(8,128)S(1)}, f32[2,1024,256]{2,1,0:T(8,128)}, u32[]{:S(2)}) copy-start(f32[2,1024,256]{2,1,0:T(8,128)} %get-tuple-element.63) | copy-start | bytes 6291460
  103.3 4.8 %collective-permute-start.17 = (bf16[2,2,2,2,64,256]{5,4,0,1,3,2:T(8,128)(2,1)S(1)}, bf16[2,2,2,2,64,256]{5,4,0,1,3,2:T(8,128)(2,1)S(1)}, u32[]{:S(2)}, u32[]{:S(2)}) collective-permute-start(bf16[2,2,2,2,64,256]{5,4,0,1,3,2:T(8,128)(2,1)S(1)} %fusion.3), channel_id=1, source_target_pairs={{0,2},{2,0},{4,6},{6,4},{8,10},{10,8},{12,14},{14,12},{16,18},{18,... | collective-permute-start | bytes 1572872 | tf_op jit(solution)/shard_map/ppermute | solution.py:45
  103.6 4.3 %copy-start.12 = (f32[2,1024,256]{2,1,0:T(8,128)S(1)}, f32[2,1024,256]{2,1,0:T(8,128)}, u32[]{:S(2)}) copy-start(f32[2,1024,256]{2,1,0:T(8,128)} %get-tuple-element.64) | copy-start | bytes 6291460
  103.7 9.2 %collective-permute-start.6 = (bf16[2,2,2,64,256]{4,3,0,1,2:T(8,128)(2,1)S(1)}, bf16[2,2,2,64,256]{4,3,0,1,2:T(8,128)(2,1)S(1)}, u32[]{:S(2)}, u32[]{:S(2)}) collective-permute-start(bf16[2,2,2,64,256]{4,3,0,1,2:T(8,128)(2,1)S(1)} %fusion.5), channel_id=1, source_target_pairs={{0,4},{2,6},{4,0},{6,2},{8,12},{10,14},{12,8},{14,10},{16,20},{18,... | collective-permute-start | bytes 786440 | tf_op jit(solution)/shard_map/ppermute | solution.py:45
  105.9 3.6 %copy-start.11 = (f32[2,1024,256]{2,1,0:T(8,128)S(1)}, f32[2,1024,256]{2,1,0:T(8,128)}, u32[]{:S(2)}) copy-start(f32[2,1024,256]{2,1,0:T(8,128)} %get-tuple-element.65) | copy-start | bytes 6291460
  106.0 10.2 %collective-permute-start.10 = (bf16[2,2,2,64,256]{4,3,0,1,2:T(8,128)(2,1)S(1)}, bf16[2,2,2,64,256]{4,3,0,1,2:T(8,128)(2,1)S(1)}, u32[]{:S(2)}, u32[]{:S(2)}) collective-permute-start(bf16[2,2,2,64,256]{4,3,0,1,2:T(8,128)(2,1)S(1)} %fusion.6), channel_id=1, source_target_pairs={{0,8},{2,10},{4,12},{6,14},{8,0},{10,2},{12,4},{14,6},{16,24},{18,... | collective-permute-start | bytes 786440 | tf_op jit(solution)/shard_map/ppermute | solution.py:45
  108.1 9.9 %collective-permute-start.14 = (bf16[2,2,2,64,256]{4,3,0,1,2:T(8,128)(2,1)S(1)}, bf16[2,2,2,64,256]{4,3,0,1,2:T(8,128)(2,1)S(1)}, u32[]{:S(2)}, u32[]{:S(2)}) collective-permute-start(bf16[2,2,2,64,256]{4,3,0,1,2:T(8,128)(2,1)S(1)} %fusion.7), channel_id=1, source_target_pairs={{0,4},{2,6},{4,0},{6,2},{8,12},{10,14},{12,8},{14,10},{16,20},{18,... | collective-permute-start | bytes 786440 | tf_op jit(solution)/shard_map/ppermute | solution.py:45
  112.9 10.3 %collective-permute-start.18 = (bf16[2,2,2,64,256]{4,3,0,1,2:T(8,128)(2,1)S(1)}, bf16[2,2,2,64,256]{4,3,0,1,2:T(8,128)(2,1)S(1)}, u32[]{:S(2)}, u32[]{:S(2)}) collective-permute-start(bf16[2,2,2,64,256]{4,3,0,1,2:T(8,128)(2,1)S(1)} %fusion.8), channel_id=1, source_target_pairs={{0,8},{2,10},{4,12},{6,14},{8,0},{10,2},{12,4},{14,6},{16,24},{18,... | collective-permute-start | bytes 786440 | tf_op jit(solution)/shard_map/ppermute | solution.py:45
  116.2 8.9 %collective-permute-start.7 = (bf16[2,2,64,256]{3,2,0,1:T(8,128)(2,1)S(1)}, bf16[2,2,64,256]{3,2,0,1:T(8,128)(2,1)S(1)}, u32[]{:S(2)}, u32[]{:S(2)}) collective-permute-start(bf16[2,2,64,256]{3,2,0,1:T(8,128)(2,1)S(1)} %fusion.9), channel_id=1, source_target_pairs={{0,8},{2,10},{4,12},{6,14},{8,0},{10,2},{12,4},{14,6},{16,24},{18,... | collective-permute-start | bytes 393224 | tf_op jit(solution)/shard_map/ppermute | solution.py:45
  118.0 7.9 %collective-permute-start.11 = (bf16[2,2,64,256]{3,2,0,1:T(8,128)(2,1)S(1)}, bf16[2,2,64,256]{3,2,0,1:T(8,128)(2,1)S(1)}, u32[]{:S(2)}, u32[]{:S(2)}) collective-permute-start(bf16[2,2,64,256]{3,2,0,1:T(8,128)(2,1)S(1)} %fusion.10), channel_id=1, source_target_pairs={{0,4},{2,6},{4,0},{6,2},{8,12},{10,14},{12,8},{14,10},{16,20},{18,... | collective-permute-start | bytes 393224 | tf_op jit(solution)/shard_map/ppermute | solution.py:45
  123.1 6.5 %collective-permute-start.15 = (bf16[2,2,64,256]{3,2,0,1:T(8,128)(2,1)S(1)}, bf16[2,2,64,256]{3,2,0,1:T(8,128)(2,1)S(1)}, u32[]{:S(2)}, u32[]{:S(2)}) collective-permute-start(bf16[2,2,64,256]{3,2,0,1:T(8,128)(2,1)S(1)} %fusion.11), channel_id=1, source_target_pairs={{0,8},{2,10},{4,12},{6,14},{8,0},{10,2},{12,4},{14,6},{16,24},{18,... | collective-permute-start | bytes 393224 | tf_op jit(solution)/shard_map/ppermute | solution.py:45
  125.2 5.7 %collective-permute-start.19 = (bf16[2,2,64,256]{3,2,0,1:T(8,128)(2,1)S(1)}, bf16[2,2,64,256]{3,2,0,1:T(8,128)(2,1)S(1)}, u32[]{:S(2)}, u32[]{:S(2)}) collective-permute-start(bf16[2,2,64,256]{3,2,0,1:T(8,128)(2,1)S(1)} %fusion.12), channel_id=1, source_target_pairs={{0,4},{2,6},{4,0},{6,2},{8,12},{10,14},{12,8},{14,10},{16,20},{18,... | collective-permute-start | bytes 393224 | tf_op jit(solution)/shard_map/ppermute | solution.py:45
  125.9 8.9 %collective-permute-start.8 = (bf16[2,64,256]{2,1,0:T(8,128)(2,1)S(1)}, bf16[2,64,256]{2,1,0:T(8,128)(2,1)S(1)}, u32[]{:S(2)}, u32[]{:S(2)}) collective-permute-start(bf16[2,64,256]{2,1,0:T(8,128)(2,1)S(1)} %fusion.17), channel_id=1, source_target_pairs={{0,16},{2,18},{4,20},{6,22},{8,24},{10,26},{12,28},{14,30},{16,0},... | collective-permute-start | bytes 196616 | tf_op jit(solution)/shard_map/ppermute | solution.py:45
  129.6 8.0 %collective-permute-start.12 = (bf16[2,64,256]{2,1,0:T(8,128)(2,1)S(1)}, bf16[2,64,256]{2,1,0:T(8,128)(2,1)S(1)}, u32[]{:S(2)}, u32[]{:S(2)}) collective-permute-start(bf16[2,64,256]{2,1,0:T(8,128)(2,1)S(1)} %fusion.18), channel_id=1, source_target_pairs={{0,16},{2,18},{4,20},{6,22},{8,24},{10,26},{12,28},{14,30},{16,0},... | collective-permute-start | bytes 196616 | tf_op jit(solution)/shard_map/ppermute | solution.py:45
  130.9 7.5 %collective-permute-start.16 = (bf16[2,64,256]{2,1,0:T(8,128)(2,1)S(1)}, bf16[2,64,256]{2,1,0:T(8,128)(2,1)S(1)}, u32[]{:S(2)}, u32[]{:S(2)}) collective-permute-start(bf16[2,64,256]{2,1,0:T(8,128)(2,1)S(1)} %fusion.19), channel_id=1, source_target_pairs={{0,16},{2,18},{4,20},{6,22},{8,24},{10,26},{12,28},{14,30},{16,0},... | collective-permute-start | bytes 196616 | tf_op jit(solution)/shard_map/ppermute | solution.py:45
  134.8 5.2 %collective-permute-start.20 = (bf16[2,64,256]{2,1,0:T(8,128)(2,1)S(1)}, bf16[2,64,256]{2,1,0:T(8,128)(2,1)S(1)}, u32[]{:S(2)}, u32[]{:S(2)}) collective-permute-start(bf16[2,64,256]{2,1,0:T(8,128)(2,1)S(1)} %fusion.20), channel_id=1, source_target_pairs={{0,16},{2,18},{4,20},{6,22},{8,24},{10,26},{12,28},{14,30},{16,0},... | collective-permute-start | bytes 196616 | tf_op jit(solution)/shard_map/ppermute | solution.py:45
  (3 other events, 3.2 us)
Sparse Core Ops, SparseCore 0:
  16.7 54.7 all-gather.1

commit v8 on v6

--- a/solution.py
+++ b/solution.py
@@ -31,10 +31,7 @@
     bits = count.bit_length() - 1
     chunk = parts.shape[axis] // count
     held = parts.reshape(parts.shape[:axis] + (2,) * bits + (chunk,) + parts.shape[axis + 1 :])
-    if bits > 2:
-        order = [0] + sorted(range(1, bits - 1), key=lambda b: (b - 1 - rotate) % (bits - 2)) + [bits - 1]
-    else:
-        order = list(range(bits))
+    order = rotated_order(bits, rotate)
     gone = []
     for bit in order:
         where = axis + bits - 1 - bit - sum(1 for done in gone if done > bit)
@@ -47,6 +44,32 @@
         )
         held = keep + arrived.astype(jnp.float32)
     return held.astype(jnp.bfloat16)
+
+
+def rotated_order(bits, rotate):
+    if bits > 2:
+        return [0] + sorted(range(1, bits - 1), key=lambda b: (b - 1 - rotate) % (bits - 2)) + [bits - 1]
+    return list(range(bits))
+
+
+def seq_all_gather(local, rotate):
+    count = lax.axis_size("seq")
+    if count & (count - 1):
+        return lax.all_gather(local, "seq", axis=0, tiled=True)
+    me = lax.axis_index("seq")
+    bits = count.bit_length() - 1
+    order = rotated_order(bits, rotate)[::-1]
+    held = local
+    for step, bit in enumerate(order):
+        mine = (me >> bit) & 1
+        arrived = lax.ppermute(held, "seq", [(source, source ^ (1 << bit)) for source in range(count)])
+        pair = jnp.stack([held, arrived], step)
+        swapped = jnp.stack([arrived, held], step)
+        held = jnp.where(mine == 0, pair, swapped)
+    placed = sorted(range(bits), key=lambda b: order.index(b))
+    axes = [placed.index(b) for b in range(bits - 1, -1, -1)]
+    held = held.transpose(axes + list(range(bits, held.ndim)))
+    return held.reshape((count * local.shape[0],) + local.shape[1:])
 
 
 def nt(left, right):
@@ -167,12 +190,13 @@
     )(seq_index, q, k, v, g, k_prev, v_prev)
 
 
-def fixed_attention(seq_index, q, k, v, g, far_kv, first_pair, pairs, head_pairs, head_dim, scale, earlier):
+def fixed_attention(seq_index, q, k, v, g, far_kv, first_pair, pairs, far_first, head_dim, scale, earlier):
     rows = q.shape[0]
     far_rows = far_kv.shape[0]
+    far_pairs = far_kv.shape[1] // (2 * head_dim)
     block = pl.BlockSpec((rows, head_dim), lambda p, s: (0, 2 * (first_pair + p) + 1))
-    far_k_spec = pl.BlockSpec((far_rows, head_dim), lambda p, s: (0, first_pair + p))
-    far_v_spec = pl.BlockSpec((far_rows, head_dim), lambda p, s: (0, head_pairs + first_pair + p))
+    far_k_spec = pl.BlockSpec((far_rows, head_dim), lambda p, s: (0, far_first + p))
+    far_v_spec = pl.BlockSpec((far_rows, head_dim), lambda p, s: (0, far_pairs + far_first + p))
     operands = [seq_index, q, k, v, g, far_kv, far_kv] + list(earlier)
     aliases = {7 + number: number for number in range(len(earlier))}
     grid_spec = pltpu.PrefetchScalarGridSpec(
@@ -260,19 +284,14 @@
     digest_v = jnp.einsum(
         "hjr,rhc->jhc", select, fixed_v, preferred_element_type=jnp.float32
     ).astype(jnp.bfloat16)
-    pair_width = head_pairs * head_dim
-    far_kv = lax.all_gather(
-        jnp.concatenate(
-            [
-                digest_k.reshape(digest_count, pair_width),
-                digest_v.reshape(digest_count, pair_width),
-            ],
-            1,
-        ),
-        "seq",
-        axis=0,
-        tiled=True,
-    )
+    gathers = 2 if head_pairs % 2 == 0 else 1
+    gather_pairs = head_pairs // gathers
+    split_dk = digest_k.reshape(digest_count, gathers, gather_pairs * head_dim)
+    split_dv = digest_v.reshape(digest_count, gathers, gather_pairs * head_dim)
+    far_parts = [
+        seq_all_gather(jnp.concatenate([split_dk[:, part], split_dv[:, part]], 1), part)
+        for part in range(gathers)
+    ]
     head_count = lax.axis_size("head")
     head_index = lax.axis_index("head")
     pieces = [cotangent] + [
@@ -298,16 +317,17 @@
     outputs = (attention, query_grad, own_dk, own_dv)
     digests = []
     for chunk in range(chunks):
+        part = chunk * pairs // gather_pairs
         *outputs, far_dkv = fixed_attention(
             seq_scalar,
             queries,
             keys,
             values,
             grad_out,
-            far_kv,
+            far_parts[part],
             chunk * pairs,
             pairs,
-            head_pairs,
+            chunk * pairs - part * gather_pairs,
             head_dim,
             score_scale,
             outputs,

time: 149 us -> 172 us (1.15)
  between operations: 14.5 us -> 1.2 us
  starting transfers between devices: 35 us -> 46 us
  other arithmetic: 7.26 us -> 17.2 us
  waiting for transfers between devices: 27.2 us -> 35.2 us
  local copies, waits for them, and re-layouts: 13 us -> 20.8 us
    ppermute x0 -> x8, waiting for transfers between devices: none -> 16.8 us  [seq_all_gather(): lax.ppermute(held, 'seq', [(source, source ^ 1 << bit) for source in rang...]
    ppermute x0 -> x8, starting transfers between devices: none -> 16.7 us  [seq_all_gather(): lax.ppermute(held, 'seq', [(source, source ^ 1 << bit) for source in rang...]
    ppermute x1, waiting for transfers between devices: 12.5 us -> 0.01 us  [on_device(): lax.ppermute(cotangent, 'head', [(source, (source + shift) % head_count)...]
    select_n x0 -> x13, other arithmetic: none -> 6.92 us  [seq_all_gather(): held = jnp.where(mine == 0, pair, swapped)]
    ppermute x16, starting transfers between devices: 23 us -> 18.7 us  [seq_reduce_scatter(): lax.ppermute(send.astype(jnp.bfloat16), 'seq', [(source, source ^ 1 << bi...]
    ppermute x16, waiting for transfers between devices: 14.7 us -> 18.5 us  [seq_reduce_scatter(): lax.ppermute(send.astype(jnp.bfloat16), 'seq', [(source, source ^ 1 << bi...]
    transpose x0 -> x1, other arithmetic: none -> 1.86 us  [seq_all_gather(): held = held.transpose(axes + list(range(bits, held.ndim)))]
    another operation x0 -> x6, other arithmetic: none -> 1.81 us  [seq_all_gather(): pair = jnp.stack([held, arrived], step)]
  transfers between devices with their start and end apart: 22 -> 29, of which waited for: 9 -> 15; matrix products, arithmetic and copies ran while one was open for 19% -> 24% of each run, Pallas kernels for 21% -> 18%
where the time goes in v8:
time: 172 us; the launch traced here: 171 us
  starting transfers between devices  46 us (27%)
  Pallas kernels  38.4 us (22%)
  waiting for transfers between devices  35.2 us (20%)
  local copies, waits for them, and re-layouts  20.8 us (12%)
  other arithmetic  17.2 us (10%)
  matrix products  12.7 us (7%)
    pallas_call x4, Pallas kernels, fixed_attention(): pl.pallas_call(functools.partial(fixed_kernel, scale=scale, unused=len(ea...  21.7 us
    ppermute x16, starting transfers between devices, seq_reduce_scatter(): lax.ppermute(send.astype(jnp.bfloat16), 'seq', [(source, source ^ 1 << bi...  18.7 us
    ppermute x16, waiting for transfers between devices, seq_reduce_scatter(): lax.ppermute(send.astype(jnp.bfloat16), 'seq', [(source, source ^ 1 << bi...  18.5 us
    ppermute x8, waiting for transfers between devices, seq_all_gather(): lax.ppermute(held, 'seq', [(source, source ^ 1 << bit) for source in rang...  16.8 us
    ppermute x8, starting transfers between devices, seq_all_gather(): lax.ppermute(held, 'seq', [(source, source ^ 1 << bit) for source in rang...  16.7 us
    dot_general x1, matrix products, on_device(): lax.dot_general(gathered.reshape(seq_rows, cotangent.shape[1]), out_weigh...  12 us
    pallas_call x1, Pallas kernels, band_attention(): pl.pallas_call(functools.partial(band_kernel, scale=scale), grid_spec=gri...  9.84 us
    ppermute x4, starting transfers between devices, passed_along(): lax.ppermute(value, axis, [(source, source + steps) for source in range(f...  8.98 us
  transfers between devices with their start and end apart: 29, of which 15 were waited for; matrix products, arithmetic and copies ran while one was open for 24% of the time, Pallas kernels for 18%

profile of v8, /device:TPU:0, one launch (start us, length us, event | category | flops | bytes accessed | tf_op | source)
XLA Modules:
  0.0 171.5 jit_solution(18432285109546356599)
XLA Ops:
  8.5 4.0 %collective-permute-start.5 = (bf16[64,1024]{1,0:T(8,128)(2,1)}, bf16[64,1024]{1,0:T(8,128)(2,1)S(1)}, u32[]{:S(2)}, u32[]{:S(2)}) collective-permute-start(bf16[64,1024]{1,0:T(8,128)(2,1)} %get-tuple-element.62), channel_id=1, source_target_pairs={{0,16},{2,18},{4,20},{6,22},{8,24},{10,26},{12,28},{14,30},{16,0},... | collective-permute-start | bytes 393224 | tf_op jit(solution)/shard_map/ppermute | solution.py:65
  14.9 2.0 %copy.103 = bf16[256,1024]{1,0:T(8,128)(2,1)} copy(bf16[256,1024]{0,1:T(8,128)(2,1)} %bitcast.180) | data formatting | bytes 1048576 | tf_op jit(solution)/shard_map/reshape;squeeze | solution.py:271
  16.9 2.1 %collective-permute-start.10 = (bf16[256,1024]{1,0:T(8,128)(2,1)}, bf16[256,1024]{1,0:T(8,128)(2,1)}, u32[]{:S(2)}, u32[]{:S(2)}) collective-permute-start(bf16[256,1024]{1,0:T(8,128)(2,1)} %copy.103), channel_id=1, source_target_pairs={{0,2},{2,4},{4,6},{6,8},{8,10},{10,12},{12,14},{14,16},{16,18},{18... | collective-permute-start | bytes 1572872 | tf_op jit(solution)/shard_map/ppermute | solution.py:21
  20.1 4.1 %collective-permute-start.9 = (bf16[256,1024]{1,0:T(8,128)(2,1)}, bf16[256,1024]{1,0:T(8,128)(2,1)}, u32[]{:S(2)}, u32[]{:S(2)}) collective-permute-start(bf16[256,1024]{1,0:T(8,128)(2,1)} %copy.102), channel_id=1, source_target_pairs={{0,2},{2,4},{4,6},{6,8},{8,10},{10,12},{12,14},{14,16},{16,18},{18... | collective-permute-start | bytes 1572872 | tf_op jit(solution)/shard_map/ppermute | solution.py:21
  27.3 6.3 %collective-permute-done.1 = bf16[64,1024]{1,0:T(8,128)(2,1)S(1)} collective-permute-done((bf16[64,1024]{1,0:T(8,128)(2,1)S(1)}, bf16[64,1024]{1,0:T(8,128)(2,1)S(1)}, u32[]{:S(2)}, u32[]{:S(2)}) %collective-permute-start.1) | collective-permute-done | bytes 131104 | tf_op jit(solution)/shard_map/ppermute | solution.py:65
  34.1 2.2 %collective-permute-done.6 = bf16[2,64,1024]{2,1,0:T(8,128)(2,1)S(1)} collective-permute-done((bf16[2,64,1024]{2,1,0:T(8,128)(2,1)S(1)}, bf16[2,64,1024]{2,1,0:T(8,128)(2,1)S(1)}, u32[]{:S(2)}, u32[]{:S(2)}) %collective-permute-start.6) | collective-permute-done | bytes 262176 | tf_op jit(solution)/shard_map/ppermute | solution.py:65
  36.4 1.7 %collective-permute-start.7 = (bf16[2,2,64,1024]{3,2,0,1:T(8,128)(2,1)S(1)}, bf16[2,2,64,1024]{3,2,0,1:T(8,128)(2,1)S(1)}, u32[]{:S(2)}, u32[]{:S(2)}) collective-permute-start(bf16[2,2,64,1024]{3,2,0,1:T(8,128)(2,1)S(1)} %maximum_select_fusion.9), channel_id=1, source_target_pairs={{0,4},{2,6},{4,0},{6,2},{8,12},{10,14},{12,8},{14,10},{16,20},{18,... | collective-permute-start | bytes 1572872 | tf_op jit(solution)/shard_map/ppermute | solution.py:65
  38.1 2.0 %collective-permute-done.2 = bf16[2,64,1024]{2,1,0:T(8,128)(2,1)S(1)} collective-permute-done((bf16[2,64,1024]{2,1,0:T(8,128)(2,1)S(1)}, bf16[2,64,1024]{2,1,0:T(8,128)(2,1)S(1)}, u32[]{:S(2)}, u32[]{:S(2)}) %collective-permute-start.2) | collective-permute-done | bytes 262176 | tf_op jit(solution)/shard_map/ppermute | solution.py:65
  40.1 4.6 %collective-permute-start.3 = (bf16[2,2,64,1024]{3,2,0,1:T(8,128)(2,1)S(1)}, bf16[2,2,64,1024]{3,2,0,1:T(8,128)(2,1)S(1)}, u32[]{:S(2)}, u32[]{:S(2)}) collective-permute-start(bf16[2,2,64,1024]{3,2,0,1:T(8,128)(2,1)S(1)} %maximum_select_fusion.7), channel_id=1, source_target_pairs={{0,8},{2,10},{4,12},{6,14},{8,0},{10,2},{12,4},{14,6},{16,24},{18,... | collective-permute-start | bytes 1572872 | tf_op jit(solution)/shard_map/ppermute | solution.py:65
  45.0 5.7 %collective-permute-done.7 = bf16[2,2,64,1024]{3,2,0,1:T(8,128)(2,1)S(1)} collective-permute-done((bf16[2,2,64,1024]{3,2,0,1:T(8,128)(2,1)S(1)}, bf16[2,2,64,1024]{3,2,0,1:T(8,128)(2,1)S(1)}, u32[]{:S(2)}, u32[]{:S(2)}) %collective-permute-start.7) | collective-permute-done | bytes 524320 | tf_op jit(solution)/shard_map/ppermute | solution.py:65
  51.9 3.5 %collective-permute-start.8 = (bf16[2,2,2,64,1024]{4,3,0,1,2:T(8,128)(2,1)}, bf16[2,2,2,64,1024]{4,3,0,1,2:T(8,128)(2,1)}, u32[]{:S(2)}, u32[]{:S(2)}) collective-permute-start(bf16[2,2,2,64,1024]{4,3,0,1,2:T(8,128)(2,1)} %maximum_select_fusion.5), channel_id=1, source_target_pairs={{0,2},{2,0},{4,6},{6,4},{8,10},{10,8},{12,14},{14,12},{16,18},{18,... | collective-permute-start | bytes 3145736 | tf_op jit(solution)/shard_map/ppermute | solution.py:65
  60.8 4.0 %fusion.2 = bf16[2,128,4096]{2,1,0:T(8,128)(2,1)} fusion(s32[]{:T(128)S(6)} %select_n.221, bf16[1,128,4096]{2,1,0:T(8,128)(2,1)} %bitcast.1, bf16[1,128,4096]{2,1,0:T(8,128)(2,1)S(1)} %bitcast.196), kind=kLoop, calls=%fused_computation.7 | loop fusion | flops 3145728 | bytes 4194308 | tf_op jit(solution)/shard_map/stack | solution.py:303
  64.8 12.0 %convolution_convert_fusion.g_ref = bf16[256,2048]{1,0:T(8,128)(2,1)} fusion(bf16[256,4096]{1,0:T(8,128)(2,1)} %bitcast.179, bf16[2048,4096]{1,0:T(8,128)(2,1)} %param.9), kind=kOutput, calls=%fused_computation.4 | convolution fusion | flops 4295491584 | bytes 19922944 | tf_op jit(solution)/shard_map/dot_general | solution.py:305
  76.9 9.8 %shard_map.93 = (bf16[256,2048]{1,0:T(8,128)(2,1)}, bf16[256,2048]{1,0:T(8,128)(2,1)}, f32[256,2048]{1,0:T(8,128)}, f32[256,2048]{1,0:T(8,128)}, bf16[256,1024]{...) custom-call(s32[1]{0:T(128)} %bitcast.seq_ref, bf16[256,2048]{1,0:T(8,128)(2,1)S(1)} %copy-done.2, ...), custom_call_target="tpu_custom_call" | custom-call | flops 1879048192 | bytes 7340032 | tf_op jit(solution)/shard_map/pallas_call | solution.py:177
  89.5 1.9 %maximum_select_fusion.1 = bf16[2,2,2,2,64,1024]{5,4,0,1,2,3:T(8,128)(2,1)S(1)} fusion(bf16[2,2,2,1,64,1024]{5,4,0,1,2,3:T(8,128)(2,1)} %bitcast.39, bf16[2,2,2,1,64,1024]{5,4,0,1,2,3:T(8,128)(2,1)S(1)} %copy-done.5, pred[]{:T(512)S(6)} %eq.14), kind=kLoop, calls=%fused_computation.10 | loop fusion | flops 3145728 | bytes 4194305 | tf_op jit(solution)/shard_map/jit(_where)/select_n | solution.py:68
  93.0 5.4 %shard_map.94 = (bf16[256,2048]{1,0:T(8,128)(2,1)}, bf16[256,2048]{1,0:T(8,128)(2,1)}, f32[256,2048]{1,0:T(8,128)}, f32[256,2048]{1,0:T(8,128)}, f32[2,1024,256]{2,1,0:T(8,128)}) custom-call(s32[1]{0:T(128)} %bitcast.seq_ref, bf16[256,2048]{1,0:T(8,128)(2,1)S(1)} %copy-done.2, ...), custom_call_target="tpu_custom_call", output_to_operand_aliasing={{0}: (7, {}), {1}: (8, {}), {2}: (9, {}), {3}: (10, {})} | custom-call | flops 1174405120 | bytes 3014656 | tf_op jit(solution)/shard_map/pallas_call | solution.py:209
  99.7 1.8 %collective-permute-start.13 = (bf16[2,2,2,2,64,256]{5,4,0,1,2,3:T(8,128)(2,1)S(1)}, bf16[2,2,2,2,64,256]{5,4,0,1,2,3:T(8,128)(2,1)S(1)}, u32[]{:S(2)}, u32[]{:S(2)}) collective-permute-start(bf16[2,2,2,2,64,256]{5,4,0,1,2,3:T(8,128)(2,1)S(1)} %fusion.6), channel_id=1, source_target_pairs={{0,2},{2,0},{4,6},{6,4},{8,10},{10,8},{12,14},{14,12},{16,18},{18,... | collective-permute-start | bytes 1572872 | tf_op jit(solution)/shard_map/ppermute | solution.py:42
  101.5 5.4 %shard_map.95 = (bf16[256,2048]{1,0:T(8,128)(2,1)}, bf16[256,2048]{1,0:T(8,128)(2,1)}, f32[256,2048]{1,0:T(8,128)}, f32[256,2048]{1,0:T(8,128)}, f32[2,1024,256]{2,1,0:T(8,128)}) custom-call(s32[1]{0:T(128)} %bitcast.seq_ref, bf16[256,2048]{1,0:T(8,128)(2,1)S(1)} %copy-done.2, ...), custom_call_target="tpu_custom_call", output_to_operand_aliasing={{0}: (7, {}), {1}: (8, {}), {2}: (9, {}), {3}: (10, {})} | custom-call | flops 1174405120 | bytes 3014656 | tf_op jit(solution)/shard_map/pallas_call | solution.py:209
  108.4 1.9 %fusion.3 = bf16[2,2,2,2,64,1024]{5,4,0,2,1,3:T(8,128)(2,1)S(1)} fusion(bf16[2,2,2,1,64,1024]{5,4,0,1,2,3:T(8,128)(2,1)} %bitcast.23, bf16[2,2,2,1,64,1024]{5,4,0,1,2,3:T(8,128)(2,1)S(1)} %copy-done.4, pred[]{:T(512)S(6)} %eq.14), kind=kLoop, calls=%fused_computation.9 | loop fusion | flops 3145728 | bytes 4194305 | tf_op jit(solution)/shard_map/transpose | solution.py:71
  111.9 5.4 %shard_map.96 = (bf16[256,2048]{1,0:T(8,128)(2,1)}, bf16[256,2048]{1,0:T(8,128)(2,1)}, f32[256,2048]{1,0:T(8,128)}, f32[256,2048]{1,0:T(8,128)}, f32[2,1024,256]{2,1,0:T(8,128)}) custom-call(s32[1]{0:T(128)} %bitcast.seq_ref, bf16[256,2048]{1,0:T(8,128)(2,1)S(1)} %copy-done.2, ...), custom_call_target="tpu_custom_call", output_to_operand_aliasing={{0}: (7, {}), {1}: (8, {}), {2}: (9, {}), {3}: (10, {})} | custom-call | flops 1174405120 | bytes 3014656 | tf_op jit(solution)/shard_map/pallas_call | solution.py:209
  119.1 5.5 %shard_map.97 = (bf16[256,2048]{1,0:T(8,128)(2,1)}, bf16[256,2048]{1,0:T(8,128)(2,1)}, f32[256,2048]{1,0:T(8,128)}, f32[256,2048]{1,0:T(8,128)}, f32[2,1024,256]{2,1,0:T(8,128)}) custom-call(s32[1]{0:T(128)} %bitcast.seq_ref, bf16[256,2048]{1,0:T(8,128)(2,1)S(1)} %copy-done.2, ...), custom_call_target="tpu_custom_call", output_to_operand_aliasing={{0}: (7, {}), {1}: (8, {}), {2}: (9, {}), {3}: (10, {})} | custom-call | flops 1174405120 | bytes 3014656 | tf_op jit(solution)/shard_map/pallas_call | solution.py:209
  126.3 2.1 %collective-permute-start.14 = (bf16[2,2,2,64,256]{4,3,0,1,2:T(8,128)(2,1)S(1)}, bf16[2,2,2,64,256]{4,3,0,1,2:T(8,128)(2,1)S(1)}, u32[]{:S(2)}, u32[]{:S(2)}) collective-permute-start(bf16[2,2,2,64,256]{4,3,0,1,2:T(8,128)(2,1)S(1)} %fusion.11), channel_id=1, source_target_pairs={{0,4},{2,6},{4,0},{6,2},{8,12},{10,14},{12,8},{14,10},{16,20},{18,... | collective-permute-start | bytes 786440 | tf_op jit(solution)/shard_map/ppermute | solution.py:42
  128.7 2.1 %collective-permute-start.18 = (bf16[2,2,2,64,256]{4,3,0,1,2:T(8,128)(2,1)S(1)}, bf16[2,2,2,64,256]{4,3,0,1,2:T(8,128)(2,1)S(1)}, u32[]{:S(2)}, u32[]{:S(2)}) collective-permute-start(bf16[2,2,2,64,256]{4,3,0,1,2:T(8,128)(2,1)S(1)} %fusion.12), channel_id=1, source_target_pairs={{0,8},{2,10},{4,12},{6,14},{8,0},{10,2},{12,4},{14,6},{16,24},{18,... | collective-permute-start | bytes 786440 | tf_op jit(solution)/shard_map/ppermute | solution.py:42
  131.2 4.3 %collective-permute-done.14 = bf16[2,2,2,64,256]{4,3,0,1,2:T(8,128)(2,1)S(1)} collective-permute-done((bf16[2,2,2,64,256]{4,3,0,1,2:T(8,128)(2,1)S(1)}, bf16[2,2,2,64,256]{4,3,0,1,2:T(8,128)(2,1)S(1)}, u32[]{:S(2)}, u32[]{:S(2)}) %collective-permute-start.14) | collective-permute-done | bytes 262176 | tf_op jit(solution)/shard_map/ppermute | solution.py:42
  135.5 2.0 %collective-permute-start.26 = (bf16[2,2,2,64,256]{4,3,0,1,2:T(8,128)(2,1)S(1)}, bf16[2,2,2,64,256]{4,3,0,1,2:T(8,128)(2,1)S(1)}, u32[]{:S(2)}, u32[]{:S(2)}) collective-permute-start(bf16[2,2,2,64,256]{4,3,0,1,2:T(8,128)(2,1)S(1)} %fusion.14), channel_id=1, source_target_pairs={{0,8},{2,10},{4,12},{6,14},{8,0},{10,2},{12,4},{14,6},{16,24},{18,... | collective-permute-start | bytes 786440 | tf_op jit(solution)/shard_map/ppermute | solution.py:42
  138.9 1.8 %collective-permute-done.22 = bf16[2,2,2,64,256]{4,3,0,1,2:T(8,128)(2,1)S(1)} collective-permute-done((bf16[2,2,2,64,256]{4,3,0,1,2:T(8,128)(2,1)S(1)}, bf16[2,2,2,64,256]{4,3,0,1,2:T(8,128)(2,1)S(1)}, u32[]{:S(2)}, u32[]{:S(2)}) %collective-permute-start.22) | collective-permute-done | bytes 262176 | tf_op jit(solution)/shard_map/ppermute | solution.py:42
  140.7 1.7 collective-permute-start.19
  142.5 2.2 %collective-permute-done.26 = bf16[2,2,2,64,256]{4,3,0,1,2:T(8,128)(2,1)S(1)} collective-permute-done((bf16[2,2,2,64,256]{4,3,0,1,2:T(8,128)(2,1)S(1)}, bf16[2,2,2,64,256]{4,3,0,1,2:T(8,128)(2,1)S(1)}, u32[]{:S(2)}, u32[]{:S(2)}) %collective-permute-start.26) | collective-permute-done | bytes 262176 | tf_op jit(solution)/shard_map/ppermute | solution.py:42
  144.7 1.7 %collective-permute-start.23 = (bf16[2,2,64,256]{3,2,0,1:T(8,128)(2,1)S(1)}, bf16[2,2,64,256]{3,2,0,1:T(8,128)(2,1)S(1)}, u32[]{:S(2)}, u32[]{:S(2)}) collective-permute-start(bf16[2,2,64,256]{3,2,0,1:T(8,128)(2,1)S(1)} %fusion.20), channel_id=1, source_target_pairs={{0,8},{2,10},{4,12},{6,14},{8,0},{10,2},{12,4},{14,6},{16,24},{18,... | collective-permute-start | bytes 393224 | tf_op jit(solution)/shard_map/ppermute | solution.py:42
  153.9 3.2 %collective-permute-done.16 = bf16[2,64,256]{2,1,0:T(8,128)(2,1)S(1)} collective-permute-done((bf16[2,64,256]{2,1,0:T(8,128)(2,1)S(1)}, bf16[2,64,256]{2,1,0:T(8,128)(2,1)S(1)}, u32[]{:S(2)}, u32[]{:S(2)}) %collective-permute-start.16) | collective-permute-done | bytes 65568 | tf_op jit(solution)/shard_map/ppermute | solution.py:42
  159.8 2.4 %collective-permute-done.28 = bf16[2,64,256]{2,1,0:T(8,128)(2,1)S(1)} collective-permute-done((bf16[2,64,256]{2,1,0:T(8,128)(2,1)S(1)}, bf16[2,64,256]{2,1,0:T(8,128)(2,1)S(1)}, u32[]{:S(2)}, u32[]{:S(2)}) %collective-permute-start.28) | collective-permute-done | bytes 65568 | tf_op jit(solution)/shard_map/ppermute | solution.py:42
  164.6 6.9 %shard_map.98 = (bf16[256,2048]{1,0:T(8,128)(2,1)}, bf16[256,2048]{1,0:T(8,128)(2,1)}) custom-call(f32[256,2048]{1,0:T(8,128)} %get-tuple-element.50.own_k_ref, f32[256,2048]{1,0:T(8,128)} %get-tuple-element.51.own_v_ref, bf16[256,1024]{1,0:T(8,128)(2,1)} %copy-done.11, bf16[256,1024]{1,0:T(8,128)(2,1)} %copy-done.12, ...), custom_call_target="tpu_custom_call" | custom-call | flops 67108864 | bytes 5242880 | tf_op jit(solution)/shard_map/pallas_call | solution.py:237
  (136 shorter events, 48.4 us)
Async XLA Ops:
  8.5 17.6 %collective-permute-start.5 = (bf16[64,1024]{1,0:T(8,128)(2,1)}, bf16[64,1024]{1,0:T(8,128)(2,1)S(1)}, u32[]{:S(2)}, u32[]{:S(2)}) collective-permute-start(bf16[64,1024]{1,0:T(8,128)(2,1)} %get-tuple-element.62), channel_id=1, source_target_pairs={{0,16},{2,18},{4,20},{6,22},{8,24},{10,26},{12,28},{14,30},{16,0},... | collective-permute-start | bytes 393224 | tf_op jit(solution)/shard_map/ppermute | solution.py:65
  12.5 48.3 %collective-permute-start = (bf16[128,4096]{1,0:T(8,128)(2,1)}, bf16[128,4096]{1,0:T(8,128)(2,1)}, u32[]{:S(2)}, u32[]{:S(2)}) collective-permute-start(bf16[128,4096]{1,0:T(8,128)(2,1)} %param.10), channel_id=1, source_target_pairs={{0,1},{1,0},{2,3},{3,2},{4,5},{5,4},{6,7},{7,6},{8,9},{9,8},{10,11... | collective-permute-start | bytes 3145736 | tf_op jit(solution)/shard_map/ppermute | solution.py:298
  16.9 59.9 %collective-permute-start.10 = (bf16[256,1024]{1,0:T(8,128)(2,1)}, bf16[256,1024]{1,0:T(8,128)(2,1)}, u32[]{:S(2)}, u32[]{:S(2)}) collective-permute-start(bf16[256,1024]{1,0:T(8,128)(2,1)} %copy.103), channel_id=1, source_target_pairs={{0,2},{2,4},{4,6},{6,8},{8,10},{10,12},{12,14},{14,16},{16,18},{18... | collective-permute-start | bytes 1572872 | tf_op jit(solution)/shard_map/ppermute | solution.py:21
  20.1 56.8 %collective-permute-start.9 = (bf16[256,1024]{1,0:T(8,128)(2,1)}, bf16[256,1024]{1,0:T(8,128)(2,1)}, u32[]{:S(2)}, u32[]{:S(2)}) collective-permute-start(bf16[256,1024]{1,0:T(8,128)(2,1)} %copy.102), channel_id=1, source_target_pairs={{0,2},{2,4},{4,6},{6,8},{8,10},{10,12},{12,14},{14,16},{16,18},{18... | collective-permute-start | bytes 1572872 | tf_op jit(solution)/shard_map/ppermute | solution.py:21
  25.1 8.5 %collective-permute-start.1 = (bf16[64,1024]{1,0:T(8,128)(2,1)S(1)}, bf16[64,1024]{1,0:T(8,128)(2,1)S(1)}, u32[]{:S(2)}, u32[]{:S(2)}) collective-permute-start(bf16[64,1024]{1,0:T(8,128)(2,1)S(1)} %get-tuple-element.69), channel_id=1, source_target_pairs={{0,16},{2,18},{4,20},{6,22},{8,24},{10,26},{12,28},{14,30},{16,0},... | collective-permute-start | bytes 393224 | tf_op jit(solution)/shard_map/ppermute | solution.py:65
  26.1 10.2 %collective-permute-start.6 = (bf16[2,64,1024]{2,1,0:T(8,128)(2,1)S(1)}, bf16[2,64,1024]{2,1,0:T(8,128)(2,1)S(1)}, u32[]{:S(2)}, u32[]{:S(2)}) collective-permute-start(bf16[2,64,1024]{2,1,0:T(8,128)(2,1)S(1)} %maximum_select_fusion.12), channel_id=1, source_target_pairs={{0,8},{2,10},{4,12},{6,14},{8,0},{10,2},{12,4},{14,6},{16,24},{18,... | collective-permute-start | bytes 786440 | tf_op jit(solution)/shard_map/ppermute | solution.py:65
  33.6 6.4 %collective-permute-start.2 = (bf16[2,64,1024]{2,1,0:T(8,128)(2,1)S(1)}, bf16[2,64,1024]{2,1,0:T(8,128)(2,1)S(1)}, u32[]{:S(2)}, u32[]{:S(2)}) collective-permute-start(bf16[2,64,1024]{2,1,0:T(8,128)(2,1)S(1)} %maximum_select_fusion.11), channel_id=1, source_target_pairs={{0,4},{2,6},{4,0},{6,2},{8,12},{10,14},{12,8},{14,10},{16,20},{18,... | collective-permute-start | bytes 786440 | tf_op jit(solution)/shard_map/ppermute | solution.py:65
  36.4 14.4 %collective-permute-start.7 = (bf16[2,2,64,1024]{3,2,0,1:T(8,128)(2,1)S(1)}, bf16[2,2,64,1024]{3,2,0,1:T(8,128)(2,1)S(1)}, u32[]{:S(2)}, u32[]{:S(2)}) collective-permute-start(bf16[2,2,64,1024]{3,2,0,1:T(8,128)(2,1)S(1)} %maximum_select_fusion.9), channel_id=1, source_target_pairs={{0,4},{2,6},{4,0},{6,2},{8,12},{10,14},{12,8},{14,10},{16,20},{18,... | collective-permute-start | bytes 1572872 | tf_op jit(solution)/shard_map/ppermute | solution.py:65
  40.1 15.8 %collective-permute-start.3 = (bf16[2,2,64,1024]{3,2,0,1:T(8,128)(2,1)S(1)}, bf16[2,2,64,1024]{3,2,0,1:T(8,128)(2,1)S(1)}, u32[]{:S(2)}, u32[]{:S(2)}) collective-permute-start(bf16[2,2,64,1024]{3,2,0,1:T(8,128)(2,1)S(1)} %maximum_select_fusion.7), channel_id=1, source_target_pairs={{0,8},{2,10},{4,12},{6,14},{8,0},{10,2},{12,4},{14,6},{16,24},{18,... | collective-permute-start | bytes 1572872 | tf_op jit(solution)/shard_map/ppermute | solution.py:65
  51.9 37.6 %collective-permute-start.8 = (bf16[2,2,2,64,1024]{4,3,0,1,2:T(8,128)(2,1)}, bf16[2,2,2,64,1024]{4,3,0,1,2:T(8,128)(2,1)}, u32[]{:S(2)}, u32[]{:S(2)}) collective-permute-start(bf16[2,2,2,64,1024]{4,3,0,1,2:T(8,128)(2,1)} %maximum_select_fusion.5), channel_id=1, source_target_pairs={{0,2},{2,0},{4,6},{6,4},{8,10},{10,8},{12,14},{14,12},{16,18},{18,... | collective-permute-start | bytes 3145736 | tf_op jit(solution)/shard_map/ppermute | solution.py:65
  57.0 51.3 %collective-permute-start.4 = (bf16[2,2,2,64,1024]{4,3,0,1,2:T(8,128)(2,1)}, bf16[2,2,2,64,1024]{4,3,0,1,2:T(8,128)(2,1)}, u32[]{:S(2)}, u32[]{:S(2)}) collective-permute-start(bf16[2,2,2,64,1024]{4,3,0,1,2:T(8,128)(2,1)} %maximum_select_fusion.3), channel_id=1, source_target_pairs={{0,2},{2,0},{4,6},{6,4},{8,10},{10,8},{12,14},{14,12},{16,18},{18,... | collective-permute-start | bytes 3145736 | tf_op jit(solution)/shard_map/ppermute | solution.py:65
  64.8 12.1 %copy-start.1 = (bf16[256,2048]{1,0:T(8,128)(2,1)S(1)}, bf16[256,2048]{1,0:T(8,128)(2,1)}, u32[]{:S(2)}) copy-start(bf16[256,2048]{1,0:T(8,128)(2,1)} %v_ref.9) | copy-start | bytes 3145732
  64.8 12.1 %copy-start.2 = (bf16[256,2048]{1,0:T(8,128)(2,1)S(1)}, bf16[256,2048]{1,0:T(8,128)(2,1)}, u32[]{:S(2)}) copy-start(bf16[256,2048]{1,0:T(8,128)(2,1)} %q_ref.9) | copy-start | bytes 3145732
  76.9 12.6 %copy-start.5 = (bf16[2,2,2,1,64,1024]{5,4,0,1,2,3:T(8,128)(2,1)S(1)}, bf16[2,2,2,1,64,1024]{5,4,0,1,2,3:T(8,128)(2,1)}, u32[]{:S(2)}) copy-start(bf16[2,2,2,1,64,1024]{5,4,0,1,2,3:T(8,128)(2,1)} %maximum_select_fusion.4) | copy-start | bytes 3145732
  86.7 76.3 %collective-permute-start.11 = (bf16[256,1024]{1,0:T(8,128)(2,1)S(1)}, bf16[256,1024]{1,0:T(8,128)(2,1)S(1)}, u32[]{:S(2)}, u32[]{:S(2)}) collective-permute-start(bf16[256,1024]{1,0:T(8,128)(2,1)S(1)} %get-tuple-element.52), channel_id=1, source_target_pairs={{2,0},{4,2},{6,4},{8,6},{10,8},{12,10},{14,12},{16,14},{18,16},{20... | collective-permute-start | bytes 1572872 | tf_op jit(solution)/shard_map/ppermute | solution.py:21
  88.0 75.0 %collective-permute-start.12 = (bf16[256,1024]{1,0:T(8,128)(2,1)S(1)}, bf16[256,1024]{1,0:T(8,128)(2,1)S(1)}, u32[]{:S(2)}, u32[]{:S(2)}) collective-permute-start(bf16[256,1024]{1,0:T(8,128)(2,1)S(1)} %get-tuple-element.53), channel_id=1, source_target_pairs={{2,0},{4,2},{6,4},{8,6},{10,8},{12,10},{14,12},{16,14},{18,16},{20... | collective-permute-start | bytes 1572872 | tf_op jit(solution)/shard_map/ppermute | solution.py:21
  99.7 26.3 %collective-permute-start.13 = (bf16[2,2,2,2,64,256]{5,4,0,1,2,3:T(8,128)(2,1)S(1)}, bf16[2,2,2,2,64,256]{5,4,0,1,2,3:T(8,128)(2,1)S(1)}, u32[]{:S(2)}, u32[]{:S(2)}) collective-permute-start(bf16[2,2,2,2,64,256]{5,4,0,1,2,3:T(8,128)(2,1)S(1)} %fusion.6), channel_id=1, source_target_pairs={{0,2},{2,0},{4,6},{6,4},{8,10},{10,8},{12,14},{14,12},{16,18},{18,... | collective-permute-start | bytes 1572872 | tf_op jit(solution)/shard_map/ppermute | solution.py:42
  108.2 18.1 %collective-permute-start.17 = (bf16[2,2,2,2,64,256]{5,4,0,1,3,2:T(8,128)(2,1)S(1)}, bf16[2,2,2,2,64,256]{5,4,0,1,3,2:T(8,128)(2,1)S(1)}, u32[]{:S(2)}, u32[]{:S(2)}) collective-permute-start(bf16[2,2,2,2,64,256]{5,4,0,1,3,2:T(8,128)(2,1)S(1)} %fusion.7), channel_id=1, source_target_pairs={{0,2},{2,0},{4,6},{6,4},{8,10},{10,8},{12,14},{14,12},{16,18},{18,... | collective-permute-start | bytes 1572872 | tf_op jit(solution)/shard_map/ppermute | solution.py:42
  118.6 10.1 %collective-permute-start.21 = (bf16[2,2,2,2,64,256]{5,4,0,1,2,3:T(8,128)(2,1)S(1)}, bf16[2,2,2,2,64,256]{5,4,0,1,2,3:T(8,128)(2,1)S(1)}, u32[]{:S(2)}, u32[]{:S(2)}) collective-permute-start(bf16[2,2,2,2,64,256]{5,4,0,1,2,3:T(8,128)(2,1)S(1)} %fusion.8), channel_id=1, source_target_pairs={{0,2},{2,0},{4,6},{6,4},{8,10},{10,8},{12,14},{14,12},{16,18},{18,... | collective-permute-start | bytes 1572872 | tf_op jit(solution)/shard_map/ppermute | solution.py:42
  126.0 4.9 %collective-permute-start.25 = (bf16[2,2,2,2,64,256]{5,4,0,1,3,2:T(8,128)(2,1)S(1)}, bf16[2,2,2,2,64,256]{5,4,0,1,3,2:T(8,128)(2,1)S(1)}, u32[]{:S(2)}, u32[]{:S(2)}) collective-permute-start(bf16[2,2,2,2,64,256]{5,4,0,1,3,2:T(8,128)(2,1)S(1)} %fusion.9), channel_id=1, source_target_pairs={{0,2},{2,0},{4,6},{6,4},{8,10},{10,8},{12,14},{14,12},{16,18},{18,... | collective-permute-start | bytes 1572872 | tf_op jit(solution)/shard_map/ppermute | solution.py:42
  126.3 9.2 %collective-permute-start.14 = (bf16[2,2,2,64,256]{4,3,0,1,2:T(8,128)(2,1)S(1)}, bf16[2,2,2,64,256]{4,3,0,1,2:T(8,128)(2,1)S(1)}, u32[]{:S(2)}, u32[]{:S(2)}) collective-permute-start(bf16[2,2,2,64,256]{4,3,0,1,2:T(8,128)(2,1)S(1)} %fusion.11), channel_id=1, source_target_pairs={{0,4},{2,6},{4,0},{6,2},{8,12},{10,14},{12,8},{14,10},{16,20},{18,... | collective-permute-start | bytes 786440 | tf_op jit(solution)/shard_map/ppermute | solution.py:42
  128.7 9.0 %collective-permute-start.18 = (bf16[2,2,2,64,256]{4,3,0,1,2:T(8,128)(2,1)S(1)}, bf16[2,2,2,64,256]{4,3,0,1,2:T(8,128)(2,1)S(1)}, u32[]{:S(2)}, u32[]{:S(2)}) collective-permute-start(bf16[2,2,2,64,256]{4,3,0,1,2:T(8,128)(2,1)S(1)} %fusion.12), channel_id=1, source_target_pairs={{0,8},{2,10},{4,12},{6,14},{8,0},{10,2},{12,4},{14,6},{16,24},{18,... | collective-permute-start | bytes 786440 | tf_op jit(solution)/shard_map/ppermute | solution.py:42
  130.9 9.8 %collective-permute-start.22 = (bf16[2,2,2,64,256]{4,3,0,1,2:T(8,128)(2,1)S(1)}, bf16[2,2,2,64,256]{4,3,0,1,2:T(8,128)(2,1)S(1)}, u32[]{:S(2)}, u32[]{:S(2)}) collective-permute-start(bf16[2,2,2,64,256]{4,3,0,1,2:T(8,128)(2,1)S(1)} %fusion.13), channel_id=1, source_target_pairs={{0,4},{2,6},{4,0},{6,2},{8,12},{10,14},{12,8},{14,10},{16,20},{18,... | collective-permute-start | bytes 786440 | tf_op jit(solution)/shard_map/ppermute | solution.py:42
  135.5 9.1 %collective-permute-start.26 = (bf16[2,2,2,64,256]{4,3,0,1,2:T(8,128)(2,1)S(1)}, bf16[2,2,2,64,256]{4,3,0,1,2:T(8,128)(2,1)S(1)}, u32[]{:S(2)}, u32[]{:S(2)}) collective-permute-start(bf16[2,2,2,64,256]{4,3,0,1,2:T(8,128)(2,1)S(1)} %fusion.14), channel_id=1, source_target_pairs={{0,8},{2,10},{4,12},{6,14},{8,0},{10,2},{12,4},{14,6},{16,24},{18,... | collective-permute-start | bytes 786440 | tf_op jit(solution)/shard_map/ppermute | solution.py:42
  137.7 9.7 %collective-permute-start.15 = (bf16[2,2,64,256]{3,2,0,1:T(8,128)(2,1)S(1)}, bf16[2,2,64,256]{3,2,0,1:T(8,128)(2,1)S(1)}, u32[]{:S(2)}, u32[]{:S(2)}) collective-permute-start(bf16[2,2,64,256]{3,2,0,1:T(8,128)(2,1)S(1)} %fusion.18), channel_id=1, source_target_pairs={{0,8},{2,10},{4,12},{6,14},{8,0},{10,2},{12,4},{14,6},{16,24},{18,... | collective-permute-start | bytes 393224 | tf_op jit(solution)/shard_map/ppermute | solution.py:42
  140.7 8.1 %collective-permute-start.19 = (bf16[2,2,64,256]{3,2,0,1:T(8,128)(2,1)S(1)}, bf16[2,2,64,256]{3,2,0,1:T(8,128)(2,1)S(1)}, u32[]{:S(2)}, u32[]{:S(2)}) collective-permute-start(bf16[2,2,64,256]{3,2,0,1:T(8,128)(2,1)S(1)} %fusion.19), channel_id=1, source_target_pairs={{0,4},{2,6},{4,0},{6,2},{8,12},{10,14},{12,8},{14,10},{16,20},{18,... | collective-permute-start | bytes 393224 | tf_op jit(solution)/shard_map/ppermute | solution.py:42
  144.7 5.7 %collective-permute-start.23 = (bf16[2,2,64,256]{3,2,0,1:T(8,128)(2,1)S(1)}, bf16[2,2,64,256]{3,2,0,1:T(8,128)(2,1)S(1)}, u32[]{:S(2)}, u32[]{:S(2)}) collective-permute-start(bf16[2,2,64,256]{3,2,0,1:T(8,128)(2,1)S(1)} %fusion.20), channel_id=1, source_target_pairs={{0,8},{2,10},{4,12},{6,14},{8,0},{10,2},{12,4},{14,6},{16,24},{18,... | collective-permute-start | bytes 393224 | tf_op jit(solution)/shard_map/ppermute | solution.py:42
  147.4 5.0 %collective-permute-start.27 = (bf16[2,2,64,256]{3,2,0,1:T(8,128)(2,1)S(1)}, bf16[2,2,64,256]{3,2,0,1:T(8,128)(2,1)S(1)}, u32[]{:S(2)}, u32[]{:S(2)}) collective-permute-start(bf16[2,2,64,256]{3,2,0,1:T(8,128)(2,1)S(1)} %fusion.21), channel_id=1, source_target_pairs={{0,4},{2,6},{4,0},{6,2},{8,12},{10,14},{12,8},{14,10},{16,20},{18,... | collective-permute-start | bytes 393224 | tf_op jit(solution)/shard_map/ppermute | solution.py:42
  148.8 8.3 %collective-permute-start.16 = (bf16[2,64,256]{2,1,0:T(8,128)(2,1)S(1)}, bf16[2,64,256]{2,1,0:T(8,128)(2,1)S(1)}, u32[]{:S(2)}, u32[]{:S(2)}) collective-permute-start(bf16[2,64,256]{2,1,0:T(8,128)(2,1)S(1)} %fusion.26), channel_id=1, source_target_pairs={{0,16},{2,18},{4,20},{6,22},{8,24},{10,26},{12,28},{14,30},{16,0},... | collective-permute-start | bytes 196616 | tf_op jit(solution)/shard_map/ppermute | solution.py:42
  150.4 8.0 %collective-permute-start.20 = (bf16[2,64,256]{2,1,0:T(8,128)(2,1)S(1)}, bf16[2,64,256]{2,1,0:T(8,128)(2,1)S(1)}, u32[]{:S(2)}, u32[]{:S(2)}) collective-permute-start(bf16[2,64,256]{2,1,0:T(8,128)(2,1)S(1)} %fusion.27), channel_id=1, source_target_pairs={{0,16},{2,18},{4,20},{6,22},{8,24},{10,26},{12,28},{14,30},{16,0},... | collective-permute-start | bytes 196616 | tf_op jit(solution)/shard_map/ppermute | solution.py:42
  152.4 7.4 %collective-permute-start.24 = (bf16[2,64,256]{2,1,0:T(8,128)(2,1)S(1)}, bf16[2,64,256]{2,1,0:T(8,128)(2,1)S(1)}, u32[]{:S(2)}, u32[]{:S(2)}) collective-permute-start(bf16[2,64,256]{2,1,0:T(8,128)(2,1)S(1)} %fusion.28), channel_id=1, source_target_pairs={{0,16},{2,18},{4,20},{6,22},{8,24},{10,26},{12,28},{14,30},{16,0},... | collective-permute-start | bytes 196616 | tf_op jit(solution)/shard_map/ppermute | solution.py:42
  157.1 5.2 %collective-permute-start.28 = (bf16[2,64,256]{2,1,0:T(8,128)(2,1)S(1)}, bf16[2,64,256]{2,1,0:T(8,128)(2,1)S(1)}, u32[]{:S(2)}, u32[]{:S(2)}) collective-permute-start(bf16[2,64,256]{2,1,0:T(8,128)(2,1)S(1)} %fusion.29), channel_id=1, source_target_pairs={{0,16},{2,18},{4,20},{6,22},{8,24},{10,26},{12,28},{14,30},{16,0},... | collective-permute-start | bytes 196616 | tf_op jit(solution)/shard_map/ppermute | solution.py:42
  (10 other events, 33.4 us)

commit v9 on v6

--- a/solution.py
+++ b/solution.py
@@ -71,10 +71,10 @@
     row_sum = w_a.sum(-1, keepdims=True) + w_b.sum(-1, keepdims=True)
     mixed = nn(w_a.astype(jnp.bfloat16), v_a) + nn(w_b.astype(jnp.bfloat16), v_b)
     out = (mixed / row_sum).astype(jnp.bfloat16)
-    log_total = row_max + jnp.log(row_sum)
     delta = jnp.sum(g.astype(jnp.float32) * out.astype(jnp.float32), -1, keepdims=True)
-    p_a = jnp.exp(s_a - log_total)
-    p_b = jnp.exp(s_b - log_total)
+    inverse = 1.0 / row_sum
+    p_a = w_a * inverse
+    p_b = w_b * inverse
     gs_a = (p_a * (nt(g, v_a) - delta)).astype(jnp.bfloat16)
     gs_b = (p_b * (nt(g, v_b) - delta)).astype(jnp.bfloat16)
     dq = ((nn(gs_a, k_a) + nn(gs_b, k_b)) * scale).astype(jnp.bfloat16)
@@ -128,8 +128,8 @@
     dq_ref[...] = dq
     dk_ref[...] = dko
     dv_ref[...] = dvo
-    dkvf_ref[0] = dkf
-    dkvf_ref[1] = dvf
+    dkvf_ref[0] = dkf.astype(dkvf_ref.dtype)
+    dkvf_ref[1] = dvf.astype(dkvf_ref.dtype)
 
 
 def attention_cost(rows, keys, head_dim, heads):
@@ -186,7 +186,7 @@
         functools.partial(fixed_kernel, scale=scale, unused=len(earlier)),
         grid_spec=grid_spec,
         out_shape=[jax.ShapeDtypeStruct(array.shape, array.dtype) for array in earlier]
-        + [jax.ShapeDtypeStruct((2, far_rows, pairs * head_dim), jnp.float32)],
+        + [jax.ShapeDtypeStruct((2, far_rows, pairs * head_dim), jnp.bfloat16)],
         input_output_aliases=aliases,
         compiler_params=pltpu.CompilerParams(vmem_limit_bytes=48 * 1024 * 1024),
         cost_estimate=attention_cost(rows, rows + far_rows, head_dim, pairs),

time: 149 us -> 147 us (0.987)
  waiting for transfers between devices: 27.2 us -> 29.3 us
  Pallas kernels: 38.2 us -> 36.3 us
  local copies, waits for them, and re-layouts: 13 us -> 11.5 us
    convert_element_type x16 -> x12, local copies, waits for them, and re-layouts: 5.61 us -> 0.31 us  [seq_reduce_scatter(): send.astype(jnp.bfloat16)]
    unnamed x22 -> x24, local copies, waits for them, and re-layouts: 3.34 us -> 6.58 us
    pallas_call x4, Pallas kernels: 21.6 us -> 19.8 us  [fixed_attention(): pl.pallas_call(functools.partial(fixed_kernel, scale=scale, unused=len(ea...]
  transfers between devices with their start and end apart: 22 -> 22, of which waited for: 9 -> 10; matrix products, arithmetic and copies ran while one was open for 19% -> 16% of each run, Pallas kernels for 21% -> 13%
where the time goes in v9:
time: 147 us; the launch traced here: 146 us
  Pallas kernels  36.3 us (25%)
  starting transfers between devices  34.2 us (23%)
  waiting for transfers between devices  29.3 us (20%)
  between operations  14.5 us (10%)
  matrix products  12.8 us (9%)
  local copies, waits for them, and re-layouts  11.5 us (8%)
  other arithmetic  7.9 us (5%)
    ppermute x16, starting transfers between devices, seq_reduce_scatter(): lax.ppermute(send.astype(jnp.bfloat16), 'seq', [(source, source ^ 1 << bi...  22.1 us
    pallas_call x4, Pallas kernels, fixed_attention(): pl.pallas_call(functools.partial(fixed_kernel, scale=scale, unused=len(ea...  19.8 us
    ppermute x16, waiting for transfers between devices, seq_reduce_scatter(): lax.ppermute(send.astype(jnp.bfloat16), 'seq', [(source, source ^ 1 << bi...  15.6 us
    ppermute x1, waiting for transfers between devices, on_device(): lax.ppermute(cotangent, 'head', [(source, (source + shift) % head_count)...  13.3 us
    dot_general x1, matrix products, on_device(): lax.dot_general(gathered.reshape(seq_rows, cotangent.shape[1]), out_weigh...  12.1 us
    pallas_call x1, Pallas kernels, band_attention(): pl.pallas_call(functools.partial(band_kernel, scale=scale), grid_spec=gri...  9.64 us
    ppermute x4, starting transfers between devices, passed_along(): lax.ppermute(value, axis, [(source, source + steps) for source in range(f...  8.97 us
    pallas_call x1, Pallas kernels, finalize(): pl.pallas_call(finalize_kernel, grid=(head_pairs,), in_specs=[wide, wide,...  6.87 us
  transfers between devices with their start and end apart: 22, of which 10 were waited for; matrix products, arithmetic and copies ran while one was open for 16% of the time, Pallas kernels for 13%

profile of v9, /device:TPU:0, one launch (start us, length us, event | category | flops | bytes accessed | tf_op | source)
XLA Modules:
  0.0 146.5 jit_solution(5790653476972013815)
XLA Ops:
  7.2 1.6 %copy.30 = bf16[256,2048]{0,1:T(8,128)(2,1)S(1)} copy(bf16[256,2048]{1,0:T(8,128)(2,1)} %k_ref.9) | data formatting | bytes 2097152 | tf_op args[1]
  11.0 3.0 %collective-permute-start = (bf16[128,4096]{1,0:T(8,128)(2,1)}, bf16[128,4096]{1,0:T(8,128)(2,1)}, u32[]{:S(2)}, u32[]{:S(2)}) collective-permute-start(bf16[128,4096]{1,0:T(8,128)(2,1)} %param.10), channel_id=1, source_target_pairs={{0,1},{1,0},{2,3},{3,2},{4,5},{5,4},{6,7},{7,6},{8,9},{9,8},{10,11... | collective-permute-start | bytes 3145736 | tf_op jit(solution)/shard_map/ppermute | solution.py:279
  14.8 2.0 %copy.46 = bf16[256,1024]{1,0:T(8,128)(2,1)} copy(bf16[256,1024]{0,1:T(8,128)(2,1)} %bitcast.136) | data formatting | bytes 1048576 | tf_op jit(solution)/shard_map/reshape;squeeze | solution.py:246
  16.9 2.3 %collective-permute-start.1 = (bf16[256,1024]{1,0:T(8,128)(2,1)}, bf16[256,1024]{1,0:T(8,128)(2,1)}, u32[]{:S(2)}, u32[]{:S(2)}) collective-permute-start(bf16[256,1024]{1,0:T(8,128)(2,1)} %copy.46), channel_id=1, source_target_pairs={{0,2},{2,4},{4,6},{6,8},{8,10},{10,12},{12,14},{14,16},{16,18},{18... | collective-permute-start | bytes 1572872 | tf_op jit(solution)/shard_map/ppermute | solution.py:21
  20.2 3.9 %collective-permute-start.2 = (bf16[256,1024]{1,0:T(8,128)(2,1)}, bf16[256,1024]{1,0:T(8,128)(2,1)}, u32[]{:S(2)}, u32[]{:S(2)}) collective-permute-start(bf16[256,1024]{1,0:T(8,128)(2,1)} %copy.47), channel_id=1, source_target_pairs={{0,2},{2,4},{4,6},{6,8},{8,10},{10,12},{12,14},{14,16},{16,18},{18... | collective-permute-start | bytes 1572872 | tf_op jit(solution)/shard_map/ppermute | solution.py:21
  24.1 13.3 %collective-permute-done = bf16[128,4096]{1,0:T(8,128)(2,1)} collective-permute-done((bf16[128,4096]{1,0:T(8,128)(2,1)}, bf16[128,4096]{1,0:T(8,128)(2,1)}, u32[]{:S(2)}, u32[]{:S(2)}) %collective-permute-start) | collective-permute-done | bytes 1048608 | tf_op jit(solution)/shard_map/ppermute | solution.py:279
  37.5 4.6 %fusion.2 = bf16[2,128,4096]{2,1,0:T(8,128)(2,1)} fusion(s32[]{:T(128)S(6)} %select_n.65, bf16[1,128,4096]{2,1,0:T(8,128)(2,1)} %bitcast.1, bf16[1,128,4096]{2,1,0:T(8,128)(2,1)} %bitcast.138), kind=kLoop, calls=%fused_computation.7 | loop fusion | flops 3145728 | bytes 4194308 | tf_op jit(solution)/shard_map/stack | solution.py:284
  42.1 12.1 %convolution_convert_fusion.g_ref = bf16[256,2048]{1,0:T(8,128)(2,1)} fusion(bf16[256,4096]{1,0:T(8,128)(2,1)} %bitcast.135, bf16[2048,4096]{1,0:T(8,128)(2,1)} %param.9), kind=kOutput, calls=%fused_computation.4 | convolution fusion | flops 4295491584 | bytes 19922944 | tf_op jit(solution)/shard_map/dot_general | solution.py:286
  54.3 9.6 %shard_map.93 = (bf16[256,2048]{1,0:T(8,128)(2,1)}, bf16[256,2048]{1,0:T(8,128)(2,1)}, f32[256,2048]{1,0:T(8,128)}, f32[256,2048]{1,0:T(8,128)}, bf16[256,1024]{...) custom-call(s32[1]{0:T(128)} %bitcast.seq_ref, bf16[256,2048]{1,0:T(8,128)(2,1)S(1)} %copy-done.2, ...), custom_call_target="tpu_custom_call" | custom-call | flops 1879048192 | bytes 7340032 | tf_op jit(solution)/shard_map/pallas_call | solution.py:154
  67.1 4.9 %shard_map.94 = (bf16[256,2048]{1,0:T(8,128)(2,1)}, bf16[256,2048]{1,0:T(8,128)(2,1)}, f32[256,2048]{1,0:T(8,128)}, f32[256,2048]{1,0:T(8,128)}, bf16[2,1024,256]{2,1,0:T(8,128)(2,1)S(1)}) custom-call(s32[1]{0:T(128)} %bitcast.seq_ref, bf16[256,2048]{1,0:T(8,128)(2,1)S(1)} %copy-done.2, ...), custom_call_target="tpu_custom_call", output_to_operand_aliasing={{0}: (7, {}), {1}: (8, {}), {2}: (9, {}), {3}: (10, {})} | custom-call | flops 1174405120 | bytes 3014656 | tf_op jit(solution)/shard_map/pallas_call | solution.py:185
  72.0 5.0 %shard_map.95 = (bf16[256,2048]{1,0:T(8,128)(2,1)}, bf16[256,2048]{1,0:T(8,128)(2,1)}, f32[256,2048]{1,0:T(8,128)}, f32[256,2048]{1,0:T(8,128)}, bf16[2,1024,256]{2,1,0:T(8,128)(2,1)S(1)}) custom-call(s32[1]{0:T(128)} %bitcast.seq_ref, bf16[256,2048]{1,0:T(8,128)(2,1)S(1)} %copy-done.2, ...), custom_call_target="tpu_custom_call", output_to_operand_aliasing={{0}: (7, {}), {1}: (8, {}), {2}: (9, {}), {3}: (10, {})} | custom-call | flops 1174405120 | bytes 3014656 | tf_op jit(solution)/shard_map/pallas_call | solution.py:185
  79.8 1.5 %collective-permute-start.4 = (bf16[256,1024]{1,0:T(8,128)(2,1)S(1)}, bf16[256,1024]{1,0:T(8,128)(2,1)S(1)}, u32[]{:S(2)}, u32[]{:S(2)}) collective-permute-start(bf16[256,1024]{1,0:T(8,128)(2,1)S(1)} %copy-done.5), channel_id=1, source_target_pairs={{2,0},{4,2},{6,4},{8,6},{10,8},{12,10},{14,12},{16,14},{18,16},{20... | collective-permute-start | bytes 1572872 | tf_op jit(solution)/shard_map/ppermute | solution.py:21
  81.3 1.8 %collective-permute-start.9 = (bf16[2,2,2,2,64,256]{5,4,0,1,3,2:T(8,128)(2,1)S(1)}, bf16[2,2,2,2,64,256]{5,4,0,1,3,2:T(8,128)(2,1)S(1)}, u32[]{:S(2)}, u32[]{:S(2)}) collective-permute-start(bf16[2,2,2,2,64,256]{5,4,0,1,3,2:T(8,128)(2,1)S(1)} %bitcast.140), channel_id=1, source_target_pairs={{0,2},{2,0},{4,6},{6,4},{8,10},{10,8},{12,14},{14,12},{16,18},{18,... | collective-permute-start | bytes 1572872 | tf_op jit(solution)/shard_map/ppermute | solution.py:45
  83.1 4.9 %shard_map.96 = (bf16[256,2048]{1,0:T(8,128)(2,1)}, bf16[256,2048]{1,0:T(8,128)(2,1)}, f32[256,2048]{1,0:T(8,128)}, f32[256,2048]{1,0:T(8,128)}, bf16[2,1024,256]{2,1,0:T(8,128)(2,1)S(1)}) custom-call(s32[1]{0:T(128)} %bitcast.seq_ref, bf16[256,2048]{1,0:T(8,128)(2,1)S(1)} %copy-done.2, ...), custom_call_target="tpu_custom_call", output_to_operand_aliasing={{0}: (7, {}), {1}: (8, {}), {2}: (9, {}), {3}: (10, {})} | custom-call | flops 1174405120 | bytes 3014656 | tf_op jit(solution)/shard_map/pallas_call | solution.py:185
  88.0 4.9 %shard_map.97 = (bf16[256,2048]{1,0:T(8,128)(2,1)}, bf16[256,2048]{1,0:T(8,128)(2,1)}, f32[256,2048]{1,0:T(8,128)}, f32[256,2048]{1,0:T(8,128)}, bf16[2,1024,256]{2,1,0:T(8,128)(2,1)S(1)}) custom-call(s32[1]{0:T(128)} %bitcast.seq_ref, bf16[256,2048]{1,0:T(8,128)(2,1)S(1)} %copy-done.2, ...), custom_call_target="tpu_custom_call", output_to_operand_aliasing={{0}: (7, {}), {1}: (8, {}), {2}: (9, {}), {3}: (10, {})} | custom-call | flops 1174405120 | bytes 3014656 | tf_op jit(solution)/shard_map/pallas_call | solution.py:185
  94.1 1.9 %collective-permute-start.6 = (bf16[2,2,2,64,256]{4,3,0,1,2:T(8,128)(2,1)S(1)}, bf16[2,2,2,64,256]{4,3,0,1,2:T(8,128)(2,1)S(1)}, u32[]{:S(2)}, u32[]{:S(2)}) collective-permute-start(bf16[2,2,2,64,256]{4,3,0,1,2:T(8,128)(2,1)S(1)} %fusion.6), channel_id=1, source_target_pairs={{0,4},{2,6},{4,0},{6,2},{8,12},{10,14},{12,8},{14,10},{16,20},{18,... | collective-permute-start | bytes 786440 | tf_op jit(solution)/shard_map/ppermute | solution.py:45
  96.2 1.7 %collective-permute-start.10 = (bf16[2,2,2,64,256]{4,3,0,1,2:T(8,128)(2,1)S(1)}, bf16[2,2,2,64,256]{4,3,0,1,2:T(8,128)(2,1)S(1)}, u32[]{:S(2)}, u32[]{:S(2)}) collective-permute-start(bf16[2,2,2,64,256]{4,3,0,1,2:T(8,128)(2,1)S(1)} %fusion.7), channel_id=1, source_target_pairs={{0,8},{2,10},{4,12},{6,14},{8,0},{10,2},{12,4},{14,6},{16,24},{18,... | collective-permute-start | bytes 786440 | tf_op jit(solution)/shard_map/ppermute | solution.py:45
  98.1 1.3 collective-permute-start.14
  99.7 3.6 %collective-permute-done.6 = bf16[2,2,2,64,256]{4,3,0,1,2:T(8,128)(2,1)S(1)} collective-permute-done((bf16[2,2,2,64,256]{4,3,0,1,2:T(8,128)(2,1)S(1)}, bf16[2,2,2,64,256]{4,3,0,1,2:T(8,128)(2,1)S(1)}, u32[]{:S(2)}, u32[]{:S(2)}) %collective-permute-start.6) | collective-permute-done | bytes 262176 | tf_op jit(solution)/shard_map/ppermute | solution.py:45
  103.3 2.8 %collective-permute-start.18 = (bf16[2,2,2,64,256]{4,3,0,1,2:T(8,128)(2,1)S(1)}, bf16[2,2,2,64,256]{4,3,0,1,2:T(8,128)(2,1)S(1)}, u32[]{:S(2)}, u32[]{:S(2)}) collective-permute-start(bf16[2,2,2,64,256]{4,3,0,1,2:T(8,128)(2,1)S(1)} %fusion.9), channel_id=1, source_target_pairs={{0,8},{2,10},{4,12},{6,14},{8,0},{10,2},{12,4},{14,6},{16,24},{18,... | collective-permute-start | bytes 786440 | tf_op jit(solution)/shard_map/ppermute | solution.py:45
  106.4 2.0 %collective-permute-done.14 = bf16[2,2,2,64,256]{4,3,0,1,2:T(8,128)(2,1)S(1)} collective-permute-done((bf16[2,2,2,64,256]{4,3,0,1,2:T(8,128)(2,1)S(1)}, bf16[2,2,2,64,256]{4,3,0,1,2:T(8,128)(2,1)S(1)}, u32[]{:S(2)}, u32[]{:S(2)}) %collective-permute-start.14) | collective-permute-done | bytes 262176 | tf_op jit(solution)/shard_map/ppermute | solution.py:45
  108.4 1.7 %collective-permute-start.11 = (bf16[2,2,64,256]{3,2,0,1:T(8,128)(2,1)S(1)}, bf16[2,2,64,256]{3,2,0,1:T(8,128)(2,1)S(1)}, u32[]{:S(2)}, u32[]{:S(2)}) collective-permute-start(bf16[2,2,64,256]{3,2,0,1:T(8,128)(2,1)S(1)} %fusion.13), channel_id=1, source_target_pairs={{0,4},{2,6},{4,0},{6,2},{8,12},{10,14},{12,8},{14,10},{16,20},{18,... | collective-permute-start | bytes 393224 | tf_op jit(solution)/shard_map/ppermute | solution.py:45
  110.2 2.2 %collective-permute-done.18 = bf16[2,2,2,64,256]{4,3,0,1,2:T(8,128)(2,1)S(1)} collective-permute-done((bf16[2,2,2,64,256]{4,3,0,1,2:T(8,128)(2,1)S(1)}, bf16[2,2,2,64,256]{4,3,0,1,2:T(8,128)(2,1)S(1)}, u32[]{:S(2)}, u32[]{:S(2)}) %collective-permute-start.18) | collective-permute-done | bytes 262176 | tf_op jit(solution)/shard_map/ppermute | solution.py:45
  112.4 2.1 %collective-permute-start.15 = (bf16[2,2,64,256]{3,2,0,1:T(8,128)(2,1)S(1)}, bf16[2,2,64,256]{3,2,0,1:T(8,128)(2,1)S(1)}, u32[]{:S(2)}, u32[]{:S(2)}) collective-permute-start(bf16[2,2,64,256]{3,2,0,1:T(8,128)(2,1)S(1)} %fusion.14), channel_id=1, source_target_pairs={{0,8},{2,10},{4,12},{6,14},{8,0},{10,2},{12,4},{14,6},{16,24},{18,... | collective-permute-start | bytes 393224 | tf_op jit(solution)/shard_map/ppermute | solution.py:45
  115.1 1.3 collective-permute-start.19
  116.4 2.2 %collective-permute-start.8 = (bf16[2,64,256]{2,1,0:T(8,128)(2,1)S(1)}, bf16[2,64,256]{2,1,0:T(8,128)(2,1)S(1)}, u32[]{:S(2)}, u32[]{:S(2)}) collective-permute-start(bf16[2,64,256]{2,1,0:T(8,128)(2,1)S(1)} %fusion.20), channel_id=1, source_target_pairs={{0,16},{2,18},{4,20},{6,22},{8,24},{10,26},{12,28},{14,30},{16,0},... | collective-permute-start | bytes 196616 | tf_op jit(solution)/shard_map/ppermute | solution.py:45
  118.7 2.8 %collective-permute-start.12 = (bf16[2,64,256]{2,1,0:T(8,128)(2,1)S(1)}, bf16[2,64,256]{2,1,0:T(8,128)(2,1)S(1)}, u32[]{:S(2)}, u32[]{:S(2)}) collective-permute-start(bf16[2,64,256]{2,1,0:T(8,128)(2,1)S(1)} %fusion.21), channel_id=1, source_target_pairs={{0,16},{2,18},{4,20},{6,22},{8,24},{10,26},{12,28},{14,30},{16,0},... | collective-permute-start | bytes 196616 | tf_op jit(solution)/shard_map/ppermute | solution.py:45
  121.6 1.4 collective-permute-start.16
  123.0 2.2 %collective-permute-done.8 = bf16[2,64,256]{2,1,0:T(8,128)(2,1)S(1)} collective-permute-done((bf16[2,64,256]{2,1,0:T(8,128)(2,1)S(1)}, bf16[2,64,256]{2,1,0:T(8,128)(2,1)S(1)}, u32[]{:S(2)}, u32[]{:S(2)}) %collective-permute-start.8) | collective-permute-done | bytes 65568 | tf_op jit(solution)/shard_map/ppermute | solution.py:45
  126.3 1.4 collective-permute-done.16
  127.7 2.6 %collective-permute-done.20 = bf16[2,64,256]{2,1,0:T(8,128)(2,1)S(1)} collective-permute-done((bf16[2,64,256]{2,1,0:T(8,128)(2,1)S(1)}, bf16[2,64,256]{2,1,0:T(8,128)(2,1)S(1)}, u32[]{:S(2)}, u32[]{:S(2)}) %collective-permute-start.20) | collective-permute-done | bytes 65568 | tf_op jit(solution)/shard_map/ppermute | solution.py:45
  132.7 6.9 %shard_map.98 = (bf16[256,2048]{1,0:T(8,128)(2,1)}, bf16[256,2048]{1,0:T(8,128)(2,1)}) custom-call(f32[256,2048]{1,0:T(8,128)} %get-tuple-element.50.own_k_ref, f32[256,2048]{1,0:T(8,128)} %get-tuple-element.51.own_v_ref, bf16[256,1024]{1,0:T(8,128)(2,1)} %copy-done.8, bf16[256,1024]{1,0:T(8,128)(2,1)} %copy-done.9, ...), custom_call_target="tpu_custom_call" | custom-call | flops 67108864 | bytes 5242880 | tf_op jit(solution)/shard_map/pallas_call | solution.py:213
  (94 shorter events, 16.2 us)
Async XLA Ops:
  7.2 1.6 %copy-start.1 = (bf16[256,2048]{1,0:T(8,128)(2,1)S(1)}, bf16[256,2048]{1,0:T(8,128)(2,1)}, u32[]{:S(2)}) copy-start(bf16[256,2048]{1,0:T(8,128)(2,1)} %v_ref.9) | copy-start | bytes 3145732
  7.2 58.7 %all-gather.2.cloned.1.call-start = ((), (), s32[]{:S(2)}) async-start(), calls=%async_computation | async-start | bytes 4456448 | tf_op jit(solution)/shard_map/all_gather | solution.py:264
  7.2 2.1 %copy-start.10 = (s32[8,32]{1,0:T(8,128)S(1)}, s32[8,32]{1,0:T(8,128)}, u32[]{:S(2)}) copy-start(s32[8,32]{1,0:T(8,128)} %param.11) | copy-start | bytes 3076
  11.0 26.5 %collective-permute-start = (bf16[128,4096]{1,0:T(8,128)(2,1)}, bf16[128,4096]{1,0:T(8,128)(2,1)}, u32[]{:S(2)}, u32[]{:S(2)}) collective-permute-start(bf16[128,4096]{1,0:T(8,128)(2,1)} %param.10), channel_id=1, source_target_pairs={{0,1},{1,0},{2,3},{3,2},{4,5},{5,4},{6,7},{7,6},{8,9},{9,8},{10,11... | collective-permute-start | bytes 3145736 | tf_op jit(solution)/shard_map/ppermute | solution.py:279
  16.9 37.4 %collective-permute-start.1 = (bf16[256,1024]{1,0:T(8,128)(2,1)}, bf16[256,1024]{1,0:T(8,128)(2,1)}, u32[]{:S(2)}, u32[]{:S(2)}) collective-permute-start(bf16[256,1024]{1,0:T(8,128)(2,1)} %copy.46), channel_id=1, source_target_pairs={{0,2},{2,4},{4,6},{6,8},{8,10},{10,12},{12,14},{14,16},{16,18},{18... | collective-permute-start | bytes 1572872 | tf_op jit(solution)/shard_map/ppermute | solution.py:21
  20.2 34.0 %collective-permute-start.2 = (bf16[256,1024]{1,0:T(8,128)(2,1)}, bf16[256,1024]{1,0:T(8,128)(2,1)}, u32[]{:S(2)}, u32[]{:S(2)}) collective-permute-start(bf16[256,1024]{1,0:T(8,128)(2,1)} %copy.47), channel_id=1, source_target_pairs={{0,2},{2,4},{4,6},{6,8},{8,10},{10,12},{12,14},{14,16},{16,18},{18... | collective-permute-start | bytes 1572872 | tf_op jit(solution)/shard_map/ppermute | solution.py:21
  42.1 12.1 %copy-start = (bf16[256,2048]{1,0:T(8,128)(2,1)S(1)}, bf16[256,2048]{1,0:T(8,128)(2,1)}, u32[]{:S(2)}) copy-start(bf16[256,2048]{1,0:T(8,128)(2,1)} %k_ref.9) | copy-start | bytes 3145732
  42.1 12.1 %copy-start.2 = (bf16[256,2048]{1,0:T(8,128)(2,1)S(1)}, bf16[256,2048]{1,0:T(8,128)(2,1)}, u32[]{:S(2)}) copy-start(bf16[256,2048]{1,0:T(8,128)(2,1)} %q_ref.9) | copy-start | bytes 3145732
  63.9 0.8 copy-start.4
  64.7 0.8 copy-start.6
  65.8 1.2 copy-start.3
  77.0 1.5 %copy-start.7 = (bf16[256,1024]{1,0:T(8,128)(2,1)S(1)}, bf16[256,1024]{1,0:T(8,128)(2,1)}, u32[]{:S(2)}) copy-start(bf16[256,1024]{1,0:T(8,128)(2,1)} %copy-done.6) | copy-start | bytes 1572868
  77.0 2.8 %copy-start.5 = (bf16[256,1024]{1,0:T(8,128)(2,1)S(1)}, bf16[256,1024]{1,0:T(8,128)(2,1)}, u32[]{:S(2)}) copy-start(bf16[256,1024]{1,0:T(8,128)(2,1)} %copy-done.4) | copy-start | bytes 1572868
  77.3 16.1 %collective-permute-start.5 = (bf16[2,2,2,2,64,256]{5,4,0,1,2,3:T(8,128)(2,1)S(1)}, bf16[2,2,2,2,64,256]{5,4,0,1,2,3:T(8,128)(2,1)S(1)}, u32[]{:S(2)}, u32[]{:S(2)}) collective-permute-start(bf16[2,2,2,2,64,256]{5,4,0,1,2,3:T(8,128)(2,1)S(1)} %bitcast.139), channel_id=1, source_target_pairs={{0,2},{2,0},{4,6},{6,4},{8,10},{10,8},{12,14},{14,12},{16,18},{18,... | collective-permute-start | bytes 1572872 | tf_op jit(solution)/shard_map/ppermute | solution.py:45
  78.5 52.7 %collective-permute-start.3 = (bf16[256,1024]{1,0:T(8,128)(2,1)S(1)}, bf16[256,1024]{1,0:T(8,128)(2,1)S(1)}, u32[]{:S(2)}, u32[]{:S(2)}) collective-permute-start(bf16[256,1024]{1,0:T(8,128)(2,1)S(1)} %copy-done.7), channel_id=1, source_target_pairs={{2,0},{4,2},{6,4},{8,6},{10,8},{12,10},{14,12},{16,14},{18,16},{20... | collective-permute-start | bytes 1572872 | tf_op jit(solution)/shard_map/ppermute | solution.py:21
  79.8 51.4 %collective-permute-start.4 = (bf16[256,1024]{1,0:T(8,128)(2,1)S(1)}, bf16[256,1024]{1,0:T(8,128)(2,1)S(1)}, u32[]{:S(2)}, u32[]{:S(2)}) collective-permute-start(bf16[256,1024]{1,0:T(8,128)(2,1)S(1)} %copy-done.5), channel_id=1, source_target_pairs={{2,0},{4,2},{6,4},{8,6},{10,8},{12,10},{14,12},{16,14},{18,16},{20... | collective-permute-start | bytes 1572872 | tf_op jit(solution)/shard_map/ppermute | solution.py:21
  81.3 12.8 %collective-permute-start.9 = (bf16[2,2,2,2,64,256]{5,4,0,1,3,2:T(8,128)(2,1)S(1)}, bf16[2,2,2,2,64,256]{5,4,0,1,3,2:T(8,128)(2,1)S(1)}, u32[]{:S(2)}, u32[]{:S(2)}) collective-permute-start(bf16[2,2,2,2,64,256]{5,4,0,1,3,2:T(8,128)(2,1)S(1)} %bitcast.140), channel_id=1, source_target_pairs={{0,2},{2,0},{4,6},{6,4},{8,10},{10,8},{12,14},{14,12},{16,18},{18,... | collective-permute-start | bytes 1572872 | tf_op jit(solution)/shard_map/ppermute | solution.py:45
  93.2 3.0 %collective-permute-start.13 = (bf16[2,2,2,2,64,256]{5,4,0,1,2,3:T(8,128)(2,1)S(1)}, bf16[2,2,2,2,64,256]{5,4,0,1,2,3:T(8,128)(2,1)S(1)}, u32[]{:S(2)}, u32[]{:S(2)}) collective-permute-start(bf16[2,2,2,2,64,256]{5,4,0,1,2,3:T(8,128)(2,1)S(1)} %bitcast.142), channel_id=1, source_target_pairs={{0,2},{2,0},{4,6},{6,4},{8,10},{10,8},{12,14},{14,12},{16,18},{18,... | collective-permute-start | bytes 1572872 | tf_op jit(solution)/shard_map/ppermute | solution.py:45
  93.4 4.7 %collective-permute-start.17 = (bf16[2,2,2,2,64,256]{5,4,0,1,3,2:T(8,128)(2,1)S(1)}, bf16[2,2,2,2,64,256]{5,4,0,1,3,2:T(8,128)(2,1)S(1)}, u32[]{:S(2)}, u32[]{:S(2)}) collective-permute-start(bf16[2,2,2,2,64,256]{5,4,0,1,3,2:T(8,128)(2,1)S(1)} %bitcast.141), channel_id=1, source_target_pairs={{0,2},{2,0},{4,6},{6,4},{8,10},{10,8},{12,14},{14,12},{16,18},{18,... | collective-permute-start | bytes 1572872 | tf_op jit(solution)/shard_map/ppermute | solution.py:45
  94.1 9.2 %collective-permute-start.6 = (bf16[2,2,2,64,256]{4,3,0,1,2:T(8,128)(2,1)S(1)}, bf16[2,2,2,64,256]{4,3,0,1,2:T(8,128)(2,1)S(1)}, u32[]{:S(2)}, u32[]{:S(2)}) collective-permute-start(bf16[2,2,2,64,256]{4,3,0,1,2:T(8,128)(2,1)S(1)} %fusion.6), channel_id=1, source_target_pairs={{0,4},{2,6},{4,0},{6,2},{8,12},{10,14},{12,8},{14,10},{16,20},{18,... | collective-permute-start | bytes 786440 | tf_op jit(solution)/shard_map/ppermute | solution.py:45
  96.2 9.9 %collective-permute-start.10 = (bf16[2,2,2,64,256]{4,3,0,1,2:T(8,128)(2,1)S(1)}, bf16[2,2,2,64,256]{4,3,0,1,2:T(8,128)(2,1)S(1)}, u32[]{:S(2)}, u32[]{:S(2)}) collective-permute-start(bf16[2,2,2,64,256]{4,3,0,1,2:T(8,128)(2,1)S(1)} %fusion.7), channel_id=1, source_target_pairs={{0,8},{2,10},{4,12},{6,14},{8,0},{10,2},{12,4},{14,6},{16,24},{18,... | collective-permute-start | bytes 786440 | tf_op jit(solution)/shard_map/ppermute | solution.py:45
  98.1 10.3 %collective-permute-start.14 = (bf16[2,2,2,64,256]{4,3,0,1,2:T(8,128)(2,1)S(1)}, bf16[2,2,2,64,256]{4,3,0,1,2:T(8,128)(2,1)S(1)}, u32[]{:S(2)}, u32[]{:S(2)}) collective-permute-start(bf16[2,2,2,64,256]{4,3,0,1,2:T(8,128)(2,1)S(1)} %fusion.8), channel_id=1, source_target_pairs={{0,4},{2,6},{4,0},{6,2},{8,12},{10,14},{12,8},{14,10},{16,20},{18,... | collective-permute-start | bytes 786440 | tf_op jit(solution)/shard_map/ppermute | solution.py:45
  103.3 9.1 %collective-permute-start.18 = (bf16[2,2,2,64,256]{4,3,0,1,2:T(8,128)(2,1)S(1)}, bf16[2,2,2,64,256]{4,3,0,1,2:T(8,128)(2,1)S(1)}, u32[]{:S(2)}, u32[]{:S(2)}) collective-permute-start(bf16[2,2,2,64,256]{4,3,0,1,2:T(8,128)(2,1)S(1)} %fusion.9), channel_id=1, source_target_pairs={{0,8},{2,10},{4,12},{6,14},{8,0},{10,2},{12,4},{14,6},{16,24},{18,... | collective-permute-start | bytes 786440 | tf_op jit(solution)/shard_map/ppermute | solution.py:45
  106.2 8.9 %collective-permute-start.7 = (bf16[2,2,64,256]{3,2,0,1:T(8,128)(2,1)S(1)}, bf16[2,2,64,256]{3,2,0,1:T(8,128)(2,1)S(1)}, u32[]{:S(2)}, u32[]{:S(2)}) collective-permute-start(bf16[2,2,64,256]{3,2,0,1:T(8,128)(2,1)S(1)} %fusion.12), channel_id=1, source_target_pairs={{0,8},{2,10},{4,12},{6,14},{8,0},{10,2},{12,4},{14,6},{16,24},{18,... | collective-permute-start | bytes 393224 | tf_op jit(solution)/shard_map/ppermute | solution.py:45
  108.4 8.0 %collective-permute-start.11 = (bf16[2,2,64,256]{3,2,0,1:T(8,128)(2,1)S(1)}, bf16[2,2,64,256]{3,2,0,1:T(8,128)(2,1)S(1)}, u32[]{:S(2)}, u32[]{:S(2)}) collective-permute-start(bf16[2,2,64,256]{3,2,0,1:T(8,128)(2,1)S(1)} %fusion.13), channel_id=1, source_target_pairs={{0,4},{2,6},{4,0},{6,2},{8,12},{10,14},{12,8},{14,10},{16,20},{18,... | collective-permute-start | bytes 393224 | tf_op jit(solution)/shard_map/ppermute | solution.py:45
  112.4 6.3 %collective-permute-start.15 = (bf16[2,2,64,256]{3,2,0,1:T(8,128)(2,1)S(1)}, bf16[2,2,64,256]{3,2,0,1:T(8,128)(2,1)S(1)}, u32[]{:S(2)}, u32[]{:S(2)}) collective-permute-start(bf16[2,2,64,256]{3,2,0,1:T(8,128)(2,1)S(1)} %fusion.14), channel_id=1, source_target_pairs={{0,8},{2,10},{4,12},{6,14},{8,0},{10,2},{12,4},{14,6},{16,24},{18,... | collective-permute-start | bytes 393224 | tf_op jit(solution)/shard_map/ppermute | solution.py:45
  115.1 6.5 %collective-permute-start.19 = (bf16[2,2,64,256]{3,2,0,1:T(8,128)(2,1)S(1)}, bf16[2,2,64,256]{3,2,0,1:T(8,128)(2,1)S(1)}, u32[]{:S(2)}, u32[]{:S(2)}) collective-permute-start(bf16[2,2,64,256]{3,2,0,1:T(8,128)(2,1)S(1)} %fusion.15), channel_id=1, source_target_pairs={{0,4},{2,6},{4,0},{6,2},{8,12},{10,14},{12,8},{14,10},{16,20},{18,... | collective-permute-start | bytes 393224 | tf_op jit(solution)/shard_map/ppermute | solution.py:45
  116.4 8.7 %collective-permute-start.8 = (bf16[2,64,256]{2,1,0:T(8,128)(2,1)S(1)}, bf16[2,64,256]{2,1,0:T(8,128)(2,1)S(1)}, u32[]{:S(2)}, u32[]{:S(2)}) collective-permute-start(bf16[2,64,256]{2,1,0:T(8,128)(2,1)S(1)} %fusion.20), channel_id=1, source_target_pairs={{0,16},{2,18},{4,20},{6,22},{8,24},{10,26},{12,28},{14,30},{16,0},... | collective-permute-start | bytes 196616 | tf_op jit(solution)/shard_map/ppermute | solution.py:45
  118.7 7.6 %collective-permute-start.12 = (bf16[2,64,256]{2,1,0:T(8,128)(2,1)S(1)}, bf16[2,64,256]{2,1,0:T(8,128)(2,1)S(1)}, u32[]{:S(2)}, u32[]{:S(2)}) collective-permute-start(bf16[2,64,256]{2,1,0:T(8,128)(2,1)S(1)} %fusion.21), channel_id=1, source_target_pairs={{0,16},{2,18},{4,20},{6,22},{8,24},{10,26},{12,28},{14,30},{16,0},... | collective-permute-start | bytes 196616 | tf_op jit(solution)/shard_map/ppermute | solution.py:45
  121.6 6.1 %collective-permute-start.16 = (bf16[2,64,256]{2,1,0:T(8,128)(2,1)S(1)}, bf16[2,64,256]{2,1,0:T(8,128)(2,1)S(1)}, u32[]{:S(2)}, u32[]{:S(2)}) collective-permute-start(bf16[2,64,256]{2,1,0:T(8,128)(2,1)S(1)} %fusion.22), channel_id=1, source_target_pairs={{0,16},{2,18},{4,20},{6,22},{8,24},{10,26},{12,28},{14,30},{16,0},... | collective-permute-start | bytes 196616 | tf_op jit(solution)/shard_map/ppermute | solution.py:45
  125.2 5.2 %collective-permute-start.20 = (bf16[2,64,256]{2,1,0:T(8,128)(2,1)S(1)}, bf16[2,64,256]{2,1,0:T(8,128)(2,1)S(1)}, u32[]{:S(2)}, u32[]{:S(2)}) collective-permute-start(bf16[2,64,256]{2,1,0:T(8,128)(2,1)S(1)} %fusion.23), channel_id=1, source_target_pairs={{0,16},{2,18},{4,20},{6,22},{8,24},{10,26},{12,28},{14,30},{16,0},... | collective-permute-start | bytes 196616 | tf_op jit(solution)/shard_map/ppermute | solution.py:45
  131.9 0.8 copy-start.9
  (1 other events, 0.8 us)
Sparse Core Ops, SparseCore 0:
  11.1 54.7 all-gather.1

commit v10 on v9

--- a/solution.py
+++ b/solution.py
@@ -193,42 +193,60 @@
     )(*operands)
 
 
-def finalize_kernel(own_k_ref, own_v_ref, back_k_ref, back_v_ref, digest_ref, select_ref, k_out, v_out):
-    hd = back_k_ref.shape[1]
+def finalize_band_kernel(own_k_ref, own_v_ref, back_k_ref, back_v_ref, k_out, v_out):
+    for own_ref, back_ref, out_ref in ((own_k_ref, back_k_ref, k_out), (own_v_ref, back_v_ref, v_out)):
+        out_ref[...] = (own_ref[...] + back_ref[...].astype(jnp.float32)).astype(out_ref.dtype)
+
+
+def finalize_fixed_kernel(own_k_ref, own_v_ref, digest_ref, select_ref, k_in, v_in, k_out, v_out):
     pick = select_ref[0]
-    for own_ref, back_ref, side, out_ref in (
-        (own_k_ref, back_k_ref, 0, k_out),
-        (own_v_ref, back_v_ref, 1, v_out),
-    ):
-        out_ref[:, :hd] = (own_ref[:, :hd] + back_ref[...].astype(jnp.float32)).astype(out_ref.dtype)
+    for own_ref, side, out_ref in ((own_k_ref, 0, k_out), (own_v_ref, 1, v_out)):
         summary = tn(pick, digest_ref[side])
-        out_ref[:, hd:] = (own_ref[:, hd:] + summary).astype(out_ref.dtype)
-
-
-def finalize(own_k, own_v, back_k, back_v, digest, select, head_pairs, head_dim):
+        out_ref[...] = (own_ref[...] + summary).astype(out_ref.dtype)
+
+
+def finalize_band(own_k, own_v, back_k, back_v, head_pairs, head_dim):
+    rows = own_k.shape[0]
+    band = pl.BlockSpec((rows, head_dim), lambda p: (0, 2 * p))
+    narrow = pl.BlockSpec((rows, head_dim), lambda p: (0, p))
+    return pl.pallas_call(
+        finalize_band_kernel,
+        grid=(head_pairs,),
+        in_specs=[band, band, narrow, narrow],
+        out_specs=[band, band],
+        out_shape=[jax.ShapeDtypeStruct(own_k.shape, jnp.bfloat16)] * 2,
+        cost_estimate=pl.CostEstimate(
+            flops=2 * rows * head_dim * head_pairs,
+            transcendentals=0,
+            bytes_accessed=rows * head_dim * head_pairs * 16,
+        ),
+    )(own_k, own_v, back_k, back_v)
+
+
+def finalize_fixed(own_k, own_v, digest, select, partial, head_pairs, head_dim):
     rows = own_k.shape[0]
     digest_rows = digest.shape[1]
-    wide = pl.BlockSpec((rows, 2 * head_dim), lambda p: (0, p))
-    narrow = pl.BlockSpec((rows, head_dim), lambda p: (0, p))
+    fixed = pl.BlockSpec((rows, head_dim), lambda p: (0, 2 * p + 1))
     return pl.pallas_call(
-        finalize_kernel,
+        finalize_fixed_kernel,
         grid=(head_pairs,),
         in_specs=[
-            wide,
-            wide,
-            narrow,
-            narrow,
+            fixed,
+            fixed,
             pl.BlockSpec((2, digest_rows, head_dim), lambda p: (0, 0, p)),
             pl.BlockSpec((1, digest_rows, rows), lambda p: (p, 0, 0)),
+            pl.BlockSpec(memory_space=pl.ANY),
+            pl.BlockSpec(memory_space=pl.ANY),
         ],
-        out_specs=[wide, wide],
+        out_specs=[fixed, fixed],
         out_shape=[jax.ShapeDtypeStruct(own_k.shape, jnp.bfloat16)] * 2,
+        input_output_aliases={4: 0, 5: 1},
         cost_estimate=pl.CostEstimate(
             flops=4 * rows * digest_rows * head_dim * head_pairs,
             transcendentals=0,
-            bytes_accessed=rows * head_dim * head_pairs * 20,
+            bytes_accessed=rows * head_dim * head_pairs * 12,
         ),
-    )(own_k, own_v, back_k, back_v, digest, select)
+    )(own_k, own_v, digest, select, *partial)
 
 
 def on_device(queries, keys, values, out_weight, cotangent, offsets):
@@ -316,8 +334,9 @@
     attention, query_grad, own_dk, own_dv = outputs
     back_k, back_v = passed_along((back_k, back_v), "seq", -1)
     digest_dkv = jnp.concatenate(digests, 2) if chunks > 1 else digests[0]
-    key_grad, value_grad = finalize(
-        own_dk, own_dv, back_k, back_v, digest_dkv, select, head_pairs, head_dim
+    partial = finalize_band(own_dk, own_dv, back_k, back_v, head_pairs, head_dim)
+    key_grad, value_grad = finalize_fixed(
+        own_dk, own_dv, digest_dkv, select, partial, head_pairs, head_dim
     )
     return attention, query_grad, key_grad, value_grad
 

time: 147 us -> 152 us (1.034)
  Pallas kernels: 36.3 us -> 41.3 us
  waiting for transfers between devices: 29.3 us -> 25 us
  other arithmetic: 7.9 us -> 11 us
    pallas_call x1 -> x2, Pallas kernels: 6.87 us -> 11.9 us  [the longest x1 6.29 us: finalize_fixed(): pl.pallas_call(finalize_fixed_kernel, grid=(head_pairs,), in_specs=[fixed...]
    ppermute x16, waiting for transfers between devices: 15.6 us -> 11.6 us  [seq_reduce_scatter(): lax.ppermute(send.astype(jnp.bfloat16), 'seq', [(source, source ^ 1 << bi...]
    unnamed x24 -> x16, local copies, waits for them, and re-layouts: 6.58 us -> 3.32 us
    add x12, other arithmetic: 0.87 us -> 4.03 us  [seq_reduce_scatter(): held = keep + arrived.astype(jnp.float32)]
    dynamic_slice x4, local copies, waits for them, and re-layouts: 0.16 us -> 1.82 us  [seq_reduce_scatter(): send = lax.dynamic_index_in_dim(held, 1 - mine, where, keepdims=False)]
  transfers between devices with their start and end apart: 22 -> 22, of which waited for: 10 -> 8; matrix products, arithmetic and copies ran while one was open for 16% -> 19% of each run, Pallas kernels for 13% -> 23%
where the time goes in v10:
time: 152 us; the launch traced here: 151 us
  Pallas kernels  41.3 us (27%)
  starting transfers between devices  35.2 us (23%)
  waiting for transfers between devices  25 us (16%)
  between operations  14.4 us (9%)
  matrix products  12.8 us (8%)
  other arithmetic  11 us (7%)
  local copies, waits for them, and re-layouts  10.9 us (7%)
    ppermute x16, starting transfers between devices, seq_reduce_scatter(): lax.ppermute(send.astype(jnp.bfloat16), 'seq', [(source, source ^ 1 << bi...  23.2 us
    pallas_call x4, Pallas kernels, fixed_attention(): pl.pallas_call(functools.partial(fixed_kernel, scale=scale, unused=len(ea...  19.8 us
    ppermute x1, waiting for transfers between devices, on_device(): lax.ppermute(cotangent, 'head', [(source, (source + shift) % head_count)...  13.4 us
    dot_general x1, matrix products, on_device(): lax.dot_general(gathered.reshape(seq_rows, cotangent.shape[1]), out_weigh...  12.1 us
    ppermute x16, waiting for transfers between devices, seq_reduce_scatter(): lax.ppermute(send.astype(jnp.bfloat16), 'seq', [(source, source ^ 1 << bi...  11.6 us
    pallas_call x1, Pallas kernels, band_attention(): pl.pallas_call(functools.partial(band_kernel, scale=scale), grid_spec=gri...  9.58 us
    ppermute x4, starting transfers between devices, passed_along(): lax.ppermute(value, axis, [(source, source + steps) for source in range(f...  8.96 us
    pallas_call x1, Pallas kernels, finalize_fixed(): pl.pallas_call(finalize_fixed_kernel, grid=(head_pairs,), in_specs=[fixed...  6.29 us
  transfers between devices with their start and end apart: 22, of which 8 were waited for; matrix products, arithmetic and copies ran while one was open for 19% of the time, Pallas kernels for 23%

profile of v10, /device:TPU:0, one launch (start us, length us, event | category | flops | bytes accessed | tf_op | source)
XLA Modules:
  0.0 150.7 jit_solution(14448168312818727879)
XLA Ops:
  7.2 1.6 %copy.32 = bf16[256,2048]{0,1:T(8,128)(2,1)S(1)} copy(bf16[256,2048]{1,0:T(8,128)(2,1)} %k_ref.9) | data formatting | bytes 2097152 | tf_op args[1]
  11.0 3.0 %collective-permute-start = (bf16[128,4096]{1,0:T(8,128)(2,1)}, bf16[128,4096]{1,0:T(8,128)(2,1)}, u32[]{:S(2)}, u32[]{:S(2)}) collective-permute-start(bf16[128,4096]{1,0:T(8,128)(2,1)} %param.10), channel_id=1, source_target_pairs={{0,1},{1,0},{2,3},{3,2},{4,5},{5,4},{6,7},{7,6},{8,9},{9,8},{10,11... | collective-permute-start | bytes 3145736 | tf_op jit(solution)/shard_map/ppermute | solution.py:297
  14.8 2.0 %copy.48 = bf16[256,1024]{1,0:T(8,128)(2,1)} copy(bf16[256,1024]{0,1:T(8,128)(2,1)} %bitcast.136) | data formatting | bytes 1048576 | tf_op jit(solution)/shard_map/reshape;squeeze | solution.py:264
  16.9 2.2 %collective-permute-start.1 = (bf16[256,1024]{1,0:T(8,128)(2,1)}, bf16[256,1024]{1,0:T(8,128)(2,1)}, u32[]{:S(2)}, u32[]{:S(2)}) collective-permute-start(bf16[256,1024]{1,0:T(8,128)(2,1)} %copy.48), channel_id=1, source_target_pairs={{0,2},{2,4},{4,6},{6,8},{8,10},{10,12},{12,14},{14,16},{16,18},{18... | collective-permute-start | bytes 1572872 | tf_op jit(solution)/shard_map/ppermute | solution.py:21
  20.2 3.9 %collective-permute-start.2 = (bf16[256,1024]{1,0:T(8,128)(2,1)}, bf16[256,1024]{1,0:T(8,128)(2,1)}, u32[]{:S(2)}, u32[]{:S(2)}) collective-permute-start(bf16[256,1024]{1,0:T(8,128)(2,1)} %copy.49), channel_id=1, source_target_pairs={{0,2},{2,4},{4,6},{6,8},{8,10},{10,12},{12,14},{14,16},{16,18},{18... | collective-permute-start | bytes 1572872 | tf_op jit(solution)/shard_map/ppermute | solution.py:21
  24.1 13.4 %collective-permute-done = bf16[128,4096]{1,0:T(8,128)(2,1)} collective-permute-done((bf16[128,4096]{1,0:T(8,128)(2,1)}, bf16[128,4096]{1,0:T(8,128)(2,1)}, u32[]{:S(2)}, u32[]{:S(2)}) %collective-permute-start) | collective-permute-done | bytes 1048608 | tf_op jit(solution)/shard_map/ppermute | solution.py:297
  37.5 4.7 %fusion.2 = bf16[2,128,4096]{2,1,0:T(8,128)(2,1)} fusion(s32[]{:T(128)S(6)} %select_n.65, bf16[1,128,4096]{2,1,0:T(8,128)(2,1)} %bitcast.1, bf16[1,128,4096]{2,1,0:T(8,128)(2,1)} %bitcast.138), kind=kLoop, calls=%fused_computation.7 | loop fusion | flops 3145728 | bytes 4194308 | tf_op jit(solution)/shard_map/stack | solution.py:302
  42.1 12.1 %convolution_convert_fusion.g_ref = bf16[256,2048]{1,0:T(8,128)(2,1)} fusion(bf16[256,4096]{1,0:T(8,128)(2,1)} %bitcast.135, bf16[2048,4096]{1,0:T(8,128)(2,1)} %param.9), kind=kOutput, calls=%fused_computation.4 | convolution fusion | flops 4295491584 | bytes 19922944 | tf_op jit(solution)/shard_map/dot_general | solution.py:304
  54.3 9.6 %shard_map.93 = (bf16[256,2048]{1,0:T(8,128)(2,1)}, bf16[256,2048]{1,0:T(8,128)(2,1)}, f32[256,2048]{1,0:T(8,128)}, f32[256,2048]{1,0:T(8,128)}, bf16[256,1024]{1,0:T(8,128)(2,1)}, /*index=5*/bf16[256,1024]{1,0:T(8,128)(2,1)}) custom-call(s32[1]{0:T(128)} %bitcast.seq_ref, bf16[256,2048]{1,0:T(8,128)(2,1)S(1)} %copy-done.2, bf16[256,2048]{1,0:T(8,128)(2,1)S(1)} %copy-done, ...), custom_call_target="tpu_custom_call" | custom-call | flops 1879048192 | bytes 7340032 | tf_op jit(solution)/shard_map/pallas_call | solution.py:154
  63.9 1.3 collective-permute-start.19
  65.1 1.5 collective-permute-start.20
  67.9 5.0 %shard_map.94 = (bf16[256,2048]{1,0:T(8,128)(2,1)}, bf16[256,2048]{1,0:T(8,128)(2,1)}, f32[256,2048]{1,0:T(8,128)}, f32[256,2048]{1,0:T(8,128)}, bf16[2,1024,256]{2,1,0:T(8,128)(2,1)S(1)}) custom-call(s32[1]{0:T(128)} %bitcast.seq_ref, bf16[256,2048]{1,0:T(8,128)(2,1)S(1)} %copy-done.2, ...), custom_call_target="tpu_custom_call", output_to_operand_aliasing={{0}: (7, {}), {1}: (8, {}), {2}: (9, {}), {3}: (10, {})} | custom-call | flops 1174405120 | bytes 3014656 | tf_op jit(solution)/shard_map/pallas_call | solution.py:185
  72.9 4.9 %shard_map.95 = (bf16[256,2048]{1,0:T(8,128)(2,1)}, bf16[256,2048]{1,0:T(8,128)(2,1)}, f32[256,2048]{1,0:T(8,128)}, f32[256,2048]{1,0:T(8,128)}, bf16[2,1024,256]{2,1,0:T(8,128)(2,1)S(1)}) custom-call(s32[1]{0:T(128)} %bitcast.seq_ref, bf16[256,2048]{1,0:T(8,128)(2,1)S(1)} %copy-done.2, ...), custom_call_target="tpu_custom_call", output_to_operand_aliasing={{0}: (7, {}), {1}: (8, {}), {2}: (9, {}), {3}: (10, {})} | custom-call | flops 1174405120 | bytes 3014656 | tf_op jit(solution)/shard_map/pallas_call | solution.py:185
  77.8 1.2 constant_dynamic-slice_fusion.5
  79.9 1.8 %collective-permute-start.3 = (bf16[2,2,2,2,64,256]{5,4,0,1,2,3:T(8,128)(2,1)}, bf16[2,2,2,2,64,256]{5,4,0,1,2,3:T(8,128)(2,1)}, u32[]{:S(2)}, u32[]{:S(2)}) collective-permute-start(bf16[2,2,2,2,64,256]{5,4,0,1,2,3:T(8,128)(2,1)} %bitcast.124), channel_id=1, source_target_pairs={{0,2},{2,0},{4,6},{6,4},{8,10},{10,8},{12,14},{14,12},{16,18},{18,... | collective-permute-start | bytes 1572872 | tf_op jit(solution)/shard_map/ppermute | solution.py:45
  83.4 5.0 %shard_map.96 = (bf16[256,2048]{1,0:T(8,128)(2,1)}, bf16[256,2048]{1,0:T(8,128)(2,1)}, f32[256,2048]{1,0:T(8,128)}, f32[256,2048]{1,0:T(8,128)}, bf16[2,1024,256]{2,1,0:T(8,128)(2,1)S(1)}) custom-call(s32[1]{0:T(128)} %bitcast.seq_ref, bf16[256,2048]{1,0:T(8,128)(2,1)S(1)} %copy-done.2, ...), custom_call_target="tpu_custom_call", output_to_operand_aliasing={{0}: (7, {}), {1}: (8, {}), {2}: (9, {}), {3}: (10, {})} | custom-call | flops 1174405120 | bytes 3014656 | tf_op jit(solution)/shard_map/pallas_call | solution.py:185
  88.3 5.0 %shard_map.97 = (bf16[256,2048]{1,0:T(8,128)(2,1)}, bf16[256,2048]{1,0:T(8,128)(2,1)}, f32[256,2048]{1,0:T(8,128)}, f32[256,2048]{1,0:T(8,128)}, bf16[2,1024,256]{2,1,0:T(8,128)(2,1)S(1)}) custom-call(s32[1]{0:T(128)} %bitcast.seq_ref, bf16[256,2048]{1,0:T(8,128)(2,1)S(1)} %copy-done.2, ...), custom_call_target="tpu_custom_call", output_to_operand_aliasing={{0}: (7, {}), {1}: (8, {}), {2}: (9, {}), {3}: (10, {})} | custom-call | flops 1174405120 | bytes 3014656 | tf_op jit(solution)/shard_map/pallas_call | solution.py:185
  94.2 5.6 %shard_map.98 = (bf16[256,2048]{1,0:T(8,128)(2,1)}, bf16[256,2048]{1,0:T(8,128)(2,1)}) custom-call(f32[256,2048]{1,0:T(8,128)} %get-tuple-element.52.own_k_ref, f32[256,2048]{1,0:T(8,128)} %get-tuple-element.53.own_v_ref, bf16[256,1024]{1,0:T(8,128)(2,1)} %collective-permute-done.19.back_k_ref, bf16[256,1024]{1,0:T(8,128)(2,1)} %collective-permute-done.20.back_v_ref), custom_call_target="tpu_custom_call" | custom-call | flops 524288 | bytes 4194304 | tf_op jit(solution)/shard_map/pallas_call | solution.py:212
  99.9 1.2 convert_add_fusion.3
  101.1 2.2 %collective-permute-start.4 = (bf16[2,2,2,64,256]{4,3,0,1,2:T(8,128)(2,1)S(1)}, bf16[2,2,2,64,256]{4,3,0,1,2:T(8,128)(2,1)S(1)}, u32[]{:S(2)}, u32[]{:S(2)}) collective-permute-start(bf16[2,2,2,64,256]{4,3,0,1,2:T(8,128)(2,1)S(1)} %fusion.6), channel_id=1, source_target_pairs={{0,4},{2,6},{4,0},{6,2},{8,12},{10,14},{12,8},{14,10},{16,20},{18,... | collective-permute-start | bytes 786440 | tf_op jit(solution)/shard_map/ppermute | solution.py:45
  104.5 1.9 %collective-permute-start.8 = (bf16[2,2,2,64,256]{4,3,0,1,2:T(8,128)(2,1)S(1)}, bf16[2,2,2,64,256]{4,3,0,1,2:T(8,128)(2,1)S(1)}, u32[]{:S(2)}, u32[]{:S(2)}) collective-permute-start(bf16[2,2,2,64,256]{4,3,0,1,2:T(8,128)(2,1)S(1)} %fusion.7), channel_id=1, source_target_pairs={{0,8},{2,10},{4,12},{6,14},{8,0},{10,2},{12,4},{14,6},{16,24},{18,... | collective-permute-start | bytes 786440 | tf_op jit(solution)/shard_map/ppermute | solution.py:45
  107.6 1.4 collective-permute-start.12
  110.0 3.8 %collective-permute-start.5 = (bf16[2,2,64,256]{3,2,0,1:T(8,128)(2,1)S(1)}, bf16[2,2,64,256]{3,2,0,1:T(8,128)(2,1)S(1)}, u32[]{:S(2)}, u32[]{:S(2)}) collective-permute-start(bf16[2,2,64,256]{3,2,0,1:T(8,128)(2,1)S(1)} %fusion.12), channel_id=1, source_target_pairs={{0,8},{2,10},{4,12},{6,14},{8,0},{10,2},{12,4},{14,6},{16,24},{18,... | collective-permute-start | bytes 393224 | tf_op jit(solution)/shard_map/ppermute | solution.py:45
  115.1 1.3 collective-permute-done.12
  116.5 2.9 %collective-permute-start.13 = (bf16[2,2,64,256]{3,2,0,1:T(8,128)(2,1)S(1)}, bf16[2,2,64,256]{3,2,0,1:T(8,128)(2,1)S(1)}, u32[]{:S(2)}, u32[]{:S(2)}) collective-permute-start(bf16[2,2,64,256]{3,2,0,1:T(8,128)(2,1)S(1)} %fusion.14), channel_id=1, source_target_pairs={{0,8},{2,10},{4,12},{6,14},{8,0},{10,2},{12,4},{14,6},{16,24},{18,... | collective-permute-start | bytes 393224 | tf_op jit(solution)/shard_map/ppermute | solution.py:45
  120.7 1.5 collective-permute-done.5
  122.3 2.9 %collective-permute-start.6 = (bf16[2,64,256]{2,1,0:T(8,128)(2,1)S(1)}, bf16[2,64,256]{2,1,0:T(8,128)(2,1)S(1)}, u32[]{:S(2)}, u32[]{:S(2)}) collective-permute-start(bf16[2,64,256]{2,1,0:T(8,128)(2,1)S(1)} %fusion.20), channel_id=1, source_target_pairs={{0,16},{2,18},{4,20},{6,22},{8,24},{10,26},{12,28},{14,30},{16,0},... | collective-permute-start | bytes 196616 | tf_op jit(solution)/shard_map/ppermute | solution.py:45
  125.5 2.9 %collective-permute-start.14 = (bf16[2,64,256]{2,1,0:T(8,128)(2,1)S(1)}, bf16[2,64,256]{2,1,0:T(8,128)(2,1)S(1)}, u32[]{:S(2)}, u32[]{:S(2)}) collective-permute-start(bf16[2,64,256]{2,1,0:T(8,128)(2,1)S(1)} %fusion.22), channel_id=1, source_target_pairs={{0,16},{2,18},{4,20},{6,22},{8,24},{10,26},{12,28},{14,30},{16,0},... | collective-permute-start | bytes 196616 | tf_op jit(solution)/shard_map/ppermute | solution.py:45
  128.6 1.8 %collective-permute-done.6 = bf16[2,64,256]{2,1,0:T(8,128)(2,1)S(1)} collective-permute-done((bf16[2,64,256]{2,1,0:T(8,128)(2,1)S(1)}, bf16[2,64,256]{2,1,0:T(8,128)(2,1)S(1)}, u32[]{:S(2)}, u32[]{:S(2)}) %collective-permute-start.6) | collective-permute-done | bytes 65568 | tf_op jit(solution)/shard_map/ppermute | solution.py:45
  130.4 3.5 %collective-permute-done.10 = bf16[2,64,256]{2,1,0:T(8,128)(2,1)S(1)} collective-permute-done((bf16[2,64,256]{2,1,0:T(8,128)(2,1)S(1)}, bf16[2,64,256]{2,1,0:T(8,128)(2,1)S(1)}, u32[]{:S(2)}, u32[]{:S(2)}) %collective-permute-start.10) | collective-permute-done | bytes 65568 | tf_op jit(solution)/shard_map/ppermute | solution.py:45
  134.0 2.1 %collective-permute-done.14 = bf16[2,64,256]{2,1,0:T(8,128)(2,1)S(1)} collective-permute-done((bf16[2,64,256]{2,1,0:T(8,128)(2,1)S(1)}, bf16[2,64,256]{2,1,0:T(8,128)(2,1)S(1)}, u32[]{:S(2)}, u32[]{:S(2)}) %collective-permute-start.14) | collective-permute-done | bytes 65568 | tf_op jit(solution)/shard_map/ppermute | solution.py:45
  137.6 6.3 %shard_map.99 = (bf16[256,2048]{1,0:T(8,128)(2,1)}, bf16[256,2048]{1,0:T(8,128)(2,1)}) custom-call(f32[256,2048]{1,0:T(8,128)} %get-tuple-element.52.own_k_ref, f32[256,2048]{1,0:T(8,128)} %get-tuple-element.53.own_v_ref, bf16[2,64,1024]{2,1,0:T(8,128)(2,1)} %pad_maximum_fusion.1.digest_ref, ...), custom_call_target="tpu_custom_call", output_to_operand_aliasing={{0}: (4, {}), {1}: (5, {})} | custom-call | flops 67108864 | bytes 3145728 | tf_op jit(solution)/shard_map/pallas_call | solution.py:230
  (87 shorter events, 16.9 us)
Async XLA Ops:
  7.2 1.6 %copy-start.1 = (bf16[256,2048]{1,0:T(8,128)(2,1)S(1)}, bf16[256,2048]{1,0:T(8,128)(2,1)}, u32[]{:S(2)}) copy-start(bf16[256,2048]{1,0:T(8,128)(2,1)} %v_ref.9) | copy-start | bytes 3145732
  7.2 59.5 %all-gather.2.cloned.1.call-start = ((), (), s32[]{:S(2)}) async-start(), calls=%async_computation | async-start | bytes 4456448 | tf_op jit(solution)/shard_map/all_gather | solution.py:282
  7.2 2.1 %copy-start.6 = (s32[8,32]{1,0:T(8,128)S(1)}, s32[8,32]{1,0:T(8,128)}, u32[]{:S(2)}) copy-start(s32[8,32]{1,0:T(8,128)} %param.11) | copy-start | bytes 3076
  11.0 26.5 %collective-permute-start = (bf16[128,4096]{1,0:T(8,128)(2,1)}, bf16[128,4096]{1,0:T(8,128)(2,1)}, u32[]{:S(2)}, u32[]{:S(2)}) collective-permute-start(bf16[128,4096]{1,0:T(8,128)(2,1)} %param.10), channel_id=1, source_target_pairs={{0,1},{1,0},{2,3},{3,2},{4,5},{5,4},{6,7},{7,6},{8,9},{9,8},{10,11... | collective-permute-start | bytes 3145736 | tf_op jit(solution)/shard_map/ppermute | solution.py:297
  16.9 37.4 %collective-permute-start.1 = (bf16[256,1024]{1,0:T(8,128)(2,1)}, bf16[256,1024]{1,0:T(8,128)(2,1)}, u32[]{:S(2)}, u32[]{:S(2)}) collective-permute-start(bf16[256,1024]{1,0:T(8,128)(2,1)} %copy.48), channel_id=1, source_target_pairs={{0,2},{2,4},{4,6},{6,8},{8,10},{10,12},{12,14},{14,16},{16,18},{18... | collective-permute-start | bytes 1572872 | tf_op jit(solution)/shard_map/ppermute | solution.py:21
  20.2 34.1 %collective-permute-start.2 = (bf16[256,1024]{1,0:T(8,128)(2,1)}, bf16[256,1024]{1,0:T(8,128)(2,1)}, u32[]{:S(2)}, u32[]{:S(2)}) collective-permute-start(bf16[256,1024]{1,0:T(8,128)(2,1)} %copy.49), channel_id=1, source_target_pairs={{0,2},{2,4},{4,6},{6,8},{8,10},{10,12},{12,14},{14,16},{16,18},{18... | collective-permute-start | bytes 1572872 | tf_op jit(solution)/shard_map/ppermute | solution.py:21
  42.1 12.1 %copy-start = (bf16[256,2048]{1,0:T(8,128)(2,1)S(1)}, bf16[256,2048]{1,0:T(8,128)(2,1)}, u32[]{:S(2)}) copy-start(bf16[256,2048]{1,0:T(8,128)(2,1)} %k_ref.9) | copy-start | bytes 3145732
  42.1 12.1 %copy-start.2 = (bf16[256,2048]{1,0:T(8,128)(2,1)S(1)}, bf16[256,2048]{1,0:T(8,128)(2,1)}, u32[]{:S(2)}) copy-start(bf16[256,2048]{1,0:T(8,128)(2,1)} %q_ref.9) | copy-start | bytes 3145732
  63.9 30.3 %collective-permute-start.19 = (bf16[256,1024]{1,0:T(8,128)(2,1)}, bf16[256,1024]{1,0:T(8,128)(2,1)}, u32[]{:S(2)}, u32[]{:S(2)}) collective-permute-start(bf16[256,1024]{1,0:T(8,128)(2,1)} %get-tuple-element.58), channel_id=1, source_target_pairs={{2,0},{4,2},{6,4},{8,6},{10,8},{12,10},{14,12},{16,14},{18,16},{20... | collective-permute-start | bytes 1572872 | tf_op jit(solution)/shard_map/ppermute | solution.py:21
  65.1 29.1 %collective-permute-start.20 = (bf16[256,1024]{1,0:T(8,128)(2,1)}, bf16[256,1024]{1,0:T(8,128)(2,1)}, u32[]{:S(2)}, u32[]{:S(2)}) collective-permute-start(bf16[256,1024]{1,0:T(8,128)(2,1)} %get-tuple-element.59), channel_id=1, source_target_pairs={{2,0},{4,2},{6,4},{8,6},{10,8},{12,10},{14,12},{16,14},{18,16},{20... | collective-permute-start | bytes 1572872 | tf_op jit(solution)/shard_map/ppermute | solution.py:21
  66.7 1.2 copy-start.3
  79.9 19.9 %collective-permute-start.3 = (bf16[2,2,2,2,64,256]{5,4,0,1,2,3:T(8,128)(2,1)}, bf16[2,2,2,2,64,256]{5,4,0,1,2,3:T(8,128)(2,1)}, u32[]{:S(2)}, u32[]{:S(2)}) collective-permute-start(bf16[2,2,2,2,64,256]{5,4,0,1,2,3:T(8,128)(2,1)} %bitcast.124), channel_id=1, source_target_pairs={{0,2},{2,0},{4,6},{6,4},{8,10},{10,8},{12,14},{14,12},{16,18},{18,... | collective-permute-start | bytes 1572872 | tf_op jit(solution)/shard_map/ppermute | solution.py:45
  83.4 19.9 %collective-permute-start.7 = (bf16[2,2,2,2,64,256]{5,4,0,1,3,2:T(8,128)(2,1)}, bf16[2,2,2,2,64,256]{5,4,0,1,3,2:T(8,128)(2,1)}, u32[]{:S(2)}, u32[]{:S(2)}) collective-permute-start(bf16[2,2,2,2,64,256]{5,4,0,1,3,2:T(8,128)(2,1)} %bitcast.123), channel_id=1, source_target_pairs={{0,2},{2,0},{4,6},{6,4},{8,10},{10,8},{12,14},{14,12},{16,18},{18,... | collective-permute-start | bytes 1572872 | tf_op jit(solution)/shard_map/ppermute | solution.py:45
  93.5 12.9 %collective-permute-start.11 = (bf16[2,2,2,2,64,256]{5,4,0,1,2,3:T(8,128)(2,1)S(1)}, bf16[2,2,2,2,64,256]{5,4,0,1,2,3:T(8,128)(2,1)}, u32[]{:S(2)}, u32[]{:S(2)}) collective-permute-start(bf16[2,2,2,2,64,256]{5,4,0,1,2,3:T(8,128)(2,1)S(1)} %bitcast.140), channel_id=1, source_target_pairs={{0,2},{2,0},{4,6},{6,4},{8,10},{10,8},{12,14},{14,12},{16,18},{18,... | collective-permute-start | bytes 1572872 | tf_op jit(solution)/shard_map/ppermute | solution.py:45
  94.1 15.0 %collective-permute-start.15 = (bf16[2,2,2,2,64,256]{5,4,0,1,3,2:T(8,128)(2,1)S(1)}, bf16[2,2,2,2,64,256]{5,4,0,1,3,2:T(8,128)(2,1)S(1)}, u32[]{:S(2)}, u32[]{:S(2)}) collective-permute-start(bf16[2,2,2,2,64,256]{5,4,0,1,3,2:T(8,128)(2,1)S(1)} %bitcast.139), channel_id=1, source_target_pairs={{0,2},{2,0},{4,6},{6,4},{8,10},{10,8},{12,14},{14,12},{16,18},{18,... | collective-permute-start | bytes 1572872 | tf_op jit(solution)/shard_map/ppermute | solution.py:45
  94.2 5.6 %copy-start.5 = (bf16[2,2,2,2,1,64,256]{6,5,4,3,2,1,0:T(8,128)(2,1)S(1)}, bf16[2,2,2,2,1,64,256]{6,5,4,3,2,1,0:T(8,128)(2,1)}, u32[]{:S(2)}) copy-start(bf16[2,2,2,2,1,64,256]{6,5,4,3,2,1,0:T(8,128)(2,1)} %get-tuple-element.75) | copy-start | bytes 1572868
  99.9 3.5 %copy-start.4 = (bf16[2,2,2,2,1,64,256]{6,5,4,3,2,1,0:T(8,128)(2,1)S(1)}, bf16[2,2,2,2,1,64,256]{6,5,4,3,2,1,0:T(8,128)(2,1)}, u32[]{:S(2)}) copy-start(bf16[2,2,2,2,1,64,256]{6,5,4,3,2,1,0:T(8,128)(2,1)} %get-tuple-element.66) | copy-start | bytes 1572868
  101.1 8.8 %collective-permute-start.4 = (bf16[2,2,2,64,256]{4,3,0,1,2:T(8,128)(2,1)S(1)}, bf16[2,2,2,64,256]{4,3,0,1,2:T(8,128)(2,1)S(1)}, u32[]{:S(2)}, u32[]{:S(2)}) collective-permute-start(bf16[2,2,2,64,256]{4,3,0,1,2:T(8,128)(2,1)S(1)} %fusion.6), channel_id=1, source_target_pairs={{0,4},{2,6},{4,0},{6,2},{8,12},{10,14},{12,8},{14,10},{16,20},{18,... | collective-permute-start | bytes 786440 | tf_op jit(solution)/shard_map/ppermute | solution.py:45
  104.5 9.3 %collective-permute-start.8 = (bf16[2,2,2,64,256]{4,3,0,1,2:T(8,128)(2,1)S(1)}, bf16[2,2,2,64,256]{4,3,0,1,2:T(8,128)(2,1)S(1)}, u32[]{:S(2)}, u32[]{:S(2)}) collective-permute-start(bf16[2,2,2,64,256]{4,3,0,1,2:T(8,128)(2,1)S(1)} %fusion.7), channel_id=1, source_target_pairs={{0,8},{2,10},{4,12},{6,14},{8,0},{10,2},{12,4},{14,6},{16,24},{18,... | collective-permute-start | bytes 786440 | tf_op jit(solution)/shard_map/ppermute | solution.py:45
  107.6 8.8 %collective-permute-start.12 = (bf16[2,2,2,64,256]{4,3,0,1,2:T(8,128)(2,1)S(1)}, bf16[2,2,2,64,256]{4,3,0,1,2:T(8,128)(2,1)S(1)}, u32[]{:S(2)}, u32[]{:S(2)}) collective-permute-start(bf16[2,2,2,64,256]{4,3,0,1,2:T(8,128)(2,1)S(1)} %fusion.8), channel_id=1, source_target_pairs={{0,4},{2,6},{4,0},{6,2},{8,12},{10,14},{12,8},{14,10},{16,20},{18,... | collective-permute-start | bytes 786440 | tf_op jit(solution)/shard_map/ppermute | solution.py:45
  109.3 10.1 %collective-permute-start.16 = (bf16[2,2,2,64,256]{4,3,0,1,2:T(8,128)(2,1)S(1)}, bf16[2,2,2,64,256]{4,3,0,1,2:T(8,128)(2,1)S(1)}, u32[]{:S(2)}, u32[]{:S(2)}) collective-permute-start(bf16[2,2,2,64,256]{4,3,0,1,2:T(8,128)(2,1)S(1)} %fusion.9), channel_id=1, source_target_pairs={{0,8},{2,10},{4,12},{6,14},{8,0},{10,2},{12,4},{14,6},{16,24},{18,... | collective-permute-start | bytes 786440 | tf_op jit(solution)/shard_map/ppermute | solution.py:45
  110.0 12.2 %collective-permute-start.5 = (bf16[2,2,64,256]{3,2,0,1:T(8,128)(2,1)S(1)}, bf16[2,2,64,256]{3,2,0,1:T(8,128)(2,1)S(1)}, u32[]{:S(2)}, u32[]{:S(2)}) collective-permute-start(bf16[2,2,64,256]{3,2,0,1:T(8,128)(2,1)S(1)} %fusion.12), channel_id=1, source_target_pairs={{0,8},{2,10},{4,12},{6,14},{8,0},{10,2},{12,4},{14,6},{16,24},{18,... | collective-permute-start | bytes 393224 | tf_op jit(solution)/shard_map/ppermute | solution.py:45
  113.9 11.3 %collective-permute-start.9 = (bf16[2,2,64,256]{3,2,0,1:T(8,128)(2,1)S(1)}, bf16[2,2,64,256]{3,2,0,1:T(8,128)(2,1)S(1)}, u32[]{:S(2)}, u32[]{:S(2)}) collective-permute-start(bf16[2,2,64,256]{3,2,0,1:T(8,128)(2,1)S(1)} %fusion.13), channel_id=1, source_target_pairs={{0,4},{2,6},{4,0},{6,2},{8,12},{10,14},{12,8},{14,10},{16,20},{18,... | collective-permute-start | bytes 393224 | tf_op jit(solution)/shard_map/ppermute | solution.py:45
  116.5 8.9 %collective-permute-start.13 = (bf16[2,2,64,256]{3,2,0,1:T(8,128)(2,1)S(1)}, bf16[2,2,64,256]{3,2,0,1:T(8,128)(2,1)S(1)}, u32[]{:S(2)}, u32[]{:S(2)}) collective-permute-start(bf16[2,2,64,256]{3,2,0,1:T(8,128)(2,1)S(1)} %fusion.14), channel_id=1, source_target_pairs={{0,8},{2,10},{4,12},{6,14},{8,0},{10,2},{12,4},{14,6},{16,24},{18,... | collective-permute-start | bytes 393224 | tf_op jit(solution)/shard_map/ppermute | solution.py:45
  119.5 8.8 %collective-permute-start.17 = (bf16[2,2,64,256]{3,2,0,1:T(8,128)(2,1)S(1)}, bf16[2,2,64,256]{3,2,0,1:T(8,128)(2,1)S(1)}, u32[]{:S(2)}, u32[]{:S(2)}) collective-permute-start(bf16[2,2,64,256]{3,2,0,1:T(8,128)(2,1)S(1)} %fusion.15), channel_id=1, source_target_pairs={{0,4},{2,6},{4,0},{6,2},{8,12},{10,14},{12,8},{14,10},{16,20},{18,... | collective-permute-start | bytes 393224 | tf_op jit(solution)/shard_map/ppermute | solution.py:45
  122.3 8.1 %collective-permute-start.6 = (bf16[2,64,256]{2,1,0:T(8,128)(2,1)S(1)}, bf16[2,64,256]{2,1,0:T(8,128)(2,1)S(1)}, u32[]{:S(2)}, u32[]{:S(2)}) collective-permute-start(bf16[2,64,256]{2,1,0:T(8,128)(2,1)S(1)} %fusion.20), channel_id=1, source_target_pairs={{0,16},{2,18},{4,20},{6,22},{8,24},{10,26},{12,28},{14,30},{16,0},... | collective-permute-start | bytes 196616 | tf_op jit(solution)/shard_map/ppermute | solution.py:45
  125.2 8.7 %collective-permute-start.10 = (bf16[2,64,256]{2,1,0:T(8,128)(2,1)S(1)}, bf16[2,64,256]{2,1,0:T(8,128)(2,1)S(1)}, u32[]{:S(2)}, u32[]{:S(2)}) collective-permute-start(bf16[2,64,256]{2,1,0:T(8,128)(2,1)S(1)} %fusion.21), channel_id=1, source_target_pairs={{0,16},{2,18},{4,20},{6,22},{8,24},{10,26},{12,28},{14,30},{16,0},... | collective-permute-start | bytes 196616 | tf_op jit(solution)/shard_map/ppermute | solution.py:45
  125.5 10.6 %collective-permute-start.14 = (bf16[2,64,256]{2,1,0:T(8,128)(2,1)S(1)}, bf16[2,64,256]{2,1,0:T(8,128)(2,1)S(1)}, u32[]{:S(2)}, u32[]{:S(2)}) collective-permute-start(bf16[2,64,256]{2,1,0:T(8,128)(2,1)S(1)} %fusion.22), channel_id=1, source_target_pairs={{0,16},{2,18},{4,20},{6,22},{8,24},{10,26},{12,28},{14,30},{16,0},... | collective-permute-start | bytes 196616 | tf_op jit(solution)/shard_map/ppermute | solution.py:45
  128.4 8.5 %collective-permute-start.18 = (bf16[2,64,256]{2,1,0:T(8,128)(2,1)S(1)}, bf16[2,64,256]{2,1,0:T(8,128)(2,1)S(1)}, u32[]{:S(2)}, u32[]{:S(2)}) collective-permute-start(bf16[2,64,256]{2,1,0:T(8,128)(2,1)S(1)} %fusion.23), channel_id=1, source_target_pairs={{0,16},{2,18},{4,20},{6,22},{8,24},{10,26},{12,28},{14,30},{16,0},... | collective-permute-start | bytes 196616 | tf_op jit(solution)/shard_map/ppermute | solution.py:45
Sparse Core Ops, SparseCore 0:
  11.1 54.7 all-gather.1

commit v11 on v9

--- a/solution.py
+++ b/solution.py
@@ -293,6 +293,8 @@
     attention, query_grad, own_dk, own_dv, back_k, back_v = band_attention(
         seq_scalar, queries, keys, values, grad_out, prev_k, prev_v, head_pairs, head_dim, score_scale
     )
+    back_k, back_v = passed_along((back_k, back_v), "seq", -1)
+    back_k, back_v, far_kv = lax.optimization_barrier((back_k, back_v, far_kv))
     chunks = 4 if head_pairs % 4 == 0 else (2 if head_pairs % 2 == 0 else 1)
     pairs = head_pairs // chunks
     outputs = (attention, query_grad, own_dk, own_dv)
@@ -314,7 +316,6 @@
         )
         digests.append(seq_reduce_scatter(far_dkv, 1, chunk))
     attention, query_grad, own_dk, own_dv = outputs
-    back_k, back_v = passed_along((back_k, back_v), "seq", -1)
     digest_dkv = jnp.concatenate(digests, 2) if chunks > 1 else digests[0]
     key_grad, value_grad = finalize(
         own_dk, own_dv, back_k, back_v, digest_dkv, select, head_pairs, head_dim

time: 147 us -> 153 us (1.041)
  starting transfers between devices: 34.2 us -> 40.4 us
  waiting for transfers between devices: 29.3 us -> 32.7 us
  local copies, waits for them, and re-layouts: 11.5 us -> 8.26 us
    ppermute x16, starting transfers between devices: 22.1 us -> 28.4 us  [seq_reduce_scatter(): lax.ppermute(send.astype(jnp.bfloat16), 'seq', [(source, source ^ 1 << bi...]
    ppermute x4, waiting for transfers between devices: 0.01 us -> 3.29 us  [passed_along(): lax.ppermute(value, axis, [(source, source + steps) for source in range(f...]
    unnamed x24 -> x12, local copies, waits for them, and re-layouts: 6.58 us -> 3.32 us
  transfers between devices with their start and end apart: 22 -> 22, of which waited for: 10 -> 12; matrix products, arithmetic and copies ran while one was open for 16% -> 15% of each run, Pallas kernels for 13% -> 13%
where the time goes in v11:
time: 153 us
  starting transfers between devices  40.4 us (26%)
  Pallas kernels  36.3 us (24%)
  waiting for transfers between devices  32.7 us (21%)
  between operations  14.4 us (9%)
  matrix products  12.8 us (8%)
  local copies, waits for them, and re-layouts  8.26 us (5%)
  other arithmetic  7.89 us (5%)
    ppermute x16, starting transfers between devices, seq_reduce_scatter(): lax.ppermute(send.astype(jnp.bfloat16), 'seq', [(source, source ^ 1 << bi...  28.4 us
    pallas_call x4, Pallas kernels, fixed_attention(): pl.pallas_call(functools.partial(fixed_kernel, scale=scale, unused=len(ea...  19.9 us
    ppermute x16, waiting for transfers between devices, seq_reduce_scatter(): lax.ppermute(send.astype(jnp.bfloat16), 'seq', [(source, source ^ 1 << bi...  16 us
    ppermute x1, waiting for transfers between devices, on_device(): lax.ppermute(cotangent, 'head', [(source, (source + shift) % head_count)...  13.4 us
    dot_general x1, matrix products, on_device(): lax.dot_general(gathered.reshape(seq_rows, cotangent.shape[1]), out_weigh...  12.1 us
    pallas_call x1, Pallas kernels, band_attention(): pl.pallas_call(functools.partial(band_kernel, scale=scale), grid_spec=gri...  9.58 us
    ppermute x4, starting transfers between devices, passed_along(): lax.ppermute(value, axis, [(source, source + steps) for source in range(f...  8.96 us
    pallas_call x1, Pallas kernels, finalize(): pl.pallas_call(finalize_kernel, grid=(head_pairs,), in_specs=[wide, wide,...  6.89 us
  transfers between devices with their start and end apart: 22, of which 12 were waited for; matrix products, arithmetic and copies ran while one was open for 15% of the time, Pallas kernels for 13%

profile of v11, /device:TPU:0, one launch (start us, length us, event | category | flops | bytes accessed | tf_op | source)
XLA Modules:
  0.0 152.8 jit_solution(15554519841497775299)
XLA Ops:
  7.2 1.6 %copy.30 = bf16[256,2048]{0,1:T(8,128)(2,1)S(1)} copy(bf16[256,2048]{1,0:T(8,128)(2,1)} %k_ref.9) | data formatting | bytes 2097152 | tf_op args[1]
  11.0 3.0 %collective-permute-start = (bf16[128,4096]{1,0:T(8,128)(2,1)}, bf16[128,4096]{1,0:T(8,128)(2,1)}, u32[]{:S(2)}, u32[]{:S(2)}) collective-permute-start(bf16[128,4096]{1,0:T(8,128)(2,1)} %param.10), channel_id=1, source_target_pairs={{0,1},{1,0},{2,3},{3,2},{4,5},{5,4},{6,7},{7,6},{8,9},{9,8},{10,11... | collective-permute-start | bytes 3145736 | tf_op jit(solution)/shard_map/ppermute | solution.py:279
  14.8 2.0 %copy.46 = bf16[256,1024]{1,0:T(8,128)(2,1)} copy(bf16[256,1024]{0,1:T(8,128)(2,1)} %bitcast.136) | data formatting | bytes 1048576 | tf_op jit(solution)/shard_map/reshape;squeeze | solution.py:246
  16.9 2.3 %collective-permute-start.1 = (bf16[256,1024]{1,0:T(8,128)(2,1)}, bf16[256,1024]{1,0:T(8,128)(2,1)}, u32[]{:S(2)}, u32[]{:S(2)}) collective-permute-start(bf16[256,1024]{1,0:T(8,128)(2,1)} %copy.46), channel_id=1, source_target_pairs={{0,2},{2,4},{4,6},{6,8},{8,10},{10,12},{12,14},{14,16},{16,18},{18... | collective-permute-start | bytes 1572872 | tf_op jit(solution)/shard_map/ppermute | solution.py:21
  20.2 3.9 %collective-permute-start.2 = (bf16[256,1024]{1,0:T(8,128)(2,1)}, bf16[256,1024]{1,0:T(8,128)(2,1)}, u32[]{:S(2)}, u32[]{:S(2)}) collective-permute-start(bf16[256,1024]{1,0:T(8,128)(2,1)} %copy.47), channel_id=1, source_target_pairs={{0,2},{2,4},{4,6},{6,8},{8,10},{10,12},{12,14},{14,16},{16,18},{18... | collective-permute-start | bytes 1572872 | tf_op jit(solution)/shard_map/ppermute | solution.py:21
  24.1 13.4 %collective-permute-done = bf16[128,4096]{1,0:T(8,128)(2,1)} collective-permute-done((bf16[128,4096]{1,0:T(8,128)(2,1)}, bf16[128,4096]{1,0:T(8,128)(2,1)}, u32[]{:S(2)}, u32[]{:S(2)}) %collective-permute-start) | collective-permute-done | bytes 1048608 | tf_op jit(solution)/shard_map/ppermute | solution.py:279
  37.5 4.7 %fusion.2 = bf16[2,128,4096]{2,1,0:T(8,128)(2,1)} fusion(s32[]{:T(128)S(6)} %select_n.65, bf16[1,128,4096]{2,1,0:T(8,128)(2,1)} %bitcast.1, bf16[1,128,4096]{2,1,0:T(8,128)(2,1)} %bitcast.138), kind=kLoop, calls=%fused_computation.7 | loop fusion | flops 3145728 | bytes 4194308 | tf_op jit(solution)/shard_map/stack | solution.py:284
  42.1 12.1 %convolution_convert_fusion.g_ref = bf16[256,2048]{1,0:T(8,128)(2,1)} fusion(bf16[256,4096]{1,0:T(8,128)(2,1)} %bitcast.135, bf16[2048,4096]{1,0:T(8,128)(2,1)} %param.9), kind=kOutput, calls=%fused_computation.4 | convolution fusion | flops 4295491584 | bytes 19922944 | tf_op jit(solution)/shard_map/dot_general | solution.py:286
  54.3 9.6 %shard_map.93 = (bf16[256,2048]{1,0:T(8,128)(2,1)}, bf16[256,2048]{1,0:T(8,128)(2,1)}, f32[256,2048]{1,0:T(8,128)}, f32[256,2048]{1,0:T(8,128)}, bf16[256,1024]{1,0:T(8,128)(2,1)}, /*index=5*/bf16[256,1024]{1,0:T(8,128)(2,1)}) custom-call(s32[1]{0:T(128)} %bitcast.seq_ref, bf16[256,2048]{1,0:T(8,128)(2,1)S(1)} %copy-done.2, bf16[256,2048]{1,0:T(8,128)(2,1)S(1)} %copy-done, ...), custom_call_target="tpu_custom_call" | custom-call | flops 1879048192 | bytes 7340032 | tf_op jit(solution)/shard_map/pallas_call | solution.py:154
  63.8 1.3 collective-permute-start.3
  65.1 1.5 collective-permute-start.4
  66.6 1.4 collective-permute-done.3.back_k_ref
  68.0 1.9 %collective-permute-done.4.back_v_ref = bf16[256,1024]{1,0:T(8,128)(2,1)} collective-permute-done((bf16[256,1024]{1,0:T(8,128)(2,1)}, bf16[256,1024]{1,0:T(8,128)(2,1)}, u32[]{:S(2)}, u32[]{:S(2)}) %collective-permute-start.4) | collective-permute-done | bytes 524320 | tf_op jit(solution)/shard_map/ppermute | solution.py:21
  71.1 4.9 %shard_map.94 = (bf16[256,2048]{1,0:T(8,128)(2,1)}, bf16[256,2048]{1,0:T(8,128)(2,1)}, f32[256,2048]{1,0:T(8,128)}, f32[256,2048]{1,0:T(8,128)}, bf16[2,1024,256]{2,1,0:T(8,128)(2,1)S(1)}) custom-call(s32[1]{0:T(128)} %bitcast.seq_ref, bf16[256,2048]{1,0:T(8,128)(2,1)S(1)} %copy-done.2, ...), custom_call_target="tpu_custom_call", output_to_operand_aliasing={{0}: (7, {}), {1}: (8, {}), {2}: (9, {}), {3}: (10, {})} | custom-call | flops 1174405120 | bytes 3014656 | tf_op jit(solution)/shard_map/pallas_call | solution.py:185
  76.1 5.0 %shard_map.95 = (bf16[256,2048]{1,0:T(8,128)(2,1)}, bf16[256,2048]{1,0:T(8,128)(2,1)}, f32[256,2048]{1,0:T(8,128)}, f32[256,2048]{1,0:T(8,128)}, bf16[2,1024,256]{2,1,0:T(8,128)(2,1)S(1)}) custom-call(s32[1]{0:T(128)} %bitcast.seq_ref, bf16[256,2048]{1,0:T(8,128)(2,1)S(1)} %copy-done.2, ...), custom_call_target="tpu_custom_call", output_to_operand_aliasing={{0}: (7, {}), {1}: (8, {}), {2}: (9, {}), {3}: (10, {})} | custom-call | flops 1174405120 | bytes 3014656 | tf_op jit(solution)/shard_map/pallas_call | solution.py:185
  81.3 10.5 %collective-permute-start.5 = (bf16[2,2,2,2,64,256]{5,4,0,1,2,3:T(8,128)(2,1)S(1)}, bf16[2,2,2,2,64,256]{5,4,0,1,2,3:T(8,128)(2,1)S(1)}, u32[]{:S(2)}, u32[]{:S(2)}) collective-permute-start(bf16[2,2,2,2,64,256]{5,4,0,1,2,3:T(8,128)(2,1)S(1)} %bitcast.140), channel_id=1, source_target_pairs={{0,2},{2,0},{4,6},{6,4},{8,10},{10,8},{12,14},{14,12},{16,18},{18,... | collective-permute-start | bytes 1572872 | tf_op jit(solution)/shard_map/ppermute | solution.py:45
  92.8 5.0 %shard_map.96 = (bf16[256,2048]{1,0:T(8,128)(2,1)}, bf16[256,2048]{1,0:T(8,128)(2,1)}, f32[256,2048]{1,0:T(8,128)}, f32[256,2048]{1,0:T(8,128)}, bf16[2,1024,256]{2,1,0:T(8,128)(2,1)S(1)}) custom-call(s32[1]{0:T(128)} %bitcast.seq_ref, bf16[256,2048]{1,0:T(8,128)(2,1)S(1)} %copy-done.2, ...), custom_call_target="tpu_custom_call", output_to_operand_aliasing={{0}: (7, {}), {1}: (8, {}), {2}: (9, {}), {3}: (10, {})} | custom-call | flops 1174405120 | bytes 3014656 | tf_op jit(solution)/shard_map/pallas_call | solution.py:185
  97.8 5.0 %shard_map.97 = (bf16[256,2048]{1,0:T(8,128)(2,1)}, bf16[256,2048]{1,0:T(8,128)(2,1)}, f32[256,2048]{1,0:T(8,128)}, f32[256,2048]{1,0:T(8,128)}, bf16[2,1024,256]{2,1,0:T(8,128)(2,1)S(1)}) custom-call(s32[1]{0:T(128)} %bitcast.seq_ref, bf16[256,2048]{1,0:T(8,128)(2,1)S(1)} %copy-done.2, ...), custom_call_target="tpu_custom_call", output_to_operand_aliasing={{0}: (7, {}), {1}: (8, {}), {2}: (9, {}), {3}: (10, {})} | custom-call | flops 1174405120 | bytes 3014656 | tf_op jit(solution)/shard_map/pallas_call | solution.py:185
  103.9 2.1 %collective-permute-start.6 = (bf16[2,2,2,64,256]{4,3,0,1,2:T(8,128)(2,1)S(1)}, bf16[2,2,2,64,256]{4,3,0,1,2:T(8,128)(2,1)S(1)}, u32[]{:S(2)}, u32[]{:S(2)}) collective-permute-start(bf16[2,2,2,64,256]{4,3,0,1,2:T(8,128)(2,1)S(1)} %fusion.6), channel_id=1, source_target_pairs={{0,4},{2,6},{4,0},{6,2},{8,12},{10,14},{12,8},{14,10},{16,20},{18,... | collective-permute-start | bytes 786440 | tf_op jit(solution)/shard_map/ppermute | solution.py:45
  106.2 1.6 %collective-permute-start.10 = (bf16[2,2,2,64,256]{4,3,0,1,2:T(8,128)(2,1)S(1)}, bf16[2,2,2,64,256]{4,3,0,1,2:T(8,128)(2,1)S(1)}, u32[]{:S(2)}, u32[]{:S(2)}) collective-permute-start(bf16[2,2,2,64,256]{4,3,0,1,2:T(8,128)(2,1)S(1)} %fusion.7), channel_id=1, source_target_pairs={{0,8},{2,10},{4,12},{6,14},{8,0},{10,2},{12,4},{14,6},{16,24},{18,... | collective-permute-start | bytes 786440 | tf_op jit(solution)/shard_map/ppermute | solution.py:45
  109.2 4.0 %collective-permute-done.6 = bf16[2,2,2,64,256]{4,3,0,1,2:T(8,128)(2,1)S(1)} collective-permute-done((bf16[2,2,2,64,256]{4,3,0,1,2:T(8,128)(2,1)S(1)}, bf16[2,2,2,64,256]{4,3,0,1,2:T(8,128)(2,1)S(1)}, u32[]{:S(2)}, u32[]{:S(2)}) %collective-permute-start.6) | collective-permute-done | bytes 262176 | tf_op jit(solution)/shard_map/ppermute | solution.py:45
  113.3 1.7 %collective-permute-start.7 = (bf16[2,2,64,256]{3,2,0,1:T(8,128)(2,1)S(1)}, bf16[2,2,64,256]{3,2,0,1:T(8,128)(2,1)S(1)}, u32[]{:S(2)}, u32[]{:S(2)}) collective-permute-start(bf16[2,2,64,256]{3,2,0,1:T(8,128)(2,1)S(1)} %fusion.12), channel_id=1, source_target_pairs={{0,8},{2,10},{4,12},{6,14},{8,0},{10,2},{12,4},{14,6},{16,24},{18,... | collective-permute-start | bytes 393224 | tf_op jit(solution)/shard_map/ppermute | solution.py:45
  115.5 1.5 collective-permute-start.11
  117.0 1.8 %collective-permute-done.14 = bf16[2,2,2,64,256]{4,3,0,1,2:T(8,128)(2,1)S(1)} collective-permute-done((bf16[2,2,2,64,256]{4,3,0,1,2:T(8,128)(2,1)S(1)}, bf16[2,2,2,64,256]{4,3,0,1,2:T(8,128)(2,1)S(1)}, u32[]{:S(2)}, u32[]{:S(2)}) %collective-permute-start.14) | collective-permute-done | bytes 262176 | tf_op jit(solution)/shard_map/ppermute | solution.py:45
  118.9 1.7 %collective-permute-start.15 = (bf16[2,2,64,256]{3,2,0,1:T(8,128)(2,1)S(1)}, bf16[2,2,64,256]{3,2,0,1:T(8,128)(2,1)S(1)}, u32[]{:S(2)}, u32[]{:S(2)}) collective-permute-start(bf16[2,2,64,256]{3,2,0,1:T(8,128)(2,1)S(1)} %fusion.14), channel_id=1, source_target_pairs={{0,8},{2,10},{4,12},{6,14},{8,0},{10,2},{12,4},{14,6},{16,24},{18,... | collective-permute-start | bytes 393224 | tf_op jit(solution)/shard_map/ppermute | solution.py:45
  121.1 1.5 collective-permute-start.19
  123.9 2.6 %collective-permute-start.8 = (bf16[2,64,256]{2,1,0:T(8,128)(2,1)S(1)}, bf16[2,64,256]{2,1,0:T(8,128)(2,1)S(1)}, u32[]{:S(2)}, u32[]{:S(2)}) collective-permute-start(bf16[2,64,256]{2,1,0:T(8,128)(2,1)S(1)} %fusion.20), channel_id=1, source_target_pairs={{0,16},{2,18},{4,20},{6,22},{8,24},{10,26},{12,28},{14,30},{16,0},... | collective-permute-start | bytes 196616 | tf_op jit(solution)/shard_map/ppermute | solution.py:45
  127.0 2.6 %collective-permute-start.16 = (bf16[2,64,256]{2,1,0:T(8,128)(2,1)S(1)}, bf16[2,64,256]{2,1,0:T(8,128)(2,1)S(1)}, u32[]{:S(2)}, u32[]{:S(2)}) collective-permute-start(bf16[2,64,256]{2,1,0:T(8,128)(2,1)S(1)} %fusion.22), channel_id=1, source_target_pairs={{0,16},{2,18},{4,20},{6,22},{8,24},{10,26},{12,28},{14,30},{16,0},... | collective-permute-start | bytes 196616 | tf_op jit(solution)/shard_map/ppermute | solution.py:45
  130.2 4.6 %collective-permute-done.8 = bf16[2,64,256]{2,1,0:T(8,128)(2,1)S(1)} collective-permute-done((bf16[2,64,256]{2,1,0:T(8,128)(2,1)S(1)}, bf16[2,64,256]{2,1,0:T(8,128)(2,1)S(1)}, u32[]{:S(2)}, u32[]{:S(2)}) %collective-permute-start.8) | collective-permute-done | bytes 65568 | tf_op jit(solution)/shard_map/ppermute | solution.py:45
  134.8 1.4 collective-permute-done.12
  136.2 1.4 collective-permute-done.16
  139.0 6.9 %shard_map.98 = (bf16[256,2048]{1,0:T(8,128)(2,1)}, bf16[256,2048]{1,0:T(8,128)(2,1)}) custom-call(f32[256,2048]{1,0:T(8,128)} %get-tuple-element.56.own_k_ref, f32[256,2048]{1,0:T(8,128)} %get-tuple-element.57.own_v_ref, bf16[256,1024]{1,0:T(8,128)(2,1)} %collective-permute-done.3.back_k_ref, bf16[256,1024]{1,0:T(8,128)(2,1)} %collective-permute-done.4.back_v_ref, ...), custom_call_target="tpu_custom_call" | custom-call | flops 67108864 | bytes 5242880 | tf_op jit(solution)/shard_map/pallas_call | solution.py:213
  (82 shorter events, 14.0 us)
Async XLA Ops:
  7.2 1.6 %copy-start.1 = (bf16[256,2048]{1,0:T(8,128)(2,1)S(1)}, bf16[256,2048]{1,0:T(8,128)(2,1)}, u32[]{:S(2)}) copy-start(bf16[256,2048]{1,0:T(8,128)(2,1)} %v_ref.9) | copy-start | bytes 3145732
  7.2 62.7 %all-gather.2.cloned.1.call-start = ((), (), s32[]{:S(2)}) async-start(), calls=%async_computation | async-start | bytes 4456448 | tf_op jit(solution)/shard_map/all_gather | solution.py:264
  7.2 2.1 %copy-start.4 = (s32[8,32]{1,0:T(8,128)S(1)}, s32[8,32]{1,0:T(8,128)}, u32[]{:S(2)}) copy-start(s32[8,32]{1,0:T(8,128)} %param.11) | copy-start | bytes 3076
  11.0 26.5 %collective-permute-start = (bf16[128,4096]{1,0:T(8,128)(2,1)}, bf16[128,4096]{1,0:T(8,128)(2,1)}, u32[]{:S(2)}, u32[]{:S(2)}) collective-permute-start(bf16[128,4096]{1,0:T(8,128)(2,1)} %param.10), channel_id=1, source_target_pairs={{0,1},{1,0},{2,3},{3,2},{4,5},{5,4},{6,7},{7,6},{8,9},{9,8},{10,11... | collective-permute-start | bytes 3145736 | tf_op jit(solution)/shard_map/ppermute | solution.py:279
  16.9 37.4 %collective-permute-start.1 = (bf16[256,1024]{1,0:T(8,128)(2,1)}, bf16[256,1024]{1,0:T(8,128)(2,1)}, u32[]{:S(2)}, u32[]{:S(2)}) collective-permute-start(bf16[256,1024]{1,0:T(8,128)(2,1)} %copy.46), channel_id=1, source_target_pairs={{0,2},{2,4},{4,6},{6,8},{8,10},{10,12},{12,14},{14,16},{16,18},{18... | collective-permute-start | bytes 1572872 | tf_op jit(solution)/shard_map/ppermute | solution.py:21
  20.2 34.1 %collective-permute-start.2 = (bf16[256,1024]{1,0:T(8,128)(2,1)}, bf16[256,1024]{1,0:T(8,128)(2,1)}, u32[]{:S(2)}, u32[]{:S(2)}) collective-permute-start(bf16[256,1024]{1,0:T(8,128)(2,1)} %copy.47), channel_id=1, source_target_pairs={{0,2},{2,4},{4,6},{6,8},{8,10},{10,12},{12,14},{14,16},{16,18},{18... | collective-permute-start | bytes 1572872 | tf_op jit(solution)/shard_map/ppermute | solution.py:21
  42.1 12.1 %copy-start = (bf16[256,2048]{1,0:T(8,128)(2,1)S(1)}, bf16[256,2048]{1,0:T(8,128)(2,1)}, u32[]{:S(2)}) copy-start(bf16[256,2048]{1,0:T(8,128)(2,1)} %k_ref.9) | copy-start | bytes 3145732
  42.1 12.1 %copy-start.2 = (bf16[256,2048]{1,0:T(8,128)(2,1)S(1)}, bf16[256,2048]{1,0:T(8,128)(2,1)}, u32[]{:S(2)}) copy-start(bf16[256,2048]{1,0:T(8,128)(2,1)} %q_ref.9) | copy-start | bytes 3145732
  63.8 4.1 %collective-permute-start.3 = (bf16[256,1024]{1,0:T(8,128)(2,1)}, bf16[256,1024]{1,0:T(8,128)(2,1)}, u32[]{:S(2)}, u32[]{:S(2)}) collective-permute-start(bf16[256,1024]{1,0:T(8,128)(2,1)} %get-tuple-element.35), channel_id=1, source_target_pairs={{2,0},{4,2},{6,4},{8,6},{10,8},{12,10},{14,12},{16,14},{18,16},{20... | collective-permute-start | bytes 1572872 | tf_op jit(solution)/shard_map/ppermute | solution.py:21
  65.1 4.8 %collective-permute-start.4 = (bf16[256,1024]{1,0:T(8,128)(2,1)}, bf16[256,1024]{1,0:T(8,128)(2,1)}, u32[]{:S(2)}, u32[]{:S(2)}) collective-permute-start(bf16[256,1024]{1,0:T(8,128)(2,1)} %get-tuple-element.36), channel_id=1, source_target_pairs={{2,0},{4,2},{6,4},{8,6},{10,8},{12,10},{14,12},{16,14},{18,16},{20... | collective-permute-start | bytes 1572872 | tf_op jit(solution)/shard_map/ppermute | solution.py:21
  69.9 1.2 copy-start.3
  81.3 22.4 %collective-permute-start.5 = (bf16[2,2,2,2,64,256]{5,4,0,1,2,3:T(8,128)(2,1)S(1)}, bf16[2,2,2,2,64,256]{5,4,0,1,2,3:T(8,128)(2,1)S(1)}, u32[]{:S(2)}, u32[]{:S(2)}) collective-permute-start(bf16[2,2,2,2,64,256]{5,4,0,1,2,3:T(8,128)(2,1)S(1)} %bitcast.140), channel_id=1, source_target_pairs={{0,2},{2,0},{4,6},{6,4},{8,10},{10,8},{12,14},{14,12},{16,18},{18,... | collective-permute-start | bytes 1572872 | tf_op jit(solution)/shard_map/ppermute | solution.py:45
  92.8 13.2 %collective-permute-start.9 = (bf16[2,2,2,2,64,256]{5,4,0,1,3,2:T(8,128)(2,1)S(1)}, bf16[2,2,2,2,64,256]{5,4,0,1,3,2:T(8,128)(2,1)S(1)}, u32[]{:S(2)}, u32[]{:S(2)}) collective-permute-start(bf16[2,2,2,2,64,256]{5,4,0,1,3,2:T(8,128)(2,1)S(1)} %bitcast.139), channel_id=1, source_target_pairs={{0,2},{2,0},{4,6},{6,4},{8,10},{10,8},{12,14},{14,12},{16,18},{18,... | collective-permute-start | bytes 1572872 | tf_op jit(solution)/shard_map/ppermute | solution.py:45
  103.1 4.8 %collective-permute-start.13 = (bf16[2,2,2,2,64,256]{5,4,0,1,2,3:T(8,128)(2,1)S(1)}, bf16[2,2,2,2,64,256]{5,4,0,1,2,3:T(8,128)(2,1)S(1)}, u32[]{:S(2)}, u32[]{:S(2)}) collective-permute-start(bf16[2,2,2,2,64,256]{5,4,0,1,2,3:T(8,128)(2,1)S(1)} %bitcast.142), channel_id=1, source_target_pairs={{0,2},{2,0},{4,6},{6,4},{8,10},{10,8},{12,14},{14,12},{16,18},{18,... | collective-permute-start | bytes 1572872 | tf_op jit(solution)/shard_map/ppermute | solution.py:45
  103.6 4.5 %collective-permute-start.17 = (bf16[2,2,2,2,64,256]{5,4,0,1,3,2:T(8,128)(2,1)S(1)}, bf16[2,2,2,2,64,256]{5,4,0,1,3,2:T(8,128)(2,1)S(1)}, u32[]{:S(2)}, u32[]{:S(2)}) collective-permute-start(bf16[2,2,2,2,64,256]{5,4,0,1,3,2:T(8,128)(2,1)S(1)} %bitcast.141), channel_id=1, source_target_pairs={{0,2},{2,0},{4,6},{6,4},{8,10},{10,8},{12,14},{14,12},{16,18},{18,... | collective-permute-start | bytes 1572872 | tf_op jit(solution)/shard_map/ppermute | solution.py:45
  103.9 9.2 %collective-permute-start.6 = (bf16[2,2,2,64,256]{4,3,0,1,2:T(8,128)(2,1)S(1)}, bf16[2,2,2,64,256]{4,3,0,1,2:T(8,128)(2,1)S(1)}, u32[]{:S(2)}, u32[]{:S(2)}) collective-permute-start(bf16[2,2,2,64,256]{4,3,0,1,2:T(8,128)(2,1)S(1)} %fusion.6), channel_id=1, source_target_pairs={{0,4},{2,6},{4,0},{6,2},{8,12},{10,14},{12,8},{14,10},{16,20},{18,... | collective-permute-start | bytes 786440 | tf_op jit(solution)/shard_map/ppermute | solution.py:45
  106.2 9.2 %collective-permute-start.10 = (bf16[2,2,2,64,256]{4,3,0,1,2:T(8,128)(2,1)S(1)}, bf16[2,2,2,64,256]{4,3,0,1,2:T(8,128)(2,1)S(1)}, u32[]{:S(2)}, u32[]{:S(2)}) collective-permute-start(bf16[2,2,2,64,256]{4,3,0,1,2:T(8,128)(2,1)S(1)} %fusion.7), channel_id=1, source_target_pairs={{0,8},{2,10},{4,12},{6,14},{8,0},{10,2},{12,4},{14,6},{16,24},{18,... | collective-permute-start | bytes 786440 | tf_op jit(solution)/shard_map/ppermute | solution.py:45
  108.0 10.8 %collective-permute-start.14 = (bf16[2,2,2,64,256]{4,3,0,1,2:T(8,128)(2,1)S(1)}, bf16[2,2,2,64,256]{4,3,0,1,2:T(8,128)(2,1)S(1)}, u32[]{:S(2)}, u32[]{:S(2)}) collective-permute-start(bf16[2,2,2,64,256]{4,3,0,1,2:T(8,128)(2,1)S(1)} %fusion.8), channel_id=1, source_target_pairs={{0,4},{2,6},{4,0},{6,2},{8,12},{10,14},{12,8},{14,10},{16,20},{18,... | collective-permute-start | bytes 786440 | tf_op jit(solution)/shard_map/ppermute | solution.py:45
  108.3 12.7 %collective-permute-start.18 = (bf16[2,2,2,64,256]{4,3,0,1,2:T(8,128)(2,1)S(1)}, bf16[2,2,2,64,256]{4,3,0,1,2:T(8,128)(2,1)S(1)}, u32[]{:S(2)}, u32[]{:S(2)}) collective-permute-start(bf16[2,2,2,64,256]{4,3,0,1,2:T(8,128)(2,1)S(1)} %fusion.9), channel_id=1, source_target_pairs={{0,8},{2,10},{4,12},{6,14},{8,0},{10,2},{12,4},{14,6},{16,24},{18,... | collective-permute-start | bytes 786440 | tf_op jit(solution)/shard_map/ppermute | solution.py:45
  113.3 10.5 %collective-permute-start.7 = (bf16[2,2,64,256]{3,2,0,1:T(8,128)(2,1)S(1)}, bf16[2,2,64,256]{3,2,0,1:T(8,128)(2,1)S(1)}, u32[]{:S(2)}, u32[]{:S(2)}) collective-permute-start(bf16[2,2,64,256]{3,2,0,1:T(8,128)(2,1)S(1)} %fusion.12), channel_id=1, source_target_pairs={{0,8},{2,10},{4,12},{6,14},{8,0},{10,2},{12,4},{14,6},{16,24},{18,... | collective-permute-start | bytes 393224 | tf_op jit(solution)/shard_map/ppermute | solution.py:45
  115.5 11.0 %collective-permute-start.11 = (bf16[2,2,64,256]{3,2,0,1:T(8,128)(2,1)S(1)}, bf16[2,2,64,256]{3,2,0,1:T(8,128)(2,1)S(1)}, u32[]{:S(2)}, u32[]{:S(2)}) collective-permute-start(bf16[2,2,64,256]{3,2,0,1:T(8,128)(2,1)S(1)} %fusion.13), channel_id=1, source_target_pairs={{0,4},{2,6},{4,0},{6,2},{8,12},{10,14},{12,8},{14,10},{16,20},{18,... | collective-permute-start | bytes 393224 | tf_op jit(solution)/shard_map/ppermute | solution.py:45
  118.9 8.1 %collective-permute-start.15 = (bf16[2,2,64,256]{3,2,0,1:T(8,128)(2,1)S(1)}, bf16[2,2,64,256]{3,2,0,1:T(8,128)(2,1)S(1)}, u32[]{:S(2)}, u32[]{:S(2)}) collective-permute-start(bf16[2,2,64,256]{3,2,0,1:T(8,128)(2,1)S(1)} %fusion.14), channel_id=1, source_target_pairs={{0,8},{2,10},{4,12},{6,14},{8,0},{10,2},{12,4},{14,6},{16,24},{18,... | collective-permute-start | bytes 393224 | tf_op jit(solution)/shard_map/ppermute | solution.py:45
  121.1 8.6 %collective-permute-start.19 = (bf16[2,2,64,256]{3,2,0,1:T(8,128)(2,1)S(1)}, bf16[2,2,64,256]{3,2,0,1:T(8,128)(2,1)S(1)}, u32[]{:S(2)}, u32[]{:S(2)}) collective-permute-start(bf16[2,2,64,256]{3,2,0,1:T(8,128)(2,1)S(1)} %fusion.15), channel_id=1, source_target_pairs={{0,4},{2,6},{4,0},{6,2},{8,12},{10,14},{12,8},{14,10},{16,20},{18,... | collective-permute-start | bytes 393224 | tf_op jit(solution)/shard_map/ppermute | solution.py:45
  123.9 10.9 %collective-permute-start.8 = (bf16[2,64,256]{2,1,0:T(8,128)(2,1)S(1)}, bf16[2,64,256]{2,1,0:T(8,128)(2,1)S(1)}, u32[]{:S(2)}, u32[]{:S(2)}) collective-permute-start(bf16[2,64,256]{2,1,0:T(8,128)(2,1)S(1)} %fusion.20), channel_id=1, source_target_pairs={{0,16},{2,18},{4,20},{6,22},{8,24},{10,26},{12,28},{14,30},{16,0},... | collective-permute-start | bytes 196616 | tf_op jit(solution)/shard_map/ppermute | solution.py:45
  126.6 9.6 %collective-permute-start.12 = (bf16[2,64,256]{2,1,0:T(8,128)(2,1)S(1)}, bf16[2,64,256]{2,1,0:T(8,128)(2,1)S(1)}, u32[]{:S(2)}, u32[]{:S(2)}) collective-permute-start(bf16[2,64,256]{2,1,0:T(8,128)(2,1)S(1)} %fusion.21), channel_id=1, source_target_pairs={{0,16},{2,18},{4,20},{6,22},{8,24},{10,26},{12,28},{14,30},{16,0},... | collective-permute-start | bytes 196616 | tf_op jit(solution)/shard_map/ppermute | solution.py:45
  127.0 10.5 %collective-permute-start.16 = (bf16[2,64,256]{2,1,0:T(8,128)(2,1)S(1)}, bf16[2,64,256]{2,1,0:T(8,128)(2,1)S(1)}, u32[]{:S(2)}, u32[]{:S(2)}) collective-permute-start(bf16[2,64,256]{2,1,0:T(8,128)(2,1)S(1)} %fusion.22), channel_id=1, source_target_pairs={{0,16},{2,18},{4,20},{6,22},{8,24},{10,26},{12,28},{14,30},{16,0},... | collective-permute-start | bytes 196616 | tf_op jit(solution)/shard_map/ppermute | solution.py:45
  129.8 8.5 %collective-permute-start.20 = (bf16[2,64,256]{2,1,0:T(8,128)(2,1)S(1)}, bf16[2,64,256]{2,1,0:T(8,128)(2,1)S(1)}, u32[]{:S(2)}, u32[]{:S(2)}) collective-permute-start(bf16[2,64,256]{2,1,0:T(8,128)(2,1)S(1)} %fusion.23), channel_id=1, source_target_pairs={{0,16},{2,18},{4,20},{6,22},{8,24},{10,26},{12,28},{14,30},{16,0},... | collective-permute-start | bytes 196616 | tf_op jit(solution)/shard_map/ppermute | solution.py:45
Sparse Core Ops, SparseCore 0:
  11.1 54.7 all-gather.1

commit v12 on v8

--- a/solution.py
+++ b/solution.py
@@ -46,12 +46,6 @@
     return held.astype(jnp.bfloat16)
 
 
-def rotated_order(bits, rotate):
-    if bits > 2:
-        return [0] + sorted(range(1, bits - 1), key=lambda b: (b - 1 - rotate) % (bits - 2)) + [bits - 1]
-    return list(range(bits))
-
-
 def seq_all_gather(local, rotate):
     count = lax.axis_size("seq")
     if count & (count - 1):
@@ -66,10 +60,15 @@
         pair = jnp.stack([held, arrived], step)
         swapped = jnp.stack([arrived, held], step)
         held = jnp.where(mine == 0, pair, swapped)
-    placed = sorted(range(bits), key=lambda b: order.index(b))
-    axes = [placed.index(b) for b in range(bits - 1, -1, -1)]
+    axes = [order.index(b) for b in range(bits - 1, -1, -1)]
     held = held.transpose(axes + list(range(bits, held.ndim)))
     return held.reshape((count * local.shape[0],) + local.shape[1:])
+
+
+def rotated_order(bits, rotate):
+    if bits > 2:
+        return [0] + sorted(range(1, bits - 1), key=lambda b: (b - 1 - rotate) % (bits - 2)) + [bits - 1]
+    return list(range(bits))
 
 
 def nt(left, right):
@@ -94,10 +93,10 @@
     row_sum = w_a.sum(-1, keepdims=True) + w_b.sum(-1, keepdims=True)
     mixed = nn(w_a.astype(jnp.bfloat16), v_a) + nn(w_b.astype(jnp.bfloat16), v_b)
     out = (mixed / row_sum).astype(jnp.bfloat16)
-    log_total = row_max + jnp.log(row_sum)
     delta = jnp.sum(g.astype(jnp.float32) * out.astype(jnp.float32), -1, keepdims=True)
-    p_a = jnp.exp(s_a - log_total)
-    p_b = jnp.exp(s_b - log_total)
+    inverse = 1.0 / row_sum
+    p_a = w_a * inverse
+    p_b = w_b * inverse
     gs_a = (p_a * (nt(g, v_a) - delta)).astype(jnp.bfloat16)
     gs_b = (p_b * (nt(g, v_b) - delta)).astype(jnp.bfloat16)
     dq = ((nn(gs_a, k_a) + nn(gs_b, k_b)) * scale).astype(jnp.bfloat16)
@@ -151,8 +150,8 @@
     dq_ref[...] = dq
     dk_ref[...] = dko
     dv_ref[...] = dvo
-    dkvf_ref[0] = dkf
-    dkvf_ref[1] = dvf
+    dkvf_ref[0] = dkf.astype(dkvf_ref.dtype)
+    dkvf_ref[1] = dvf.astype(dkvf_ref.dtype)
 
 
 def attention_cost(rows, keys, head_dim, heads):
@@ -210,7 +209,7 @@
         functools.partial(fixed_kernel, scale=scale, unused=len(earlier)),
         grid_spec=grid_spec,
         out_shape=[jax.ShapeDtypeStruct(array.shape, array.dtype) for array in earlier]
-        + [jax.ShapeDtypeStruct((2, far_rows, pairs * head_dim), jnp.float32)],
+        + [jax.ShapeDtypeStruct((2, far_rows, pairs * head_dim), jnp.bfloat16)],
         input_output_aliases=aliases,
         compiler_params=pltpu.CompilerParams(vmem_limit_bytes=48 * 1024 * 1024),
         cost_estimate=attention_cost(rows, rows + far_rows, head_dim, pairs),
@@ -288,10 +287,13 @@
     gather_pairs = head_pairs // gathers
     split_dk = digest_k.reshape(digest_count, gathers, gather_pairs * head_dim)
     split_dv = digest_v.reshape(digest_count, gathers, gather_pairs * head_dim)
-    far_parts = [
-        seq_all_gather(jnp.concatenate([split_dk[:, part], split_dv[:, part]], 1), part)
-        for part in range(gathers)
-    ]
+    far_parts = []
+    for part in range(gathers):
+        joined = jnp.concatenate([split_dk[:, part], split_dv[:, part]], 1)
+        if part == 0:
+            far_parts.append(lax.all_gather(joined, "seq", axis=0, tiled=True))
+        else:
+            far_parts.append(seq_all_gather(joined, 0))
     head_count = lax.axis_size("head")
     head_index = lax.axis_index("head")
     pieces = [cotangent] + [

time: 172 us -> 175 us (1.017)
  between operations: 1.2 us -> 14.6 us
  local copies, waits for them, and re-layouts: 20.8 us -> 12 us
  other arithmetic: 17.2 us -> 14.1 us
  waiting for transfers between devices: 35.2 us -> 37.6 us
  Pallas kernels: 38.4 us -> 36.2 us
    ppermute x16, starting transfers between devices: 18.7 us -> 26.4 us  [seq_reduce_scatter(): lax.ppermute(send.astype(jnp.bfloat16), 'seq', [(source, source ^ 1 << bi...]
    ppermute x8 -> x4, waiting for transfers between devices: 16.8 us -> 23.4 us  [seq_all_gather(): lax.ppermute(held, 'seq', [(source, source ^ 1 << bit) for source in rang...]
    ppermute x8 -> x4, starting transfers between devices: 16.7 us -> 10.5 us  [seq_all_gather(): lax.ppermute(held, 'seq', [(source, source ^ 1 << bit) for source in rang...]
    convert_element_type x16 -> x12, local copies, waits for them, and re-layouts: 5.6 us -> 0.31 us  [seq_reduce_scatter(): send.astype(jnp.bfloat16)]
    ppermute x16, waiting for transfers between devices: 18.5 us -> 14.1 us  [seq_reduce_scatter(): lax.ppermute(send.astype(jnp.bfloat16), 'seq', [(source, source ^ 1 << bi...]
    pallas_call x4, Pallas kernels: 21.7 us -> 19.7 us  [fixed_attention(): pl.pallas_call(functools.partial(fixed_kernel, scale=scale, unused=len(ea...]
    transpose x1 -> x0, other arithmetic: 1.86 us -> none  [seq_all_gather(): held = held.transpose(axes + list(range(bits, held.ndim)))]
    unnamed x29 -> x18, local copies, waits for them, and re-layouts: 4.28 us -> 3.33 us
  transfers between devices with their start and end apart: 29 -> 26, of which waited for: 15 -> 10; matrix products, arithmetic and copies ran while one was open for 24% -> 18% of each run, Pallas kernels for 18% -> 17%
where the time goes in v12:
time: 175 us
  starting transfers between devices  47.6 us (27%)
  waiting for transfers between devices  37.6 us (21%)
  Pallas kernels  36.2 us (21%)
  between operations  14.6 us (8%)
  other arithmetic  14.1 us (8%)
  matrix products  12.7 us (7%)
  local copies, waits for them, and re-layouts  12 us (7%)
    ppermute x16, starting transfers between devices, seq_reduce_scatter(): lax.ppermute(send.astype(jnp.bfloat16), 'seq', [(source, source ^ 1 << bi...  26.4 us
    ppermute x4, waiting for transfers between devices, seq_all_gather(): lax.ppermute(held, 'seq', [(source, source ^ 1 << bit) for source in rang...  23.4 us
    pallas_call x4, Pallas kernels, fixed_attention(): pl.pallas_call(functools.partial(fixed_kernel, scale=scale, unused=len(ea...  19.7 us
    ppermute x16, waiting for transfers between devices, seq_reduce_scatter(): lax.ppermute(send.astype(jnp.bfloat16), 'seq', [(source, source ^ 1 << bi...  14.1 us
    dot_general x1, matrix products, on_device(): lax.dot_general(gathered.reshape(seq_rows, cotangent.shape[1]), out_weigh...  12 us
    ppermute x4, starting transfers between devices, seq_all_gather(): lax.ppermute(held, 'seq', [(source, source ^ 1 << bit) for source in rang...  10.5 us
    pallas_call x1, Pallas kernels, band_attention(): pl.pallas_call(functools.partial(band_kernel, scale=scale), grid_spec=gri...  9.67 us
    ppermute x4, starting transfers between devices, passed_along(): lax.ppermute(value, axis, [(source, source + steps) for source in range(f...  9.15 us
  transfers between devices with their start and end apart: 26, of which 10 were waited for; matrix products, arithmetic and copies ran while one was open for 18% of the time, Pallas kernels for 17%

profile of v12, /device:TPU:0, one launch (start us, length us, event | category | flops | bytes accessed | tf_op | source)
XLA Modules:
  0.0 174.7 jit_solution(1467648172924559052)
XLA Ops:
  7.2 1.6 copy.49
  13.8 4.0 %collective-permute-start.1 = (bf16[64,1024]{1,0:T(8,128)(2,1)S(1)}, bf16[64,1024]{1,0:T(8,128)(2,1)S(1)}, u32[]{:S(2)}, u32[]{:S(2)}) collective-permute-start(bf16[64,1024]{1,0:T(8,128)(2,1)S(1)} %get-tuple-element.74), channel_id=1, source_target_pairs={{0,16},{2,18},{4,20},{6,22},{8,24},{10,26},{12,28},{14,30},{16,0},... | collective-permute-start | bytes 393224 | tf_op jit(solution)/shard_map/ppermute | solution.py:59
  17.9 6.3 %collective-permute-done.1 = bf16[64,1024]{1,0:T(8,128)(2,1)S(1)} collective-permute-done((bf16[64,1024]{1,0:T(8,128)(2,1)S(1)}, bf16[64,1024]{1,0:T(8,128)(2,1)S(1)}, u32[]{:S(2)}, u32[]{:S(2)}) %collective-permute-start.1) | collective-permute-done | bytes 131104 | tf_op jit(solution)/shard_map/ppermute | solution.py:59
  28.0 2.0 %copy.69 = bf16[256,1024]{1,0:T(8,128)(2,1)} copy(bf16[256,1024]{0,1:T(8,128)(2,1)} %bitcast.161) | data formatting | bytes 1048576 | tf_op jit(solution)/shard_map/reshape;squeeze | solution.py:269
  30.0 2.3 %collective-permute-start.5 = (bf16[256,1024]{1,0:T(8,128)(2,1)}, bf16[256,1024]{1,0:T(8,128)(2,1)}, u32[]{:S(2)}, u32[]{:S(2)}) collective-permute-start(bf16[256,1024]{1,0:T(8,128)(2,1)} %copy.69), channel_id=1, source_target_pairs={{0,2},{2,4},{4,6},{6,8},{8,10},{10,12},{12,14},{14,16},{16,18},{18... | collective-permute-start | bytes 1572872 | tf_op jit(solution)/shard_map/ppermute | solution.py:21
  33.4 4.1 %collective-permute-start.6 = (bf16[256,1024]{1,0:T(8,128)(2,1)}, bf16[256,1024]{1,0:T(8,128)(2,1)}, u32[]{:S(2)}, u32[]{:S(2)}) collective-permute-start(bf16[256,1024]{1,0:T(8,128)(2,1)} %copy.70), channel_id=1, source_target_pairs={{0,2},{2,4},{4,6},{6,8},{8,10},{10,12},{12,14},{14,16},{16,18},{18... | collective-permute-start | bytes 1572872 | tf_op jit(solution)/shard_map/ppermute | solution.py:21
  40.2 17.1 %collective-permute-done.3 = bf16[2,2,64,1024]{3,2,0,1:T(8,128)(2,1)S(1)} collective-permute-done((bf16[2,2,64,1024]{3,2,0,1:T(8,128)(2,1)S(1)}, bf16[2,2,64,1024]{3,2,0,1:T(8,128)(2,1)S(1)}, u32[]{:S(2)}, u32[]{:S(2)}) %collective-permute-start.3) | collective-permute-done | bytes 524320 | tf_op jit(solution)/shard_map/ppermute | solution.py:59
  58.4 5.2 %collective-permute-start.4 = (bf16[2,2,2,64,1024]{4,3,0,1,2:T(8,128)(2,1)}, bf16[2,2,2,64,1024]{4,3,0,1,2:T(8,128)(2,1)}, u32[]{:S(2)}, u32[]{:S(2)}) collective-permute-start(bf16[2,2,2,64,1024]{4,3,0,1,2:T(8,128)(2,1)} %maximum_select_fusion.2), channel_id=1, source_target_pairs={{0,2},{2,0},{4,6},{6,4},{8,10},{10,8},{12,14},{14,12},{16,18},{18,... | collective-permute-start | bytes 3145736 | tf_op jit(solution)/shard_map/ppermute | solution.py:59
  64.7 4.1 %fusion.2 = bf16[2,128,4096]{2,1,0:T(8,128)(2,1)} fusion(s32[]{:T(128)S(6)} %select_n.152, bf16[1,128,4096]{2,1,0:T(8,128)(2,1)} %bitcast.1, bf16[1,128,4096]{2,1,0:T(8,128)(2,1)S(1)} %bitcast.166), kind=kLoop, calls=%fused_computation.7 | loop fusion | flops 3145728 | bytes 4194308 | tf_op jit(solution)/shard_map/stack | solution.py:305
  68.8 12.0 %convolution_convert_fusion.g_ref = bf16[256,2048]{1,0:T(8,128)(2,1)} fusion(bf16[256,4096]{1,0:T(8,128)(2,1)} %bitcast.160, bf16[2048,4096]{1,0:T(8,128)(2,1)} %param.9), kind=kOutput, calls=%fused_computation.4 | convolution fusion | flops 4295491584 | bytes 19922944 | tf_op jit(solution)/shard_map/dot_general | solution.py:307
  80.9 9.7 %shard_map.93 = (bf16[256,2048]{1,0:T(8,128)(2,1)}, bf16[256,2048]{1,0:T(8,128)(2,1)}, f32[256,2048]{1,0:T(8,128)}, f32[256,2048]{1,0:T(8,128)}, bf16[256,1024]{1,0:T(8,128)(2,1)}, /*index=5*/bf16[256,1024]{1,0:T(8,128)(2,1)}) custom-call(s32[1]{0:T(128)} %bitcast.seq_ref, bf16[256,2048]{1,0:T(8,128)(2,1)S(1)} %copy-done.2, bf16[256,2048]{1,0:T(8,128)(2,1)S(1)} %copy-done, ...), custom_call_target="tpu_custom_call" | custom-call | flops 1879048192 | bytes 7340032 | tf_op jit(solution)/shard_map/pallas_call | solution.py:176
  93.3 1.9 %maximum_select_fusion = bf16[2,2,2,2,64,1024]{5,4,0,1,2,3:T(8,128)(2,1)S(1)} fusion(bf16[2,2,2,1,64,1024]{5,4,0,1,2,3:T(8,128)(2,1)} %bitcast.23, bf16[2,2,2,1,64,1024]{5,4,0,1,2,3:T(8,128)(2,1)S(1)} %copy-done.4, pred[]{:T(512)S(6)} %eq.25), kind=kLoop, calls=%fused_computation.8 | loop fusion | flops 3145728 | bytes 4194305 | tf_op jit(solution)/shard_map/jit(_where)/select_n | solution.py:62
  95.2 1.5 copy.56
  98.0 4.9 %shard_map.94 = (bf16[256,2048]{1,0:T(8,128)(2,1)}, bf16[256,2048]{1,0:T(8,128)(2,1)}, f32[256,2048]{1,0:T(8,128)}, f32[256,2048]{1,0:T(8,128)}, bf16[2,1024,256]{2,1,0:T(8,128)(2,1)S(1)}) custom-call(s32[1]{0:T(128)} %bitcast.seq_ref, bf16[256,2048]{1,0:T(8,128)(2,1)S(1)} %copy-done.2, ...), custom_call_target="tpu_custom_call", output_to_operand_aliasing={{0}: (7, {}), {1}: (8, {}), {2}: (9, {}), {3}: (10, {})} | custom-call | flops 1174405120 | bytes 3014656 | tf_op jit(solution)/shard_map/pallas_call | solution.py:208
  103.1 1.8 %collective-permute-start.9 = (bf16[2,2,2,2,64,256]{5,4,0,1,2,3:T(8,128)(2,1)S(1)}, bf16[2,2,2,2,64,256]{5,4,0,1,2,3:T(8,128)(2,1)S(1)}, u32[]{:S(2)}, u32[]{:S(2)}) collective-permute-start(bf16[2,2,2,2,64,256]{5,4,0,1,2,3:T(8,128)(2,1)S(1)} %bitcast.167), channel_id=1, source_target_pairs={{0,2},{2,0},{4,6},{6,4},{8,10},{10,8},{12,14},{14,12},{16,18},{18,... | collective-permute-start | bytes 1572872 | tf_op jit(solution)/shard_map/ppermute | solution.py:42
  104.9 4.9 %shard_map.95 = (bf16[256,2048]{1,0:T(8,128)(2,1)}, bf16[256,2048]{1,0:T(8,128)(2,1)}, f32[256,2048]{1,0:T(8,128)}, f32[256,2048]{1,0:T(8,128)}, bf16[2,1024,256]{2,1,0:T(8,128)(2,1)S(1)}) custom-call(s32[1]{0:T(128)} %bitcast.seq_ref, bf16[256,2048]{1,0:T(8,128)(2,1)S(1)} %copy-done.2, ...), custom_call_target="tpu_custom_call", output_to_operand_aliasing={{0}: (7, {}), {1}: (8, {}), {2}: (9, {}), {3}: (10, {})} | custom-call | flops 1174405120 | bytes 3014656 | tf_op jit(solution)/shard_map/pallas_call | solution.py:208
  110.1 4.9 %shard_map.96 = (bf16[256,2048]{1,0:T(8,128)(2,1)}, bf16[256,2048]{1,0:T(8,128)(2,1)}, f32[256,2048]{1,0:T(8,128)}, f32[256,2048]{1,0:T(8,128)}, bf16[2,1024,256]{2,1,0:T(8,128)(2,1)S(1)}) custom-call(s32[1]{0:T(128)} %bitcast.seq_ref, bf16[256,2048]{1,0:T(8,128)(2,1)S(1)} %copy-done.2, ...), custom_call_target="tpu_custom_call", output_to_operand_aliasing={{0}: (7, {}), {1}: (8, {}), {2}: (9, {}), {3}: (10, {})} | custom-call | flops 1174405120 | bytes 3014656 | tf_op jit(solution)/shard_map/pallas_call | solution.py:208
  115.7 4.9 %shard_map.97 = (bf16[256,2048]{1,0:T(8,128)(2,1)}, bf16[256,2048]{1,0:T(8,128)(2,1)}, f32[256,2048]{1,0:T(8,128)}, f32[256,2048]{1,0:T(8,128)}, bf16[2,1024,256]{2,1,0:T(8,128)(2,1)S(1)}) custom-call(s32[1]{0:T(128)} %bitcast.seq_ref, bf16[256,2048]{1,0:T(8,128)(2,1)S(1)} %copy-done.2, ...), custom_call_target="tpu_custom_call", output_to_operand_aliasing={{0}: (7, {}), {1}: (8, {}), {2}: (9, {}), {3}: (10, {})} | custom-call | flops 1174405120 | bytes 3014656 | tf_op jit(solution)/shard_map/pallas_call | solution.py:208
  121.1 2.2 %collective-permute-start.10 = (bf16[2,2,2,64,256]{4,3,0,1,2:T(8,128)(2,1)S(1)}, bf16[2,2,2,64,256]{4,3,0,1,2:T(8,128)(2,1)S(1)}, u32[]{:S(2)}, u32[]{:S(2)}) collective-permute-start(bf16[2,2,2,64,256]{4,3,0,1,2:T(8,128)(2,1)S(1)} %fusion.6), channel_id=1, source_target_pairs={{0,4},{2,6},{4,0},{6,2},{8,12},{10,14},{12,8},{14,10},{16,20},{18,... | collective-permute-start | bytes 786440 | tf_op jit(solution)/shard_map/ppermute | solution.py:42
  123.5 3.6 %collective-permute-start.14 = (bf16[2,2,2,64,256]{4,3,0,1,2:T(8,128)(2,1)S(1)}, bf16[2,2,2,64,256]{4,3,0,1,2:T(8,128)(2,1)S(1)}, u32[]{:S(2)}, u32[]{:S(2)}) collective-permute-start(bf16[2,2,2,64,256]{4,3,0,1,2:T(8,128)(2,1)S(1)} %fusion.7), channel_id=1, source_target_pairs={{0,8},{2,10},{4,12},{6,14},{8,0},{10,2},{12,4},{14,6},{16,24},{18,... | collective-permute-start | bytes 786440 | tf_op jit(solution)/shard_map/ppermute | solution.py:42
  127.6 2.9 %collective-permute-done.10 = bf16[2,2,2,64,256]{4,3,0,1,2:T(8,128)(2,1)S(1)} collective-permute-done((bf16[2,2,2,64,256]{4,3,0,1,2:T(8,128)(2,1)S(1)}, bf16[2,2,2,64,256]{4,3,0,1,2:T(8,128)(2,1)S(1)}, u32[]{:S(2)}, u32[]{:S(2)}) %collective-permute-start.10) | collective-permute-done | bytes 262176 | tf_op jit(solution)/shard_map/ppermute | solution.py:42
  130.5 3.5 %collective-permute-start.22 = (bf16[2,2,2,64,256]{4,3,0,1,2:T(8,128)(2,1)S(1)}, bf16[2,2,2,64,256]{4,3,0,1,2:T(8,128)(2,1)S(1)}, u32[]{:S(2)}, u32[]{:S(2)}) collective-permute-start(bf16[2,2,2,64,256]{4,3,0,1,2:T(8,128)(2,1)S(1)} %fusion.9), channel_id=1, source_target_pairs={{0,8},{2,10},{4,12},{6,14},{8,0},{10,2},{12,4},{14,6},{16,24},{18,... | collective-permute-start | bytes 786440 | tf_op jit(solution)/shard_map/ppermute | solution.py:42
  135.8 1.7 collective-permute-start.15
  137.7 3.5 %collective-permute-done.22 = bf16[2,2,2,64,256]{4,3,0,1,2:T(8,128)(2,1)S(1)} collective-permute-done((bf16[2,2,2,64,256]{4,3,0,1,2:T(8,128)(2,1)S(1)}, bf16[2,2,2,64,256]{4,3,0,1,2:T(8,128)(2,1)S(1)}, u32[]{:S(2)}, u32[]{:S(2)}) %collective-permute-start.22) | collective-permute-done | bytes 262176 | tf_op jit(solution)/shard_map/ppermute | solution.py:42
  141.2 2.0 %collective-permute-start.19 = (bf16[2,2,64,256]{3,2,0,1:T(8,128)(2,1)S(1)}, bf16[2,2,64,256]{3,2,0,1:T(8,128)(2,1)S(1)}, u32[]{:S(2)}, u32[]{:S(2)}) collective-permute-start(bf16[2,2,64,256]{3,2,0,1:T(8,128)(2,1)S(1)} %fusion.14), channel_id=1, source_target_pairs={{0,8},{2,10},{4,12},{6,14},{8,0},{10,2},{12,4},{14,6},{16,24},{18,... | collective-permute-start | bytes 393224 | tf_op jit(solution)/shard_map/ppermute | solution.py:42
  144.0 1.8 %collective-permute-start.23 = (bf16[2,2,64,256]{3,2,0,1:T(8,128)(2,1)S(1)}, bf16[2,2,64,256]{3,2,0,1:T(8,128)(2,1)S(1)}, u32[]{:S(2)}, u32[]{:S(2)}) collective-permute-start(bf16[2,2,64,256]{3,2,0,1:T(8,128)(2,1)S(1)} %fusion.15), channel_id=1, source_target_pairs={{0,4},{2,6},{4,0},{6,2},{8,12},{10,14},{12,8},{14,10},{16,20},{18,... | collective-permute-start | bytes 393224 | tf_op jit(solution)/shard_map/ppermute | solution.py:42
  145.8 3.9 %collective-permute-start.12 = (bf16[2,64,256]{2,1,0:T(8,128)(2,1)S(1)}, bf16[2,64,256]{2,1,0:T(8,128)(2,1)S(1)}, u32[]{:S(2)}, u32[]{:S(2)}) collective-permute-start(bf16[2,64,256]{2,1,0:T(8,128)(2,1)S(1)} %fusion.20), channel_id=1, source_target_pairs={{0,16},{2,18},{4,20},{6,22},{8,24},{10,26},{12,28},{14,30},{16,0},... | collective-permute-start | bytes 196616 | tf_op jit(solution)/shard_map/ppermute | solution.py:42
  150.7 2.2 %collective-permute-start.20 = (bf16[2,64,256]{2,1,0:T(8,128)(2,1)S(1)}, bf16[2,64,256]{2,1,0:T(8,128)(2,1)S(1)}, u32[]{:S(2)}, u32[]{:S(2)}) collective-permute-start(bf16[2,64,256]{2,1,0:T(8,128)(2,1)S(1)} %fusion.22), channel_id=1, source_target_pairs={{0,16},{2,18},{4,20},{6,22},{8,24},{10,26},{12,28},{14,30},{16,0},... | collective-permute-start | bytes 196616 | tf_op jit(solution)/shard_map/ppermute | solution.py:42
  153.0 2.1 %collective-permute-done.12 = bf16[2,64,256]{2,1,0:T(8,128)(2,1)S(1)} collective-permute-done((bf16[2,64,256]{2,1,0:T(8,128)(2,1)S(1)}, bf16[2,64,256]{2,1,0:T(8,128)(2,1)S(1)}, u32[]{:S(2)}, u32[]{:S(2)}) %collective-permute-start.12) | collective-permute-done | bytes 65568 | tf_op jit(solution)/shard_map/ppermute | solution.py:42
  155.6 2.3 %collective-permute-done.16 = bf16[2,64,256]{2,1,0:T(8,128)(2,1)S(1)} collective-permute-done((bf16[2,64,256]{2,1,0:T(8,128)(2,1)S(1)}, bf16[2,64,256]{2,1,0:T(8,128)(2,1)S(1)}, u32[]{:S(2)}, u32[]{:S(2)}) %collective-permute-start.16) | collective-permute-done | bytes 65568 | tf_op jit(solution)/shard_map/ppermute | solution.py:42
  158.6 1.6 collective-permute-done.24
  161.0 6.9 %shard_map.98 = (bf16[256,2048]{1,0:T(8,128)(2,1)}, bf16[256,2048]{1,0:T(8,128)(2,1)}) custom-call(f32[256,2048]{1,0:T(8,128)} %get-tuple-element.50.own_k_ref, f32[256,2048]{1,0:T(8,128)} %get-tuple-element.51.own_v_ref, bf16[256,1024]{1,0:T(8,128)(2,1)} %collective-permute-done.7.back_k_ref, bf16[256,1024]{1,0:T(8,128)(2,1)} %collective-permute-done.8.back_v_ref, ...), custom_call_target="tpu_custom_call" | custom-call | flops 67108864 | bytes 5242880 | tf_op jit(solution)/shard_map/pallas_call | solution.py:236
  (115 shorter events, 26.7 us)
Async XLA Ops:
  7.2 89.6 %all-gather.2.cloned.1.call-start = ((), (), s32[]{:S(2)}) async-start(), calls=%async_computation | async-start | bytes 2228224 | tf_op jit(solution)/shard_map/all_gather | solution.py:294
  7.2 2.1 %copy-start.7 = (s32[8,32]{1,0:T(8,128)S(1)}, s32[8,32]{1,0:T(8,128)}, u32[]{:S(2)}) copy-start(s32[8,32]{1,0:T(8,128)} %param.11) | copy-start | bytes 3076
  13.8 10.3 %collective-permute-start.1 = (bf16[64,1024]{1,0:T(8,128)(2,1)S(1)}, bf16[64,1024]{1,0:T(8,128)(2,1)S(1)}, u32[]{:S(2)}, u32[]{:S(2)}) collective-permute-start(bf16[64,1024]{1,0:T(8,128)(2,1)S(1)} %get-tuple-element.74), channel_id=1, source_target_pairs={{0,16},{2,18},{4,20},{6,22},{8,24},{10,26},{12,28},{14,30},{16,0},... | collective-permute-start | bytes 393224 | tf_op jit(solution)/shard_map/ppermute | solution.py:59
  24.9 13.6 %collective-permute-start.2 = (bf16[2,64,1024]{2,1,0:T(8,128)(2,1)}, bf16[2,64,1024]{2,1,0:T(8,128)(2,1)S(1)}, u32[]{:S(2)}, u32[]{:S(2)}) collective-permute-start(bf16[2,64,1024]{2,1,0:T(8,128)(2,1)} %maximum_select_fusion.6), channel_id=1, source_target_pairs={{0,8},{2,10},{4,12},{6,14},{8,0},{10,2},{12,4},{14,6},{16,24},{18,... | collective-permute-start | bytes 786440 | tf_op jit(solution)/shard_map/ppermute | solution.py:59
  25.6 39.1 %collective-permute-start = (bf16[128,4096]{1,0:T(8,128)(2,1)}, bf16[128,4096]{1,0:T(8,128)(2,1)}, u32[]{:S(2)}, u32[]{:S(2)}) collective-permute-start(bf16[128,4096]{1,0:T(8,128)(2,1)} %param.10), channel_id=1, source_target_pairs={{0,1},{1,0},{2,3},{3,2},{4,5},{5,4},{6,7},{7,6},{8,9},{9,8},{10,11... | collective-permute-start | bytes 3145736 | tf_op jit(solution)/shard_map/ppermute | solution.py:300
  30.0 10.0 %copy-start.5 = (bf16[1,1,64,1024]{3,2,0,1:T(8,128)(2,1)S(1)}, bf16[1,1,64,1024]{3,2,0,1:T(8,128)(2,1)}, u32[]{:S(2)}) copy-start(bf16[1,1,64,1024]{3,2,0,1:T(8,128)(2,1)} %get-tuple-element.72) | copy-start | bytes 393220
  30.0 50.8 %collective-permute-start.5 = (bf16[256,1024]{1,0:T(8,128)(2,1)}, bf16[256,1024]{1,0:T(8,128)(2,1)}, u32[]{:S(2)}, u32[]{:S(2)}) collective-permute-start(bf16[256,1024]{1,0:T(8,128)(2,1)} %copy.69), channel_id=1, source_target_pairs={{0,2},{2,4},{4,6},{6,8},{8,10},{10,12},{12,14},{14,16},{16,18},{18... | collective-permute-start | bytes 1572872 | tf_op jit(solution)/shard_map/ppermute | solution.py:21
  33.4 47.4 %collective-permute-start.6 = (bf16[256,1024]{1,0:T(8,128)(2,1)}, bf16[256,1024]{1,0:T(8,128)(2,1)}, u32[]{:S(2)}, u32[]{:S(2)}) collective-permute-start(bf16[256,1024]{1,0:T(8,128)(2,1)} %copy.70), channel_id=1, source_target_pairs={{0,2},{2,4},{4,6},{6,8},{8,10},{10,12},{12,14},{14,16},{16,18},{18... | collective-permute-start | bytes 1572872 | tf_op jit(solution)/shard_map/ppermute | solution.py:21
  38.6 18.7 %collective-permute-start.3 = (bf16[2,2,64,1024]{3,2,0,1:T(8,128)(2,1)S(1)}, bf16[2,2,64,1024]{3,2,0,1:T(8,128)(2,1)S(1)}, u32[]{:S(2)}, u32[]{:S(2)}) collective-permute-start(bf16[2,2,64,1024]{3,2,0,1:T(8,128)(2,1)S(1)} %maximum_select_fusion.4), channel_id=1, source_target_pairs={{0,4},{2,6},{4,0},{6,2},{8,12},{10,14},{12,8},{14,10},{16,20},{18,... | collective-permute-start | bytes 1572872 | tf_op jit(solution)/shard_map/ppermute | solution.py:59
  57.3 7.4 %copy-start.6 = (bf16[128,4096]{1,0:T(8,128)(2,1)S(1)}, bf16[128,4096]{1,0:T(8,128)(2,1)}, u32[]{:S(2)}) copy-start(bf16[128,4096]{1,0:T(8,128)(2,1)} %param.10) | copy-start | bytes 3145732
  58.4 34.9 %collective-permute-start.4 = (bf16[2,2,2,64,1024]{4,3,0,1,2:T(8,128)(2,1)}, bf16[2,2,2,64,1024]{4,3,0,1,2:T(8,128)(2,1)}, u32[]{:S(2)}, u32[]{:S(2)}) collective-permute-start(bf16[2,2,2,64,1024]{4,3,0,1,2:T(8,128)(2,1)} %maximum_select_fusion.2), channel_id=1, source_target_pairs={{0,2},{2,0},{4,6},{6,4},{8,10},{10,8},{12,14},{14,12},{16,18},{18,... | collective-permute-start | bytes 3145736 | tf_op jit(solution)/shard_map/ppermute | solution.py:59
  68.8 12.1 %copy-start = (bf16[256,2048]{1,0:T(8,128)(2,1)S(1)}, bf16[256,2048]{1,0:T(8,128)(2,1)}, u32[]{:S(2)}) copy-start(bf16[256,2048]{1,0:T(8,128)(2,1)} %k_ref.9) | copy-start | bytes 3145732
  68.8 12.1 %copy-start.2 = (bf16[256,2048]{1,0:T(8,128)(2,1)S(1)}, bf16[256,2048]{1,0:T(8,128)(2,1)}, u32[]{:S(2)}) copy-start(bf16[256,2048]{1,0:T(8,128)(2,1)} %q_ref.9) | copy-start | bytes 3145732
  80.9 12.5 %copy-start.4 = (bf16[2,2,2,1,64,1024]{5,4,0,1,2,3:T(8,128)(2,1)S(1)}, bf16[2,2,2,1,64,1024]{5,4,0,1,2,3:T(8,128)(2,1)}, u32[]{:S(2)}) copy-start(bf16[2,2,2,1,64,1024]{5,4,0,1,2,3:T(8,128)(2,1)} %maximum_select_fusion.1) | copy-start | bytes 3145732
  90.5 70.5 %collective-permute-start.7 = (bf16[256,1024]{1,0:T(8,128)(2,1)}, bf16[256,1024]{1,0:T(8,128)(2,1)}, u32[]{:S(2)}, u32[]{:S(2)}) collective-permute-start(bf16[256,1024]{1,0:T(8,128)(2,1)} %get-tuple-element.52), channel_id=1, source_target_pairs={{2,0},{4,2},{6,4},{8,6},{10,8},{12,10},{14,12},{16,14},{18,16},{20... | collective-permute-start | bytes 1572872 | tf_op jit(solution)/shard_map/ppermute | solution.py:21
  91.8 69.2 %collective-permute-start.8 = (bf16[256,1024]{1,0:T(8,128)(2,1)}, bf16[256,1024]{1,0:T(8,128)(2,1)}, u32[]{:S(2)}, u32[]{:S(2)}) collective-permute-start(bf16[256,1024]{1,0:T(8,128)(2,1)} %get-tuple-element.53), channel_id=1, source_target_pairs={{2,0},{4,2},{6,4},{8,6},{10,8},{12,10},{14,12},{16,14},{18,16},{20... | collective-permute-start | bytes 1572872 | tf_op jit(solution)/shard_map/ppermute | solution.py:21
  103.1 17.7 %collective-permute-start.9 = (bf16[2,2,2,2,64,256]{5,4,0,1,2,3:T(8,128)(2,1)S(1)}, bf16[2,2,2,2,64,256]{5,4,0,1,2,3:T(8,128)(2,1)S(1)}, u32[]{:S(2)}, u32[]{:S(2)}) collective-permute-start(bf16[2,2,2,2,64,256]{5,4,0,1,2,3:T(8,128)(2,1)S(1)} %bitcast.167), channel_id=1, source_target_pairs={{0,2},{2,0},{4,6},{6,4},{8,10},{10,8},{12,14},{14,12},{16,18},{18,... | collective-permute-start | bytes 1572872 | tf_op jit(solution)/shard_map/ppermute | solution.py:42
  110.0 11.1 %collective-permute-start.13 = (bf16[2,2,2,2,64,256]{5,4,0,1,3,2:T(8,128)(2,1)S(1)}, bf16[2,2,2,2,64,256]{5,4,0,1,3,2:T(8,128)(2,1)S(1)}, u32[]{:S(2)}, u32[]{:S(2)}) collective-permute-start(bf16[2,2,2,2,64,256]{5,4,0,1,3,2:T(8,128)(2,1)S(1)} %bitcast.168), channel_id=1, source_target_pairs={{0,2},{2,0},{4,6},{6,4},{8,10},{10,8},{12,14},{14,12},{16,18},{18,... | collective-permute-start | bytes 1572872 | tf_op jit(solution)/shard_map/ppermute | solution.py:42
  115.2 8.3 %collective-permute-start.17 = (bf16[2,2,2,2,64,256]{5,4,0,1,2,3:T(8,128)(2,1)S(1)}, bf16[2,2,2,2,64,256]{5,4,0,1,2,3:T(8,128)(2,1)S(1)}, u32[]{:S(2)}, u32[]{:S(2)}) collective-permute-start(bf16[2,2,2,2,64,256]{5,4,0,1,2,3:T(8,128)(2,1)S(1)} %bitcast.169), channel_id=1, source_target_pairs={{0,2},{2,0},{4,6},{6,4},{8,10},{10,8},{12,14},{14,12},{16,18},{18,... | collective-permute-start | bytes 1572872 | tf_op jit(solution)/shard_map/ppermute | solution.py:42
  120.7 6.5 %collective-permute-start.21 = (bf16[2,2,2,2,64,256]{5,4,0,1,3,2:T(8,128)(2,1)S(1)}, bf16[2,2,2,2,64,256]{5,4,0,1,3,2:T(8,128)(2,1)S(1)}, u32[]{:S(2)}, u32[]{:S(2)}) collective-permute-start(bf16[2,2,2,2,64,256]{5,4,0,1,3,2:T(8,128)(2,1)S(1)} %bitcast.170), channel_id=1, source_target_pairs={{0,2},{2,0},{4,6},{6,4},{8,10},{10,8},{12,14},{14,12},{16,18},{18,... | collective-permute-start | bytes 1572872 | tf_op jit(solution)/shard_map/ppermute | solution.py:42
  121.1 9.4 %collective-permute-start.10 = (bf16[2,2,2,64,256]{4,3,0,1,2:T(8,128)(2,1)S(1)}, bf16[2,2,2,64,256]{4,3,0,1,2:T(8,128)(2,1)S(1)}, u32[]{:S(2)}, u32[]{:S(2)}) collective-permute-start(bf16[2,2,2,64,256]{4,3,0,1,2:T(8,128)(2,1)S(1)} %fusion.6), channel_id=1, source_target_pairs={{0,4},{2,6},{4,0},{6,2},{8,12},{10,14},{12,8},{14,10},{16,20},{18,... | collective-permute-start | bytes 786440 | tf_op jit(solution)/shard_map/ppermute | solution.py:42
  123.5 10.6 %collective-permute-start.14 = (bf16[2,2,2,64,256]{4,3,0,1,2:T(8,128)(2,1)S(1)}, bf16[2,2,2,64,256]{4,3,0,1,2:T(8,128)(2,1)S(1)}, u32[]{:S(2)}, u32[]{:S(2)}) collective-permute-start(bf16[2,2,2,64,256]{4,3,0,1,2:T(8,128)(2,1)S(1)} %fusion.7), channel_id=1, source_target_pairs={{0,8},{2,10},{4,12},{6,14},{8,0},{10,2},{12,4},{14,6},{16,24},{18,... | collective-permute-start | bytes 786440 | tf_op jit(solution)/shard_map/ppermute | solution.py:42
  127.2 8.6 %collective-permute-start.18 = (bf16[2,2,2,64,256]{4,3,0,1,2:T(8,128)(2,1)S(1)}, bf16[2,2,2,64,256]{4,3,0,1,2:T(8,128)(2,1)S(1)}, u32[]{:S(2)}, u32[]{:S(2)}) collective-permute-start(bf16[2,2,2,64,256]{4,3,0,1,2:T(8,128)(2,1)S(1)} %fusion.8), channel_id=1, source_target_pairs={{0,4},{2,6},{4,0},{6,2},{8,12},{10,14},{12,8},{14,10},{16,20},{18,... | collective-permute-start | bytes 786440 | tf_op jit(solution)/shard_map/ppermute | solution.py:42
  130.5 10.7 %collective-permute-start.22 = (bf16[2,2,2,64,256]{4,3,0,1,2:T(8,128)(2,1)S(1)}, bf16[2,2,2,64,256]{4,3,0,1,2:T(8,128)(2,1)S(1)}, u32[]{:S(2)}, u32[]{:S(2)}) collective-permute-start(bf16[2,2,2,64,256]{4,3,0,1,2:T(8,128)(2,1)S(1)} %fusion.9), channel_id=1, source_target_pairs={{0,8},{2,10},{4,12},{6,14},{8,0},{10,2},{12,4},{14,6},{16,24},{18,... | collective-permute-start | bytes 786440 | tf_op jit(solution)/shard_map/ppermute | solution.py:42
  134.1 9.9 %collective-permute-start.11 = (bf16[2,2,64,256]{3,2,0,1:T(8,128)(2,1)S(1)}, bf16[2,2,64,256]{3,2,0,1:T(8,128)(2,1)S(1)}, u32[]{:S(2)}, u32[]{:S(2)}) collective-permute-start(bf16[2,2,64,256]{3,2,0,1:T(8,128)(2,1)S(1)} %fusion.12), channel_id=1, source_target_pairs={{0,8},{2,10},{4,12},{6,14},{8,0},{10,2},{12,4},{14,6},{16,24},{18,... | collective-permute-start | bytes 393224 | tf_op jit(solution)/shard_map/ppermute | solution.py:42
  135.8 10.0 %collective-permute-start.15 = (bf16[2,2,64,256]{3,2,0,1:T(8,128)(2,1)S(1)}, bf16[2,2,64,256]{3,2,0,1:T(8,128)(2,1)S(1)}, u32[]{:S(2)}, u32[]{:S(2)}) collective-permute-start(bf16[2,2,64,256]{3,2,0,1:T(8,128)(2,1)S(1)} %fusion.13), channel_id=1, source_target_pairs={{0,4},{2,6},{4,0},{6,2},{8,12},{10,14},{12,8},{14,10},{16,20},{18,... | collective-permute-start | bytes 393224 | tf_op jit(solution)/shard_map/ppermute | solution.py:42
  141.2 8.6 %collective-permute-start.19 = (bf16[2,2,64,256]{3,2,0,1:T(8,128)(2,1)S(1)}, bf16[2,2,64,256]{3,2,0,1:T(8,128)(2,1)S(1)}, u32[]{:S(2)}, u32[]{:S(2)}) collective-permute-start(bf16[2,2,64,256]{3,2,0,1:T(8,128)(2,1)S(1)} %fusion.14), channel_id=1, source_target_pairs={{0,8},{2,10},{4,12},{6,14},{8,0},{10,2},{12,4},{14,6},{16,24},{18,... | collective-permute-start | bytes 393224 | tf_op jit(solution)/shard_map/ppermute | solution.py:42
  144.0 6.7 %collective-permute-start.23 = (bf16[2,2,64,256]{3,2,0,1:T(8,128)(2,1)S(1)}, bf16[2,2,64,256]{3,2,0,1:T(8,128)(2,1)S(1)}, u32[]{:S(2)}, u32[]{:S(2)}) collective-permute-start(bf16[2,2,64,256]{3,2,0,1:T(8,128)(2,1)S(1)} %fusion.15), channel_id=1, source_target_pairs={{0,4},{2,6},{4,0},{6,2},{8,12},{10,14},{12,8},{14,10},{16,20},{18,... | collective-permute-start | bytes 393224 | tf_op jit(solution)/shard_map/ppermute | solution.py:42
  145.8 9.2 %collective-permute-start.12 = (bf16[2,64,256]{2,1,0:T(8,128)(2,1)S(1)}, bf16[2,64,256]{2,1,0:T(8,128)(2,1)S(1)}, u32[]{:S(2)}, u32[]{:S(2)}) collective-permute-start(bf16[2,64,256]{2,1,0:T(8,128)(2,1)S(1)} %fusion.20), channel_id=1, source_target_pairs={{0,16},{2,18},{4,20},{6,22},{8,24},{10,26},{12,28},{14,30},{16,0},... | collective-permute-start | bytes 196616 | tf_op jit(solution)/shard_map/ppermute | solution.py:42
  149.8 8.1 %collective-permute-start.16 = (bf16[2,64,256]{2,1,0:T(8,128)(2,1)S(1)}, bf16[2,64,256]{2,1,0:T(8,128)(2,1)S(1)}, u32[]{:S(2)}, u32[]{:S(2)}) collective-permute-start(bf16[2,64,256]{2,1,0:T(8,128)(2,1)S(1)} %fusion.21), channel_id=1, source_target_pairs={{0,16},{2,18},{4,20},{6,22},{8,24},{10,26},{12,28},{14,30},{16,0},... | collective-permute-start | bytes 196616 | tf_op jit(solution)/shard_map/ppermute | solution.py:42
  150.7 7.9 %collective-permute-start.20 = (bf16[2,64,256]{2,1,0:T(8,128)(2,1)S(1)}, bf16[2,64,256]{2,1,0:T(8,128)(2,1)S(1)}, u32[]{:S(2)}, u32[]{:S(2)}) collective-permute-start(bf16[2,64,256]{2,1,0:T(8,128)(2,1)S(1)} %fusion.22), channel_id=1, source_target_pairs={{0,16},{2,18},{4,20},{6,22},{8,24},{10,26},{12,28},{14,30},{16,0},... | collective-permute-start | bytes 196616 | tf_op jit(solution)/shard_map/ppermute | solution.py:42
  155.1 5.2 %collective-permute-start.24 = (bf16[2,64,256]{2,1,0:T(8,128)(2,1)S(1)}, bf16[2,64,256]{2,1,0:T(8,128)(2,1)S(1)}, u32[]{:S(2)}, u32[]{:S(2)}) collective-permute-start(bf16[2,64,256]{2,1,0:T(8,128)(2,1)S(1)} %fusion.23), channel_id=1, source_target_pairs={{0,16},{2,18},{4,20},{6,22},{8,24},{10,26},{12,28},{14,30},{16,0},... | collective-permute-start | bytes 196616 | tf_op jit(solution)/shard_map/ppermute | solution.py:42
  (2 other events, 2.9 us)
Sparse Core Ops, SparseCore 0:
  13.2 53.8 all-gather.1

commit v13 on v9

--- a/solution.py
+++ b/solution.py
@@ -85,7 +85,7 @@
     return out, dq, (dk_a, dv_a), (dk_b, dv_b)
 
 
-def band_kernel(seq_ref, q_ref, k_ref, v_ref, g_ref, kp_ref, vp_ref, out_ref, dq_ref, dk_ref, dv_ref, dkp_ref, dvp_ref, *, scale):
+def band_kernel(seq_ref, q_ref, k_ref, v_ref, g_ref, kvp_ref, out_ref, dq_ref, dk_ref, dv_ref, dkvp_ref, *, scale):
     rows = q_ref.shape[0]
     qi = lax.broadcasted_iota(jnp.int32, (rows, rows), 0)
     kj = lax.broadcasted_iota(jnp.int32, (rows, rows), 1)
@@ -94,7 +94,7 @@
     out, dq, (dkp, dvp), (dko, dvo) = two_part_attention(
         q_ref[...],
         g_ref[...],
-        (kp_ref[...], vp_ref[...], prev_mask),
+        (kvp_ref[0], kvp_ref[1], prev_mask),
         (k_ref[...], v_ref[...], own_mask),
         scale,
     )
@@ -102,8 +102,8 @@
     dq_ref[...] = dq
     dk_ref[...] = dko
     dv_ref[...] = dvo
-    dkp_ref[...] = dkp.astype(dkp_ref.dtype)
-    dvp_ref[...] = dvp.astype(dvp_ref.dtype)
+    dkvp_ref[0] = dkp.astype(dkvp_ref.dtype)
+    dkvp_ref[1] = dvp.astype(dkvp_ref.dtype)
 
 
 def fixed_kernel(seq_ref, q_ref, k_ref, v_ref, g_ref, kf_ref, vf_ref, *refs, scale, unused):
@@ -140,16 +140,16 @@
     )
 
 
-def band_attention(seq_index, q, k, v, g, k_prev, v_prev, head_pairs, head_dim, scale):
+def band_attention(seq_index, q, k, v, g, kv_prev, head_pairs, head_dim, scale):
     rows = q.shape[0]
     block = pl.BlockSpec((rows, head_dim), lambda p, s: (0, 2 * p))
-    narrow = pl.BlockSpec((rows, head_dim), lambda p, s: (0, p))
+    narrow = pl.BlockSpec((2, rows, head_dim), lambda p, s: (0, 0, p))
     width = 2 * head_pairs * head_dim
     grid_spec = pltpu.PrefetchScalarGridSpec(
         num_scalar_prefetch=1,
         grid=(head_pairs,),
-        in_specs=[block] * 4 + [narrow] * 2,
-        out_specs=[block] * 4 + [narrow] * 2,
+        in_specs=[block] * 4 + [narrow],
+        out_specs=[block] * 4 + [narrow],
     )
     return pl.pallas_call(
         functools.partial(band_kernel, scale=scale),
@@ -159,12 +159,11 @@
             jax.ShapeDtypeStruct((rows, width), jnp.bfloat16),
             jax.ShapeDtypeStruct((rows, width), jnp.float32),
             jax.ShapeDtypeStruct((rows, width), jnp.float32),
-            jax.ShapeDtypeStruct((rows, head_pairs * head_dim), jnp.bfloat16),
-            jax.ShapeDtypeStruct((rows, head_pairs * head_dim), jnp.bfloat16),
+            jax.ShapeDtypeStruct((2, rows, head_pairs * head_dim), jnp.bfloat16),
         ],
         compiler_params=pltpu.CompilerParams(vmem_limit_bytes=48 * 1024 * 1024),
         cost_estimate=attention_cost(rows, 2 * rows, head_dim, head_pairs),
-    )(seq_index, q, k, v, g, k_prev, v_prev)
+    )(seq_index, q, k, v, g, kv_prev)
 
 
 def fixed_attention(seq_index, q, k, v, g, far_kv, first_pair, pairs, head_pairs, head_dim, scale, earlier):
@@ -193,30 +192,26 @@
     )(*operands)
 
 
-def finalize_kernel(own_k_ref, own_v_ref, back_k_ref, back_v_ref, digest_ref, select_ref, k_out, v_out):
-    hd = back_k_ref.shape[1]
+def finalize_kernel(own_k_ref, own_v_ref, back_ref, digest_ref, select_ref, k_out, v_out):
+    hd = back_ref.shape[2]
     pick = select_ref[0]
-    for own_ref, back_ref, side, out_ref in (
-        (own_k_ref, back_k_ref, 0, k_out),
-        (own_v_ref, back_v_ref, 1, v_out),
-    ):
-        out_ref[:, :hd] = (own_ref[:, :hd] + back_ref[...].astype(jnp.float32)).astype(out_ref.dtype)
+    for own_ref, side, out_ref in ((own_k_ref, 0, k_out), (own_v_ref, 1, v_out)):
+        out_ref[:, :hd] = (own_ref[:, :hd] + back_ref[side].astype(jnp.float32)).astype(out_ref.dtype)
         summary = tn(pick, digest_ref[side])
         out_ref[:, hd:] = (own_ref[:, hd:] + summary).astype(out_ref.dtype)
 
 
-def finalize(own_k, own_v, back_k, back_v, digest, select, head_pairs, head_dim):
+def finalize(own_k, own_v, back_kv, digest, select, head_pairs, head_dim):
     rows = own_k.shape[0]
     digest_rows = digest.shape[1]
     wide = pl.BlockSpec((rows, 2 * head_dim), lambda p: (0, p))
-    narrow = pl.BlockSpec((rows, head_dim), lambda p: (0, p))
+    narrow = pl.BlockSpec((2, rows, head_dim), lambda p: (0, 0, p))
     return pl.pallas_call(
         finalize_kernel,
         grid=(head_pairs,),
         in_specs=[
             wide,
             wide,
-            narrow,
             narrow,
             pl.BlockSpec((2, digest_rows, head_dim), lambda p: (0, 0, p)),
             pl.BlockSpec((1, digest_rows, rows), lambda p: (p, 0, 0)),
@@ -228,7 +223,7 @@
             transcendentals=0,
             bytes_accessed=rows * head_dim * head_pairs * 20,
         ),
-    )(own_k, own_v, back_k, back_v, digest, select)
+    )(own_k, own_v, back_kv, digest, select)
 
 
 def on_device(queries, keys, values, out_weight, cotangent, offsets):
@@ -243,9 +238,10 @@
     split_v = values.reshape(seq_rows, head_pairs, 2, head_dim)
     fixed_k = split_k[:, :, 1]
     fixed_v = split_v[:, :, 1]
-    band_k = split_k[:, :, 0].reshape(seq_rows, head_pairs * head_dim)
-    band_v = split_v[:, :, 0].reshape(seq_rows, head_pairs * head_dim)
-    prev_k, prev_v = passed_along((band_k, band_v), "seq", 1)
+    band_kv = jnp.stack([split_k[:, :, 0], split_v[:, :, 0]], 0).reshape(
+        2, seq_rows, head_pairs * head_dim
+    )
+    prev_kv = passed_along(band_kv, "seq", 1)
     digest_count = seq_rows // BLOCK * SUMM
     offset_table = jnp.tile(offsets.T, (seq_rows // BLOCK, 1))
     digest_rows = (jnp.arange(digest_count, dtype=jnp.int32) // SUMM * BLOCK)[
@@ -290,8 +286,8 @@
         preferred_element_type=jnp.float32,
     ).astype(jnp.bfloat16)
     seq_scalar = seq_index.reshape(1).astype(jnp.int32)
-    attention, query_grad, own_dk, own_dv, back_k, back_v = band_attention(
-        seq_scalar, queries, keys, values, grad_out, prev_k, prev_v, head_pairs, head_dim, score_scale
+    attention, query_grad, own_dk, own_dv, back_kv = band_attention(
+        seq_scalar, queries, keys, values, grad_out, prev_kv, head_pairs, head_dim, score_scale
     )
     chunks = 4 if head_pairs % 4 == 0 else (2 if head_pairs % 2 == 0 else 1)
     pairs = head_pairs // chunks
@@ -314,10 +310,10 @@
         )
         digests.append(seq_reduce_scatter(far_dkv, 1, chunk))
     attention, query_grad, own_dk, own_dv = outputs
-    back_k, back_v = passed_along((back_k, back_v), "seq", -1)
+    back_kv = passed_along(back_kv, "seq", -1)
     digest_dkv = jnp.concatenate(digests, 2) if chunks > 1 else digests[0]
     key_grad, value_grad = finalize(
-        own_dk, own_dv, back_k, back_v, digest_dkv, select, head_pairs, head_dim
+        own_dk, own_dv, back_kv, digest_dkv, select, head_pairs, head_dim
     )
     return attention, query_grad, key_grad, value_grad
 

time: 147 us -> 140 us (0.952)
  starting transfers between devices: 34.2 us -> 26.4 us
  local copies, waits for them, and re-layouts: 11.5 us -> 7.86 us
  waiting for transfers between devices: 29.3 us -> 32.7 us
    ppermute x4 -> x2, starting transfers between devices: 8.97 us -> 3.91 us  [passed_along(): lax.ppermute(value, axis, [(source, source + steps) for source in range(f...]
    ppermute x1, waiting for transfers between devices: 13.3 us -> 16.8 us  [on_device(): lax.ppermute(cotangent, 'head', [(source, (source + shift) % head_count)...]
    ppermute x16, starting transfers between devices: 22.1 us -> 19.5 us  [seq_reduce_scatter(): lax.ppermute(send.astype(jnp.bfloat16), 'seq', [(source, source ^ 1 << bi...]
    unnamed x24 -> x16, local copies, waits for them, and re-layouts: 6.58 us -> 4.54 us
    another operation x2, local copies, waits for them, and re-layouts: 3.04 us -> 1.46 us  [on_device(): jnp.stack([split_k[:, :, 0], split_v[:, :, 0]], 0)]
  transfers between devices with their start and end apart: 22 -> 20, of which waited for: 10 -> 8; matrix products, arithmetic and copies ran while one was open for 16% -> 17% of each run, Pallas kernels for 13% -> 21%
where the time goes in v13:
time: 140 us; the launch traced here: 139 us
  Pallas kernels  36.4 us (26%)
  waiting for transfers between devices  32.7 us (23%)
  starting transfers between devices  26.4 us (19%)
  between operations  14.4 us (10%)
  matrix products  12.8 us (9%)
  other arithmetic  8.34 us (6%)
  local copies, waits for them, and re-layouts  7.86 us (6%)
    pallas_call x4, Pallas kernels, fixed_attention(): pl.pallas_call(functools.partial(fixed_kernel, scale=scale, unused=len(ea...  19.8 us
    ppermute x16, starting transfers between devices, seq_reduce_scatter(): lax.ppermute(send.astype(jnp.bfloat16), 'seq', [(source, source ^ 1 << bi...  19.5 us
    ppermute x1, waiting for transfers between devices, on_device(): lax.ppermute(cotangent, 'head', [(source, (source + shift) % head_count)...  16.8 us
    ppermute x16, waiting for transfers between devices, seq_reduce_scatter(): lax.ppermute(send.astype(jnp.bfloat16), 'seq', [(source, source ^ 1 << bi...  15.9 us
    dot_general x1, matrix products, on_device(): lax.dot_general(gathered.reshape(seq_rows, cotangent.shape[1]), out_weigh...  12.1 us
    pallas_call x1, Pallas kernels, band_attention(): pl.pallas_call(functools.partial(band_kernel, scale=scale), grid_spec=gri...  9.6 us
    pallas_call x1, Pallas kernels, finalize(): pl.pallas_call(finalize_kernel, grid=(head_pairs,), in_specs=[wide, wide,...  7.02 us
    unnamed x16, local copies, waits for them, and re-layouts  4.54 us
  transfers between devices with their start and end apart: 20, of which 8 were waited for; matrix products, arithmetic and copies ran while one was open for 17% of the time, Pallas kernels for 21%

profile of v13, /device:TPU:0, one launch (start us, length us, event | category | flops | bytes accessed | tf_op | source)
XLA Modules:
  0.0 139.0 jit_solution(13116446980592423529)
XLA Ops:
  7.2 1.6 %copy.30 = bf16[256,2048]{0,1:T(8,128)(2,1)S(1)} copy(bf16[256,2048]{1,0:T(8,128)(2,1)} %k_ref.9) | data formatting | bytes 2097152 | tf_op args[1]
  10.9 3.0 %collective-permute-start = (bf16[128,4096]{1,0:T(8,128)(2,1)}, bf16[128,4096]{1,0:T(8,128)(2,1)}, u32[]{:S(2)}, u32[]{:S(2)}) collective-permute-start(bf16[128,4096]{1,0:T(8,128)(2,1)} %param.10), channel_id=1, source_target_pairs={{0,1},{1,0},{2,3},{3,2},{4,5},{5,4},{6,7},{7,6},{8,9},{9,8},{10,11... | collective-permute-start | bytes 3145736 | tf_op jit(solution)/shard_map/ppermute | solution.py:275
  14.8 1.3 copy.46
  17.4 2.5 %collective-permute-start.1 = (bf16[2,256,1024]{2,1,0:T(8,128)(2,1)}, bf16[2,256,1024]{2,1,0:T(8,128)(2,1)}, u32[]{:S(2)}, u32[]{:S(2)}) collective-permute-start(bf16[2,256,1024]{2,1,0:T(8,128)(2,1)} %pad_maximum_fusion), channel_id=1, source_target_pairs={{0,2},{2,4},{4,6},{6,8},{8,10},{10,12},{12,14},{14,16},{16,18},{18... | collective-permute-start | bytes 3145736 | tf_op jit(solution)/shard_map/ppermute | solution.py:21
  20.7 16.8 %collective-permute-done = bf16[128,4096]{1,0:T(8,128)(2,1)} collective-permute-done((bf16[128,4096]{1,0:T(8,128)(2,1)}, bf16[128,4096]{1,0:T(8,128)(2,1)}, u32[]{:S(2)}, u32[]{:S(2)}) %collective-permute-start) | collective-permute-done | bytes 1048608 | tf_op jit(solution)/shard_map/ppermute | solution.py:275
  37.5 4.1 %fusion.2 = bf16[2,128,4096]{2,1,0:T(8,128)(2,1)} fusion(s32[]{:T(128)S(6)} %select_n.65, bf16[1,128,4096]{2,1,0:T(8,128)(2,1)} %bitcast.1, bf16[1,128,4096]{2,1,0:T(8,128)(2,1)S(1)} %bitcast.136), kind=kLoop, calls=%fused_computation.7 | loop fusion | flops 3145728 | bytes 4194308 | tf_op jit(solution)/shard_map/stack | solution.py:280
  41.5 12.1 %convolution_convert_fusion.g_ref = bf16[256,2048]{1,0:T(8,128)(2,1)} fusion(bf16[256,4096]{1,0:T(8,128)(2,1)} %bitcast.133, bf16[2048,4096]{1,0:T(8,128)(2,1)} %param.9), kind=kOutput, calls=%fused_computation.4 | convolution fusion | flops 4295491584 | bytes 19922944 | tf_op jit(solution)/shard_map/dot_general | solution.py:282
  53.7 1.2 copy-done.3
  54.9 9.6 %shard_map.93 = (bf16[256,2048]{1,0:T(8,128)(2,1)}, bf16[256,2048]{1,0:T(8,128)(2,1)}, f32[256,2048]{1,0:T(8,128)}, f32[256,2048]{1,0:T(8,128)}, bf16[2,256,1024]{2,1,0:T(8,128)(2,1)}) custom-call(s32[1]{0:T(128)} %bitcast.seq_ref, bf16[256,2048]{1,0:T(8,128)(2,1)S(1)} %copy-done.2, bf16[256,2048]{1,0:T(8,128)(2,1)S(1)} %copy-done, ...), custom_call_target="tpu_custom_call" | custom-call | flops 1879048192 | bytes 7340032 | tf_op jit(solution)/shard_map/pallas_call | solution.py:154
  64.5 1.5 %collective-permute-start.2 = (bf16[2,256,1024]{2,1,0:T(8,128)(2,1)}, bf16[2,256,1024]{2,1,0:T(8,128)(2,1)}, u32[]{:S(2)}, u32[]{:S(2)}) collective-permute-start(bf16[2,256,1024]{2,1,0:T(8,128)(2,1)} %get-tuple-element.51), channel_id=1, source_target_pairs={{2,0},{4,2},{6,4},{8,6},{10,8},{12,10},{14,12},{16,14},{18,16},{20... | collective-permute-start | bytes 3145736 | tf_op jit(solution)/shard_map/ppermute | solution.py:21
  66.0 1.2 copy-done.4
  67.2 5.0 %shard_map.94 = (bf16[256,2048]{1,0:T(8,128)(2,1)}, bf16[256,2048]{1,0:T(8,128)(2,1)}, f32[256,2048]{1,0:T(8,128)}, f32[256,2048]{1,0:T(8,128)}, bf16[2,1024,256]{2,1,0:T(8,128)(2,1)S(1)}) custom-call(s32[1]{0:T(128)} %bitcast.seq_ref, bf16[256,2048]{1,0:T(8,128)(2,1)S(1)} %copy-done.2, ...), custom_call_target="tpu_custom_call", output_to_operand_aliasing={{0}: (7, {}), {1}: (8, {}), {2}: (9, {}), {3}: (10, {})} | custom-call | flops 1174405120 | bytes 3014656 | tf_op jit(solution)/shard_map/pallas_call | solution.py:184
  72.3 1.2 collective-permute-start.3
  73.5 4.9 %shard_map.95 = (bf16[256,2048]{1,0:T(8,128)(2,1)}, bf16[256,2048]{1,0:T(8,128)(2,1)}, f32[256,2048]{1,0:T(8,128)}, f32[256,2048]{1,0:T(8,128)}, bf16[2,1024,256]{2,1,0:T(8,128)(2,1)S(1)}) custom-call(s32[1]{0:T(128)} %bitcast.seq_ref, bf16[256,2048]{1,0:T(8,128)(2,1)S(1)} %copy-done.2, ...), custom_call_target="tpu_custom_call", output_to_operand_aliasing={{0}: (7, {}), {1}: (8, {}), {2}: (9, {}), {3}: (10, {})} | custom-call | flops 1174405120 | bytes 3014656 | tf_op jit(solution)/shard_map/pallas_call | solution.py:184
  78.7 4.9 %shard_map.96 = (bf16[256,2048]{1,0:T(8,128)(2,1)}, bf16[256,2048]{1,0:T(8,128)(2,1)}, f32[256,2048]{1,0:T(8,128)}, f32[256,2048]{1,0:T(8,128)}, bf16[2,1024,256]{2,1,0:T(8,128)(2,1)S(1)}) custom-call(s32[1]{0:T(128)} %bitcast.seq_ref, bf16[256,2048]{1,0:T(8,128)(2,1)S(1)} %copy-done.2, ...), custom_call_target="tpu_custom_call", output_to_operand_aliasing={{0}: (7, {}), {1}: (8, {}), {2}: (9, {}), {3}: (10, {})} | custom-call | flops 1174405120 | bytes 3014656 | tf_op jit(solution)/shard_map/pallas_call | solution.py:184
  84.4 4.9 %shard_map.97 = (bf16[256,2048]{1,0:T(8,128)(2,1)}, bf16[256,2048]{1,0:T(8,128)(2,1)}, f32[256,2048]{1,0:T(8,128)}, f32[256,2048]{1,0:T(8,128)}, bf16[2,1024,256]{2,1,0:T(8,128)(2,1)S(1)}) custom-call(s32[1]{0:T(128)} %bitcast.seq_ref, bf16[256,2048]{1,0:T(8,128)(2,1)S(1)} %copy-done.2, ...), custom_call_target="tpu_custom_call", output_to_operand_aliasing={{0}: (7, {}), {1}: (8, {}), {2}: (9, {}), {3}: (10, {})} | custom-call | flops 1174405120 | bytes 3014656 | tf_op jit(solution)/shard_map/pallas_call | solution.py:184
  89.8 1.9 %collective-permute-start.4 = (bf16[2,2,2,64,256]{4,3,0,1,2:T(8,128)(2,1)S(1)}, bf16[2,2,2,64,256]{4,3,0,1,2:T(8,128)(2,1)S(1)}, u32[]{:S(2)}, u32[]{:S(2)}) collective-permute-start(bf16[2,2,2,64,256]{4,3,0,1,2:T(8,128)(2,1)S(1)} %fusion.6), channel_id=1, source_target_pairs={{0,4},{2,6},{4,0},{6,2},{8,12},{10,14},{12,8},{14,10},{16,20},{18,... | collective-permute-start | bytes 786440 | tf_op jit(solution)/shard_map/ppermute | solution.py:45
  91.8 1.5 %collective-permute-start.8 = (bf16[2,2,2,64,256]{4,3,0,1,2:T(8,128)(2,1)S(1)}, bf16[2,2,2,64,256]{4,3,0,1,2:T(8,128)(2,1)S(1)}, u32[]{:S(2)}, u32[]{:S(2)}) collective-permute-start(bf16[2,2,2,64,256]{4,3,0,1,2:T(8,128)(2,1)S(1)} %fusion.7), channel_id=1, source_target_pairs={{0,8},{2,10},{4,12},{6,14},{8,0},{10,2},{12,4},{14,6},{16,24},{18,... | collective-permute-start | bytes 786440 | tf_op jit(solution)/shard_map/ppermute | solution.py:45
  94.8 4.1 %collective-permute-done.4 = bf16[2,2,2,64,256]{4,3,0,1,2:T(8,128)(2,1)S(1)} collective-permute-done((bf16[2,2,2,64,256]{4,3,0,1,2:T(8,128)(2,1)S(1)}, bf16[2,2,2,64,256]{4,3,0,1,2:T(8,128)(2,1)S(1)}, u32[]{:S(2)}, u32[]{:S(2)}) %collective-permute-start.4) | collective-permute-done | bytes 262176 | tf_op jit(solution)/shard_map/ppermute | solution.py:45
  99.0 2.3 %collective-permute-start.5 = (bf16[2,2,64,256]{3,2,0,1:T(8,128)(2,1)S(1)}, bf16[2,2,64,256]{3,2,0,1:T(8,128)(2,1)S(1)}, u32[]{:S(2)}, u32[]{:S(2)}) collective-permute-start(bf16[2,2,64,256]{3,2,0,1:T(8,128)(2,1)S(1)} %fusion.12), channel_id=1, source_target_pairs={{0,8},{2,10},{4,12},{6,14},{8,0},{10,2},{12,4},{14,6},{16,24},{18,... | collective-permute-start | bytes 393224 | tf_op jit(solution)/shard_map/ppermute | solution.py:45
  101.4 1.1 collective-permute-start.9
  102.6 2.0 %collective-permute-done.12 = bf16[2,2,2,64,256]{4,3,0,1,2:T(8,128)(2,1)S(1)} collective-permute-done((bf16[2,2,2,64,256]{4,3,0,1,2:T(8,128)(2,1)S(1)}, bf16[2,2,2,64,256]{4,3,0,1,2:T(8,128)(2,1)S(1)}, u32[]{:S(2)}, u32[]{:S(2)}) %collective-permute-start.12) | collective-permute-done | bytes 262176 | tf_op jit(solution)/shard_map/ppermute | solution.py:45
  104.6 2.3 %collective-permute-start.13 = (bf16[2,2,64,256]{3,2,0,1:T(8,128)(2,1)S(1)}, bf16[2,2,64,256]{3,2,0,1:T(8,128)(2,1)S(1)}, u32[]{:S(2)}, u32[]{:S(2)}) collective-permute-start(bf16[2,2,64,256]{3,2,0,1:T(8,128)(2,1)S(1)} %fusion.14), channel_id=1, source_target_pairs={{0,8},{2,10},{4,12},{6,14},{8,0},{10,2},{12,4},{14,6},{16,24},{18,... | collective-permute-start | bytes 393224 | tf_op jit(solution)/shard_map/ppermute | solution.py:45
  107.0 1.1 collective-permute-start.17
  108.2 1.3 collective-permute-done.5
  109.5 2.8 %collective-permute-start.6 = (bf16[2,64,256]{2,1,0:T(8,128)(2,1)S(1)}, bf16[2,64,256]{2,1,0:T(8,128)(2,1)S(1)}, u32[]{:S(2)}, u32[]{:S(2)}) collective-permute-start(bf16[2,64,256]{2,1,0:T(8,128)(2,1)S(1)} %fusion.20), channel_id=1, source_target_pairs={{0,16},{2,18},{4,20},{6,22},{8,24},{10,26},{12,28},{14,30},{16,0},... | collective-permute-start | bytes 196616 | tf_op jit(solution)/shard_map/ppermute | solution.py:45
  112.7 2.8 %collective-permute-start.14 = (bf16[2,64,256]{2,1,0:T(8,128)(2,1)S(1)}, bf16[2,64,256]{2,1,0:T(8,128)(2,1)S(1)}, u32[]{:S(2)}, u32[]{:S(2)}) collective-permute-start(bf16[2,64,256]{2,1,0:T(8,128)(2,1)S(1)} %fusion.22), channel_id=1, source_target_pairs={{0,16},{2,18},{4,20},{6,22},{8,24},{10,26},{12,28},{14,30},{16,0},... | collective-permute-start | bytes 196616 | tf_op jit(solution)/shard_map/ppermute | solution.py:45
  115.8 1.8 %collective-permute-done.6 = bf16[2,64,256]{2,1,0:T(8,128)(2,1)S(1)} collective-permute-done((bf16[2,64,256]{2,1,0:T(8,128)(2,1)S(1)}, bf16[2,64,256]{2,1,0:T(8,128)(2,1)S(1)}, u32[]{:S(2)}, u32[]{:S(2)}) %collective-permute-start.6) | collective-permute-done | bytes 65568 | tf_op jit(solution)/shard_map/ppermute | solution.py:45
  117.7 3.5 %collective-permute-done.10 = bf16[2,64,256]{2,1,0:T(8,128)(2,1)S(1)} collective-permute-done((bf16[2,64,256]{2,1,0:T(8,128)(2,1)S(1)}, bf16[2,64,256]{2,1,0:T(8,128)(2,1)S(1)}, u32[]{:S(2)}, u32[]{:S(2)}) %collective-permute-start.10) | collective-permute-done | bytes 65568 | tf_op jit(solution)/shard_map/ppermute | solution.py:45
  121.2 2.1 %collective-permute-done.14 = bf16[2,64,256]{2,1,0:T(8,128)(2,1)S(1)} collective-permute-done((bf16[2,64,256]{2,1,0:T(8,128)(2,1)S(1)}, bf16[2,64,256]{2,1,0:T(8,128)(2,1)S(1)}, u32[]{:S(2)}, u32[]{:S(2)}) %collective-permute-start.14) | collective-permute-done | bytes 65568 | tf_op jit(solution)/shard_map/ppermute | solution.py:45
  123.3 1.1 collective-permute-done.18
  125.1 7.0 %shard_map.98 = (bf16[256,2048]{1,0:T(8,128)(2,1)}, bf16[256,2048]{1,0:T(8,128)(2,1)}) custom-call(f32[256,2048]{1,0:T(8,128)} %get-tuple-element.49.own_k_ref, f32[256,2048]{1,0:T(8,128)} %get-tuple-element.50.own_v_ref, bf16[2,256,1024]{2,1,0:T(8,128)(2,1)} %collective-permute-done.2.back_ref, bf16[2,64,1024]{2,1,0:T(8,128)(2,1)} %pad_maximum_fusion.2.digest_ref, ...), custom_call_target="tpu_custom_call" | custom-call | flops 67108864 | bytes 5242880 | tf_op jit(solution)/shard_map/pallas_call | solution.py:209
  (84 shorter events, 9.9 us)
Async XLA Ops:
  7.2 1.6 %copy-start.1 = (bf16[256,2048]{1,0:T(8,128)(2,1)S(1)}, bf16[256,2048]{1,0:T(8,128)(2,1)}, u32[]{:S(2)}) copy-start(bf16[256,2048]{1,0:T(8,128)(2,1)} %v_ref.9) | copy-start | bytes 3145732
  7.2 58.8 %all-gather.2.cloned.1.call-start = ((), (), s32[]{:S(2)}) async-start(), calls=%async_computation | async-start | bytes 4456448 | tf_op jit(solution)/shard_map/all_gather | solution.py:260
  7.2 2.1 %copy-start.6 = (s32[8,32]{1,0:T(8,128)S(1)}, s32[8,32]{1,0:T(8,128)}, u32[]{:S(2)}) copy-start(s32[8,32]{1,0:T(8,128)} %param.11) | copy-start | bytes 3076
  10.9 26.5 %collective-permute-start = (bf16[128,4096]{1,0:T(8,128)(2,1)}, bf16[128,4096]{1,0:T(8,128)(2,1)}, u32[]{:S(2)}, u32[]{:S(2)}) collective-permute-start(bf16[128,4096]{1,0:T(8,128)(2,1)} %param.10), channel_id=1, source_target_pairs={{0,1},{1,0},{2,3},{3,2},{4,5},{5,4},{6,7},{7,6},{8,9},{9,8},{10,11... | collective-permute-start | bytes 3145736 | tf_op jit(solution)/shard_map/ppermute | solution.py:275
  16.3 21.1 %copy-start.5 = (bf16[128,4096]{1,0:T(8,128)(2,1)S(1)}, bf16[128,4096]{1,0:T(8,128)(2,1)}, u32[]{:S(2)}) copy-start(bf16[128,4096]{1,0:T(8,128)(2,1)} %param.10) | copy-start | bytes 3145732
  17.4 36.3 %collective-permute-start.1 = (bf16[2,256,1024]{2,1,0:T(8,128)(2,1)}, bf16[2,256,1024]{2,1,0:T(8,128)(2,1)}, u32[]{:S(2)}, u32[]{:S(2)}) collective-permute-start(bf16[2,256,1024]{2,1,0:T(8,128)(2,1)} %pad_maximum_fusion), channel_id=1, source_target_pairs={{0,2},{2,4},{4,6},{6,8},{8,10},{10,12},{12,14},{14,16},{16,18},{18... | collective-permute-start | bytes 3145736 | tf_op jit(solution)/shard_map/ppermute | solution.py:21
  41.5 12.1 %copy-start = (bf16[256,2048]{1,0:T(8,128)(2,1)S(1)}, bf16[256,2048]{1,0:T(8,128)(2,1)}, u32[]{:S(2)}) copy-start(bf16[256,2048]{1,0:T(8,128)(2,1)} %k_ref.9) | copy-start | bytes 3145732
  41.5 12.1 %copy-start.2 = (bf16[256,2048]{1,0:T(8,128)(2,1)S(1)}, bf16[256,2048]{1,0:T(8,128)(2,1)}, u32[]{:S(2)}) copy-start(bf16[256,2048]{1,0:T(8,128)(2,1)} %q_ref.9) | copy-start | bytes 3145732
  53.7 1.2 copy-start.3
  64.5 60.6 %collective-permute-start.2 = (bf16[2,256,1024]{2,1,0:T(8,128)(2,1)}, bf16[2,256,1024]{2,1,0:T(8,128)(2,1)}, u32[]{:S(2)}, u32[]{:S(2)}) collective-permute-start(bf16[2,256,1024]{2,1,0:T(8,128)(2,1)} %get-tuple-element.51), channel_id=1, source_target_pairs={{2,0},{4,2},{6,4},{8,6},{10,8},{12,10},{14,12},{16,14},{18,16},{20... | collective-permute-start | bytes 3145736 | tf_op jit(solution)/shard_map/ppermute | solution.py:21
  66.0 1.2 copy-start.4
  72.3 17.2 %collective-permute-start.3 = (bf16[2,2,2,2,64,256]{5,4,0,1,2,3:T(8,128)(2,1)S(1)}, bf16[2,2,2,2,64,256]{5,4,0,1,2,3:T(8,128)(2,1)S(1)}, u32[]{:S(2)}, u32[]{:S(2)}) collective-permute-start(bf16[2,2,2,2,64,256]{5,4,0,1,2,3:T(8,128)(2,1)S(1)} %bitcast.137), channel_id=1, source_target_pairs={{0,2},{2,0},{4,6},{6,4},{8,10},{10,8},{12,14},{14,12},{16,18},{18,... | collective-permute-start | bytes 1572872 | tf_op jit(solution)/shard_map/ppermute | solution.py:45
  78.6 13.0 %collective-permute-start.7 = (bf16[2,2,2,2,64,256]{5,4,0,1,3,2:T(8,128)(2,1)S(1)}, bf16[2,2,2,2,64,256]{5,4,0,1,3,2:T(8,128)(2,1)S(1)}, u32[]{:S(2)}, u32[]{:S(2)}) collective-permute-start(bf16[2,2,2,2,64,256]{5,4,0,1,3,2:T(8,128)(2,1)S(1)} %bitcast.138), channel_id=1, source_target_pairs={{0,2},{2,0},{4,6},{6,4},{8,10},{10,8},{12,14},{14,12},{16,18},{18,... | collective-permute-start | bytes 1572872 | tf_op jit(solution)/shard_map/ppermute | solution.py:45
  83.8 9.6 %collective-permute-start.11 = (bf16[2,2,2,2,64,256]{5,4,0,1,2,3:T(8,128)(2,1)S(1)}, bf16[2,2,2,2,64,256]{5,4,0,1,2,3:T(8,128)(2,1)S(1)}, u32[]{:S(2)}, u32[]{:S(2)}) collective-permute-start(bf16[2,2,2,2,64,256]{5,4,0,1,2,3:T(8,128)(2,1)S(1)} %bitcast.139), channel_id=1, source_target_pairs={{0,2},{2,0},{4,6},{6,4},{8,10},{10,8},{12,14},{14,12},{16,18},{18,... | collective-permute-start | bytes 1572872 | tf_op jit(solution)/shard_map/ppermute | solution.py:45
  89.5 5.1 %collective-permute-start.15 = (bf16[2,2,2,2,64,256]{5,4,0,1,3,2:T(8,128)(2,1)S(1)}, bf16[2,2,2,2,64,256]{5,4,0,1,3,2:T(8,128)(2,1)S(1)}, u32[]{:S(2)}, u32[]{:S(2)}) collective-permute-start(bf16[2,2,2,2,64,256]{5,4,0,1,3,2:T(8,128)(2,1)S(1)} %bitcast.140), channel_id=1, source_target_pairs={{0,2},{2,0},{4,6},{6,4},{8,10},{10,8},{12,14},{14,12},{16,18},{18,... | collective-permute-start | bytes 1572872 | tf_op jit(solution)/shard_map/ppermute | solution.py:45
  89.8 9.2 %collective-permute-start.4 = (bf16[2,2,2,64,256]{4,3,0,1,2:T(8,128)(2,1)S(1)}, bf16[2,2,2,64,256]{4,3,0,1,2:T(8,128)(2,1)S(1)}, u32[]{:S(2)}, u32[]{:S(2)}) collective-permute-start(bf16[2,2,2,64,256]{4,3,0,1,2:T(8,128)(2,1)S(1)} %fusion.6), channel_id=1, source_target_pairs={{0,4},{2,6},{4,0},{6,2},{8,12},{10,14},{12,8},{14,10},{16,20},{18,... | collective-permute-start | bytes 786440 | tf_op jit(solution)/shard_map/ppermute | solution.py:45
  91.8 9.5 %collective-permute-start.8 = (bf16[2,2,2,64,256]{4,3,0,1,2:T(8,128)(2,1)S(1)}, bf16[2,2,2,64,256]{4,3,0,1,2:T(8,128)(2,1)S(1)}, u32[]{:S(2)}, u32[]{:S(2)}) collective-permute-start(bf16[2,2,2,64,256]{4,3,0,1,2:T(8,128)(2,1)S(1)} %fusion.7), channel_id=1, source_target_pairs={{0,8},{2,10},{4,12},{6,14},{8,0},{10,2},{12,4},{14,6},{16,24},{18,... | collective-permute-start | bytes 786440 | tf_op jit(solution)/shard_map/ppermute | solution.py:45
  93.6 11.0 %collective-permute-start.12 = (bf16[2,2,2,64,256]{4,3,0,1,2:T(8,128)(2,1)S(1)}, bf16[2,2,2,64,256]{4,3,0,1,2:T(8,128)(2,1)S(1)}, u32[]{:S(2)}, u32[]{:S(2)}) collective-permute-start(bf16[2,2,2,64,256]{4,3,0,1,2:T(8,128)(2,1)S(1)} %fusion.8), channel_id=1, source_target_pairs={{0,4},{2,6},{4,0},{6,2},{8,12},{10,14},{12,8},{14,10},{16,20},{18,... | collective-permute-start | bytes 786440 | tf_op jit(solution)/shard_map/ppermute | solution.py:45
  94.8 12.2 %collective-permute-start.16 = (bf16[2,2,2,64,256]{4,3,0,1,2:T(8,128)(2,1)S(1)}, bf16[2,2,2,64,256]{4,3,0,1,2:T(8,128)(2,1)S(1)}, u32[]{:S(2)}, u32[]{:S(2)}) collective-permute-start(bf16[2,2,2,64,256]{4,3,0,1,2:T(8,128)(2,1)S(1)} %fusion.9), channel_id=1, source_target_pairs={{0,8},{2,10},{4,12},{6,14},{8,0},{10,2},{12,4},{14,6},{16,24},{18,... | collective-permute-start | bytes 786440 | tf_op jit(solution)/shard_map/ppermute | solution.py:45
  99.0 10.5 %collective-permute-start.5 = (bf16[2,2,64,256]{3,2,0,1:T(8,128)(2,1)S(1)}, bf16[2,2,64,256]{3,2,0,1:T(8,128)(2,1)S(1)}, u32[]{:S(2)}, u32[]{:S(2)}) collective-permute-start(bf16[2,2,64,256]{3,2,0,1:T(8,128)(2,1)S(1)} %fusion.12), channel_id=1, source_target_pairs={{0,8},{2,10},{4,12},{6,14},{8,0},{10,2},{12,4},{14,6},{16,24},{18,... | collective-permute-start | bytes 393224 | tf_op jit(solution)/shard_map/ppermute | solution.py:45
  101.4 11.0 %collective-permute-start.9 = (bf16[2,2,64,256]{3,2,0,1:T(8,128)(2,1)S(1)}, bf16[2,2,64,256]{3,2,0,1:T(8,128)(2,1)S(1)}, u32[]{:S(2)}, u32[]{:S(2)}) collective-permute-start(bf16[2,2,64,256]{3,2,0,1:T(8,128)(2,1)S(1)} %fusion.13), channel_id=1, source_target_pairs={{0,4},{2,6},{4,0},{6,2},{8,12},{10,14},{12,8},{14,10},{16,20},{18,... | collective-permute-start | bytes 393224 | tf_op jit(solution)/shard_map/ppermute | solution.py:45
  104.6 8.0 %collective-permute-start.13 = (bf16[2,2,64,256]{3,2,0,1:T(8,128)(2,1)S(1)}, bf16[2,2,64,256]{3,2,0,1:T(8,128)(2,1)S(1)}, u32[]{:S(2)}, u32[]{:S(2)}) collective-permute-start(bf16[2,2,64,256]{3,2,0,1:T(8,128)(2,1)S(1)} %fusion.14), channel_id=1, source_target_pairs={{0,8},{2,10},{4,12},{6,14},{8,0},{10,2},{12,4},{14,6},{16,24},{18,... | collective-permute-start | bytes 393224 | tf_op jit(solution)/shard_map/ppermute | solution.py:45
  107.0 8.5 %collective-permute-start.17 = (bf16[2,2,64,256]{3,2,0,1:T(8,128)(2,1)S(1)}, bf16[2,2,64,256]{3,2,0,1:T(8,128)(2,1)S(1)}, u32[]{:S(2)}, u32[]{:S(2)}) collective-permute-start(bf16[2,2,64,256]{3,2,0,1:T(8,128)(2,1)S(1)} %fusion.15), channel_id=1, source_target_pairs={{0,4},{2,6},{4,0},{6,2},{8,12},{10,14},{12,8},{14,10},{16,20},{18,... | collective-permute-start | bytes 393224 | tf_op jit(solution)/shard_map/ppermute | solution.py:45
  109.5 8.1 %collective-permute-start.6 = (bf16[2,64,256]{2,1,0:T(8,128)(2,1)S(1)}, bf16[2,64,256]{2,1,0:T(8,128)(2,1)S(1)}, u32[]{:S(2)}, u32[]{:S(2)}) collective-permute-start(bf16[2,64,256]{2,1,0:T(8,128)(2,1)S(1)} %fusion.20), channel_id=1, source_target_pairs={{0,16},{2,18},{4,20},{6,22},{8,24},{10,26},{12,28},{14,30},{16,0},... | collective-permute-start | bytes 196616 | tf_op jit(solution)/shard_map/ppermute | solution.py:45
  112.4 8.7 %collective-permute-start.10 = (bf16[2,64,256]{2,1,0:T(8,128)(2,1)S(1)}, bf16[2,64,256]{2,1,0:T(8,128)(2,1)S(1)}, u32[]{:S(2)}, u32[]{:S(2)}) collective-permute-start(bf16[2,64,256]{2,1,0:T(8,128)(2,1)S(1)} %fusion.21), channel_id=1, source_target_pairs={{0,16},{2,18},{4,20},{6,22},{8,24},{10,26},{12,28},{14,30},{16,0},... | collective-permute-start | bytes 196616 | tf_op jit(solution)/shard_map/ppermute | solution.py:45
  112.7 10.6 %collective-permute-start.14 = (bf16[2,64,256]{2,1,0:T(8,128)(2,1)S(1)}, bf16[2,64,256]{2,1,0:T(8,128)(2,1)S(1)}, u32[]{:S(2)}, u32[]{:S(2)}) collective-permute-start(bf16[2,64,256]{2,1,0:T(8,128)(2,1)S(1)} %fusion.22), channel_id=1, source_target_pairs={{0,16},{2,18},{4,20},{6,22},{8,24},{10,26},{12,28},{14,30},{16,0},... | collective-permute-start | bytes 196616 | tf_op jit(solution)/shard_map/ppermute | solution.py:45
  115.6 8.8 %collective-permute-start.18 = (bf16[2,64,256]{2,1,0:T(8,128)(2,1)S(1)}, bf16[2,64,256]{2,1,0:T(8,128)(2,1)S(1)}, u32[]{:S(2)}, u32[]{:S(2)}) collective-permute-start(bf16[2,64,256]{2,1,0:T(8,128)(2,1)S(1)} %fusion.23), channel_id=1, source_target_pairs={{0,16},{2,18},{4,20},{6,22},{8,24},{10,26},{12,28},{14,30},{16,0},... | collective-permute-start | bytes 196616 | tf_op jit(solution)/shard_map/ppermute | solution.py:45
Sparse Core Ops, SparseCore 0:
  11.1 54.6 all-gather.1

commit v14 on v13

--- a/solution.py
+++ b/solution.py
@@ -289,7 +289,7 @@
     attention, query_grad, own_dk, own_dv, back_kv = band_attention(
         seq_scalar, queries, keys, values, grad_out, prev_kv, head_pairs, head_dim, score_scale
     )
-    chunks = 4 if head_pairs % 4 == 0 else (2 if head_pairs % 2 == 0 else 1)
+    chunks = 2 if head_pairs % 2 == 0 else 1
     pairs = head_pairs // chunks
     outputs = (attention, query_grad, own_dk, own_dv)
     digests = []

time: 140 us -> 157 us (1.12)
  local copies, waits for them, and re-layouts: 7.86 us -> 15.7 us
  waiting for transfers between devices: 32.7 us -> 40 us
  other arithmetic: 8.34 us -> 11.2 us
  Pallas kernels: 36.4 us -> 34.5 us
    ppermute x16 -> x8, waiting for transfers between devices: 15.9 us -> 22.2 us  [seq_reduce_scatter(): lax.ppermute(send.astype(jnp.bfloat16), 'seq', [(source, source ^ 1 << bi...]
    dynamic_slice x4 -> x2, local copies, waits for them, and re-layouts: 0.39 us -> 4.49 us  [seq_reduce_scatter(): keep = lax.dynamic_index_in_dim(held, mine, where, keepdims=False)]
    add x12 -> x6, other arithmetic: 0.88 us -> 3.7 us  [seq_reduce_scatter(): held = keep + arrived.astype(jnp.float32)]
    unnamed x16 -> x24, local copies, waits for them, and re-layouts: 4.54 us -> 7.3 us
    pallas_call x4 -> x2, Pallas kernels: 19.8 us -> 17.7 us  [fixed_attention(): pl.pallas_call(functools.partial(fixed_kernel, scale=scale, unused=len(ea...]
    ppermute x16 -> x8, starting transfers between devices: 19.5 us -> 21.1 us  [seq_reduce_scatter(): lax.ppermute(send.astype(jnp.bfloat16), 'seq', [(source, source ^ 1 << bi...]
  transfers between devices with their start and end apart: 20 -> 12, of which waited for: 8 -> 6; matrix products, arithmetic and copies ran while one was open for 17% -> 17% of each run, Pallas kernels for 21% -> 12%
where the time goes in v14:
time: 157 us; the launch traced here: 156 us
  waiting for transfers between devices  40 us (25%)
  Pallas kernels  34.5 us (22%)
  starting transfers between devices  27.9 us (18%)
  local copies, waits for them, and re-layouts  15.7 us (10%)
  between operations  14.3 us (9%)
  matrix products  12.8 us (8%)
  other arithmetic  11.2 us (7%)
    ppermute x8, waiting for transfers between devices, seq_reduce_scatter(): lax.ppermute(send.astype(jnp.bfloat16), 'seq', [(source, source ^ 1 << bi...  22.2 us
    ppermute x8, starting transfers between devices, seq_reduce_scatter(): lax.ppermute(send.astype(jnp.bfloat16), 'seq', [(source, source ^ 1 << bi...  21.1 us
    pallas_call x2, Pallas kernels, fixed_attention(): pl.pallas_call(functools.partial(fixed_kernel, scale=scale, unused=len(ea...  17.7 us
    ppermute x1, waiting for transfers between devices, on_device(): lax.ppermute(cotangent, 'head', [(source, (source + shift) % head_count)...  17.6 us
    dot_general x1, matrix products, on_device(): lax.dot_general(gathered.reshape(seq_rows, cotangent.shape[1]), out_weigh...  12.1 us
    pallas_call x1, Pallas kernels, band_attention(): pl.pallas_call(functools.partial(band_kernel, scale=scale), grid_spec=gri...  9.72 us
    unnamed x24, local copies, waits for them, and re-layouts  7.3 us
    pallas_call x1, Pallas kernels, finalize(): pl.pallas_call(finalize_kernel, grid=(head_pairs,), in_specs=[wide, wide,...  7.04 us
  transfers between devices with their start and end apart: 12, of which 6 were waited for; matrix products, arithmetic and copies ran while one was open for 17% of the time, Pallas kernels for 12%

profile of v14, /device:TPU:0, one launch (start us, length us, event | category | flops | bytes accessed | tf_op | source)
XLA Modules:
  0.0 156.4 jit_solution(7605036812374058363)
XLA Ops:
  7.2 1.6 copy.22
  11.0 3.0 %collective-permute-start = (bf16[128,4096]{1,0:T(8,128)(2,1)}, bf16[128,4096]{1,0:T(8,128)(2,1)}, u32[]{:S(2)}, u32[]{:S(2)}) collective-permute-start(bf16[128,4096]{1,0:T(8,128)(2,1)} %param.10), channel_id=1, source_target_pairs={{0,1},{1,0},{2,3},{3,2},{4,5},{5,4},{6,7},{7,6},{8,9},{9,8},{10,11... | collective-permute-start | bytes 3145736 | tf_op jit(solution)/shard_map/ppermute | solution.py:275
  14.9 1.3 copy.34
  16.3 1.1 pad_maximum_fusion
  17.4 2.5 %collective-permute-start.1 = (bf16[2,256,1024]{2,1,0:T(8,128)(2,1)}, bf16[2,256,1024]{2,1,0:T(8,128)(2,1)}, u32[]{:S(2)}, u32[]{:S(2)}) collective-permute-start(bf16[2,256,1024]{2,1,0:T(8,128)(2,1)} %pad_maximum_fusion), channel_id=1, source_target_pairs={{0,2},{2,4},{4,6},{6,8},{8,10},{10,12},{12,14},{14,16},{16,18},{18... | collective-permute-start | bytes 3145736 | tf_op jit(solution)/shard_map/ppermute | solution.py:21
  19.9 17.6 %collective-permute-done = bf16[128,4096]{1,0:T(8,128)(2,1)} collective-permute-done((bf16[128,4096]{1,0:T(8,128)(2,1)}, bf16[128,4096]{1,0:T(8,128)(2,1)}, u32[]{:S(2)}, u32[]{:S(2)}) %collective-permute-start) | collective-permute-done | bytes 1048608 | tf_op jit(solution)/shard_map/ppermute | solution.py:275
  37.5 4.0 %fusion.2 = bf16[2,128,4096]{2,1,0:T(8,128)(2,1)} fusion(s32[]{:T(128)S(6)} %select_n.49, bf16[1,128,4096]{2,1,0:T(8,128)(2,1)} %bitcast.1, bf16[1,128,4096]{2,1,0:T(8,128)(2,1)S(1)} %bitcast.88), kind=kLoop, calls=%fused_computation.7 | loop fusion | flops 3145728 | bytes 4194308 | tf_op jit(solution)/shard_map/stack | solution.py:280
  41.5 12.1 %convolution_convert_fusion.g_ref = bf16[256,2048]{1,0:T(8,128)(2,1)} fusion(bf16[256,4096]{1,0:T(8,128)(2,1)} %bitcast.85, bf16[2048,4096]{1,0:T(8,128)(2,1)} %param.9), kind=kOutput, calls=%fused_computation.4 | convolution fusion | flops 4295491584 | bytes 19922944 | tf_op jit(solution)/shard_map/dot_general | solution.py:282
  53.7 1.2 copy-done.3
  54.9 9.7 %shard_map.93 = (bf16[256,2048]{1,0:T(8,128)(2,1)}, bf16[256,2048]{1,0:T(8,128)(2,1)}, f32[256,2048]{1,0:T(8,128)}, f32[256,2048]{1,0:T(8,128)}, bf16[2,256,1024]{2,1,0:T(8,128)(2,1)S(1)}) custom-call(s32[1]{0:T(128)} %bitcast.seq_ref, bf16[256,2048]{1,0:T(8,128)(2,1)S(1)} %copy-done.2, bf16[256,2048]{1,0:T(8,128)(2,1)S(1)} %copy-done, ...), custom_call_target="tpu_custom_call" | custom-call | flops 1879048192 | bytes 7340032 | tf_op jit(solution)/shard_map/pallas_call | solution.py:154
  64.6 1.0 copy-done.5
  65.8 1.2 copy-done.4
  67.0 8.9 %shard_map.94 = (bf16[256,2048]{1,0:T(8,128)(2,1)}, bf16[256,2048]{1,0:T(8,128)(2,1)}, f32[256,2048]{1,0:T(8,128)}, f32[256,2048]{1,0:T(8,128)}, bf16[2,1024,512]{2,1,0:T(8,128)(2,1)}) custom-call(s32[1]{0:T(128)} %bitcast.seq_ref, bf16[256,2048]{1,0:T(8,128)(2,1)S(1)} %copy-done.2, ...), custom_call_target="tpu_custom_call", output_to_operand_aliasing={{0}: (7, {}), {1}: (8, {}), {2}: (9, {}), {3}: (10, {})} | custom-call | flops 2348810240 | bytes 6029312 | tf_op jit(solution)/shard_map/pallas_call | solution.py:184
  75.9 2.7 %constant_dynamic-slice_fusion.3 = (bf16[2,2,2,2,1,64,512]{6,5,4,3,2,1,0:T(8,128)(2,1)}, bf16[2,2,2,2,1,64,512]{6,5,4,3,2,1,0:T(8,128)(2,1)S(1)}) fusion(bf16[2,2,2,2,2,64,512]{6,5,4,3,2,1,0:T(8,128)(2,1)} %bitcast.84, s32[]{:T(128)S(6)} %select_n.51, s32[]{:T(128)S(6)} %select_n.52), kind=kLoop, calls=%fused_computation.52 | loop fusion | bytes 4194312 | tf_op jit(solution)/shard_map/jit(dynamic_index_in_dim)/dynamic_slice | solution.py:43
  78.6 1.1 copy.53
  79.9 8.9 %shard_map.95 = (bf16[256,2048]{1,0:T(8,128)(2,1)}, bf16[256,2048]{1,0:T(8,128)(2,1)}, f32[256,2048]{1,0:T(8,128)}, f32[256,2048]{1,0:T(8,128)}, bf16[2,1024,512]{2,1,0:T(8,128)(2,1)}) custom-call(s32[1]{0:T(128)} %bitcast.seq_ref, bf16[256,2048]{1,0:T(8,128)(2,1)S(1)} %copy-done.2, ...), custom_call_target="tpu_custom_call", output_to_operand_aliasing={{0}: (7, {}), {1}: (8, {}), {2}: (9, {}), {3}: (10, {})} | custom-call | flops 2348810240 | bytes 6029312 | tf_op jit(solution)/shard_map/pallas_call | solution.py:184
  88.8 1.8 %constant_dynamic-slice_fusion.1 = (bf16[2,2,2,2,1,64,512]{6,5,4,3,2,1,0:T(8,128)(2,1)S(1)}, bf16[2,2,2,2,1,64,512]{6,5,4,3,2,1,0:T(8,128)(2,1)S(1)}) fusion(bf16[2,2,2,2,2,64,512]{6,5,4,3,2,1,0:T(8,128)(2,1)} %bitcast.83, s32[]{:T(128)S(6)} %select_n.51, s32[]{:T(128)S(6)} %select_n.52), kind=kLoop, calls=%fused_computation.50 | loop fusion | bytes 4194312 | tf_op jit(solution)/shard_map/jit(dynamic_index_in_dim)/dynamic_slice | solution.py:43
  91.8 1.5 convert_add_fusion.1
  93.4 1.5 collective-permute-start.4
  94.9 1.6 %convert_add_fusion = f32[2,2,2,2,64,512]{5,4,0,1,3,2:T(8,128)S(1)} fusion(bf16[2,2,2,2,64,512]{5,4,0,1,3,2:T(8,128)(2,1)} %collective-permute-done.7, bf16[2,2,2,2,1,64,512]{6,5,4,3,2,1,0:T(8,128)(2,1)S(1)} %get-tuple-element.40), kind=kLoop, calls=%fused_computation.8 | loop fusion | flops 1572864 | bytes 4194304 | tf_op jit(solution)/shard_map/add | solution.py:48
  96.6 1.5 collective-permute-start.8
  98.2 0.8 fusion.7.select_ref
  99.0 1.3 collective-permute-start.2
  100.3 7.3 %collective-permute-done.4 = bf16[2,2,2,64,512]{4,3,0,1,2:T(8,128)(2,1)S(1)} collective-permute-done((bf16[2,2,2,64,512]{4,3,0,1,2:T(8,128)(2,1)S(1)}, bf16[2,2,2,64,512]{4,3,0,1,2:T(8,128)(2,1)S(1)}, u32[]{:S(2)}, u32[]{:S(2)}) %collective-permute-start.4) | collective-permute-done | bytes 524320 | tf_op jit(solution)/shard_map/ppermute | solution.py:45
  107.8 11.9 %collective-permute-start.5 = (bf16[2,2,64,512]{3,2,0,1:T(8,128)(2,1)S(1)}, bf16[2,2,64,512]{3,2,0,1:T(8,128)(2,1)S(1)}, u32[]{:S(2)}, u32[]{:S(2)}) collective-permute-start(bf16[2,2,64,512]{3,2,0,1:T(8,128)(2,1)S(1)} %fusion.8), channel_id=1, source_target_pairs={{0,8},{2,10},{4,12},{6,14},{8,0},{10,2},{12,4},{14,6},{16,24},{18,... | collective-permute-start | bytes 786440 | tf_op jit(solution)/shard_map/ppermute | solution.py:45
  120.0 2.5 %collective-permute-start.9 = (bf16[2,2,64,512]{3,2,0,1:T(8,128)(2,1)S(1)}, bf16[2,2,64,512]{3,2,0,1:T(8,128)(2,1)S(1)}, u32[]{:S(2)}, u32[]{:S(2)}) collective-permute-start(bf16[2,2,64,512]{3,2,0,1:T(8,128)(2,1)S(1)} %fusion.9), channel_id=1, source_target_pairs={{0,4},{2,6},{4,0},{6,2},{8,12},{10,14},{12,8},{14,10},{16,20},{18,... | collective-permute-start | bytes 786440 | tf_op jit(solution)/shard_map/ppermute | solution.py:45
  122.5 5.1 %collective-permute-done.5 = bf16[2,2,64,512]{3,2,0,1:T(8,128)(2,1)S(1)} collective-permute-done((bf16[2,2,64,512]{3,2,0,1:T(8,128)(2,1)S(1)}, bf16[2,2,64,512]{3,2,0,1:T(8,128)(2,1)S(1)}, u32[]{:S(2)}, u32[]{:S(2)}) %collective-permute-start.5) | collective-permute-done | bytes 262176 | tf_op jit(solution)/shard_map/ppermute | solution.py:45
  127.7 2.6 %collective-permute-start.6 = (bf16[2,64,512]{2,1,0:T(8,128)(2,1)S(1)}, bf16[2,64,512]{2,1,0:T(8,128)(2,1)S(1)}, u32[]{:S(2)}, u32[]{:S(2)}) collective-permute-start(bf16[2,64,512]{2,1,0:T(8,128)(2,1)S(1)} %fusion.14), channel_id=1, source_target_pairs={{0,16},{2,18},{4,20},{6,22},{8,24},{10,26},{12,28},{14,30},{16,0},... | collective-permute-start | bytes 393224 | tf_op jit(solution)/shard_map/ppermute | solution.py:45
  130.9 7.2 %collective-permute-done.6 = bf16[2,64,512]{2,1,0:T(8,128)(2,1)S(1)} collective-permute-done((bf16[2,64,512]{2,1,0:T(8,128)(2,1)S(1)}, bf16[2,64,512]{2,1,0:T(8,128)(2,1)S(1)}, u32[]{:S(2)}, u32[]{:S(2)}) %collective-permute-start.6) | collective-permute-done | bytes 131104 | tf_op jit(solution)/shard_map/ppermute | solution.py:45
  138.1 2.7 %collective-permute-done.10 = bf16[2,64,512]{2,1,0:T(8,128)(2,1)S(1)} collective-permute-done((bf16[2,64,512]{2,1,0:T(8,128)(2,1)S(1)}, bf16[2,64,512]{2,1,0:T(8,128)(2,1)S(1)}, u32[]{:S(2)}, u32[]{:S(2)}) %collective-permute-start.10) | collective-permute-done | bytes 131104 | tf_op jit(solution)/shard_map/ppermute | solution.py:45
  141.6 1.0 copy-done.9
  142.5 7.0 %shard_map.96 = (bf16[256,2048]{1,0:T(8,128)(2,1)}, bf16[256,2048]{1,0:T(8,128)(2,1)}) custom-call(f32[256,2048]{1,0:T(8,128)} %get-tuple-element.31.own_k_ref, f32[256,2048]{1,0:T(8,128)} %get-tuple-element.32.own_v_ref, bf16[2,256,1024]{2,1,0:T(8,128)(2,1)} %copy-done.9, bf16[2,64,1024]{2,1,0:T(8,128)(2,1)} %pad_maximum_fusion.2.digest_ref, ...), custom_call_target="tpu_custom_call" | custom-call | flops 67108864 | bytes 5242880 | tf_op jit(solution)/shard_map/pallas_call | solution.py:209
  (56 shorter events, 7.0 us)
Async XLA Ops:
  7.2 1.6 %copy-start.1 = (bf16[256,2048]{1,0:T(8,128)(2,1)S(1)}, bf16[256,2048]{1,0:T(8,128)(2,1)}, u32[]{:S(2)}) copy-start(bf16[256,2048]{1,0:T(8,128)(2,1)} %v_ref.5) | copy-start | bytes 3145732
  7.2 58.6 %all-gather.2.cloned.1.call-start = ((), (), s32[]{:S(2)}) async-start(), calls=%async_computation | async-start | bytes 4456448 | tf_op jit(solution)/shard_map/all_gather | solution.py:260
  7.2 2.1 %copy-start.10 = (s32[8,32]{1,0:T(8,128)S(1)}, s32[8,32]{1,0:T(8,128)}, u32[]{:S(2)}) copy-start(s32[8,32]{1,0:T(8,128)} %param.11) | copy-start | bytes 3076
  11.0 26.5 %collective-permute-start = (bf16[128,4096]{1,0:T(8,128)(2,1)}, bf16[128,4096]{1,0:T(8,128)(2,1)}, u32[]{:S(2)}, u32[]{:S(2)}) collective-permute-start(bf16[128,4096]{1,0:T(8,128)(2,1)} %param.10), channel_id=1, source_target_pairs={{0,1},{1,0},{2,3},{3,2},{4,5},{5,4},{6,7},{7,6},{8,9},{9,8},{10,11... | collective-permute-start | bytes 3145736 | tf_op jit(solution)/shard_map/ppermute | solution.py:275
  16.3 21.1 %copy-start.8 = (bf16[128,4096]{1,0:T(8,128)(2,1)S(1)}, bf16[128,4096]{1,0:T(8,128)(2,1)}, u32[]{:S(2)}) copy-start(bf16[128,4096]{1,0:T(8,128)(2,1)} %param.10) | copy-start | bytes 3145732
  17.4 36.3 %collective-permute-start.1 = (bf16[2,256,1024]{2,1,0:T(8,128)(2,1)}, bf16[2,256,1024]{2,1,0:T(8,128)(2,1)}, u32[]{:S(2)}, u32[]{:S(2)}) collective-permute-start(bf16[2,256,1024]{2,1,0:T(8,128)(2,1)} %pad_maximum_fusion), channel_id=1, source_target_pairs={{0,2},{2,4},{4,6},{6,8},{8,10},{10,12},{12,14},{14,16},{16,18},{18... | collective-permute-start | bytes 3145736 | tf_op jit(solution)/shard_map/ppermute | solution.py:21
  41.5 12.1 %copy-start = (bf16[256,2048]{1,0:T(8,128)(2,1)S(1)}, bf16[256,2048]{1,0:T(8,128)(2,1)}, u32[]{:S(2)}) copy-start(bf16[256,2048]{1,0:T(8,128)(2,1)} %k_ref.5) | copy-start | bytes 3145732
  41.5 12.1 %copy-start.2 = (bf16[256,2048]{1,0:T(8,128)(2,1)S(1)}, bf16[256,2048]{1,0:T(8,128)(2,1)}, u32[]{:S(2)}) copy-start(bf16[256,2048]{1,0:T(8,128)(2,1)} %q_ref.5) | copy-start | bytes 3145732
  53.7 1.2 copy-start.3
  64.6 1.0 copy-start.5
  65.8 1.2 copy-start.4
  79.7 11.3 %collective-permute-start.3 = (bf16[2,2,2,2,64,512]{5,4,0,1,2,3:T(8,128)(2,1)}, bf16[2,2,2,2,64,512]{5,4,0,1,2,3:T(8,128)(2,1)}, u32[]{:S(2)}, u32[]{:S(2)}) collective-permute-start(bf16[2,2,2,2,64,512]{5,4,0,1,2,3:T(8,128)(2,1)} %bitcast.78), channel_id=1, source_target_pairs={{0,2},{2,0},{4,6},{6,4},{8,10},{10,8},{12,14},{14,12},{16,18},{18,... | collective-permute-start | bytes 3145736 | tf_op jit(solution)/shard_map/ppermute | solution.py:45
  90.6 1.2 copy-start.7
  90.7 4.2 %collective-permute-start.7 = (bf16[2,2,2,2,64,512]{5,4,0,1,3,2:T(8,128)(2,1)S(1)}, bf16[2,2,2,2,64,512]{5,4,0,1,3,2:T(8,128)(2,1)}, u32[]{:S(2)}, u32[]{:S(2)}) collective-permute-start(bf16[2,2,2,2,64,512]{5,4,0,1,3,2:T(8,128)(2,1)S(1)} %bitcast.89), channel_id=1, source_target_pairs={{0,2},{2,0},{4,6},{6,4},{8,10},{10,8},{12,14},{14,12},{16,18},{18,... | collective-permute-start | bytes 3145736 | tf_op jit(solution)/shard_map/ppermute | solution.py:45
  93.4 14.2 %collective-permute-start.4 = (bf16[2,2,2,64,512]{4,3,0,1,2:T(8,128)(2,1)S(1)}, bf16[2,2,2,64,512]{4,3,0,1,2:T(8,128)(2,1)S(1)}, u32[]{:S(2)}, u32[]{:S(2)}) collective-permute-start(bf16[2,2,2,64,512]{4,3,0,1,2:T(8,128)(2,1)S(1)} %fusion.5), channel_id=1, source_target_pairs={{0,4},{2,6},{4,0},{6,2},{8,12},{10,14},{12,8},{14,10},{16,20},{18,... | collective-permute-start | bytes 1572872 | tf_op jit(solution)/shard_map/ppermute | solution.py:45
  94.9 4.1 %copy-start.6 = (bf16[2,256,1024]{2,1,0:T(8,128)(2,1)S(1)}, bf16[2,256,1024]{2,1,0:T(8,128)(2,1)}, u32[]{:S(2)}) copy-start(bf16[2,256,1024]{2,1,0:T(8,128)(2,1)} %copy-done.5) | copy-start | bytes 3145732
  96.6 23.1 %collective-permute-start.8 = (bf16[2,2,2,64,512]{4,3,0,1,2:T(8,128)(2,1)S(1)}, bf16[2,2,2,64,512]{4,3,0,1,2:T(8,128)(2,1)S(1)}, u32[]{:S(2)}, u32[]{:S(2)}) collective-permute-start(bf16[2,2,2,64,512]{4,3,0,1,2:T(8,128)(2,1)S(1)} %fusion.6), channel_id=1, source_target_pairs={{0,8},{2,10},{4,12},{6,14},{8,0},{10,2},{12,4},{14,6},{16,24},{18,... | collective-permute-start | bytes 1572872 | tf_op jit(solution)/shard_map/ppermute | solution.py:45
  99.0 42.5 %collective-permute-start.2 = (bf16[2,256,1024]{2,1,0:T(8,128)(2,1)S(1)}, bf16[2,256,1024]{2,1,0:T(8,128)(2,1)S(1)}, u32[]{:S(2)}, u32[]{:S(2)}) collective-permute-start(bf16[2,256,1024]{2,1,0:T(8,128)(2,1)S(1)} %copy-done.6), channel_id=1, source_target_pairs={{2,0},{4,2},{6,4},{8,6},{10,8},{12,10},{14,12},{16,14},{18,16},{20... | collective-permute-start | bytes 3145736 | tf_op jit(solution)/shard_map/ppermute | solution.py:21
  107.8 19.8 %collective-permute-start.5 = (bf16[2,2,64,512]{3,2,0,1:T(8,128)(2,1)S(1)}, bf16[2,2,64,512]{3,2,0,1:T(8,128)(2,1)S(1)}, u32[]{:S(2)}, u32[]{:S(2)}) collective-permute-start(bf16[2,2,64,512]{3,2,0,1:T(8,128)(2,1)S(1)} %fusion.8), channel_id=1, source_target_pairs={{0,8},{2,10},{4,12},{6,14},{8,0},{10,2},{12,4},{14,6},{16,24},{18,... | collective-permute-start | bytes 786440 | tf_op jit(solution)/shard_map/ppermute | solution.py:45
  120.0 10.3 %collective-permute-start.9 = (bf16[2,2,64,512]{3,2,0,1:T(8,128)(2,1)S(1)}, bf16[2,2,64,512]{3,2,0,1:T(8,128)(2,1)S(1)}, u32[]{:S(2)}, u32[]{:S(2)}) collective-permute-start(bf16[2,2,64,512]{3,2,0,1:T(8,128)(2,1)S(1)} %fusion.9), channel_id=1, source_target_pairs={{0,4},{2,6},{4,0},{6,2},{8,12},{10,14},{12,8},{14,10},{16,20},{18,... | collective-permute-start | bytes 786440 | tf_op jit(solution)/shard_map/ppermute | solution.py:45
  127.7 10.4 %collective-permute-start.6 = (bf16[2,64,512]{2,1,0:T(8,128)(2,1)S(1)}, bf16[2,64,512]{2,1,0:T(8,128)(2,1)S(1)}, u32[]{:S(2)}, u32[]{:S(2)}) collective-permute-start(bf16[2,64,512]{2,1,0:T(8,128)(2,1)S(1)} %fusion.14), channel_id=1, source_target_pairs={{0,16},{2,18},{4,20},{6,22},{8,24},{10,26},{12,28},{14,30},{16,0},... | collective-permute-start | bytes 393224 | tf_op jit(solution)/shard_map/ppermute | solution.py:45
  130.4 10.4 %collective-permute-start.10 = (bf16[2,64,512]{2,1,0:T(8,128)(2,1)S(1)}, bf16[2,64,512]{2,1,0:T(8,128)(2,1)S(1)}, u32[]{:S(2)}, u32[]{:S(2)}) collective-permute-start(bf16[2,64,512]{2,1,0:T(8,128)(2,1)S(1)} %fusion.15), channel_id=1, source_target_pairs={{0,16},{2,18},{4,20},{6,22},{8,24},{10,26},{12,28},{14,30},{16,0},... | collective-permute-start | bytes 393224 | tf_op jit(solution)/shard_map/ppermute | solution.py:45
  141.6 1.0 copy-start.9
Sparse Core Ops, SparseCore 0:
  11.1 54.6 all-gather.1

commit v15 on v14

--- a/solution.py
+++ b/solution.py
@@ -289,7 +289,7 @@
     attention, query_grad, own_dk, own_dv, back_kv = band_attention(
         seq_scalar, queries, keys, values, grad_out, prev_kv, head_pairs, head_dim, score_scale
     )
-    chunks = 2 if head_pairs % 2 == 0 else 1
+    chunks = 8 if head_pairs % 8 == 0 else (4 if head_pairs % 4 == 0 else (2 if head_pairs % 2 == 0 else 1))
     pairs = head_pairs // chunks
     outputs = (attention, query_grad, own_dk, own_dv)
     digests = []

time: 157 us -> 168 us (1.070)
  starting transfers between devices: 27.9 us -> 42.4 us
  Pallas kernels: 34.5 us -> 42 us
  local copies, waits for them, and re-layouts: 15.7 us -> 8.62 us
  other arithmetic: 11.2 us -> 7.7 us
    ppermute x8 -> x32, starting transfers between devices: 21.1 us -> 35.5 us  [seq_reduce_scatter(): lax.ppermute(send.astype(jnp.bfloat16), 'seq', [(source, source ^ 1 << bi...]
    pallas_call x2 -> x8, Pallas kernels: 17.7 us -> 25.4 us  [fixed_attention(): pl.pallas_call(functools.partial(fixed_kernel, scale=scale, unused=len(ea...]
    dynamic_slice x2 -> x8, local copies, waits for them, and re-layouts: 4.49 us -> 0.3 us  [seq_reduce_scatter(): keep = lax.dynamic_index_in_dim(held, mine, where, keepdims=False)]
    add x6 -> x24, other arithmetic: 3.7 us -> 0.81 us  [seq_reduce_scatter(): held = keep + arrived.astype(jnp.float32)]
    unnamed x24 -> x18, local copies, waits for them, and re-layouts: 7.3 us -> 5.23 us
    ppermute x8 -> x32, waiting for transfers between devices: 22.2 us -> 22 us  [seq_reduce_scatter(): lax.ppermute(send.astype(jnp.bfloat16), 'seq', [(source, source ^ 1 << bi...]
  transfers between devices with their start and end apart: 12 -> 36, of which waited for: 6 -> 10; matrix products, arithmetic and copies ran while one was open for 17% -> 13% of each run, Pallas kernels for 12% -> 21%
where the time goes in v15:
time: 168 us; the launch traced here: 167 us
  starting transfers between devices  42.4 us (25%)
  Pallas kernels  42 us (25%)
  waiting for transfers between devices  38.8 us (23%)
  between operations  14.8 us (9%)
  matrix products  12.8 us (8%)
  local copies, waits for them, and re-layouts  8.62 us (5%)
  other arithmetic  7.7 us (5%)
    ppermute x32, starting transfers between devices, seq_reduce_scatter(): lax.ppermute(send.astype(jnp.bfloat16), 'seq', [(source, source ^ 1 << bi...  35.5 us
    pallas_call x8, Pallas kernels, fixed_attention(): pl.pallas_call(functools.partial(fixed_kernel, scale=scale, unused=len(ea...  25.4 us
    ppermute x32, waiting for transfers between devices, seq_reduce_scatter(): lax.ppermute(send.astype(jnp.bfloat16), 'seq', [(source, source ^ 1 << bi...  22 us
    ppermute x1, waiting for transfers between devices, on_device(): lax.ppermute(cotangent, 'head', [(source, (source + shift) % head_count)...  16.8 us
    dot_general x1, matrix products, on_device(): lax.dot_general(gathered.reshape(seq_rows, cotangent.shape[1]), out_weigh...  12.1 us
    pallas_call x1, Pallas kernels, band_attention(): pl.pallas_call(functools.partial(band_kernel, scale=scale), grid_spec=gri...  9.6 us
    pallas_call x1, Pallas kernels, finalize(): pl.pallas_call(finalize_kernel, grid=(head_pairs,), in_specs=[wide, wide,...  7.02 us
    unnamed x18, local copies, waits for them, and re-layouts  5.23 us
  transfers between devices with their start and end apart: 36, of which 10 were waited for; matrix products, arithmetic and copies ran while one was open for 13% of the time, Pallas kernels for 21%

profile of v15, /device:TPU:0, one launch (start us, length us, event | category | flops | bytes accessed | tf_op | source)
XLA Modules:
  0.0 167.2 jit_solution(6348163499720849405)
XLA Ops:
  7.2 1.6 copy.46
  11.0 3.0 %collective-permute-start = (bf16[128,4096]{1,0:T(8,128)(2,1)}, bf16[128,4096]{1,0:T(8,128)(2,1)}, u32[]{:S(2)}, u32[]{:S(2)}) collective-permute-start(bf16[128,4096]{1,0:T(8,128)(2,1)} %param.10), channel_id=1, source_target_pairs={{0,1},{1,0},{2,3},{3,2},{4,5},{5,4},{6,7},{7,6},{8,9},{9,8},{10,11... | collective-permute-start | bytes 3145736 | tf_op jit(solution)/shard_map/ppermute | solution.py:275
  17.4 2.4 %collective-permute-start.1 = (bf16[2,256,1024]{2,1,0:T(8,128)(2,1)}, bf16[2,256,1024]{2,1,0:T(8,128)(2,1)}, u32[]{:S(2)}, u32[]{:S(2)}) collective-permute-start(bf16[2,256,1024]{2,1,0:T(8,128)(2,1)} %pad_maximum_fusion), channel_id=1, source_target_pairs={{0,2},{2,4},{4,6},{6,8},{8,10},{10,12},{12,14},{14,16},{16,18},{18... | collective-permute-start | bytes 3145736 | tf_op jit(solution)/shard_map/ppermute | solution.py:21
  20.7 16.8 %collective-permute-done = bf16[128,4096]{1,0:T(8,128)(2,1)} collective-permute-done((bf16[128,4096]{1,0:T(8,128)(2,1)}, bf16[128,4096]{1,0:T(8,128)(2,1)}, u32[]{:S(2)}, u32[]{:S(2)}) %collective-permute-start) | collective-permute-done | bytes 1048608 | tf_op jit(solution)/shard_map/ppermute | solution.py:275
  37.5 4.0 %fusion.2 = bf16[2,128,4096]{2,1,0:T(8,128)(2,1)} fusion(s32[]{:T(128)S(6)} %select_n.97, bf16[1,128,4096]{2,1,0:T(8,128)(2,1)} %bitcast.1, bf16[1,128,4096]{2,1,0:T(8,128)(2,1)S(1)} %bitcast.248), kind=kLoop, calls=%fused_computation.7 | loop fusion | flops 3145728 | bytes 4194308 | tf_op jit(solution)/shard_map/stack | solution.py:280
  41.5 12.1 %convolution_convert_fusion.g_ref = bf16[256,2048]{1,0:T(8,128)(2,1)} fusion(bf16[256,4096]{1,0:T(8,128)(2,1)} %bitcast.245, bf16[2048,4096]{1,0:T(8,128)(2,1)} %param.9), kind=kOutput, calls=%fused_computation.4 | convolution fusion | flops 4295491584 | bytes 19922944 | tf_op jit(solution)/shard_map/dot_general | solution.py:282
  54.9 9.6 %shard_map.93 = (bf16[256,2048]{1,0:T(8,128)(2,1)}, bf16[256,2048]{1,0:T(8,128)(2,1)}, f32[256,2048]{1,0:T(8,128)}, f32[256,2048]{1,0:T(8,128)}, bf16[2,256,1024]{2,1,0:T(8,128)(2,1)}) custom-call(s32[1]{0:T(128)} %bitcast.seq_ref, bf16[256,2048]{1,0:T(8,128)(2,1)S(1)} %copy-done.2, bf16[256,2048]{1,0:T(8,128)(2,1)S(1)} %copy-done, ...), custom_call_target="tpu_custom_call" | custom-call | flops 1879048192 | bytes 7340032 | tf_op jit(solution)/shard_map/pallas_call | solution.py:154
  64.5 1.5 collective-permute-start.2
  67.2 3.1 %shard_map.94 = (bf16[256,2048]{1,0:T(8,128)(2,1)}, bf16[256,2048]{1,0:T(8,128)(2,1)}, f32[256,2048]{1,0:T(8,128)}, f32[256,2048]{1,0:T(8,128)}, bf16[2,1024,128]{2,1,0:T(8,128)(2,1)S(1)}) custom-call(s32[1]{0:T(128)} %bitcast.seq_ref, bf16[256,2048]{1,0:T(8,128)(2,1)S(1)} %copy-done.2, ...), custom_call_target="tpu_custom_call", output_to_operand_aliasing={{0}: (7, {}), {1}: (8, {}), {2}: (9, {}), {3}: (10, {})} | custom-call | flops 587202560 | bytes 1507328 | tf_op jit(solution)/shard_map/pallas_call | solution.py:184
  70.4 3.1 %shard_map.95 = (bf16[256,2048]{1,0:T(8,128)(2,1)}, bf16[256,2048]{1,0:T(8,128)(2,1)}, f32[256,2048]{1,0:T(8,128)}, f32[256,2048]{1,0:T(8,128)}, bf16[2,1024,128]{2,1,0:T(8,128)(2,1)S(1)}) custom-call(s32[1]{0:T(128)} %bitcast.seq_ref, bf16[256,2048]{1,0:T(8,128)(2,1)S(1)} %copy-done.2, ...), custom_call_target="tpu_custom_call", output_to_operand_aliasing={{0}: (7, {}), {1}: (8, {}), {2}: (9, {}), {3}: (10, {})} | custom-call | flops 587202560 | bytes 1507328 | tf_op jit(solution)/shard_map/pallas_call | solution.py:184
  73.5 3.1 %shard_map.96 = (bf16[256,2048]{1,0:T(8,128)(2,1)}, bf16[256,2048]{1,0:T(8,128)(2,1)}, f32[256,2048]{1,0:T(8,128)}, f32[256,2048]{1,0:T(8,128)}, bf16[2,1024,128]{2,1,0:T(8,128)(2,1)S(1)}) custom-call(s32[1]{0:T(128)} %bitcast.seq_ref, bf16[256,2048]{1,0:T(8,128)(2,1)S(1)} %copy-done.2, ...), custom_call_target="tpu_custom_call", output_to_operand_aliasing={{0}: (7, {}), {1}: (8, {}), {2}: (9, {}), {3}: (10, {})} | custom-call | flops 587202560 | bytes 1507328 | tf_op jit(solution)/shard_map/pallas_call | solution.py:184
  76.6 3.1 %shard_map.97 = (bf16[256,2048]{1,0:T(8,128)(2,1)}, bf16[256,2048]{1,0:T(8,128)(2,1)}, f32[256,2048]{1,0:T(8,128)}, f32[256,2048]{1,0:T(8,128)}, bf16[2,1024,128]{2,1,0:T(8,128)(2,1)S(1)}) custom-call(s32[1]{0:T(128)} %bitcast.seq_ref, bf16[256,2048]{1,0:T(8,128)(2,1)S(1)} %copy-done.2, ...), custom_call_target="tpu_custom_call", output_to_operand_aliasing={{0}: (7, {}), {1}: (8, {}), {2}: (9, {}), {3}: (10, {})} | custom-call | flops 587202560 | bytes 1507328 | tf_op jit(solution)/shard_map/pallas_call | solution.py:184
  79.8 3.2 %shard_map.98 = (bf16[256,2048]{1,0:T(8,128)(2,1)}, bf16[256,2048]{1,0:T(8,128)(2,1)}, f32[256,2048]{1,0:T(8,128)}, f32[256,2048]{1,0:T(8,128)}, bf16[2,1024,128]{2,1,0:T(8,128)(2,1)S(1)}) custom-call(s32[1]{0:T(128)} %bitcast.seq_ref, bf16[256,2048]{1,0:T(8,128)(2,1)S(1)} %copy-done.2, ...), custom_call_target="tpu_custom_call", output_to_operand_aliasing={{0}: (7, {}), {1}: (8, {}), {2}: (9, {}), {3}: (10, {})} | custom-call | flops 587202560 | bytes 1507328 | tf_op jit(solution)/shard_map/pallas_call | solution.py:184
  82.9 3.1 %shard_map.99 = (bf16[256,2048]{1,0:T(8,128)(2,1)}, bf16[256,2048]{1,0:T(8,128)(2,1)}, f32[256,2048]{1,0:T(8,128)}, f32[256,2048]{1,0:T(8,128)}, bf16[2,1024,128]{2,1,0:T(8,128)(2,1)S(1)}) custom-call(s32[1]{0:T(128)} %bitcast.seq_ref, bf16[256,2048]{1,0:T(8,128)(2,1)S(1)} %copy-done.2, ...), custom_call_target="tpu_custom_call", output_to_operand_aliasing={{0}: (7, {}), {1}: (8, {}), {2}: (9, {}), {3}: (10, {})} | custom-call | flops 587202560 | bytes 1507328 | tf_op jit(solution)/shard_map/pallas_call | solution.py:184
  86.1 3.2 %shard_map.100 = (bf16[256,2048]{1,0:T(8,128)(2,1)}, bf16[256,2048]{1,0:T(8,128)(2,1)}, f32[256,2048]{1,0:T(8,128)}, f32[256,2048]{1,0:T(8,128)}, bf16[2,1024,128]{2,1,0:T(8,128)(2,1)S(1)}) custom-call(s32[1]{0:T(128)} %bitcast.seq_ref, bf16[256,2048]{1,0:T(8,128)(2,1)S(1)} %copy-done.2, ...), custom_call_target="tpu_custom_call", output_to_operand_aliasing={{0}: (7, {}), {1}: (8, {}), {2}: (9, {}), {3}: (10, {})} | custom-call | flops 587202560 | bytes 1507328 | tf_op jit(solution)/shard_map/pallas_call | solution.py:184
  89.2 3.4 %shard_map.101 = (bf16[256,2048]{1,0:T(8,128)(2,1)}, bf16[256,2048]{1,0:T(8,128)(2,1)}, f32[256,2048]{1,0:T(8,128)}, f32[256,2048]{1,0:T(8,128)}, bf16[2,1024,128]{2,1,0:T(8,128)(2,1)S(1)}) custom-call(s32[1]{0:T(128)} %bitcast.seq_ref, bf16[256,2048]{1,0:T(8,128)(2,1)S(1)} %copy-done.2, ...), custom_call_target="tpu_custom_call", output_to_operand_aliasing={{0}: (7, {}), {1}: (8, {}), {2}: (9, {}), {3}: (10, {})} | custom-call | flops 587202560 | bytes 1507328 | tf_op jit(solution)/shard_map/pallas_call | solution.py:184
  96.8 2.3 %collective-permute-start.32 = (bf16[2,2,2,64,128]{4,3,0,1,2:T(8,128)(2,1)S(1)}, bf16[2,2,2,64,128]{4,3,0,1,2:T(8,128)(2,1)S(1)}, u32[]{:S(2)}, u32[]{:S(2)}) collective-permute-start(bf16[2,2,2,64,128]{4,3,0,1,2:T(8,128)(2,1)S(1)} %fusion.15), channel_id=1, source_target_pairs={{0,8},{2,10},{4,12},{6,14},{8,0},{10,2},{12,4},{14,6},{16,24},{18,... | collective-permute-start | bytes 393224 | tf_op jit(solution)/shard_map/ppermute | solution.py:45
  103.0 2.5 %collective-permute-start.16 = (bf16[2,2,2,64,128]{4,3,0,1,2:T(8,128)(2,1)S(1)}, bf16[2,2,2,64,128]{4,3,0,1,2:T(8,128)(2,1)S(1)}, u32[]{:S(2)}, u32[]{:S(2)}) collective-permute-start(bf16[2,2,2,64,128]{4,3,0,1,2:T(8,128)(2,1)S(1)} %fusion.11), channel_id=1, source_target_pairs={{0,8},{2,10},{4,12},{6,14},{8,0},{10,2},{12,4},{14,6},{16,24},{18,... | collective-permute-start | bytes 393224 | tf_op jit(solution)/shard_map/ppermute | solution.py:45
  105.5 1.3 collective-permute-done.24
  107.9 1.5 collective-permute-start.8
  112.8 1.8 %collective-permute-start.29 = (bf16[2,2,64,128]{3,2,0,1:T(8,128)(2,1)S(1)}, bf16[2,2,64,128]{3,2,0,1:T(8,128)(2,1)S(1)}, u32[]{:S(2)}, u32[]{:S(2)}) collective-permute-start(bf16[2,2,64,128]{3,2,0,1:T(8,128)(2,1)S(1)} %fusion.22), channel_id=1, source_target_pairs={{0,8},{2,10},{4,12},{6,14},{8,0},{10,2},{12,4},{14,6},{16,24},{18,... | collective-permute-start | bytes 196616 | tf_op jit(solution)/shard_map/ppermute | solution.py:45
  117.0 1.4 collective-permute-start.17
  119.3 1.6 collective-permute-start.9
  121.6 3.1 %collective-permute-start.34 = (bf16[2,64,128]{2,1,0:T(8,128)(2,1)S(1)}, bf16[2,64,128]{2,1,0:T(8,128)(2,1)S(1)}, u32[]{:S(2)}, u32[]{:S(2)}) collective-permute-start(bf16[2,64,128]{2,1,0:T(8,128)(2,1)S(1)} %fusion.39), channel_id=1, source_target_pairs={{0,16},{2,18},{4,20},{6,22},{8,24},{10,26},{12,28},{14,30},{16,0},... | collective-permute-start | bytes 98312 | tf_op jit(solution)/shard_map/ppermute | solution.py:45
  124.8 1.5 collective-permute-start.30
  126.3 2.0 %collective-permute-start.26 = (bf16[2,64,128]{2,1,0:T(8,128)(2,1)S(1)}, bf16[2,64,128]{2,1,0:T(8,128)(2,1)S(1)}, u32[]{:S(2)}, u32[]{:S(2)}) collective-permute-start(bf16[2,64,128]{2,1,0:T(8,128)(2,1)S(1)} %fusion.37), channel_id=1, source_target_pairs={{0,16},{2,18},{4,20},{6,22},{8,24},{10,26},{12,28},{14,30},{16,0},... | collective-permute-start | bytes 98312 | tf_op jit(solution)/shard_map/ppermute | solution.py:45
  129.4 3.8 %collective-permute-done.6 = bf16[2,64,128]{2,1,0:T(8,128)(2,1)S(1)} collective-permute-done((bf16[2,64,128]{2,1,0:T(8,128)(2,1)S(1)}, bf16[2,64,128]{2,1,0:T(8,128)(2,1)S(1)}, u32[]{:S(2)}, u32[]{:S(2)}) %collective-permute-start.6) | collective-permute-done | bytes 32800 | tf_op jit(solution)/shard_map/ppermute | solution.py:45
  134.2 3.8 %collective-permute-done.10 = bf16[2,64,128]{2,1,0:T(8,128)(2,1)S(1)} collective-permute-done((bf16[2,64,128]{2,1,0:T(8,128)(2,1)S(1)}, bf16[2,64,128]{2,1,0:T(8,128)(2,1)S(1)}, u32[]{:S(2)}, u32[]{:S(2)}) %collective-permute-start.10) | collective-permute-done | bytes 32800 | tf_op jit(solution)/shard_map/ppermute | solution.py:45
  139.1 3.8 %collective-permute-done.14 = bf16[2,64,128]{2,1,0:T(8,128)(2,1)S(1)} collective-permute-done((bf16[2,64,128]{2,1,0:T(8,128)(2,1)S(1)}, bf16[2,64,128]{2,1,0:T(8,128)(2,1)S(1)}, u32[]{:S(2)}, u32[]{:S(2)}) %collective-permute-start.14) | collective-permute-done | bytes 32800 | tf_op jit(solution)/shard_map/ppermute | solution.py:45
  144.2 3.5 %collective-permute-done.18 = bf16[2,64,128]{2,1,0:T(8,128)(2,1)S(1)} collective-permute-done((bf16[2,64,128]{2,1,0:T(8,128)(2,1)S(1)}, bf16[2,64,128]{2,1,0:T(8,128)(2,1)S(1)}, u32[]{:S(2)}, u32[]{:S(2)}) %collective-permute-start.18) | collective-permute-done | bytes 32800 | tf_op jit(solution)/shard_map/ppermute | solution.py:45
  149.0 3.5 %collective-permute-done.22 = bf16[2,64,128]{2,1,0:T(8,128)(2,1)S(1)} collective-permute-done((bf16[2,64,128]{2,1,0:T(8,128)(2,1)S(1)}, bf16[2,64,128]{2,1,0:T(8,128)(2,1)S(1)}, u32[]{:S(2)}, u32[]{:S(2)}) %collective-permute-start.22) | collective-permute-done | bytes 32800 | tf_op jit(solution)/shard_map/ppermute | solution.py:45
  153.4 7.0 %shard_map.102 = (bf16[256,2048]{1,0:T(8,128)(2,1)}, bf16[256,2048]{1,0:T(8,128)(2,1)}) custom-call(f32[256,2048]{1,0:T(8,128)} %get-tuple-element.85.own_k_ref, f32[256,2048]{1,0:T(8,128)} %get-tuple-element.86.own_v_ref, bf16[2,256,1024]{2,1,0:T(8,128)(2,1)} %collective-permute-done.2.back_ref, bf16[2,64,1024]{2,1,0:T(8,128)(2,1)} %copy-done.6, ...), custom_call_target="tpu_custom_call" | custom-call | flops 67108864 | bytes 5242880 | tf_op jit(solution)/shard_map/pallas_call | solution.py:209
  (157 shorter events, 31.6 us)
Async XLA Ops:
  7.2 58.8 %all-gather.2.cloned.1.call-start = ((), (), s32[]{:S(2)}) async-start(), calls=%async_computation | async-start | bytes 4456448 | tf_op jit(solution)/shard_map/all_gather | solution.py:260
  11.0 26.5 %collective-permute-start = (bf16[128,4096]{1,0:T(8,128)(2,1)}, bf16[128,4096]{1,0:T(8,128)(2,1)}, u32[]{:S(2)}, u32[]{:S(2)}) collective-permute-start(bf16[128,4096]{1,0:T(8,128)(2,1)} %param.10), channel_id=1, source_target_pairs={{0,1},{1,0},{2,3},{3,2},{4,5},{5,4},{6,7},{7,6},{8,9},{9,8},{10,11... | collective-permute-start | bytes 3145736 | tf_op jit(solution)/shard_map/ppermute | solution.py:275
  17.4 36.3 %collective-permute-start.1 = (bf16[2,256,1024]{2,1,0:T(8,128)(2,1)}, bf16[2,256,1024]{2,1,0:T(8,128)(2,1)}, u32[]{:S(2)}, u32[]{:S(2)}) collective-permute-start(bf16[2,256,1024]{2,1,0:T(8,128)(2,1)} %pad_maximum_fusion), channel_id=1, source_target_pairs={{0,2},{2,4},{4,6},{6,8},{8,10},{10,12},{12,14},{14,16},{16,18},{18... | collective-permute-start | bytes 3145736 | tf_op jit(solution)/shard_map/ppermute | solution.py:21
  64.5 88.2 %collective-permute-start.2 = (bf16[2,256,1024]{2,1,0:T(8,128)(2,1)}, bf16[2,256,1024]{2,1,0:T(8,128)(2,1)}, u32[]{:S(2)}, u32[]{:S(2)}) collective-permute-start(bf16[2,256,1024]{2,1,0:T(8,128)(2,1)} %get-tuple-element.87), channel_id=1, source_target_pairs={{2,0},{4,2},{6,4},{8,6},{10,8},{12,10},{14,12},{16,14},{18,16},{20... | collective-permute-start | bytes 3145736 | tf_op jit(solution)/shard_map/ppermute | solution.py:21
  92.7 2.4 %collective-permute-start.31 = (bf16[2,2,2,2,64,128]{5,4,0,1,3,2:T(8,128)(2,1)S(1)}, bf16[2,2,2,2,64,128]{5,4,0,1,3,2:T(8,128)(2,1)S(1)}, u32[]{:S(2)}, u32[]{:S(2)}) collective-permute-start(bf16[2,2,2,2,64,128]{5,4,0,1,3,2:T(8,128)(2,1)S(1)} %bitcast.254), channel_id=1, source_target_pairs={{0,2},{2,0},{4,6},{6,4},{8,10},{10,8},{12,14},{14,12},{16,18},{18,... | collective-permute-start | bytes 786440 | tf_op jit(solution)/shard_map/ppermute | solution.py:45
  95.7 3.4 %collective-permute-start.11 = (bf16[2,2,2,2,64,128]{5,4,0,1,2,3:T(8,128)(2,1)S(1)}, bf16[2,2,2,2,64,128]{5,4,0,1,2,3:T(8,128)(2,1)S(1)}, u32[]{:S(2)}, u32[]{:S(2)}) collective-permute-start(bf16[2,2,2,2,64,128]{5,4,0,1,2,3:T(8,128)(2,1)S(1)} %bitcast.255), channel_id=1, source_target_pairs={{0,2},{2,0},{4,6},{6,4},{8,10},{10,8},{12,14},{14,12},{16,18},{18,... | collective-permute-start | bytes 786440 | tf_op jit(solution)/shard_map/ppermute | solution.py:45
  95.9 4.6 %collective-permute-start.7 = (bf16[2,2,2,2,64,128]{5,4,0,1,3,2:T(8,128)(2,1)S(1)}, bf16[2,2,2,2,64,128]{5,4,0,1,3,2:T(8,128)(2,1)S(1)}, u32[]{:S(2)}, u32[]{:S(2)}) collective-permute-start(bf16[2,2,2,2,64,128]{5,4,0,1,3,2:T(8,128)(2,1)S(1)} %bitcast.250), channel_id=1, source_target_pairs={{0,2},{2,0},{4,6},{6,4},{8,10},{10,8},{12,14},{14,12},{16,18},{18,... | collective-permute-start | bytes 786440 | tf_op jit(solution)/shard_map/ppermute | solution.py:45
  96.5 4.7 %collective-permute-start.3 = (bf16[2,2,2,2,64,128]{5,4,0,1,2,3:T(8,128)(2,1)S(1)}, bf16[2,2,2,2,64,128]{5,4,0,1,2,3:T(8,128)(2,1)S(1)}, u32[]{:S(2)}, u32[]{:S(2)}) collective-permute-start(bf16[2,2,2,2,64,128]{5,4,0,1,2,3:T(8,128)(2,1)S(1)} %bitcast.249), channel_id=1, source_target_pairs={{0,2},{2,0},{4,6},{6,4},{8,10},{10,8},{12,14},{14,12},{16,18},{18,... | collective-permute-start | bytes 786440 | tf_op jit(solution)/shard_map/ppermute | solution.py:45
  96.8 6.2 %collective-permute-start.32 = (bf16[2,2,2,64,128]{4,3,0,1,2:T(8,128)(2,1)S(1)}, bf16[2,2,2,64,128]{4,3,0,1,2:T(8,128)(2,1)S(1)}, u32[]{:S(2)}, u32[]{:S(2)}) collective-permute-start(bf16[2,2,2,64,128]{4,3,0,1,2:T(8,128)(2,1)S(1)} %fusion.15), channel_id=1, source_target_pairs={{0,8},{2,10},{4,12},{6,14},{8,0},{10,2},{12,4},{14,6},{16,24},{18,... | collective-permute-start | bytes 393224 | tf_op jit(solution)/shard_map/ppermute | solution.py:45
  99.2 8.7 %collective-permute-start.28 = (bf16[2,2,2,64,128]{4,3,0,1,2:T(8,128)(2,1)S(1)}, bf16[2,2,2,64,128]{4,3,0,1,2:T(8,128)(2,1)S(1)}, u32[]{:S(2)}, u32[]{:S(2)}) collective-permute-start(bf16[2,2,2,64,128]{4,3,0,1,2:T(8,128)(2,1)S(1)} %fusion.14), channel_id=1, source_target_pairs={{0,4},{2,6},{4,0},{6,2},{8,12},{10,14},{12,8},{14,10},{16,20},{18,... | collective-permute-start | bytes 393224 | tf_op jit(solution)/shard_map/ppermute | solution.py:45
  100.5 6.3 %collective-permute-start.24 = (bf16[2,2,2,64,128]{4,3,0,1,2:T(8,128)(2,1)S(1)}, bf16[2,2,2,64,128]{4,3,0,1,2:T(8,128)(2,1)S(1)}, u32[]{:S(2)}, u32[]{:S(2)}) collective-permute-start(bf16[2,2,2,64,128]{4,3,0,1,2:T(8,128)(2,1)S(1)} %fusion.13), channel_id=1, source_target_pairs={{0,8},{2,10},{4,12},{6,14},{8,0},{10,2},{12,4},{14,6},{16,24},{18,... | collective-permute-start | bytes 393224 | tf_op jit(solution)/shard_map/ppermute | solution.py:45
  101.2 8.2 %collective-permute-start.20 = (bf16[2,2,2,64,128]{4,3,0,1,2:T(8,128)(2,1)S(1)}, bf16[2,2,2,64,128]{4,3,0,1,2:T(8,128)(2,1)S(1)}, u32[]{:S(2)}, u32[]{:S(2)}) collective-permute-start(bf16[2,2,2,64,128]{4,3,0,1,2:T(8,128)(2,1)S(1)} %fusion.12), channel_id=1, source_target_pairs={{0,4},{2,6},{4,0},{6,2},{8,12},{10,14},{12,8},{14,10},{16,20},{18,... | collective-permute-start | bytes 393224 | tf_op jit(solution)/shard_map/ppermute | solution.py:45
  103.0 7.6 %collective-permute-start.16 = (bf16[2,2,2,64,128]{4,3,0,1,2:T(8,128)(2,1)S(1)}, bf16[2,2,2,64,128]{4,3,0,1,2:T(8,128)(2,1)S(1)}, u32[]{:S(2)}, u32[]{:S(2)}) collective-permute-start(bf16[2,2,2,64,128]{4,3,0,1,2:T(8,128)(2,1)S(1)} %fusion.11), channel_id=1, source_target_pairs={{0,8},{2,10},{4,12},{6,14},{8,0},{10,2},{12,4},{14,6},{16,24},{18,... | collective-permute-start | bytes 393224 | tf_op jit(solution)/shard_map/ppermute | solution.py:45
  106.8 6.0 %collective-permute-start.12 = (bf16[2,2,2,64,128]{4,3,0,1,2:T(8,128)(2,1)S(1)}, bf16[2,2,2,64,128]{4,3,0,1,2:T(8,128)(2,1)S(1)}, u32[]{:S(2)}, u32[]{:S(2)}) collective-permute-start(bf16[2,2,2,64,128]{4,3,0,1,2:T(8,128)(2,1)S(1)} %fusion.10), channel_id=1, source_target_pairs={{0,4},{2,6},{4,0},{6,2},{8,12},{10,14},{12,8},{14,10},{16,20},{18,... | collective-permute-start | bytes 393224 | tf_op jit(solution)/shard_map/ppermute | solution.py:45
  107.9 6.8 %collective-permute-start.8 = (bf16[2,2,2,64,128]{4,3,0,1,2:T(8,128)(2,1)S(1)}, bf16[2,2,2,64,128]{4,3,0,1,2:T(8,128)(2,1)S(1)}, u32[]{:S(2)}, u32[]{:S(2)}) collective-permute-start(bf16[2,2,2,64,128]{4,3,0,1,2:T(8,128)(2,1)S(1)} %fusion.9), channel_id=1, source_target_pairs={{0,8},{2,10},{4,12},{6,14},{8,0},{10,2},{12,4},{14,6},{16,24},{18,... | collective-permute-start | bytes 393224 | tf_op jit(solution)/shard_map/ppermute | solution.py:45
  109.5 6.5 %collective-permute-start.4 = (bf16[2,2,2,64,128]{4,3,0,1,2:T(8,128)(2,1)S(1)}, bf16[2,2,2,64,128]{4,3,0,1,2:T(8,128)(2,1)S(1)}, u32[]{:S(2)}, u32[]{:S(2)}) collective-permute-start(bf16[2,2,2,64,128]{4,3,0,1,2:T(8,128)(2,1)S(1)} %fusion.8), channel_id=1, source_target_pairs={{0,4},{2,6},{4,0},{6,2},{8,12},{10,14},{12,8},{14,10},{16,20},{18,... | collective-permute-start | bytes 393224 | tf_op jit(solution)/shard_map/ppermute | solution.py:45
  110.6 6.4 %collective-permute-start.33 = (bf16[2,2,64,128]{3,2,0,1:T(8,128)(2,1)S(1)}, bf16[2,2,64,128]{3,2,0,1:T(8,128)(2,1)S(1)}, u32[]{:S(2)}, u32[]{:S(2)}) collective-permute-start(bf16[2,2,64,128]{3,2,0,1:T(8,128)(2,1)S(1)} %fusion.23), channel_id=1, source_target_pairs={{0,4},{2,6},{4,0},{6,2},{8,12},{10,14},{12,8},{14,10},{16,20},{18,... | collective-permute-start | bytes 196616 | tf_op jit(solution)/shard_map/ppermute | solution.py:45
  112.8 5.6 %collective-permute-start.29 = (bf16[2,2,64,128]{3,2,0,1:T(8,128)(2,1)S(1)}, bf16[2,2,64,128]{3,2,0,1:T(8,128)(2,1)S(1)}, u32[]{:S(2)}, u32[]{:S(2)}) collective-permute-start(bf16[2,2,64,128]{3,2,0,1:T(8,128)(2,1)S(1)} %fusion.22), channel_id=1, source_target_pairs={{0,8},{2,10},{4,12},{6,14},{8,0},{10,2},{12,4},{14,6},{16,24},{18,... | collective-permute-start | bytes 196616 | tf_op jit(solution)/shard_map/ppermute | solution.py:45
  114.7 4.6 %collective-permute-start.25 = (bf16[2,2,64,128]{3,2,0,1:T(8,128)(2,1)S(1)}, bf16[2,2,64,128]{3,2,0,1:T(8,128)(2,1)S(1)}, u32[]{:S(2)}, u32[]{:S(2)}) collective-permute-start(bf16[2,2,64,128]{3,2,0,1:T(8,128)(2,1)S(1)} %fusion.21), channel_id=1, source_target_pairs={{0,4},{2,6},{4,0},{6,2},{8,12},{10,14},{12,8},{14,10},{16,20},{18,... | collective-permute-start | bytes 196616 | tf_op jit(solution)/shard_map/ppermute | solution.py:45
  116.0 5.0 %collective-permute-start.21 = (bf16[2,2,64,128]{3,2,0,1:T(8,128)(2,1)S(1)}, bf16[2,2,64,128]{3,2,0,1:T(8,128)(2,1)S(1)}, u32[]{:S(2)}, u32[]{:S(2)}) collective-permute-start(bf16[2,2,64,128]{3,2,0,1:T(8,128)(2,1)S(1)} %fusion.20), channel_id=1, source_target_pairs={{0,8},{2,10},{4,12},{6,14},{8,0},{10,2},{12,4},{14,6},{16,24},{18,... | collective-permute-start | bytes 196616 | tf_op jit(solution)/shard_map/ppermute | solution.py:45
  117.0 4.6 %collective-permute-start.17 = (bf16[2,2,64,128]{3,2,0,1:T(8,128)(2,1)S(1)}, bf16[2,2,64,128]{3,2,0,1:T(8,128)(2,1)S(1)}, u32[]{:S(2)}, u32[]{:S(2)}) collective-permute-start(bf16[2,2,64,128]{3,2,0,1:T(8,128)(2,1)S(1)} %fusion.19), channel_id=1, source_target_pairs={{0,4},{2,6},{4,0},{6,2},{8,12},{10,14},{12,8},{14,10},{16,20},{18,... | collective-permute-start | bytes 196616 | tf_op jit(solution)/shard_map/ppermute | solution.py:45
  118.4 6.3 %collective-permute-start.13 = (bf16[2,2,64,128]{3,2,0,1:T(8,128)(2,1)S(1)}, bf16[2,2,64,128]{3,2,0,1:T(8,128)(2,1)S(1)}, u32[]{:S(2)}, u32[]{:S(2)}) collective-permute-start(bf16[2,2,64,128]{3,2,0,1:T(8,128)(2,1)S(1)} %fusion.18), channel_id=1, source_target_pairs={{0,8},{2,10},{4,12},{6,14},{8,0},{10,2},{12,4},{14,6},{16,24},{18,... | collective-permute-start | bytes 196616 | tf_op jit(solution)/shard_map/ppermute | solution.py:45
  119.3 9.1 %collective-permute-start.9 = (bf16[2,2,64,128]{3,2,0,1:T(8,128)(2,1)S(1)}, bf16[2,2,64,128]{3,2,0,1:T(8,128)(2,1)S(1)}, u32[]{:S(2)}, u32[]{:S(2)}) collective-permute-start(bf16[2,2,64,128]{3,2,0,1:T(8,128)(2,1)S(1)} %fusion.17), channel_id=1, source_target_pairs={{0,4},{2,6},{4,0},{6,2},{8,12},{10,14},{12,8},{14,10},{16,20},{18,... | collective-permute-start | bytes 196616 | tf_op jit(solution)/shard_map/ppermute | solution.py:45
  121.0 5.3 %collective-permute-start.5 = (bf16[2,2,64,128]{3,2,0,1:T(8,128)(2,1)S(1)}, bf16[2,2,64,128]{3,2,0,1:T(8,128)(2,1)S(1)}, u32[]{:S(2)}, u32[]{:S(2)}) collective-permute-start(bf16[2,2,64,128]{3,2,0,1:T(8,128)(2,1)S(1)} %fusion.16), channel_id=1, source_target_pairs={{0,8},{2,10},{4,12},{6,14},{8,0},{10,2},{12,4},{14,6},{16,24},{18,... | collective-permute-start | bytes 196616 | tf_op jit(solution)/shard_map/ppermute | solution.py:45
  121.6 31.0 %collective-permute-start.34 = (bf16[2,64,128]{2,1,0:T(8,128)(2,1)S(1)}, bf16[2,64,128]{2,1,0:T(8,128)(2,1)S(1)}, u32[]{:S(2)}, u32[]{:S(2)}) collective-permute-start(bf16[2,64,128]{2,1,0:T(8,128)(2,1)S(1)} %fusion.39), channel_id=1, source_target_pairs={{0,16},{2,18},{4,20},{6,22},{8,24},{10,26},{12,28},{14,30},{16,0},... | collective-permute-start | bytes 98312 | tf_op jit(solution)/shard_map/ppermute | solution.py:45
  124.8 27.8 %collective-permute-start.30 = (bf16[2,64,128]{2,1,0:T(8,128)(2,1)S(1)}, bf16[2,64,128]{2,1,0:T(8,128)(2,1)S(1)}, u32[]{:S(2)}, u32[]{:S(2)}) collective-permute-start(bf16[2,64,128]{2,1,0:T(8,128)(2,1)S(1)} %fusion.38), channel_id=1, source_target_pairs={{0,16},{2,18},{4,20},{6,22},{8,24},{10,26},{12,28},{14,30},{16,0},... | collective-permute-start | bytes 98312 | tf_op jit(solution)/shard_map/ppermute | solution.py:45
  126.3 26.2 %collective-permute-start.26 = (bf16[2,64,128]{2,1,0:T(8,128)(2,1)S(1)}, bf16[2,64,128]{2,1,0:T(8,128)(2,1)S(1)}, u32[]{:S(2)}, u32[]{:S(2)}) collective-permute-start(bf16[2,64,128]{2,1,0:T(8,128)(2,1)S(1)} %fusion.37), channel_id=1, source_target_pairs={{0,16},{2,18},{4,20},{6,22},{8,24},{10,26},{12,28},{14,30},{16,0},... | collective-permute-start | bytes 98312 | tf_op jit(solution)/shard_map/ppermute | solution.py:45
  128.4 4.9 %collective-permute-start.6 = (bf16[2,64,128]{2,1,0:T(8,128)(2,1)S(1)}, bf16[2,64,128]{2,1,0:T(8,128)(2,1)S(1)}, u32[]{:S(2)}, u32[]{:S(2)}) collective-permute-start(bf16[2,64,128]{2,1,0:T(8,128)(2,1)S(1)} %fusion.32), channel_id=1, source_target_pairs={{0,16},{2,18},{4,20},{6,22},{8,24},{10,26},{12,28},{14,30},{16,0},... | collective-permute-start | bytes 98312 | tf_op jit(solution)/shard_map/ppermute | solution.py:45
  133.2 4.8 %collective-permute-start.10 = (bf16[2,64,128]{2,1,0:T(8,128)(2,1)S(1)}, bf16[2,64,128]{2,1,0:T(8,128)(2,1)S(1)}, u32[]{:S(2)}, u32[]{:S(2)}) collective-permute-start(bf16[2,64,128]{2,1,0:T(8,128)(2,1)S(1)} %fusion.33), channel_id=1, source_target_pairs={{0,16},{2,18},{4,20},{6,22},{8,24},{10,26},{12,28},{14,30},{16,0},... | collective-permute-start | bytes 98312 | tf_op jit(solution)/shard_map/ppermute | solution.py:45
  138.1 4.8 %collective-permute-start.14 = (bf16[2,64,128]{2,1,0:T(8,128)(2,1)S(1)}, bf16[2,64,128]{2,1,0:T(8,128)(2,1)S(1)}, u32[]{:S(2)}, u32[]{:S(2)}) collective-permute-start(bf16[2,64,128]{2,1,0:T(8,128)(2,1)S(1)} %fusion.34), channel_id=1, source_target_pairs={{0,16},{2,18},{4,20},{6,22},{8,24},{10,26},{12,28},{14,30},{16,0},... | collective-permute-start | bytes 98312 | tf_op jit(solution)/shard_map/ppermute | solution.py:45
  142.9 4.8 %collective-permute-start.18 = (bf16[2,64,128]{2,1,0:T(8,128)(2,1)S(1)}, bf16[2,64,128]{2,1,0:T(8,128)(2,1)S(1)}, u32[]{:S(2)}, u32[]{:S(2)}) collective-permute-start(bf16[2,64,128]{2,1,0:T(8,128)(2,1)S(1)} %fusion.35), channel_id=1, source_target_pairs={{0,16},{2,18},{4,20},{6,22},{8,24},{10,26},{12,28},{14,30},{16,0},... | collective-permute-start | bytes 98312 | tf_op jit(solution)/shard_map/ppermute | solution.py:45
  147.7 4.8 %collective-permute-start.22 = (bf16[2,64,128]{2,1,0:T(8,128)(2,1)S(1)}, bf16[2,64,128]{2,1,0:T(8,128)(2,1)S(1)}, u32[]{:S(2)}, u32[]{:S(2)}) collective-permute-start(bf16[2,64,128]{2,1,0:T(8,128)(2,1)S(1)} %fusion.36), channel_id=1, source_target_pairs={{0,16},{2,18},{4,20},{6,22},{8,24},{10,26},{12,28},{14,30},{16,0},... | collective-permute-start | bytes 98312 | tf_op jit(solution)/shard_map/ppermute | solution.py:45
  (12 other events, 59.5 us)
Sparse Core Ops, SparseCore 0:
  11.1 54.6 all-gather.1

commit v16 on v13

--- a/solution.py
+++ b/solution.py
@@ -250,24 +250,12 @@
     select = (
         digest_rows.T[:, :, None] == jnp.arange(seq_rows, dtype=jnp.int32)[None, None, :]
     ).astype(jnp.bfloat16)
-    digest_k = jnp.einsum(
-        "hjr,rhc->jhc", select, fixed_k, preferred_element_type=jnp.float32
+    fixed_kv = jnp.stack([fixed_k, fixed_v], 1)
+    digest_kv = jnp.einsum(
+        "hjr,rthc->jthc", select, fixed_kv, preferred_element_type=jnp.float32
     ).astype(jnp.bfloat16)
-    digest_v = jnp.einsum(
-        "hjr,rhc->jhc", select, fixed_v, preferred_element_type=jnp.float32
-    ).astype(jnp.bfloat16)
-    pair_width = head_pairs * head_dim
     far_kv = lax.all_gather(
-        jnp.concatenate(
-            [
-                digest_k.reshape(digest_count, pair_width),
-                digest_v.reshape(digest_count, pair_width),
-            ],
-            1,
-        ),
-        "seq",
-        axis=0,
-        tiled=True,
+        digest_kv.reshape(digest_count, 2 * head_pairs * head_dim), "seq", axis=0, tiled=True
     )
     head_count = lax.axis_size("head")
     head_index = lax.axis_index("head")

time: 140 us -> 147 us (1.050)
  local copies, waits for them, and re-layouts: 7.86 us -> 13.3 us
  starting transfers between devices: 26.4 us -> 28.1 us
    unnamed x16 -> x23, local copies, waits for them, and re-layouts: 4.54 us -> 9.89 us
    ppermute x1, waiting for transfers between devices: 16.8 us -> 19.5 us  [on_device(): lax.ppermute(cotangent, 'head', [(source, (source + shift) % head_count)...]
    ppermute x16, waiting for transfers between devices: 15.9 us -> 13.9 us  [seq_reduce_scatter(): lax.ppermute(send.astype(jnp.bfloat16), 'seq', [(source, source ^ 1 << bi...]
    ppermute x16, starting transfers between devices: 19.5 us -> 21.1 us  [seq_reduce_scatter(): lax.ppermute(send.astype(jnp.bfloat16), 'seq', [(source, source ^ 1 << bi...]
  transfers between devices with their start and end apart: 20 -> 20, of which waited for: 8 -> 8; matrix products, arithmetic and copies ran while one was open for 17% -> 15% of each run, Pallas kernels for 21% -> 13%
where the time goes in v16:
time: 147 us; the launch traced here: 146 us
  Pallas kernels  36.6 us (25%)
  waiting for transfers between devices  33.4 us (23%)
  starting transfers between devices  28.1 us (19%)
  between operations  14.4 us (10%)
  local copies, waits for them, and re-layouts  13.3 us (9%)
  matrix products  12.4 us (8%)
  other arithmetic  8.28 us (6%)
    ppermute x16, starting transfers between devices, seq_reduce_scatter(): lax.ppermute(send.astype(jnp.bfloat16), 'seq', [(source, source ^ 1 << bi...  21.1 us
    pallas_call x4, Pallas kernels, fixed_attention(): pl.pallas_call(functools.partial(fixed_kernel, scale=scale, unused=len(ea...  19.8 us
    ppermute x1, waiting for transfers between devices, on_device(): lax.ppermute(cotangent, 'head', [(source, (source + shift) % head_count)...  19.5 us
    ppermute x16, waiting for transfers between devices, seq_reduce_scatter(): lax.ppermute(send.astype(jnp.bfloat16), 'seq', [(source, source ^ 1 << bi...  13.9 us
    dot_general x1, matrix products, on_device(): lax.dot_general(gathered.reshape(seq_rows, cotangent.shape[1]), out_weigh...  12.1 us
    unnamed x23, local copies, waits for them, and re-layouts  9.89 us
    pallas_call x1, Pallas kernels, band_attention(): pl.pallas_call(functools.partial(band_kernel, scale=scale), grid_spec=gri...  9.74 us
    pallas_call x1, Pallas kernels, finalize(): pl.pallas_call(finalize_kernel, grid=(head_pairs,), in_specs=[wide, wide,...  7.02 us
  transfers between devices with their start and end apart: 20, of which 8 were waited for; matrix products, arithmetic and copies ran while one was open for 15% of the time, Pallas kernels for 13%

profile of v16, /device:TPU:0, one launch (start us, length us, event | category | flops | bytes accessed | tf_op | source)
XLA Modules:
  0.0 146.4 jit_solution(7257639668464530137)
XLA Ops:
  7.2 1.6 %copy.29 = bf16[256,2048]{0,1:T(8,128)(2,1)S(1)} copy(bf16[256,2048]{1,0:T(8,128)(2,1)} %k_ref.9) | data formatting | bytes 2097152 | tf_op args[1]
  11.1 1.3 copy.47
  12.4 1.3 copy.48
  15.1 3.0 %collective-permute-start = (bf16[128,4096]{1,0:T(8,128)(2,1)}, bf16[128,4096]{1,0:T(8,128)(2,1)}, u32[]{:S(2)}, u32[]{:S(2)}) collective-permute-start(bf16[128,4096]{1,0:T(8,128)(2,1)} %param.10), channel_id=1, source_target_pairs={{0,1},{1,0},{2,3},{3,2},{4,5},{5,4},{6,7},{7,6},{8,9},{9,8},{10,11... | collective-permute-start | bytes 3145736 | tf_op jit(solution)/shard_map/ppermute | solution.py:263
  18.6 1.1 pad_maximum_fusion
  19.6 2.4 %collective-permute-start.1 = (bf16[2,256,1024]{2,1,0:T(8,128)(2,1)}, bf16[2,256,1024]{2,1,0:T(8,128)(2,1)}, u32[]{:S(2)}, u32[]{:S(2)}) collective-permute-start(bf16[2,256,1024]{2,1,0:T(8,128)(2,1)} %pad_maximum_fusion), channel_id=1, source_target_pairs={{0,2},{2,4},{4,6},{6,8},{8,10},{10,12},{12,14},{14,16},{16,18},{18... | collective-permute-start | bytes 3145736 | tf_op jit(solution)/shard_map/ppermute | solution.py:21
  22.1 19.5 %collective-permute-done = bf16[128,4096]{1,0:T(8,128)(2,1)} collective-permute-done((bf16[128,4096]{1,0:T(8,128)(2,1)}, bf16[128,4096]{1,0:T(8,128)(2,1)}, u32[]{:S(2)}, u32[]{:S(2)}) %collective-permute-start) | collective-permute-done | bytes 1048608 | tf_op jit(solution)/shard_map/ppermute | solution.py:263
  41.6 4.7 %fusion.2 = bf16[2,128,4096]{2,1,0:T(8,128)(2,1)} fusion(s32[]{:T(128)S(6)} %select_n.65, bf16[1,128,4096]{2,1,0:T(8,128)(2,1)} %bitcast.1, bf16[1,128,4096]{2,1,0:T(8,128)(2,1)} %bitcast.2), kind=kLoop, calls=%fused_computation.7 | loop fusion | flops 3145728 | bytes 4194308 | tf_op jit(solution)/shard_map/stack | solution.py:268
  46.3 12.1 %convolution_convert_fusion.g_ref = bf16[256,2048]{1,0:T(8,128)(2,1)} fusion(bf16[256,4096]{1,0:T(8,128)(2,1)} %bitcast.127, bf16[2048,4096]{1,0:T(8,128)(2,1)} %param.9), kind=kOutput, calls=%fused_computation.4 | convolution fusion | flops 4295491584 | bytes 19922944 | tf_op jit(solution)/shard_map/dot_general | solution.py:270
  58.4 1.2 copy-done.3
  59.6 9.7 %shard_map.93 = (bf16[256,2048]{1,0:T(8,128)(2,1)}, bf16[256,2048]{1,0:T(8,128)(2,1)}, f32[256,2048]{1,0:T(8,128)}, f32[256,2048]{1,0:T(8,128)}, bf16[2,256,1024]{2,1,0:T(8,128)(2,1)S(1)}) custom-call(s32[1]{0:T(128)} %bitcast.seq_ref, bf16[256,2048]{1,0:T(8,128)(2,1)S(1)} %copy-done.2, bf16[256,2048]{1,0:T(8,128)(2,1)S(1)} %copy-done, ...), custom_call_target="tpu_custom_call" | custom-call | flops 1879048192 | bytes 7340032 | tf_op jit(solution)/shard_map/pallas_call | solution.py:154
  70.4 1.2 copy-done.4
  71.6 4.9 %shard_map.94 = (bf16[256,2048]{1,0:T(8,128)(2,1)}, bf16[256,2048]{1,0:T(8,128)(2,1)}, f32[256,2048]{1,0:T(8,128)}, f32[256,2048]{1,0:T(8,128)}, bf16[2,1024,256]{2,1,0:T(8,128)(2,1)S(1)}) custom-call(s32[1]{0:T(128)} %bitcast.seq_ref, bf16[256,2048]{1,0:T(8,128)(2,1)S(1)} %copy-done.2, ...), custom_call_target="tpu_custom_call", output_to_operand_aliasing={{0}: (7, {}), {1}: (8, {}), {2}: (9, {}), {3}: (10, {})} | custom-call | flops 1174405120 | bytes 3014656 | tf_op jit(solution)/shard_map/pallas_call | solution.py:184
  76.5 5.0 %shard_map.95 = (bf16[256,2048]{1,0:T(8,128)(2,1)}, bf16[256,2048]{1,0:T(8,128)(2,1)}, f32[256,2048]{1,0:T(8,128)}, f32[256,2048]{1,0:T(8,128)}, bf16[2,1024,256]{2,1,0:T(8,128)(2,1)S(1)}) custom-call(s32[1]{0:T(128)} %bitcast.seq_ref, bf16[256,2048]{1,0:T(8,128)(2,1)S(1)} %copy-done.2, ...), custom_call_target="tpu_custom_call", output_to_operand_aliasing={{0}: (7, {}), {1}: (8, {}), {2}: (9, {}), {3}: (10, {})} | custom-call | flops 1174405120 | bytes 3014656 | tf_op jit(solution)/shard_map/pallas_call | solution.py:184
  82.7 1.5 %collective-permute-start.2 = (bf16[2,256,1024]{2,1,0:T(8,128)(2,1)S(1)}, bf16[2,256,1024]{2,1,0:T(8,128)(2,1)S(1)}, u32[]{:S(2)}, u32[]{:S(2)}) collective-permute-start(bf16[2,256,1024]{2,1,0:T(8,128)(2,1)S(1)} %copy-done.6), channel_id=1, source_target_pairs={{2,0},{4,2},{6,4},{8,6},{10,8},{12,10},{14,12},{16,14},{18,16},{20... | collective-permute-start | bytes 3145736 | tf_op jit(solution)/shard_map/ppermute | solution.py:21
  84.3 1.2 collective-permute-start.7
  85.5 4.9 %shard_map.96 = (bf16[256,2048]{1,0:T(8,128)(2,1)}, bf16[256,2048]{1,0:T(8,128)(2,1)}, f32[256,2048]{1,0:T(8,128)}, f32[256,2048]{1,0:T(8,128)}, bf16[2,1024,256]{2,1,0:T(8,128)(2,1)S(1)}) custom-call(s32[1]{0:T(128)} %bitcast.seq_ref, bf16[256,2048]{1,0:T(8,128)(2,1)S(1)} %copy-done.2, ...), custom_call_target="tpu_custom_call", output_to_operand_aliasing={{0}: (7, {}), {1}: (8, {}), {2}: (9, {}), {3}: (10, {})} | custom-call | flops 1174405120 | bytes 3014656 | tf_op jit(solution)/shard_map/pallas_call | solution.py:184
  90.4 5.0 %shard_map.97 = (bf16[256,2048]{1,0:T(8,128)(2,1)}, bf16[256,2048]{1,0:T(8,128)(2,1)}, f32[256,2048]{1,0:T(8,128)}, f32[256,2048]{1,0:T(8,128)}, bf16[2,1024,256]{2,1,0:T(8,128)(2,1)S(1)}) custom-call(s32[1]{0:T(128)} %bitcast.seq_ref, bf16[256,2048]{1,0:T(8,128)(2,1)S(1)} %copy-done.2, ...), custom_call_target="tpu_custom_call", output_to_operand_aliasing={{0}: (7, {}), {1}: (8, {}), {2}: (9, {}), {3}: (10, {})} | custom-call | flops 1174405120 | bytes 3014656 | tf_op jit(solution)/shard_map/pallas_call | solution.py:184
  96.6 1.9 %collective-permute-start.4 = (bf16[2,2,2,64,256]{4,3,0,1,2:T(8,128)(2,1)S(1)}, bf16[2,2,2,64,256]{4,3,0,1,2:T(8,128)(2,1)S(1)}, u32[]{:S(2)}, u32[]{:S(2)}) collective-permute-start(bf16[2,2,2,64,256]{4,3,0,1,2:T(8,128)(2,1)S(1)} %fusion.10), channel_id=1, source_target_pairs={{0,4},{2,6},{4,0},{6,2},{8,12},{10,14},{12,8},{14,10},{16,20},{18,... | collective-permute-start | bytes 786440 | tf_op jit(solution)/shard_map/ppermute | solution.py:45
  98.6 1.8 %collective-permute-start.8 = (bf16[2,2,2,64,256]{4,3,0,1,2:T(8,128)(2,1)S(1)}, bf16[2,2,2,64,256]{4,3,0,1,2:T(8,128)(2,1)S(1)}, u32[]{:S(2)}, u32[]{:S(2)}) collective-permute-start(bf16[2,2,2,64,256]{4,3,0,1,2:T(8,128)(2,1)S(1)} %fusion.11), channel_id=1, source_target_pairs={{0,8},{2,10},{4,12},{6,14},{8,0},{10,2},{12,4},{14,6},{16,24},{18,... | collective-permute-start | bytes 786440 | tf_op jit(solution)/shard_map/ppermute | solution.py:45
  100.6 1.5 %collective-permute-start.12 = (bf16[2,2,2,64,256]{4,3,0,1,2:T(8,128)(2,1)S(1)}, bf16[2,2,2,64,256]{4,3,0,1,2:T(8,128)(2,1)S(1)}, u32[]{:S(2)}, u32[]{:S(2)}) collective-permute-start(bf16[2,2,2,64,256]{4,3,0,1,2:T(8,128)(2,1)S(1)} %fusion.12), channel_id=1, source_target_pairs={{0,4},{2,6},{4,0},{6,2},{8,12},{10,14},{12,8},{14,10},{16,20},{18,... | collective-permute-start | bytes 786440 | tf_op jit(solution)/shard_map/ppermute | solution.py:45
  102.4 3.4 %collective-permute-done.4 = bf16[2,2,2,64,256]{4,3,0,1,2:T(8,128)(2,1)S(1)} collective-permute-done((bf16[2,2,2,64,256]{4,3,0,1,2:T(8,128)(2,1)S(1)}, bf16[2,2,2,64,256]{4,3,0,1,2:T(8,128)(2,1)S(1)}, u32[]{:S(2)}, u32[]{:S(2)}) %collective-permute-start.4) | collective-permute-done | bytes 262176 | tf_op jit(solution)/shard_map/ppermute | solution.py:45
  105.9 3.0 %collective-permute-start.5 = (bf16[2,2,64,256]{3,2,0,1:T(8,128)(2,1)S(1)}, bf16[2,2,64,256]{3,2,0,1:T(8,128)(2,1)S(1)}, u32[]{:S(2)}, u32[]{:S(2)}) collective-permute-start(bf16[2,2,64,256]{3,2,0,1:T(8,128)(2,1)S(1)} %fusion.15), channel_id=1, source_target_pairs={{0,8},{2,10},{4,12},{6,14},{8,0},{10,2},{12,4},{14,6},{16,24},{18,... | collective-permute-start | bytes 393224 | tf_op jit(solution)/shard_map/ppermute | solution.py:45
  109.7 1.4 collective-permute-done.12
  111.2 3.3 %collective-permute-start.13 = (bf16[2,2,64,256]{3,2,0,1:T(8,128)(2,1)S(1)}, bf16[2,2,64,256]{3,2,0,1:T(8,128)(2,1)S(1)}, u32[]{:S(2)}, u32[]{:S(2)}) collective-permute-start(bf16[2,2,64,256]{3,2,0,1:T(8,128)(2,1)S(1)} %fusion.17), channel_id=1, source_target_pairs={{0,8},{2,10},{4,12},{6,14},{8,0},{10,2},{12,4},{14,6},{16,24},{18,... | collective-permute-start | bytes 393224 | tf_op jit(solution)/shard_map/ppermute | solution.py:45
  116.4 2.8 %collective-permute-start.6 = (bf16[2,64,256]{2,1,0:T(8,128)(2,1)S(1)}, bf16[2,64,256]{2,1,0:T(8,128)(2,1)S(1)}, u32[]{:S(2)}, u32[]{:S(2)}) collective-permute-start(bf16[2,64,256]{2,1,0:T(8,128)(2,1)S(1)} %fusion.23), channel_id=1, source_target_pairs={{0,16},{2,18},{4,20},{6,22},{8,24},{10,26},{12,28},{14,30},{16,0},... | collective-permute-start | bytes 196616 | tf_op jit(solution)/shard_map/ppermute | solution.py:45
  119.5 2.8 %collective-permute-start.14 = (bf16[2,64,256]{2,1,0:T(8,128)(2,1)S(1)}, bf16[2,64,256]{2,1,0:T(8,128)(2,1)S(1)}, u32[]{:S(2)}, u32[]{:S(2)}) collective-permute-start(bf16[2,64,256]{2,1,0:T(8,128)(2,1)S(1)} %fusion.25), channel_id=1, source_target_pairs={{0,16},{2,18},{4,20},{6,22},{8,24},{10,26},{12,28},{14,30},{16,0},... | collective-permute-start | bytes 196616 | tf_op jit(solution)/shard_map/ppermute | solution.py:45
  122.6 1.8 %collective-permute-done.6 = bf16[2,64,256]{2,1,0:T(8,128)(2,1)S(1)} collective-permute-done((bf16[2,64,256]{2,1,0:T(8,128)(2,1)S(1)}, bf16[2,64,256]{2,1,0:T(8,128)(2,1)S(1)}, u32[]{:S(2)}, u32[]{:S(2)}) %collective-permute-start.6) | collective-permute-done | bytes 65568 | tf_op jit(solution)/shard_map/ppermute | solution.py:45
  124.4 3.5 %collective-permute-done.10 = bf16[2,64,256]{2,1,0:T(8,128)(2,1)S(1)} collective-permute-done((bf16[2,64,256]{2,1,0:T(8,128)(2,1)S(1)}, bf16[2,64,256]{2,1,0:T(8,128)(2,1)S(1)}, u32[]{:S(2)}, u32[]{:S(2)}) %collective-permute-start.10) | collective-permute-done | bytes 65568 | tf_op jit(solution)/shard_map/ppermute | solution.py:45
  128.0 2.1 %collective-permute-done.14 = bf16[2,64,256]{2,1,0:T(8,128)(2,1)S(1)} collective-permute-done((bf16[2,64,256]{2,1,0:T(8,128)(2,1)S(1)}, bf16[2,64,256]{2,1,0:T(8,128)(2,1)S(1)}, u32[]{:S(2)}, u32[]{:S(2)}) %collective-permute-start.14) | collective-permute-done | bytes 65568 | tf_op jit(solution)/shard_map/ppermute | solution.py:45
  131.6 1.0 copy-done.7
  132.6 7.0 %shard_map.98 = (bf16[256,2048]{1,0:T(8,128)(2,1)}, bf16[256,2048]{1,0:T(8,128)(2,1)}) custom-call(f32[256,2048]{1,0:T(8,128)} %get-tuple-element.49.own_k_ref, f32[256,2048]{1,0:T(8,128)} %get-tuple-element.50.own_v_ref, bf16[2,256,1024]{2,1,0:T(8,128)(2,1)} %copy-done.7, bf16[2,64,1024]{2,1,0:T(8,128)(2,1)} %pad_maximum_fusion.1.digest_ref, ...), custom_call_target="tpu_custom_call" | custom-call | flops 67108864 | bytes 5242880 | tf_op jit(solution)/shard_map/pallas_call | solution.py:209
  (87 shorter events, 13.3 us)
Async XLA Ops:
  7.2 63.2 %all-gather.2.cloned.1.call-start = ((), (), s32[]{:S(2)}) async-start(), calls=%async_computation | async-start | bytes 4456448 | tf_op jit(solution)/shard_map/all_gather | solution.py:257
  7.2 2.5 %copy-start.1 = (bf16[256,2048]{1,0:T(8,128)(2,1)S(1)}, bf16[256,2048]{1,0:T(8,128)(2,1)}, u32[]{:S(2)}) copy-start(bf16[256,2048]{1,0:T(8,128)(2,1)} %v_ref.9) | copy-start | bytes 3145732
  10.2 3.5 %copy-start.8 = (s32[8,32]{1,0:T(8,128)S(1)}, s32[8,32]{1,0:T(8,128)}, u32[]{:S(2)}) copy-start(s32[8,32]{1,0:T(8,128)} %param.11) | copy-start | bytes 3076
  15.1 26.5 %collective-permute-start = (bf16[128,4096]{1,0:T(8,128)(2,1)}, bf16[128,4096]{1,0:T(8,128)(2,1)}, u32[]{:S(2)}, u32[]{:S(2)}) collective-permute-start(bf16[128,4096]{1,0:T(8,128)(2,1)} %param.10), channel_id=1, source_target_pairs={{0,1},{1,0},{2,3},{3,2},{4,5},{5,4},{6,7},{7,6},{8,9},{9,8},{10,11... | collective-permute-start | bytes 3145736 | tf_op jit(solution)/shard_map/ppermute | solution.py:263
  19.6 38.8 %collective-permute-start.1 = (bf16[2,256,1024]{2,1,0:T(8,128)(2,1)}, bf16[2,256,1024]{2,1,0:T(8,128)(2,1)}, u32[]{:S(2)}, u32[]{:S(2)}) collective-permute-start(bf16[2,256,1024]{2,1,0:T(8,128)(2,1)} %pad_maximum_fusion), channel_id=1, source_target_pairs={{0,2},{2,4},{4,6},{6,8},{8,10},{10,12},{12,14},{14,16},{16,18},{18... | collective-permute-start | bytes 3145736 | tf_op jit(solution)/shard_map/ppermute | solution.py:21
  46.3 12.1 %copy-start = (bf16[256,2048]{1,0:T(8,128)(2,1)S(1)}, bf16[256,2048]{1,0:T(8,128)(2,1)}, u32[]{:S(2)}) copy-start(bf16[256,2048]{1,0:T(8,128)(2,1)} %k_ref.9) | copy-start | bytes 3145732
  46.3 12.1 %copy-start.2 = (bf16[256,2048]{1,0:T(8,128)(2,1)S(1)}, bf16[256,2048]{1,0:T(8,128)(2,1)}, u32[]{:S(2)}) copy-start(bf16[256,2048]{1,0:T(8,128)(2,1)} %q_ref.9) | copy-start | bytes 3145732
  58.4 1.2 copy-start.3
  69.4 1.0 copy-start.5
  70.4 1.2 copy-start.4
  81.5 1.3 copy-start.6
  81.8 14.6 %collective-permute-start.3 = (bf16[2,2,2,2,64,256]{5,4,0,1,2,3:T(8,128)(2,1)S(1)}, bf16[2,2,2,2,64,256]{5,4,0,1,2,3:T(8,128)(2,1)S(1)}, u32[]{:S(2)}, u32[]{:S(2)}) collective-permute-start(bf16[2,2,2,2,64,256]{5,4,0,1,2,3:T(8,128)(2,1)S(1)} %bitcast.132), channel_id=1, source_target_pairs={{0,2},{2,0},{4,6},{6,4},{8,10},{10,8},{12,14},{14,12},{16,18},{18,... | collective-permute-start | bytes 1572872 | tf_op jit(solution)/shard_map/ppermute | solution.py:45
  82.7 48.9 %collective-permute-start.2 = (bf16[2,256,1024]{2,1,0:T(8,128)(2,1)S(1)}, bf16[2,256,1024]{2,1,0:T(8,128)(2,1)S(1)}, u32[]{:S(2)}, u32[]{:S(2)}) collective-permute-start(bf16[2,256,1024]{2,1,0:T(8,128)(2,1)S(1)} %copy-done.6), channel_id=1, source_target_pairs={{2,0},{4,2},{6,4},{8,6},{10,8},{12,10},{14,12},{16,14},{18,16},{20... | collective-permute-start | bytes 3145736 | tf_op jit(solution)/shard_map/ppermute | solution.py:21
  84.3 14.2 %collective-permute-start.7 = (bf16[2,2,2,2,64,256]{5,4,0,1,3,2:T(8,128)(2,1)S(1)}, bf16[2,2,2,2,64,256]{5,4,0,1,3,2:T(8,128)(2,1)S(1)}, u32[]{:S(2)}, u32[]{:S(2)}) collective-permute-start(bf16[2,2,2,2,64,256]{5,4,0,1,3,2:T(8,128)(2,1)S(1)} %bitcast.133), channel_id=1, source_target_pairs={{0,2},{2,0},{4,6},{6,4},{8,10},{10,8},{12,14},{14,12},{16,18},{18,... | collective-permute-start | bytes 1572872 | tf_op jit(solution)/shard_map/ppermute | solution.py:45
  95.7 4.7 %collective-permute-start.11 = (bf16[2,2,2,2,64,256]{5,4,0,1,2,3:T(8,128)(2,1)S(1)}, bf16[2,2,2,2,64,256]{5,4,0,1,2,3:T(8,128)(2,1)S(1)}, u32[]{:S(2)}, u32[]{:S(2)}) collective-permute-start(bf16[2,2,2,2,64,256]{5,4,0,1,2,3:T(8,128)(2,1)S(1)} %bitcast.135), channel_id=1, source_target_pairs={{0,2},{2,0},{4,6},{6,4},{8,10},{10,8},{12,14},{14,12},{16,18},{18,... | collective-permute-start | bytes 1572872 | tf_op jit(solution)/shard_map/ppermute | solution.py:45
  95.9 6.3 %collective-permute-start.15 = (bf16[2,2,2,2,64,256]{5,4,0,1,3,2:T(8,128)(2,1)S(1)}, bf16[2,2,2,2,64,256]{5,4,0,1,3,2:T(8,128)(2,1)S(1)}, u32[]{:S(2)}, u32[]{:S(2)}) collective-permute-start(bf16[2,2,2,2,64,256]{5,4,0,1,3,2:T(8,128)(2,1)S(1)} %bitcast.134), channel_id=1, source_target_pairs={{0,2},{2,0},{4,6},{6,4},{8,10},{10,8},{12,14},{14,12},{16,18},{18,... | collective-permute-start | bytes 1572872 | tf_op jit(solution)/shard_map/ppermute | solution.py:45
  96.6 9.2 %collective-permute-start.4 = (bf16[2,2,2,64,256]{4,3,0,1,2:T(8,128)(2,1)S(1)}, bf16[2,2,2,64,256]{4,3,0,1,2:T(8,128)(2,1)S(1)}, u32[]{:S(2)}, u32[]{:S(2)}) collective-permute-start(bf16[2,2,2,64,256]{4,3,0,1,2:T(8,128)(2,1)S(1)} %fusion.10), channel_id=1, source_target_pairs={{0,4},{2,6},{4,0},{6,2},{8,12},{10,14},{12,8},{14,10},{16,20},{18,... | collective-permute-start | bytes 786440 | tf_op jit(solution)/shard_map/ppermute | solution.py:45
  98.6 10.2 %collective-permute-start.8 = (bf16[2,2,2,64,256]{4,3,0,1,2:T(8,128)(2,1)S(1)}, bf16[2,2,2,64,256]{4,3,0,1,2:T(8,128)(2,1)S(1)}, u32[]{:S(2)}, u32[]{:S(2)}) collective-permute-start(bf16[2,2,2,64,256]{4,3,0,1,2:T(8,128)(2,1)S(1)} %fusion.11), channel_id=1, source_target_pairs={{0,8},{2,10},{4,12},{6,14},{8,0},{10,2},{12,4},{14,6},{16,24},{18,... | collective-permute-start | bytes 786440 | tf_op jit(solution)/shard_map/ppermute | solution.py:45
  100.6 10.5 %collective-permute-start.12 = (bf16[2,2,2,64,256]{4,3,0,1,2:T(8,128)(2,1)S(1)}, bf16[2,2,2,64,256]{4,3,0,1,2:T(8,128)(2,1)S(1)}, u32[]{:S(2)}, u32[]{:S(2)}) collective-permute-start(bf16[2,2,2,64,256]{4,3,0,1,2:T(8,128)(2,1)S(1)} %fusion.12), channel_id=1, source_target_pairs={{0,4},{2,6},{4,0},{6,2},{8,12},{10,14},{12,8},{14,10},{16,20},{18,... | collective-permute-start | bytes 786440 | tf_op jit(solution)/shard_map/ppermute | solution.py:45
  102.3 12.2 %collective-permute-start.16 = (bf16[2,2,2,64,256]{4,3,0,1,2:T(8,128)(2,1)S(1)}, bf16[2,2,2,64,256]{4,3,0,1,2:T(8,128)(2,1)S(1)}, u32[]{:S(2)}, u32[]{:S(2)}) collective-permute-start(bf16[2,2,2,64,256]{4,3,0,1,2:T(8,128)(2,1)S(1)} %fusion.13), channel_id=1, source_target_pairs={{0,8},{2,10},{4,12},{6,14},{8,0},{10,2},{12,4},{14,6},{16,24},{18,... | collective-permute-start | bytes 786440 | tf_op jit(solution)/shard_map/ppermute | solution.py:45
  105.9 10.4 %collective-permute-start.5 = (bf16[2,2,64,256]{3,2,0,1:T(8,128)(2,1)S(1)}, bf16[2,2,64,256]{3,2,0,1:T(8,128)(2,1)S(1)}, u32[]{:S(2)}, u32[]{:S(2)}) collective-permute-start(bf16[2,2,64,256]{3,2,0,1:T(8,128)(2,1)S(1)} %fusion.15), channel_id=1, source_target_pairs={{0,8},{2,10},{4,12},{6,14},{8,0},{10,2},{12,4},{14,6},{16,24},{18,... | collective-permute-start | bytes 393224 | tf_op jit(solution)/shard_map/ppermute | solution.py:45
  108.9 10.2 %collective-permute-start.9 = (bf16[2,2,64,256]{3,2,0,1:T(8,128)(2,1)S(1)}, bf16[2,2,64,256]{3,2,0,1:T(8,128)(2,1)S(1)}, u32[]{:S(2)}, u32[]{:S(2)}) collective-permute-start(bf16[2,2,64,256]{3,2,0,1:T(8,128)(2,1)S(1)} %fusion.16), channel_id=1, source_target_pairs={{0,4},{2,6},{4,0},{6,2},{8,12},{10,14},{12,8},{14,10},{16,20},{18,... | collective-permute-start | bytes 393224 | tf_op jit(solution)/shard_map/ppermute | solution.py:45
  111.2 8.3 %collective-permute-start.13 = (bf16[2,2,64,256]{3,2,0,1:T(8,128)(2,1)S(1)}, bf16[2,2,64,256]{3,2,0,1:T(8,128)(2,1)S(1)}, u32[]{:S(2)}, u32[]{:S(2)}) collective-permute-start(bf16[2,2,64,256]{3,2,0,1:T(8,128)(2,1)S(1)} %fusion.17), channel_id=1, source_target_pairs={{0,8},{2,10},{4,12},{6,14},{8,0},{10,2},{12,4},{14,6},{16,24},{18,... | collective-permute-start | bytes 393224 | tf_op jit(solution)/shard_map/ppermute | solution.py:45
  114.6 7.7 %collective-permute-start.17 = (bf16[2,2,64,256]{3,2,0,1:T(8,128)(2,1)S(1)}, bf16[2,2,64,256]{3,2,0,1:T(8,128)(2,1)S(1)}, u32[]{:S(2)}, u32[]{:S(2)}) collective-permute-start(bf16[2,2,64,256]{3,2,0,1:T(8,128)(2,1)S(1)} %fusion.18), channel_id=1, source_target_pairs={{0,4},{2,6},{4,0},{6,2},{8,12},{10,14},{12,8},{14,10},{16,20},{18,... | collective-permute-start | bytes 393224 | tf_op jit(solution)/shard_map/ppermute | solution.py:45
  116.4 8.1 %collective-permute-start.6 = (bf16[2,64,256]{2,1,0:T(8,128)(2,1)S(1)}, bf16[2,64,256]{2,1,0:T(8,128)(2,1)S(1)}, u32[]{:S(2)}, u32[]{:S(2)}) collective-permute-start(bf16[2,64,256]{2,1,0:T(8,128)(2,1)S(1)} %fusion.23), channel_id=1, source_target_pairs={{0,16},{2,18},{4,20},{6,22},{8,24},{10,26},{12,28},{14,30},{16,0},... | collective-permute-start | bytes 196616 | tf_op jit(solution)/shard_map/ppermute | solution.py:45
  119.2 8.8 %collective-permute-start.10 = (bf16[2,64,256]{2,1,0:T(8,128)(2,1)S(1)}, bf16[2,64,256]{2,1,0:T(8,128)(2,1)S(1)}, u32[]{:S(2)}, u32[]{:S(2)}) collective-permute-start(bf16[2,64,256]{2,1,0:T(8,128)(2,1)S(1)} %fusion.24), channel_id=1, source_target_pairs={{0,16},{2,18},{4,20},{6,22},{8,24},{10,26},{12,28},{14,30},{16,0},... | collective-permute-start | bytes 196616 | tf_op jit(solution)/shard_map/ppermute | solution.py:45
  119.5 10.5 %collective-permute-start.14 = (bf16[2,64,256]{2,1,0:T(8,128)(2,1)S(1)}, bf16[2,64,256]{2,1,0:T(8,128)(2,1)S(1)}, u32[]{:S(2)}, u32[]{:S(2)}) collective-permute-start(bf16[2,64,256]{2,1,0:T(8,128)(2,1)S(1)} %fusion.25), channel_id=1, source_target_pairs={{0,16},{2,18},{4,20},{6,22},{8,24},{10,26},{12,28},{14,30},{16,0},... | collective-permute-start | bytes 196616 | tf_op jit(solution)/shard_map/ppermute | solution.py:45
  122.4 8.5 %collective-permute-start.18 = (bf16[2,64,256]{2,1,0:T(8,128)(2,1)S(1)}, bf16[2,64,256]{2,1,0:T(8,128)(2,1)S(1)}, u32[]{:S(2)}, u32[]{:S(2)}) collective-permute-start(bf16[2,64,256]{2,1,0:T(8,128)(2,1)S(1)} %fusion.26), channel_id=1, source_target_pairs={{0,16},{2,18},{4,20},{6,22},{8,24},{10,26},{12,28},{14,30},{16,0},... | collective-permute-start | bytes 196616 | tf_op jit(solution)/shard_map/ppermute | solution.py:45
  131.6 1.0 copy-start.7
Sparse Core Ops, SparseCore 0:
  15.2 54.7 all-gather.1
